TPU v7x, 32 devices: a whole 2x2x4 slice. The times are simulated.
32 devices in a mesh: space: 8 (over z, y), match: 4 (over x, core).
Axes of the slice: x: 2, y: 2, z: 4, core: 2. Of those that a mesh axis runs over, the one named last changes fastest.
Arguments:
- source: bfloat16 [32, 256, 128], P('space', 'match'), may hold values from -200 to 200
- targets: bfloat16 [8192, 128], P('match'), may hold values from -200 to 200
- conv_in: bfloat16 [3, 3, 128, 128], replicated, may hold values from -0.1875 to 0.1875
- flow_proj: float32 [2, 128], replicated, may hold values from -4 to 4
- in_bias: float32 [128], replicated, may hold values from -3 to 3
- conv_out: bfloat16 [2, 3, 3, 128], replicated, may hold values from -0.1875 to 0.1875
Outputs:
- refined: float32 [2, 32, 256], P(None, 'space', 'match')
All inputs are finite; a program needn't handle non-finite values.
Results may differ from a plain program's by a relative error of at most 0.0066.
Values may be sent and summed in bfloat16 or wider, within the bound.
No kernel may reach another device: no remote copies, remote signals or barrier semaphores. Data moves between devices by JAX's collectives and lax.ppermute only.
A program may use at most 64 MiB of HBM per device.

v0:
```python
import math

import jax
import jax.numpy as jnp
from jax import lax
from jax.sharding import PartitionSpec as P


def extended(block, sides, width):
    for axis, dim in sides:
        count = lax.axis_size(axis)
        forward = [(i, i + 1) for i in range(count - 1)]
        backward = [(target, source) for source, target in forward]
        low = lax.ppermute(
            lax.slice_in_dim(block, block.shape[dim] - width, None, axis=dim), axis, forward
        )
        high = lax.ppermute(lax.slice_in_dim(block, 0, width, axis=dim), axis, backward)
        block = jnp.concatenate([low, block, high], axis=dim)
    return block


def block_terms(query, keys, start, width):
    scale = 1.0 / math.sqrt(query.shape[1])
    scores = (
        lax.dot_general(query, keys, (((1,), (1,)), ((), ())), preferred_element_type=jnp.float32)
        * scale
    )
    peak = jnp.max(scores, axis=1)
    weight = jnp.exp(scores - peak[:, None])
    probs = weight.astype(jnp.bfloat16)
    total = jnp.sum(weight, axis=1)
    accum = jnp.dot(probs, keys, preferred_element_type=jnp.float32)
    index = start + jnp.arange(keys.shape[0], dtype=jnp.int32)
    col_pos = (index % width).astype(jnp.float32) / width
    row_pos = (index // width).astype(jnp.float32) / width
    sum_x = jnp.sum(weight * col_pos[None, :], axis=1)
    sum_y = jnp.sum(weight * row_pos[None, :], axis=1)
    return (peak, total, accum, sum_x, sum_y)


def band_terms(queries, keys, start, width):
    count = queries.shape[0]
    step_rows = math.gcd(count, 512)
    blocks = queries.reshape(count // step_rows, step_rows, queries.shape[1])
    peak, total, accum, sum_x, sum_y = lax.map(
        lambda blk: block_terms(blk, keys, start, width), blocks
    )
    return (
        peak.reshape(count),
        total.reshape(count),
        accum.reshape(count, -1),
        sum_x.reshape(count),
        sum_y.reshape(count),
    )


def conv_first(padded, conv_in, rows, cols):
    result = jnp.zeros((rows, cols, conv_in.shape[3]), jnp.float32)
    for tap_a in range(3):
        for tap_b in range(3):
            result = result + jnp.einsum(
                "hwc,cd->hwd",
                padded[tap_a : tap_a + rows, tap_b : tap_b + cols],
                conv_in[tap_a, tap_b].astype(jnp.float32),
                precision=lax.Precision.HIGHEST,
                preferred_element_type=jnp.float32,
            )
    return result


def conv_second(padded, conv_out, rows, cols):
    result = jnp.zeros((2, rows, cols), jnp.float32)
    for tap_a in range(3):
        for tap_b in range(3):
            result = result + jnp.einsum(
                "hwc,oc->ohw",
                padded[tap_a : tap_a + rows, tap_b : tap_b + cols],
                conv_out[:, tap_a, tap_b, :],
                preferred_element_type=jnp.float32,
            )
    return result


def local(source, targets, conv_in, flow_proj, in_bias, conv_out):
    rows, cols, chans = source.shape
    width = cols * lax.axis_size("match")
    row_first = lax.axis_index("space") * rows
    col_first = lax.axis_index("match") * cols
    target_first = lax.axis_index("match") * targets.shape[0]
    band = lax.all_gather(source, "match", axis=1, tiled=True)
    peak, total, accum, sum_x, sum_y = band_terms(
        band.reshape(rows * width, chans), targets, target_first, width
    )
    peak = peak.reshape(rows, width)
    overall = lax.pmax(peak, "match")
    factor = jnp.exp(peak - overall)
    accum, total, sum_x, sum_y = (
        lax.psum_scatter(
            accum.reshape(rows, width, chans) * factor[..., None],
            "match",
            scatter_dimension=1,
            tiled=True,
        ),
        lax.psum_scatter(
            total.reshape(rows, width) * factor, "match", scatter_dimension=1, tiled=True
        ),
        lax.psum_scatter(
            sum_x.reshape(rows, width) * factor, "match", scatter_dimension=1, tiled=True
        ),
        lax.psum_scatter(
            sum_y.reshape(rows, width) * factor, "match", scatter_dimension=1, tiled=True
        ),
    )
    warped = accum / total[..., None]
    col_pos = (col_first + jnp.arange(cols, dtype=jnp.int32)).astype(jnp.float32) / width
    row_pos = (row_first + jnp.arange(rows, dtype=jnp.int32)).astype(jnp.float32) / width
    flow_x = sum_x / total - col_pos[None, :]
    flow_y = sum_y / total - row_pos[:, None]
    padded = extended(warped, (("space", 0), ("match", 1)), 1)
    pre = conv_first(padded, conv_in, rows, cols)
    pre = pre + flow_x[:, :, None] * flow_proj[0] + flow_y[:, :, None] * flow_proj[1] + in_bias
    hidden = jax.nn.silu(pre).astype(jnp.bfloat16)
    hpad = extended(hidden, (("space", 0), ("match", 1)), 1)
    delta = conv_second(hpad, conv_out, rows, cols)
    return jnp.stack([flow_x, flow_y]) + delta


def solution(mesh):
    in_specs = (P("space", "match", None), P("match", None), P(), P(), P(), P())
    out_specs = P(None, "space", "match")
    return jax.shard_map(local, mesh=mesh, in_specs=in_specs, out_specs=out_specs, check_vma=False)
```

profile of v0, /device:TPU:0, one launch (start us, length us, event | category | flops | bytes accessed | tf_op | source)
XLA Modules:
  0.0 169.4 jit_solution(7408028364116758490)
XLA Ops:
  6.5 7.4 %all_gather.3 = bf16[4,256,128]{2,1,0:T(8,128)(2,1)S(1)} all-gather(bf16[4,64,128]{2,1,0:T(8,128)(2,1)} %param.8), channel_id=1, replica_groups=mesh['space'=8,'match'=4] {'match'}, dimensions={1}, use_global_device_ids=true | all-gather | bytes 327680 | tf_op jit(solution)/shard_map/all_gather | solution.py:90
  13.9 17.2 %while.20 = (s32[]{:T(128)}, f32[2,512]{1,0:T(2,128)S(1)}, f32[2,512]{1,0:T(2,128)S(1)}, f32[2,512,128]{2,1,0:T(8,128)S(1)}, f32[2,512]{1,0:T(2,128)S(1)}, /*ind...) while((s32[]{:T(128)}, f32[2,512]{1,0:T(2,128)S(1)}, ...), condition=%wide.region_5.6_spmd, body=%wide.region_0.5_spmd.sunk | while | flops 549500928 | bytes 32960704 | solution.py:45
  13.9 1.9 %multiply_reduce_fusion.5 = (f32[512]{0:T(512)S(1)}, f32[512,2048]{1,0:T(8,128)S(1)}) fusion(bf16[2048,128]{1,0:T(8,128)(2,1)} %get-tuple-element.273, bf16[2,512,128]{2,1,0:T(8,128)(2,1)S(1)} %get-tuple-element.272, s32[]{:T(128)} %get-tuple-element.255), kind=kOutput, calls=%fused_computation.3.clone.1 | convolution fusion | flops 270532096 | bytes 4851716 | tf_op jit(solution)/shard_map/while/body/eval_jaxpr/dot_general | solution.py:25
  15.9 1.9 %copy-done = f32[512,2048]{1,0:T(8,128)} copy-done((f32[512,2048]{1,0:T(8,128)}, f32[512,2048]{1,0:T(8,128)S(1)}, u32[]{:S(2)}) %copy-start) | copy-done | bytes 4194328 | tf_op jit(solution)/shard_map/while
  17.8 1.5 multiply_reduce_fusion.6
  19.4 3.0 %fusion.136 = f32[2,512,128]{2,1,0:T(8,128)S(1)} fusion(f32[2,512,128]{2,1,0:T(8,128)S(1)} %get-tuple-element.258, s32[]{:T(128)} %get-tuple-element.255, bf16[2048,128]{1,0:T(8,128)(2,1)S(1)} %copy-done.1, f32[512,2048]{1,0:T(8,128)} %copy-done, f32[512]{0:T(512)S(1)} %get-tuple-element.237), kind=kOutput, calls=%fused_computation.7.clone.1 | convolution fusion | flops 271581184 | bytes 4982788 | tf_op jit(solution)/shard_map/while/body/eval_jaxpr/dot_general | solution.py:32
  22.5 1.9 %multiply_reduce_fusion.5 = (f32[512]{0:T(512)S(1)}, f32[512,2048]{1,0:T(8,128)S(1)}) fusion(bf16[2048,128]{1,0:T(8,128)(2,1)} %get-tuple-element.273, bf16[2,512,128]{2,1,0:T(8,128)(2,1)S(1)} %get-tuple-element.272, s32[]{:T(128)} %get-tuple-element.255), kind=kOutput, calls=%fused_computation.3.clone.1 | convolution fusion | flops 270532096 | bytes 4851716 | tf_op jit(solution)/shard_map/while/body/eval_jaxpr/dot_general | solution.py:25
  24.5 1.9 %copy-done = f32[512,2048]{1,0:T(8,128)} copy-done((f32[512,2048]{1,0:T(8,128)}, f32[512,2048]{1,0:T(8,128)S(1)}, u32[]{:S(2)}) %copy-start) | copy-done | bytes 4194328 | tf_op jit(solution)/shard_map/while
  26.4 1.5 multiply_reduce_fusion.6
  28.0 3.0 %fusion.136 = f32[2,512,128]{2,1,0:T(8,128)S(1)} fusion(f32[2,512,128]{2,1,0:T(8,128)S(1)} %get-tuple-element.258, s32[]{:T(128)} %get-tuple-element.255, bf16[2048,128]{1,0:T(8,128)(2,1)S(1)} %copy-done.1, f32[512,2048]{1,0:T(8,128)} %copy-done, f32[512]{0:T(512)S(1)} %get-tuple-element.237), kind=kOutput, calls=%fused_computation.7.clone.1 | convolution fusion | flops 271581184 | bytes 4982788 | tf_op jit(solution)/shard_map/while/body/eval_jaxpr/dot_general | solution.py:32
  31.1 7.1 %pmax.7 = f32[4,256]{1,0:T(4,128)S(1)} all-reduce(f32[4,256]{1,0:T(4,128)S(1)} %reshape_reshape.20), channel_id=1, replica_groups=mesh['space'=8,'match'=4] {'match'}, use_global_device_ids=true, to_apply=%region_6.7 | all-reduce | flops 1024 | bytes 8192 | tf_op jit(solution)/shard_map/pmax | solution.py:95
  38.3 0.8 copy.12
  39.2 0.8 copy.14
  40.1 0.8 copy.10
  41.0 1.0 broadcast_multiply_fusion
  42.0 17.2 %reduce-scatter.15.cloned.1.call-done = f32[64,4]{1,0:T(8,128)} async-done(((f32[256,4]{1,0:T(8,128)}), f32[64,4]{1,0:T(8,128)}) %reduce-scatter.15.cloned.1.call-update) | async-done | bytes 1040
  59.2 0.8 copy.13
  60.1 21.3 %reduce-scatter.17.cloned.1.call-done = f32[64,4]{1,0:T(8,128)} async-done(((f32[256,4]{1,0:T(8,128)}), f32[64,4]{1,0:T(8,128)}) %reduce-scatter.17.cloned.1.call-update) | async-done | bytes 1040
  81.4 0.8 copy.15
  82.2 21.2 %reduce-scatter.13.cloned.1.call-done = f32[64,4]{1,0:T(8,128)} async-done(((f32[256,4]{1,0:T(8,128)}), f32[64,4]{1,0:T(8,128)}) %reduce-scatter.13.cloned.1.call-update) | async-done | bytes 1040
  103.4 0.8 copy.11
  104.3 23.3 %reduce-scatter.11.cloned.1.call-done = f32[4,64,128]{2,1,0:T(8,128)} async-done(((f32[4,256,128]{2,1,0:T(8,128)}), f32[4,64,128]{2,1,0:T(8,128)}) %reduce-scatter.11.cloned.1.call-update) | async-done | bytes 131088 | tf_op jit(solution)/shard_map/reduce_scatter | solution.py:98
  127.6 1.0 broadcast_divide_fusion
  128.6 3.4 %collective-permute-start = (f32[1,64,128]{2,1,0:T(8,128)S(1)}, f32[1,64,128]{2,1,0:T(8,128)S(1)}, u32[]{:S(2)}, u32[]{:S(2)}) collective-permute-start(f32[1,64,128]{2,1,0:T(8,128)S(1)} %get-tuple-element.161), channel_id=1, source_target_pairs={{0,4},{4,8},{8,12},{12,16},{16,20},{20,24},{24,28},{1,5},{5,9},{9,... | collective-permute-start | bytes 98312 | tf_op jit(solution)/shard_map/ppermute | solution.py:14
  132.0 1.3 collective-permute-start.1
  133.3 0.2 fusion.81
  133.6 4.2 %collective-permute-done.1 = f32[1,64,128]{2,1,0:T(8,128)S(1)} collective-permute-done((f32[1,64,128]{2,1,0:T(8,128)S(1)}, f32[1,64,128]{2,1,0:T(8,128)S(1)}, u32[]{:S(2)}, u32[]{:S(2)}) %collective-permute-start.1) | collective-permute-done | bytes 32800 | tf_op jit(solution)/shard_map/ppermute | solution.py:17
  137.8 1.3 collective-permute-start.2
  139.1 1.3 collective-permute-start.3
  140.4 0.2 fusion.39
  140.6 0.2 fusion.43
  140.9 2.1 %collective-permute-done.3 = f32[6,1,128]{2,1,0:T(1,128)S(1)} collective-permute-done((f32[6,1,128]{2,1,0:T(1,128)S(1)}, f32[6,1,128]{2,1,0:T(1,128)S(1)}, u32[]{:S(2)}, u32[]{:S(2)}) %collective-permute-start.3) | collective-permute-done | bytes 3104 | tf_op jit(solution)/shard_map/ppermute | solution.py:17
  143.0 0.2 fusion.54
  143.2 0.2 fusion.47
  143.4 0.2 fusion.52
  143.6 0.2 fusion.49
  143.8 0.2 fusion.24
  144.1 0.3 multiply_convert_fusion
  144.3 4.3 %collective-permute-start.4 = (bf16[1,64,128]{2,1,0:T(8,128)(2,1)S(1)}, bf16[1,64,128]{2,1,0:T(8,128)(2,1)S(1)}, u32[]{:S(2)}, u32[]{:S(2)}) collective-permute-start(bf16[1,64,128]{2,1,0:T(8,128)(2,1)S(1)} %get-tuple-element.167), channel_id=1, source_target_pairs={{0,4},{4,8},{8,12},{12,16},{16,20},{20,24},{24,28},{1,5},{5,9},{9,... | collective-permute-start | bytes 49160 | tf_op jit(solution)/shard_map/ppermute | solution.py:14
  148.6 1.3 collective-permute-start.5
  150.1 4.2 %collective-permute-done.5 = bf16[1,64,128]{2,1,0:T(8,128)(2,1)S(1)} collective-permute-done((bf16[1,64,128]{2,1,0:T(8,128)(2,1)S(1)}, bf16[1,64,128]{2,1,0:T(8,128)(2,1)S(1)}, u32[]{:S(2)}, u32[]{:S(2)}) %collective-permute-start.5) | collective-permute-done | bytes 16416 | tf_op jit(solution)/shard_map/ppermute | solution.py:17
  154.3 2.8 %collective-permute-start.6 = (bf16[6,1,128]{2,1,0:T(2,128)(2,1)S(1)}, bf16[6,1,128]{2,1,0:T(2,128)(2,1)S(1)}, u32[]{:S(2)}, u32[]{:S(2)}) collective-permute-start(bf16[6,1,128]{2,1,0:T(2,128)(2,1)S(1)} %get-tuple-element.165), channel_id=1, source_target_pairs={{0,1},{1,2},{2,3},{4,5},{5,6},{6,7},{8,9},{9,10},{10,11},{12,13},{... | collective-permute-start | bytes 4616 | tf_op jit(solution)/shard_map/ppermute | solution.py:14
  157.1 1.3 collective-permute-start.7
  158.7 2.4 %collective-permute-done.7 = bf16[6,1,128]{2,1,0:T(2,128)(2,1)S(1)} collective-permute-done((bf16[6,1,128]{2,1,0:T(2,128)(2,1)S(1)}, bf16[6,1,128]{2,1,0:T(2,128)(2,1)S(1)}, u32[]{:S(2)}, u32[]{:S(2)}) %collective-permute-start.7) | collective-permute-done | bytes 1568 | tf_op jit(solution)/shard_map/ppermute | solution.py:17
  161.4 0.2 fusion.67
  161.9 0.2 fusion.38
  162.0 0.2 fusion.35
  162.2 0.6 copy.9
  (63 shorter events, 1.9 us)
Async XLA Ops:
  6.5 52.7 %reduce-scatter.15.cloned.1.call-start = ((), (), s32[]{:S(2)}) async-start(), calls=%async_computation.6 | async-start | bytes 163840
  13.9 28.1 %copy-start.3 = (f32[2,128]{1,0:T(2,128)S(1)}, f32[2,128]{1,0:T(2,128)}, u32[]{:S(2)}) copy-start(f32[2,128]{1,0:T(2,128)} %param.11) | copy-start | bytes 3076
  13.9 119.4 %copy-start.2 = (bf16[3,3,128,128]{3,2,1,0:T(8,128)(2,1)S(1)}, bf16[3,3,128,128]{3,2,1,0:T(8,128)(2,1)}, u32[]{:S(2)}) copy-start(bf16[3,3,128,128]{3,2,1,0:T(8,128)(2,1)} %param.10) | copy-start | bytes 884740
  13.9 5.5 %copy-start.1 = (bf16[2048,128]{1,0:T(8,128)(2,1)S(1)}, bf16[2048,128]{1,0:T(8,128)(2,1)}, u32[]{:S(2)}) copy-start(bf16[2048,128]{1,0:T(8,128)(2,1)} %get-tuple-element.273) | copy-start | bytes 1572868 | tf_op jit(solution)/shard_map/while
  15.8 2.0 %copy-start = (f32[512,2048]{1,0:T(8,128)}, f32[512,2048]{1,0:T(8,128)S(1)}, u32[]{:S(2)}) copy-start(f32[512,2048]{1,0:T(8,128)S(1)} %get-tuple-element.239) | copy-start | bytes 12582916 | tf_op jit(solution)/shard_map/while
  22.5 5.5 %copy-start.1 = (bf16[2048,128]{1,0:T(8,128)(2,1)S(1)}, bf16[2048,128]{1,0:T(8,128)(2,1)}, u32[]{:S(2)}) copy-start(bf16[2048,128]{1,0:T(8,128)(2,1)} %get-tuple-element.273) | copy-start | bytes 1572868 | tf_op jit(solution)/shard_map/while
  24.4 2.0 %copy-start = (f32[512,2048]{1,0:T(8,128)}, f32[512,2048]{1,0:T(8,128)S(1)}, u32[]{:S(2)}) copy-start(f32[512,2048]{1,0:T(8,128)S(1)} %get-tuple-element.239) | copy-start | bytes 12582916 | tf_op jit(solution)/shard_map/while
  31.1 112.9 %copy-start.5 = (f32[128]{0:T(128)S(1)}, f32[128]{0:T(128)}, u32[]{:S(2)}) copy-start(f32[128]{0:T(128)} %param.12) | copy-start | bytes 1540
  31.1 118.8 %copy-start.4 = (bf16[2,3,3,128]{3,0,2,1:T(2,128)(2,1)S(1)}, bf16[2,3,3,128]{3,0,2,1:T(2,128)(2,1)}, u32[]{:S(2)}) copy-start(bf16[2,3,3,128]{3,0,2,1:T(2,128)(2,1)} %param.13) | copy-start | bytes 13828
  39.2 42.2 %reduce-scatter.17.cloned.1.call-start = ((), (), s32[]{:S(2)}) async-start(), calls=%async_computation.7 | async-start | bytes 163840
  40.0 63.4 %reduce-scatter.13.cloned.1.call-start = ((), (), s32[]{:S(2)}) async-start(), calls=%async_computation.5 | async-start | bytes 163840
  40.9 86.7 %reduce-scatter.11.cloned.1.call-start = ((), (), s32[]{:S(2)}) async-start(), calls=%async_computation.4 | async-start | bytes 655360 | tf_op jit(solution)/shard_map/reduce_scatter | solution.py:98
  128.6 5.0 %collective-permute-start = (f32[1,64,128]{2,1,0:T(8,128)S(1)}, f32[1,64,128]{2,1,0:T(8,128)S(1)}, u32[]{:S(2)}, u32[]{:S(2)}) collective-permute-start(f32[1,64,128]{2,1,0:T(8,128)S(1)} %get-tuple-element.161), channel_id=1, source_target_pairs={{0,4},{4,8},{8,12},{12,16},{16,20},{20,24},{24,28},{1,5},{5,9},{9,... | collective-permute-start | bytes 98312 | tf_op jit(solution)/shard_map/ppermute | solution.py:14
  132.0 5.8 %collective-permute-start.1 = (f32[1,64,128]{2,1,0:T(8,128)S(1)}, f32[1,64,128]{2,1,0:T(8,128)S(1)}, u32[]{:S(2)}, u32[]{:S(2)}) collective-permute-start(f32[1,64,128]{2,1,0:T(8,128)S(1)} %get-tuple-element.162), channel_id=1, source_target_pairs={{4,0},{8,4},{12,8},{16,12},{20,16},{24,20},{28,24},{5,1},{9,5},{13... | collective-permute-start | bytes 98312 | tf_op jit(solution)/shard_map/ppermute | solution.py:17
  137.8 3.0 %collective-permute-start.2 = (f32[6,1,128]{2,1,0:T(1,128)S(1)}, f32[6,1,128]{2,1,0:T(1,128)S(1)}, u32[]{:S(2)}, u32[]{:S(2)}) collective-permute-start(f32[6,1,128]{2,1,0:T(1,128)S(1)} %get-tuple-element.159), channel_id=1, source_target_pairs={{0,1},{1,2},{2,3},{4,5},{5,6},{6,7},{8,9},{9,10},{10,11},{12,13},{... | collective-permute-start | bytes 9224 | tf_op jit(solution)/shard_map/ppermute | solution.py:14
  139.1 3.8 %collective-permute-start.3 = (f32[6,1,128]{2,1,0:T(1,128)S(1)}, f32[6,1,128]{2,1,0:T(1,128)S(1)}, u32[]{:S(2)}, u32[]{:S(2)}) collective-permute-start(f32[6,1,128]{2,1,0:T(1,128)S(1)} %get-tuple-element.160), channel_id=1, source_target_pairs={{1,0},{2,1},{3,2},{5,4},{6,5},{7,6},{9,8},{10,9},{11,10},{13,12},{... | collective-permute-start | bytes 9224 | tf_op jit(solution)/shard_map/ppermute | solution.py:17
  144.3 5.8 %collective-permute-start.4 = (bf16[1,64,128]{2,1,0:T(8,128)(2,1)S(1)}, bf16[1,64,128]{2,1,0:T(8,128)(2,1)S(1)}, u32[]{:S(2)}, u32[]{:S(2)}) collective-permute-start(bf16[1,64,128]{2,1,0:T(8,128)(2,1)S(1)} %get-tuple-element.167), channel_id=1, source_target_pairs={{0,4},{4,8},{8,12},{12,16},{16,20},{20,24},{24,28},{1,5},{5,9},{9,... | collective-permute-start | bytes 49160 | tf_op jit(solution)/shard_map/ppermute | solution.py:14
  148.6 5.6 %collective-permute-start.5 = (bf16[1,64,128]{2,1,0:T(8,128)(2,1)S(1)}, bf16[1,64,128]{2,1,0:T(8,128)(2,1)S(1)}, u32[]{:S(2)}, u32[]{:S(2)}) collective-permute-start(bf16[1,64,128]{2,1,0:T(8,128)(2,1)S(1)} %get-tuple-element.168), channel_id=1, source_target_pairs={{4,0},{8,4},{12,8},{16,12},{20,16},{24,20},{28,24},{5,1},{9,5},{13... | collective-permute-start | bytes 49160 | tf_op jit(solution)/shard_map/ppermute | solution.py:17
  154.3 4.5 %collective-permute-start.6 = (bf16[6,1,128]{2,1,0:T(2,128)(2,1)S(1)}, bf16[6,1,128]{2,1,0:T(2,128)(2,1)S(1)}, u32[]{:S(2)}, u32[]{:S(2)}) collective-permute-start(bf16[6,1,128]{2,1,0:T(2,128)(2,1)S(1)} %get-tuple-element.165), channel_id=1, source_target_pairs={{0,1},{1,2},{2,3},{4,5},{5,6},{6,7},{8,9},{9,10},{10,11},{12,13},{... | collective-permute-start | bytes 4616 | tf_op jit(solution)/shard_map/ppermute | solution.py:14
  157.1 4.0 %collective-permute-start.7 = (bf16[6,1,128]{2,1,0:T(2,128)(2,1)S(1)}, bf16[6,1,128]{2,1,0:T(2,128)(2,1)S(1)}, u32[]{:S(2)}, u32[]{:S(2)}) collective-permute-start(bf16[6,1,128]{2,1,0:T(2,128)(2,1)S(1)} %get-tuple-element.166), channel_id=1, source_target_pairs={{1,0},{2,1},{3,2},{5,4},{6,5},{7,6},{9,8},{10,9},{11,10},{13,12},{... | collective-permute-start | bytes 4616 | tf_op jit(solution)/shard_map/ppermute | solution.py:17
Sparse Core Ops, SparseCore 0:
  39.3 19.8 reduce-scatter.14
  61.8 19.5 reduce-scatter.16
  83.8 19.5 reduce-scatter.12
  105.9 21.6 reduce-scatter.10
where the time goes:
time: 172 us; the launch traced here: 169 us
  waiting for transfers between devices  96 us (56%)
  starting transfers between devices  17.1 us (10%)
  blocking collectives  14.5 us (8%)
  between operations  13.4 us (8%)
  matrix products  13.2 us (8%)
  local copies, waits for them, and re-layouts  9.77 us (6%)
  other arithmetic  5.23 us (3%)
    unnamed x7, waiting for transfers between devices  59.8 us
    reduce_scatter x1, waiting for transfers between devices, local(): lax.psum_scatter(accum.reshape(rows, width, chans) * factor[..., None], '...  23.3 us
    ppermute x4, waiting for transfers between devices, extended(): lax.ppermute(lax.slice_in_dim(block, 0, width, axis=dim), axis, backward)  12.9 us
    ppermute x4, starting transfers between devices, extended(): lax.ppermute(lax.slice_in_dim(block, block.shape[dim] - width, None, axis...  11.8 us
    all_gather x1, blocking collectives, local(): band = lax.all_gather(source, 'match', axis=1, tiled=True)  7.39 us
    pmax x1, blocking collectives, local(): overall = lax.pmax(peak, 'match')  7.14 us
    dot_general x2, matrix products, block_terms(): accum = jnp.dot(probs, keys, preferred_element_type=jnp.float32)  6.06 us
    ppermute x4, starting transfers between devices, extended(): lax.ppermute(lax.slice_in_dim(block, 0, width, axis=dim), axis, backward)  5.17 us
  transfers between devices with their start and end apart: 12, of which 9 were waited for; matrix products, arithmetic and copies ran while one was open for 4% of the time, Pallas kernels for 0%

commit v1 on v0

v1 whole, which is shorter than its diff:
```python
import functools
import math

import jax
import jax.numpy as jnp
from jax import lax
from jax.experimental import pallas as pl
from jax.experimental.pallas import tpu as pltpu
from jax.sharding import PartitionSpec as P

HALO = 2


def extended(block, sides, width):
    for axis, dim in sides:
        count = lax.axis_size(axis)
        forward = [(i, i + 1) for i in range(count - 1)]
        backward = [(target, source) for source, target in forward]
        low = lax.ppermute(
            lax.slice_in_dim(block, block.shape[dim] - width, None, axis=dim), axis, forward
        )
        high = lax.ppermute(lax.slice_in_dim(block, 0, width, axis=dim), axis, backward)
        block = jnp.concatenate([low, block, high], axis=dim)
    return block


def match_kernel(q_ref, k_ref, pos_ref, warped_ref, flow_ref,
                 m_ref, acc_ref, tot_ref, sx_ref, sy_ref, *, scale, tk, nk):
    phase = pl.program_id(1)
    kb = pl.program_id(2)
    s = lax.dot_general(
        q_ref[...], k_ref[...], (((1,), (1,)), ((), ())),
        preferred_element_type=jnp.float32,
    ) * scale

    @pl.when((phase == 0) & (kb == 0))
    def _():
        m_ref[...] = jnp.full(m_ref.shape, -jnp.inf, jnp.float32)

    @pl.when(phase == 0)
    def _():
        m_ref[...] = jnp.maximum(m_ref[...], jnp.max(s, axis=1, keepdims=True))

    @pl.when((phase == 1) & (kb == 0))
    def _():
        acc_ref[...] = jnp.zeros(acc_ref.shape, jnp.float32)
        tot_ref[...] = jnp.zeros(tot_ref.shape, jnp.float32)
        sx_ref[...] = jnp.zeros(sx_ref.shape, jnp.float32)
        sy_ref[...] = jnp.zeros(sy_ref.shape, jnp.float32)

    @pl.when(phase == 1)
    def _():
        w = jnp.exp(s - m_ref[...])
        acc_ref[...] += jnp.dot(
            w.astype(jnp.bfloat16), k_ref[...], preferred_element_type=jnp.float32
        )
        tot = tot_ref[...]
        sx = sx_ref[...]
        sy = sy_ref[...]
        for c in range(tk // 128):
            part = w[:, c * 128:(c + 1) * 128]
            tot = tot + part
            sx = sx + part * pos_ref[0:1, c * 128:(c + 1) * 128]
            sy = sy + part * pos_ref[1:2, c * 128:(c + 1) * 128]
        tot_ref[...] = tot
        sx_ref[...] = sx
        sy_ref[...] = sy

    @pl.when((phase == 1) & (kb == nk - 1))
    def _():
        total = jnp.sum(tot_ref[...], axis=1, keepdims=True)
        warped_ref[...] = acc_ref[...] / total
        fx = jnp.sum(sx_ref[...], axis=1, keepdims=True) / total
        fy = jnp.sum(sy_ref[...], axis=1, keepdims=True) / total
        lane = lax.broadcasted_iota(jnp.int32, flow_ref.shape, 1)
        flow_ref[...] = jnp.where(lane == 0, fx, jnp.where(lane == 1, fy, 0.0))


def match(queries, keys, pos):
    count, chans = queries.shape
    total_keys = keys.shape[0]
    nq = -(-count // 1024)
    tq = -(-count // nq)
    tq = -(-tq // 8) * 8
    padded = tq * nq
    if padded != count:
        queries = jnp.pad(queries, ((0, padded - count), (0, 0)))
    tk = math.gcd(total_keys, 2048)
    nk = total_keys // tk
    kernel = functools.partial(
        match_kernel, scale=1.0 / math.sqrt(chans), tk=tk, nk=nk
    )
    warped, flow = pl.pallas_call(
        kernel,
        grid=(nq, 2, nk),
        in_specs=[
            pl.BlockSpec((tq, chans), lambda i, p, k: (i, 0)),
            pl.BlockSpec((tk, chans), lambda i, p, k: (k, 0)),
            pl.BlockSpec((8, tk), lambda i, p, k: (0, k)),
        ],
        out_specs=[
            pl.BlockSpec((tq, chans), lambda i, p, k: (i, 0)),
            pl.BlockSpec((tq, 128), lambda i, p, k: (i, 0)),
        ],
        out_shape=[
            jax.ShapeDtypeStruct((padded, chans), jnp.float32),
            jax.ShapeDtypeStruct((padded, 128), jnp.float32),
        ],
        scratch_shapes=[
            pltpu.VMEM((tq, 1), jnp.float32),
            pltpu.VMEM((tq, chans), jnp.float32),
            pltpu.VMEM((tq, 128), jnp.float32),
            pltpu.VMEM((tq, 128), jnp.float32),
            pltpu.VMEM((tq, 128), jnp.float32),
        ],
        compiler_params=pltpu.CompilerParams(
            dimension_semantics=("arbitrary", "arbitrary", "arbitrary"),
        ),
    )(queries, keys, pos)
    return warped[:count], flow[:count, 0], flow[:count, 1]


def local(source, targets, conv_in, flow_proj, in_bias, conv_out):
    rows, cols, chans = source.shape
    all_rows = rows * lax.axis_size("space")
    width = cols * lax.axis_size("match")
    row_first = lax.axis_index("space") * rows
    col_first = lax.axis_index("match") * cols
    keys = lax.all_gather(targets, "match", axis=0, tiled=True)
    index = jnp.arange(keys.shape[0], dtype=jnp.int32)
    pos = jnp.zeros((8, keys.shape[0]), jnp.float32)
    pos = pos.at[0].set((index % width).astype(jnp.float32) / width)
    pos = pos.at[1].set((index // width).astype(jnp.float32) / width)

    ext = extended(source, (("match", 1), ("space", 0)), HALO)
    erows, ecols = rows + 2 * HALO, cols + 2 * HALO
    warped, sum_x, sum_y = match(ext.reshape(erows * ecols, chans), keys, pos)
    warped = warped.reshape(erows, ecols, chans)
    grow = row_first - HALO + jnp.arange(erows, dtype=jnp.int32)
    gcol = col_first - HALO + jnp.arange(ecols, dtype=jnp.int32)
    inside = ((grow >= 0) & (grow < all_rows))[:, None] & ((gcol >= 0) & (gcol < width))[None, :]
    warped = jnp.where(inside[:, :, None], warped, 0.0)
    col_pos = gcol.astype(jnp.float32) / width
    row_pos = grow.astype(jnp.float32) / width
    flow_x = sum_x.reshape(erows, ecols) - col_pos[None, :]
    flow_y = sum_y.reshape(erows, ecols) - row_pos[:, None]

    pre = lax.conv_general_dilated(
        warped[None], conv_in.astype(jnp.float32), (1, 1), "VALID",
        dimension_numbers=("NHWC", "HWIO", "NHWC"),
        precision=lax.Precision.HIGHEST,
        preferred_element_type=jnp.float32,
    )[0]
    fx1 = flow_x[1:-1, 1:-1]
    fy1 = flow_y[1:-1, 1:-1]
    pre = pre + fx1[:, :, None] * flow_proj[0] + fy1[:, :, None] * flow_proj[1] + in_bias
    hidden = jax.nn.silu(pre).astype(jnp.bfloat16)
    hidden = jnp.where(inside[1:-1, 1:-1, None], hidden, jnp.zeros((), jnp.bfloat16))
    delta = lax.conv_general_dilated(
        hidden[None], jnp.transpose(conv_out, (1, 2, 3, 0)), (1, 1), "VALID",
        dimension_numbers=("NHWC", "HWIO", "NHWC"),
        preferred_element_type=jnp.float32,
    )[0]
    flows = jnp.stack([flow_x[HALO:-HALO, HALO:-HALO], flow_y[HALO:-HALO, HALO:-HALO]])
    return flows + jnp.transpose(delta, (2, 0, 1))


def solution(mesh):
    in_specs = (P("space", "match", None), P("match", None), P(), P(), P(), P())
    out_specs = P(None, "space", "match")
    return jax.shard_map(local, mesh=mesh, in_specs=in_specs, out_specs=out_specs, check_vma=False)
```

time: 172 us -> 69.8 us (0.41); the launches traced: 169 us -> 69.4 us
  waiting for transfers between devices: 96 us -> 18.9 us
  Pallas kernels: 0 us -> 16.7 us
  blocking collectives: 14.5 us -> 0 us
  matrix products: 13.2 us -> 2.64 us
  starting transfers between devices: 17.1 us -> 8.36 us
  local copies, waits for them, and re-layouts: 9.77 us -> 6.07 us
  other arithmetic: 5.23 us -> 3.04 us
    unnamed x7 -> x1, waiting for transfers between devices: 59.8 us -> 0.02 us
    reduce_scatter x1 -> x0, waiting for transfers between devices: 23.3 us -> none  [local(): lax.psum_scatter(accum.reshape(rows, width, chans) * factor[..., None], '...]
    pallas_call x0 -> x1, Pallas kernels: none -> 16.7 us  [match(): pl.pallas_call(kernel, grid=(nq, 2, nk), in_specs=[pl.BlockSpec((tq, chan...]
    dot_general x22 -> x0, matrix products: 13.2 us -> none  [the longest x2 6.06 us: block_terms(): accum = jnp.dot(probs, keys, preferred_element_type=jnp.float32)]
    all_gather x0 -> x1, waiting for transfers between devices: none -> 11.9 us  [local(): keys = lax.all_gather(targets, 'match', axis=0, tiled=True)]
    all_gather x1 -> x0, blocking collectives: 7.39 us -> none  [local(): band = lax.all_gather(source, 'match', axis=1, tiled=True)]
    pmax x1 -> x0, blocking collectives: 7.14 us -> none  [local(): overall = lax.pmax(peak, 'match')]
    ppermute x4 -> x2, starting transfers between devices: 11.8 us -> 5.77 us  [extended(): lax.ppermute(lax.slice_in_dim(block, block.shape[dim] - width, None, axis...]
  transfers between devices with their start and end apart: 12 -> 5, of which waited for: 9 -> 3; matrix products, arithmetic and copies ran while one was open for 4% -> 5% of each run, Pallas kernels for 0% -> 0%
where the time goes in v1:
time: 69.8 us; the launch traced here: 69.4 us
  waiting for transfers between devices  18.9 us (27%)
  Pallas kernels  16.7 us (24%)
  between operations  13.7 us (20%)
  starting transfers between devices  8.36 us (12%)
  local copies, waits for them, and re-layouts  6.07 us (9%)
  other arithmetic  3.04 us (4%)
  matrix products  2.64 us (4%)
    pallas_call x1, Pallas kernels, match(): pl.pallas_call(kernel, grid=(nq, 2, nk), in_specs=[pl.BlockSpec((tq, chan...  16.7 us
    all_gather x1, waiting for transfers between devices, local(): keys = lax.all_gather(targets, 'match', axis=0, tiled=True)  11.9 us
    ppermute x2, waiting for transfers between devices, extended(): lax.ppermute(lax.slice_in_dim(block, 0, width, axis=dim), axis, backward)  6.97 us
    ppermute x2, starting transfers between devices, extended(): lax.ppermute(lax.slice_in_dim(block, block.shape[dim] - width, None, axis...  5.77 us
    ppermute x2, starting transfers between devices, extended(): lax.ppermute(lax.slice_in_dim(block, 0, width, axis=dim), axis, backward)  2.58 us
    concatenate x2, other arithmetic, extended(): block = jnp.concatenate([low, block, high], axis=dim)  1.74 us
    conv_general_dilated x1, matrix products, local(): lax.conv_general_dilated(hidden[None], jnp.transpose(conv_out, (1, 2, 3,...  1.7 us
  transfers between devices with their start and end apart: 5, of which 3 were waited for; matrix products, arithmetic and copies ran while one was open for 5% of the time, Pallas kernels for 0%

profile of v1, /device:TPU:0, one launch (start us, length us, event | category | flops | bytes accessed | tf_op | source)
XLA Modules:
  0.0 69.4 jit_solution(13281733584283535733)
XLA Ops:
  6.5 0.0 copy-start
  6.5 0.0 all-gather.2.cloned.1.call-start
  6.5 0.8 %fusion.29 = (bf16[4,2,128]{2,1,0:T(2,128)(2,1)S(1)}, bf16[4,2,128]{2,1,0:T(2,128)(2,1)S(1)}) fusion(bf16[4,64,128]{2,1,0:T(8,128)(2,1)} %param.10), kind=kLoop, calls=%fused_computation.59 | loop fusion | bytes 8192 | tf_op jit(solution)/shard_map/slice | solution.py:20
  7.3 2.3 %collective-permute-start = (bf16[4,2,128]{2,1,0:T(2,128)(2,1)S(1)}, bf16[4,2,128]{2,1,0:T(2,128)(2,1)S(1)}, u32[]{:S(2)}, u32[]{:S(2)}) collective-permute-start(bf16[4,2,128]{2,1,0:T(2,128)(2,1)S(1)} %get-tuple-element.37), channel_id=1, source_target_pairs={{0,1},{1,2},{2,3},{4,5},{5,6},{6,7},{8,9},{9,10},{10,11},{12,13},{... | collective-permute-start | bytes 6152 | tf_op jit(solution)/shard_map/ppermute | solution.py:19
  9.7 1.3 %collective-permute-start.1 = (bf16[4,2,128]{2,1,0:T(2,128)(2,1)S(1)}, bf16[4,2,128]{2,1,0:T(2,128)(2,1)S(1)}, u32[]{:S(2)}, u32[]{:S(2)}) collective-permute-start(bf16[4,2,128]{2,1,0:T(2,128)(2,1)S(1)} %get-tuple-element.38), channel_id=1, source_target_pairs={{1,0},{2,1},{3,2},{5,4},{6,5},{7,6},{9,8},{10,9},{11,10},{13,12},{... | collective-permute-start | bytes 6152 | tf_op jit(solution)/shard_map/ppermute | solution.py:22
  11.0 0.0 all-gather.2.cloned.1.call-update
  11.0 0.8 %slice_bitcast_fusion.5 = (f32[128]{0:T(128)S(1)}, f32[128]{0:T(128)S(1)}) fusion(f32[2,128]{1,0:T(2,128)} %param.13), kind=kLoop, calls=%fused_computation.47 | loop fusion | bytes 2048 | tf_op jit(solution)/shard_map/mul | solution.py:156
  11.8 0.1 broadcast_and_fusion
  12.0 0.0 collective-permute-done
  12.0 2.8 %collective-permute-done.1 = bf16[4,2,128]{2,1,0:T(2,128)(2,1)S(1)} collective-permute-done((bf16[4,2,128]{2,1,0:T(2,128)(2,1)S(1)}, bf16[4,2,128]{2,1,0:T(2,128)(2,1)S(1)}, u32[]{:S(2)}, u32[]{:S(2)}) %collective-permute-start.1) | collective-permute-done | bytes 2080 | tf_op jit(solution)/shard_map/ppermute | solution.py:22
  14.8 0.9 %pad_maximum_fusion.1 = bf16[4,68,128]{2,1,0:T(8,128)(2,1)S(1)} fusion(bf16[4,2,128]{2,1,0:T(2,128)(2,1)S(1)} %collective-permute-done.1, bf16[4,64,128]{2,1,0:T(8,128)(2,1)} %param.10, bf16[4,2,128]{2,1,0:T(2,128)(2,1)S(1)} %collective-permute-done), kind=kLoop, calls=%fused_computation.28 | loop fusion | flops 208896 | bytes 139264 | tf_op jit(solution)/shard_map/concatenate | solution.py:23
  15.7 3.4 %collective-permute-start.2 = (bf16[2,68,128]{2,1,0:T(8,128)(2,1)S(1)}, bf16[2,68,128]{2,1,0:T(8,128)(2,1)S(1)}, u32[]{:S(2)}, u32[]{:S(2)}) collective-permute-start(bf16[2,68,128]{2,1,0:T(8,128)(2,1)S(1)} %get-tuple-element.35), channel_id=1, source_target_pairs={{0,4},{4,8},{8,12},{12,16},{16,20},{20,24},{24,28},{1,5},{5,9},{9,... | collective-permute-start | bytes 104456 | tf_op jit(solution)/shard_map/ppermute | solution.py:19
  19.1 1.3 %collective-permute-start.3 = (bf16[2,68,128]{2,1,0:T(8,128)(2,1)S(1)}, bf16[2,68,128]{2,1,0:T(8,128)(2,1)S(1)}, u32[]{:S(2)}, u32[]{:S(2)}) collective-permute-start(bf16[2,68,128]{2,1,0:T(8,128)(2,1)S(1)} %get-tuple-element.36), channel_id=1, source_target_pairs={{4,0},{8,4},{12,8},{16,12},{20,16},{24,20},{28,24},{5,1},{9,5},{13... | collective-permute-start | bytes 104456 | tf_op jit(solution)/shard_map/ppermute | solution.py:22
  20.5 0.1 slice.76
  20.5 0.1 copy.7
  20.7 0.1 scatter.9.pos_ref
  20.8 0.0 copy-start.1
  20.8 0.0 collective-permute-done.2
  20.9 4.1 %collective-permute-done.3 = bf16[2,68,128]{2,1,0:T(8,128)(2,1)S(1)} collective-permute-done((bf16[2,68,128]{2,1,0:T(8,128)(2,1)S(1)}, bf16[2,68,128]{2,1,0:T(8,128)(2,1)S(1)}, u32[]{:S(2)}, u32[]{:S(2)}) %collective-permute-start.3) | collective-permute-done | bytes 34848 | tf_op jit(solution)/shard_map/ppermute | solution.py:22
  25.0 0.9 %pad_maximum_fusion = bf16[8,68,128]{2,1,0:T(8,128)(2,1)S(1)} fusion(bf16[2,68,128]{2,1,0:T(8,128)(2,1)S(1)} %collective-permute-done.3, bf16[4,2,128]{2,1,0:T(2,128)(2,1)S(1)} %collective-permute-done.1, bf16[4,64,128]{2,1,0:T(8,128)(2,1)} %param.10, bf16[4,2,128]{2,1,0:T(2,128)(2,1)S(1)} %collective-permute-done, ...), kind=kLoop, calls=%fused_computation.19 | loop fusion | flops 696320 | bytes 278528 | tf_op jit(solution)/shard_map/concatenate | solution.py:23
  25.9 0.7 reshape.165.q_ref
  26.5 11.9 %all-gather.2.cloned.1.call-done.k_ref = bf16[8192,128]{1,0:T(8,128)(2,1)} async-done(((bf16[2048,128]{1,0:T(8,128)(2,1)}), bf16[8192,128]{1,0:T(8,128)(2,1)}) %all-gather.2.cloned.1.call-update) | async-done | bytes 2097168 | tf_op jit(solution)/shard_map/all_gather | solution.py:129
  38.4 0.0 copy-done.1
  38.4 16.7 %shard_map.64 = (f32[544,128]{1,0:T(8,128)}, f32[544,128]{1,0:T(8,128)}) custom-call(bf16[544,128]{1,0:T(8,128)(2,1)} %reshape.165.q_ref, bf16[8192,128]{1,0:T(8,128)(2,1)} %all-gather.2.cloned.1.call-done.k_ref, f32[8,8192]{1,0:T(8,128)} %copy-done.1), custom_call_target="tpu_custom_call" | custom-call | tf_op jit(solution)/shard_map/pallas_call | solution.py:93
  55.2 1.4 %slice_reduce_fusion.1 = (f32[544]{0:T(1024)S(1)}, f32[544]{0:T(1024)S(1)}) fusion(f32[544,128]{1,0:T(8,128)} %get-tuple-element.31), kind=kLoop, calls=%fused_computation.9 | loop fusion | bytes 8704 | tf_op jit(solution)/shard_map/slice | solution.py:120
  56.6 0.1 reshape_squeeze.6
  56.6 0.1 slice.77
  56.7 0.1 reshape_squeeze.7
  56.8 0.1 broadcast_subtract_fusion
  56.9 0.1 slice.79
  56.9 0.1 slice_bitcast_fusion.2
  57.0 1.0 %reshape.166 = f32[1,8,68,128]{3,2,1,0:T(8,128)S(1)} reshape(f32[544,128]{1,0:T(8,128)} %get-tuple-element.32) | data formatting | bytes 557056 | tf_op jit(solution)/shard_map/reshape | solution.py:138
  58.0 0.0 copy-start.2
  58.0 0.1 select_bitcast_fusion
  58.2 0.1 copy.20
  58.2 0.0 copy-start.3
  58.2 0.0 copy-start.4
  58.3 0.1 copy.10
  58.4 0.0 copy-done
  58.4 0.9 %convolution_select_fusion = f32[6,8,9,128]{3,1,2,0:T(8,128)S(1)} fusion(bf16[3,3,128,128]{3,2,1,0:T(8,128)(2,1)S(1)} %copy-done, f32[8,1,7,2,128]{4,2,3,0,1:T(8,128)S(1)} %slice.87, f32[8,1,8,9,128]{4,2,3,0,1:T(8,128)S(1)} %copy.10, pred[8,9]{0,1:T(8,128)(4,1)S(1)} %copy-done.5), kind=kOutput, calls=%fused_computation | convolution fusion | flops 764737536 | bytes 868424 | tf_op jit(solution)/shard_map/conv_general_dilated | solution.py:148
  59.3 0.1 copy.11
  59.4 0.1 copy.12
  59.5 0.1 copy.13
  59.6 0.3 select_bitcast_fusion.1
  60.0 1.7 %convolution_select_fusion.1 = f32[4,8,9,2]{1,3,2,0:T(2,128)S(1)} fusion(bf16[2,3,3,128]{3,0,2,1:T(2,128)(2,1)S(1)} %copy-done.3, bf16[6,1,7,2,128]{4,2,3,0,1:T(8,128)(2,1)S(1)} %slice.89, bf16[6,1,8,9,128]{4,2,3,0,1:T(8,128)(2,1)S(1)} %copy.15, pred[8,9]{0,1:T(8,128)(4,1)S(1)} %copy-done.4), kind=kOutput, calls=%fused_computation.1 | convolution fusion | flops 1733184 | bytes 139080 | tf_op jit(solution)/shard_map/conv_general_dilated | solution.py:159
  61.7 0.1 copy.18
  61.9 0.1 reshape.192
  61.9 0.6 fusion.21
  (19 shorter events, 0.2 us)
Async XLA Ops:
  6.5 51.8 %copy-start = (bf16[3,3,128,128]{3,2,1,0:T(8,128)(2,1)S(1)}, bf16[3,3,128,128]{3,2,1,0:T(8,128)(2,1)}, u32[]{:S(2)}) copy-start(bf16[3,3,128,128]{3,2,1,0:T(8,128)(2,1)} %param.12) | copy-start | bytes 884740
  6.5 31.9 %all-gather.2.cloned.1.call-start = ((), (), s32[]{:S(2)}) async-start(), calls=%async_computation | async-start | bytes 2621440 | tf_op jit(solution)/shard_map/all_gather | solution.py:129
  7.3 4.7 %collective-permute-start = (bf16[4,2,128]{2,1,0:T(2,128)(2,1)S(1)}, bf16[4,2,128]{2,1,0:T(2,128)(2,1)S(1)}, u32[]{:S(2)}, u32[]{:S(2)}) collective-permute-start(bf16[4,2,128]{2,1,0:T(2,128)(2,1)S(1)} %get-tuple-element.37), channel_id=1, source_target_pairs={{0,1},{1,2},{2,3},{4,5},{5,6},{6,7},{8,9},{9,10},{10,11},{12,13},{... | collective-permute-start | bytes 6152 | tf_op jit(solution)/shard_map/ppermute | solution.py:19
  9.7 5.2 %collective-permute-start.1 = (bf16[4,2,128]{2,1,0:T(2,128)(2,1)S(1)}, bf16[4,2,128]{2,1,0:T(2,128)(2,1)S(1)}, u32[]{:S(2)}, u32[]{:S(2)}) collective-permute-start(bf16[4,2,128]{2,1,0:T(2,128)(2,1)S(1)} %get-tuple-element.38), channel_id=1, source_target_pairs={{1,0},{2,1},{3,2},{5,4},{6,5},{7,6},{9,8},{10,9},{11,10},{13,12},{... | collective-permute-start | bytes 6152 | tf_op jit(solution)/shard_map/ppermute | solution.py:22
  15.7 5.1 %collective-permute-start.2 = (bf16[2,68,128]{2,1,0:T(8,128)(2,1)S(1)}, bf16[2,68,128]{2,1,0:T(8,128)(2,1)S(1)}, u32[]{:S(2)}, u32[]{:S(2)}) collective-permute-start(bf16[2,68,128]{2,1,0:T(8,128)(2,1)S(1)} %get-tuple-element.35), channel_id=1, source_target_pairs={{0,4},{4,8},{8,12},{12,16},{16,20},{20,24},{24,28},{1,5},{5,9},{9,... | collective-permute-start | bytes 104456 | tf_op jit(solution)/shard_map/ppermute | solution.py:19
  19.1 5.9 %collective-permute-start.3 = (bf16[2,68,128]{2,1,0:T(8,128)(2,1)S(1)}, bf16[2,68,128]{2,1,0:T(8,128)(2,1)S(1)}, u32[]{:S(2)}, u32[]{:S(2)}) collective-permute-start(bf16[2,68,128]{2,1,0:T(8,128)(2,1)S(1)} %get-tuple-element.36), channel_id=1, source_target_pairs={{4,0},{8,4},{12,8},{16,12},{20,16},{24,20},{28,24},{5,1},{9,5},{13... | collective-permute-start | bytes 104456 | tf_op jit(solution)/shard_map/ppermute | solution.py:22
  20.8 17.6 %copy-start.1 = (f32[8,8192]{1,0:T(8,128)}, f32[8,8192]{1,0:T(8,128)S(1)}, u32[]{:S(2)}) copy-start(f32[8,8192]{1,0:T(8,128)S(1)} %scatter.9.pos_ref) | copy-start | bytes 786436
  55.2 3.2 %copy-start.5 = (pred[8,9]{0,1:T(8,128)(4,1)S(1)}, pred[8,9]{0,1:T(8,128)(4,1)}, u32[]{:S(2)}) copy-start(pred[8,9]{0,1:T(8,128)(4,1)} %constant.134) | copy-start | bytes 220
  58.0 1.6 %copy-start.2 = (f32[128]{0:T(128)S(1)}, f32[128]{0:T(128)}, u32[]{:S(2)}) copy-start(f32[128]{0:T(128)} %param.14) | copy-start | bytes 1540
  58.2 1.8 %copy-start.3 = (bf16[2,3,3,128]{3,0,2,1:T(2,128)(2,1)S(1)}, bf16[2,3,3,128]{3,0,2,1:T(2,128)(2,1)}, u32[]{:S(2)}) copy-start(bf16[2,3,3,128]{3,0,2,1:T(2,128)(2,1)} %param.15) | copy-start | bytes 13828
  58.2 1.8 %copy-start.4 = (pred[8,9]{0,1:T(8,128)(4,1)S(1)}, pred[8,9]{0,1:T(8,128)(4,1)}, u32[]{:S(2)}) copy-start(pred[8,9]{0,1:T(8,128)(4,1)} %constant.133) | copy-start | bytes 220
Sparse Core Ops, SparseCore 0:
  11.1 27.2 all-gather.1

commit v2 on v1

v2 whole, which is shorter than its diff:
```python
import functools
import math

import jax
import jax.numpy as jnp
from jax import lax
from jax.experimental import pallas as pl
from jax.experimental.pallas import tpu as pltpu
from jax.sharding import PartitionSpec as P

HALO = 2


def extended(block, sides, width):
    for axis, dim in sides:
        count = lax.axis_size(axis)
        forward = [(i, i + 1) for i in range(count - 1)]
        backward = [(target, source) for source, target in forward]
        low = lax.ppermute(
            lax.slice_in_dim(block, block.shape[dim] - width, None, axis=dim), axis, forward
        )
        high = lax.ppermute(lax.slice_in_dim(block, 0, width, axis=dim), axis, backward)
        block = jnp.concatenate([low, block, high], axis=dim)
    return block


def shard_kernel(*refs, scale, chans, first, last):
    if first:
        q_ref, km_ref = refs[:2]
        outs = refs[2:]
    else:
        q_ref, km_ref, m_ref, acc_ref, st_ref = refs[:5]
        outs = refs[5:]
    s = lax.dot_general(
        q_ref[...], km_ref[:, 0:chans], (((1,), (1,)), ((), ())),
        preferred_element_type=jnp.float32,
    ) * scale
    peak = jnp.max(s, axis=1, keepdims=True)
    if not first:
        old = m_ref[:, 0:1]
        peak = jnp.maximum(old, peak)
    w = jnp.exp(s - peak)
    hi = w.astype(jnp.bfloat16)
    lo = (w - hi.astype(jnp.float32)).astype(jnp.bfloat16)
    both = jnp.dot(hi, km_ref[...], preferred_element_type=jnp.float32)
    acc = both[:, 0:chans]
    st = both[:, chans:] + jnp.dot(
        lo, km_ref[:, chans:], preferred_element_type=jnp.float32
    )
    if not first:
        alpha = jnp.exp(old - peak)
        acc = acc_ref[...] * alpha + acc
        st = st_ref[...] * alpha + st
    if last:
        warped_ref, flow_ref = outs
        total = st[:, 0:1]
        warped_ref[...] = acc / total
        fx = (st[:, 1:2] + st[:, 2:3]) / total
        fy = (st[:, 3:4] + st[:, 4:5]) / total
        lane = lax.broadcasted_iota(jnp.int32, flow_ref.shape, 1)
        flow_ref[...] = jnp.where(lane == 0, fx, jnp.where(lane == 1, fy, 0.0))
    else:
        m_out, acc_out, st_out = outs
        m_out[...] = jnp.broadcast_to(peak, m_out.shape)
        acc_out[...] = acc
        st_out[...] = st


def split_bf16(x):
    hi = x.astype(jnp.bfloat16)
    return hi, (x - hi.astype(jnp.float32)).astype(jnp.bfloat16)


def with_positions(keys, offset, width):
    count = keys.shape[0]
    index = offset + jnp.arange(count, dtype=jnp.int32)
    col_hi, col_lo = split_bf16((index % width).astype(jnp.float32) / width)
    row_hi, row_lo = split_bf16((index // width).astype(jnp.float32) / width)
    cols = jnp.stack(
        [jnp.ones((count,), jnp.bfloat16), col_hi, col_lo, row_hi, row_lo], axis=1
    )
    cols = jnp.pad(cols, ((0, 0), (0, 128 - cols.shape[1])))
    return jnp.concatenate([keys, cols], axis=1)


def match_step(queries, km, state, tq, first, last):
    padded, chans = queries.shape
    nq = padded // tq
    tk = km.shape[0]
    kernel = functools.partial(
        shard_kernel, scale=1.0 / math.sqrt(chans), chans=chans, first=first, last=last
    )
    row_spec = lambda width: pl.BlockSpec((tq, width), lambda i: (i, 0))
    in_specs = [row_spec(chans), pl.BlockSpec((tk, km.shape[1]), lambda i: (0, 0))]
    args = [queries, km]
    if not first:
        in_specs += [row_spec(128), row_spec(chans), row_spec(128)]
        args += list(state)
    if last:
        out_specs = [row_spec(chans), row_spec(128)]
        out_shape = [
            jax.ShapeDtypeStruct((padded, chans), jnp.float32),
            jax.ShapeDtypeStruct((padded, 128), jnp.float32),
        ]
    else:
        out_specs = [row_spec(128), row_spec(chans), row_spec(128)]
        out_shape = [
            jax.ShapeDtypeStruct((padded, 128), jnp.float32),
            jax.ShapeDtypeStruct((padded, chans), jnp.float32),
            jax.ShapeDtypeStruct((padded, 128), jnp.float32),
        ]
    return pl.pallas_call(
        kernel,
        grid=(nq,),
        in_specs=in_specs,
        out_specs=out_specs,
        out_shape=out_shape,
        compiler_params=pltpu.CompilerParams(dimension_semantics=("arbitrary",)),
    )(*args)


def match(queries, targets, width):
    count, chans = queries.shape
    tk = targets.shape[0]
    cap = max(8, (1024 * 2048 // tk) // 8 * 8)
    nq = -(-count // cap)
    tq = -(-(-(-count // nq)) // 8) * 8
    padded = tq * nq
    if padded != count:
        queries = jnp.pad(queries, ((0, padded - count), (0, 0)))
    n = lax.axis_size("match")
    me = lax.axis_index("match")
    shards = [(targets, me)]
    for shift in range(1, n):
        moved = lax.ppermute(targets, "match", [(j, (j + shift) % n) for j in range(n)])
        shards.append((moved, (me - shift) % n))
    state = None
    for step, (keys, owner) in enumerate(shards):
        km = with_positions(keys, owner * tk, width)
        state = match_step(queries, km, state, tq, step == 0, step == n - 1)
    warped, flow = state
    return warped[:count], flow[:count, 0], flow[:count, 1]


def local(source, targets, conv_in, flow_proj, in_bias, conv_out):
    rows, cols, chans = source.shape
    all_rows = rows * lax.axis_size("space")
    width = cols * lax.axis_size("match")
    row_first = lax.axis_index("space") * rows
    col_first = lax.axis_index("match") * cols
    ext = extended(source, (("match", 1), ("space", 0)), HALO)
    erows, ecols = rows + 2 * HALO, cols + 2 * HALO
    warped, sum_x, sum_y = match(ext.reshape(erows * ecols, chans), targets, width)
    warped = warped.reshape(erows, ecols, chans)
    grow = row_first - HALO + jnp.arange(erows, dtype=jnp.int32)
    gcol = col_first - HALO + jnp.arange(ecols, dtype=jnp.int32)
    inside = ((grow >= 0) & (grow < all_rows))[:, None] & ((gcol >= 0) & (gcol < width))[None, :]
    warped = jnp.where(inside[:, :, None], warped, 0.0)
    col_pos = gcol.astype(jnp.float32) / width
    row_pos = grow.astype(jnp.float32) / width
    flow_x = sum_x.reshape(erows, ecols) - col_pos[None, :]
    flow_y = sum_y.reshape(erows, ecols) - row_pos[:, None]

    pre = lax.conv_general_dilated(
        warped[None], conv_in.astype(jnp.float32), (1, 1), "VALID",
        dimension_numbers=("NHWC", "HWIO", "NHWC"),
        precision=lax.Precision.HIGHEST,
        preferred_element_type=jnp.float32,
    )[0]
    fx1 = flow_x[1:-1, 1:-1]
    fy1 = flow_y[1:-1, 1:-1]
    pre = pre + fx1[:, :, None] * flow_proj[0] + fy1[:, :, None] * flow_proj[1] + in_bias
    hidden = jax.nn.silu(pre).astype(jnp.bfloat16)
    hidden = jnp.where(inside[1:-1, 1:-1, None], hidden, jnp.zeros((), jnp.bfloat16))
    delta = lax.conv_general_dilated(
        hidden[None], jnp.transpose(conv_out, (1, 2, 3, 0)), (1, 1), "VALID",
        dimension_numbers=("NHWC", "HWIO", "NHWC"),
        preferred_element_type=jnp.float32,
    )[0]
    flows = jnp.stack([flow_x[HALO:-HALO, HALO:-HALO], flow_y[HALO:-HALO, HALO:-HALO]])
    return flows + jnp.transpose(delta, (2, 0, 1))


def solution(mesh):
    in_specs = (P("space", "match", None), P("match", None), P(), P(), P(), P())
    out_specs = P(None, "space", "match")
    return jax.shard_map(local, mesh=mesh, in_specs=in_specs, out_specs=out_specs, check_vma=False)
```

time: 69.8 us -> 69.4 us (level)
  the two profiles are of different devices: /device:TPU:0 before, /device:TPU:14 now
where the time goes in v2:
time: 69.4 us; the launch traced here: 68.9 us
  Pallas kernels  19.2 us (28%)
  waiting for transfers between devices  17.2 us (25%)
  starting transfers between devices  13.4 us (19%)
  other arithmetic  8.84 us (13%)
  local copies, waits for them, and re-layouts  7.21 us (10%)
  matrix products  2.64 us (4%)
    pallas_call x4, Pallas kernels, match_step(): pl.pallas_call(kernel, grid=(nq,), in_specs=in_specs, out_specs=out_specs...  19.2 us
    ppermute x2, waiting for transfers between devices, extended(): lax.ppermute(lax.slice_in_dim(block, block.shape[dim] - width, None, axis...  14.3 us
    concatenate x4, other arithmetic, with_positions(): return jnp.concatenate([keys, cols], axis=1)  6.89 us
    ppermute x2, starting transfers between devices, extended(): lax.ppermute(lax.slice_in_dim(block, 0, width, axis=dim), axis, backward)  6.06 us
    ppermute x2, starting transfers between devices, extended(): lax.ppermute(lax.slice_in_dim(block, block.shape[dim] - width, None, axis...  5.34 us
    ppermute x2, waiting for transfers between devices, extended(): lax.ppermute(lax.slice_in_dim(block, 0, width, axis=dim), axis, backward)  2.93 us
    ppermute x3, starting transfers between devices, match(): lax.ppermute(targets, 'match', [(j, (j + shift) % n) for j in range(n)])  1.99 us
    conv_general_dilated x1, matrix products, local(): lax.conv_general_dilated(hidden[None], jnp.transpose(conv_out, (1, 2, 3,...  1.7 us
  transfers between devices with their start and end apart: 7, of which 2 were waited for; matrix products, arithmetic and copies ran while one was open for 14% of the time, Pallas kernels for 20%

profile of v2, /device:TPU:14, one launch (start us, length us, event | category | flops | bytes accessed | tf_op | source)
XLA Modules:
  0.0 68.9 jit_solution(6067831642700658003)
XLA Ops:
  0.0 0.6 collective-permute-start.5
  0.6 1.4 %collective-permute-start.4 = (bf16[2048,128]{1,0:T(8,128)(2,1)}, bf16[2048,128]{1,0:T(8,128)(2,1)S(1)}, u32[]{:S(2)}, u32[]{:S(2)}) collective-permute-start(bf16[2048,128]{1,0:T(8,128)(2,1)} %param.7), channel_id=1, source_target_pairs={{0,3},{1,0},{2,1},{3,2},{4,7},{5,4},{6,5},{7,6},{8,11},{9,8},{10,9... | collective-permute-start | bytes 1572872 | tf_op jit(solution)/shard_map/ppermute | solution.py:135
  2.0 0.7 %fusion.49 = (bf16[4,2,128]{2,1,0:T(2,128)(2,1)S(1)}, bf16[4,2,128]{2,1,0:T(2,128)(2,1)S(1)}) fusion(bf16[4,64,128]{2,1,0:T(8,128)(2,1)} %param.6), kind=kLoop, calls=%fused_computation.111 | loop fusion | bytes 8192 | tf_op jit(solution)/shard_map/slice | solution.py:20
  2.7 1.9 %collective-permute-start = (bf16[4,2,128]{2,1,0:T(2,128)(2,1)S(1)}, bf16[4,2,128]{2,1,0:T(2,128)(2,1)S(1)}, u32[]{:S(2)}, u32[]{:S(2)}) collective-permute-start(bf16[4,2,128]{2,1,0:T(2,128)(2,1)S(1)} %get-tuple-element.31), channel_id=1, source_target_pairs={{0,1},{1,2},{2,3},{4,5},{5,6},{6,7},{8,9},{9,10},{10,11},{12,13},{... | collective-permute-start | bytes 6152 | tf_op jit(solution)/shard_map/ppermute | solution.py:19
  4.6 3.6 %collective-permute-start.1 = (bf16[4,2,128]{2,1,0:T(2,128)(2,1)S(1)}, bf16[4,2,128]{2,1,0:T(2,128)(2,1)S(1)}, u32[]{:S(2)}, u32[]{:S(2)}) collective-permute-start(bf16[4,2,128]{2,1,0:T(2,128)(2,1)S(1)} %get-tuple-element.32), channel_id=1, source_target_pairs={{1,0},{2,1},{3,2},{5,4},{6,5},{7,6},{9,8},{10,9},{11,10},{13,12},{... | collective-permute-start | bytes 6152 | tf_op jit(solution)/shard_map/ppermute | solution.py:22
  8.3 0.1 subtract_convert_fusion.2
  8.4 0.1 fusion.35
  8.5 0.1 subtract_convert_fusion
  8.6 0.1 fusion.36
  8.7 0.1 subtract_convert_fusion.4
  8.8 0.1 fusion.34
  8.9 0.1 subtract_convert_fusion.6
  9.0 0.1 fusion.40
  9.2 0.3 copy.21
  9.5 1.2 %fusion.7.refs_1_ = bf16[2048,256]{1,0:T(8,128)(2,1)} fusion(bf16[2048,5]{1,0:T(8,128)(2,1)S(1)} %copy.21, bf16[2048,128]{1,0:T(8,128)(2,1)S(1)} %copy-done.1), kind=kLoop, calls=%fused_computation.10 | loop fusion | flops 3145728 | bytes 1593344 | tf_op jit(solution)/shard_map/concatenate | solution.py:83
  10.8 0.1 broadcast_and_fusion
  10.8 14.3 %collective-permute-done = bf16[4,2,128]{2,1,0:T(2,128)(2,1)S(1)} collective-permute-done((bf16[4,2,128]{2,1,0:T(2,128)(2,1)S(1)}, bf16[4,2,128]{2,1,0:T(2,128)(2,1)S(1)}, u32[]{:S(2)}, u32[]{:S(2)}) %collective-permute-start) | collective-permute-done | bytes 2080 | tf_op jit(solution)/shard_map/ppermute | solution.py:19
  25.2 3.4 %collective-permute-start.2 = (bf16[2,68,128]{2,1,0:T(8,128)(2,1)S(1)}, bf16[2,68,128]{2,1,0:T(8,128)(2,1)S(1)}, u32[]{:S(2)}, u32[]{:S(2)}) collective-permute-start(bf16[2,68,128]{2,1,0:T(8,128)(2,1)S(1)} %get-tuple-element.29), channel_id=1, source_target_pairs={{0,4},{4,8},{8,12},{12,16},{16,20},{20,24},{24,28},{1,5},{5,9},{9,... | collective-permute-start | bytes 104456 | tf_op jit(solution)/shard_map/ppermute | solution.py:19
  28.6 2.4 %collective-permute-start.3 = (bf16[2,68,128]{2,1,0:T(8,128)(2,1)S(1)}, bf16[2,68,128]{2,1,0:T(8,128)(2,1)S(1)}, u32[]{:S(2)}, u32[]{:S(2)}) collective-permute-start(bf16[2,68,128]{2,1,0:T(8,128)(2,1)S(1)} %get-tuple-element.30), channel_id=1, source_target_pairs={{4,0},{8,4},{12,8},{16,12},{20,16},{24,20},{28,24},{5,1},{9,5},{13... | collective-permute-start | bytes 104456 | tf_op jit(solution)/shard_map/ppermute | solution.py:22
  31.1 0.3 copy.20
  31.5 0.3 copy.19
  31.9 0.3 copy.18
  32.2 0.1 slice.47
  32.3 0.1 copy.22
  32.4 2.9 %collective-permute-done.3 = bf16[2,68,128]{2,1,0:T(8,128)(2,1)S(1)} collective-permute-done((bf16[2,68,128]{2,1,0:T(8,128)(2,1)S(1)}, bf16[2,68,128]{2,1,0:T(8,128)(2,1)S(1)}, u32[]{:S(2)}, u32[]{:S(2)}) %collective-permute-start.3) | collective-permute-done | bytes 34848 | tf_op jit(solution)/shard_map/ppermute | solution.py:22
  35.4 0.7 reshape.517.refs_0_
  36.1 4.2 %shard_map.64 = (f32[544,128]{1,0:T(8,128)}, f32[544,128]{1,0:T(8,128)}, f32[544,128]{1,0:T(8,128)}) custom-call(bf16[544,128]{1,0:T(8,128)(2,1)} %reshape.517.refs_0_, bf16[2048,256]{1,0:T(8,128)(2,1)} %fusion.7.refs_1_), custom_call_target="tpu_custom_call" | custom-call | tf_op jit(solution)/shard_map/pallas_call | solution.py:112
  40.3 2.2 %fusion.6.refs_1_ = bf16[2048,256]{1,0:T(8,128)(2,1)} fusion(bf16[2048,5]{1,0:T(8,128)(2,1)S(1)} %copy.20, bf16[2048,128]{1,0:T(8,128)(2,1)} %collective-permute-done.6), kind=kLoop, calls=%fused_computation.9 | loop fusion | flops 3145728 | bytes 1593344 | tf_op jit(solution)/shard_map/concatenate | solution.py:83
  42.5 4.9 %shard_map.65 = (f32[544,128]{1,0:T(8,128)}, f32[544,128]{1,0:T(8,128)}, f32[544,128]{1,0:T(8,128)}) custom-call(bf16[544,128]{1,0:T(8,128)(2,1)} %reshape.517.refs_0_, bf16[2048,256]{1,0:T(8,128)(2,1)} %fusion.6.refs_1_, f32[544,128]{1,0:T(8,128)} %get-tuple-element.16.refs_2_, f32[544,128]{1,0:T(8,128)} %get-tuple-element.17.refs_3_, ...), custom_call_target="tpu_custom_call" | custom-call | tf_op jit(solution)/shard_map/pallas_call | solution.py:112
  47.4 2.2 %fusion.5.refs_1_ = bf16[2048,256]{1,0:T(8,128)(2,1)} fusion(bf16[2048,5]{1,0:T(8,128)(2,1)S(1)} %copy.19, bf16[2048,128]{1,0:T(8,128)(2,1)} %collective-permute-done.5), kind=kLoop, calls=%fused_computation.8 | loop fusion | flops 3145728 | bytes 1593344 | tf_op jit(solution)/shard_map/concatenate | solution.py:83
  49.7 4.9 %shard_map.66 = (f32[544,128]{1,0:T(8,128)}, f32[544,128]{1,0:T(8,128)}, f32[544,128]{1,0:T(8,128)}) custom-call(bf16[544,128]{1,0:T(8,128)(2,1)} %reshape.517.refs_0_, bf16[2048,256]{1,0:T(8,128)(2,1)} %fusion.5.refs_1_, f32[544,128]{1,0:T(8,128)} %get-tuple-element.19.refs_2_, f32[544,128]{1,0:T(8,128)} %get-tuple-element.20.refs_3_, ...), custom_call_target="tpu_custom_call" | custom-call | tf_op jit(solution)/shard_map/pallas_call | solution.py:112
  54.5 1.2 %fusion.4.refs_1_ = bf16[2048,256]{1,0:T(8,128)(2,1)} fusion(bf16[2048,5]{1,0:T(8,128)(2,1)S(1)} %copy.18, bf16[2048,128]{1,0:T(8,128)(2,1)S(1)} %collective-permute-done.4), kind=kLoop, calls=%fused_computation.7 | loop fusion | flops 3145728 | bytes 1593344 | tf_op jit(solution)/shard_map/concatenate | solution.py:83
  55.7 5.3 %shard_map.67 = (f32[544,128]{1,0:T(8,128)}, f32[544,128]{1,0:T(8,128)}) custom-call(bf16[544,128]{1,0:T(8,128)(2,1)} %reshape.517.refs_0_, bf16[2048,256]{1,0:T(8,128)(2,1)} %fusion.4.refs_1_, f32[544,128]{1,0:T(8,128)} %get-tuple-element.22.refs_2_, f32[544,128]{1,0:T(8,128)} %get-tuple-element.23.refs_3_, f32[544,128]{1,0:T(8,128)} %get-tuple-element.24.refs_4_), custom_call_target="tpu_custom_call" | custom-call | tf_op jit(solution)/shard_map/pallas_call | solution.py:112
  61.0 1.4 %slice_reduce_fusion.1 = (f32[544]{0:T(1024)S(1)}, f32[544]{0:T(1024)S(1)}) fusion(f32[544,128]{1,0:T(8,128)} %get-tuple-element.25), kind=kLoop, calls=%fused_computation.18 | loop fusion | bytes 8704 | tf_op jit(solution)/shard_map/slice | solution.py:142
  62.4 0.1 reshape_squeeze.6
  62.5 0.1 slice.48
  62.7 0.1 slice.50
  62.9 1.0 %reshape.518 = f32[1,8,68,128]{3,2,1,0:T(8,128)S(1)} reshape(f32[544,128]{1,0:T(8,128)} %get-tuple-element.26) | data formatting | bytes 557056 | tf_op jit(solution)/shard_map/reshape | solution.py:154
  63.9 0.1 select_bitcast_fusion
  64.2 0.5 copy-done.7
  64.7 0.9 %convolution_select_fusion = f32[6,8,9,128]{3,1,2,0:T(8,128)S(1)} fusion(bf16[3,3,128,128]{3,2,1,0:T(8,128)(2,1)S(1)} %copy-done, f32[8,1,7,2,128]{4,2,3,0,1:T(8,128)S(1)} %slice.58, f32[8,1,8,9,128]{4,2,3,0,1:T(8,128)S(1)} %copy.25, pred[8,9]{0,1:T(8,128)(4,1)S(1)} %copy-done.7), kind=kOutput, calls=%fused_computation.5 | convolution fusion | flops 764737536 | bytes 868424 | tf_op jit(solution)/shard_map/conv_general_dilated | solution.py:164
  65.8 0.1 copy.27
  65.9 0.1 copy.28
  66.0 0.3 select_bitcast_fusion.1
  66.4 1.7 %convolution_select_fusion.1 = f32[4,8,9,2]{1,3,2,0:T(2,128)S(1)} fusion(bf16[2,3,3,128]{3,0,2,1:T(2,128)(2,1)S(1)} %copy-done.5, bf16[6,1,7,2,128]{4,2,3,0,1:T(8,128)(2,1)S(1)} %slice.60, bf16[6,1,8,9,128]{4,2,3,0,1:T(8,128)(2,1)S(1)} %copy.30, pred[8,9]{0,1:T(8,128)(4,1)S(1)} %copy-done.6), kind=kOutput, calls=%fused_computation.6 | convolution fusion | flops 1733184 | bytes 139080 | tf_op jit(solution)/shard_map/conv_general_dilated | solution.py:175
  68.1 0.1 copy.33
  68.2 0.1 reshape.544
  68.3 0.6 fusion.33
  (47 shorter events, 1.0 us)
Async XLA Ops:
  0.0 64.2 %copy-start = (bf16[3,3,128,128]{3,2,1,0:T(8,128)(2,1)S(1)}, bf16[3,3,128,128]{3,2,1,0:T(8,128)(2,1)}, u32[]{:S(2)}) copy-start(bf16[3,3,128,128]{3,2,1,0:T(8,128)(2,1)} %param.8) | copy-start | bytes 884740
  0.0 9.5 %copy-start.1 = (bf16[2048,128]{1,0:T(8,128)(2,1)S(1)}, bf16[2048,128]{1,0:T(8,128)(2,1)}, u32[]{:S(2)}) copy-start(bf16[2048,128]{1,0:T(8,128)(2,1)} %param.7) | copy-start | bytes 1572868
  0.0 40.3 %collective-permute-start.6 = (bf16[2048,128]{1,0:T(8,128)(2,1)}, bf16[2048,128]{1,0:T(8,128)(2,1)}, u32[]{:S(2)}, u32[]{:S(2)}) collective-permute-start(bf16[2048,128]{1,0:T(8,128)(2,1)} %param.7), channel_id=1, source_target_pairs={{0,1},{1,2},{2,3},{3,0},{4,5},{5,6},{6,7},{7,4},{8,9},{9,10},{10,1... | collective-permute-start | bytes 1572872 | tf_op jit(solution)/shard_map/ppermute | solution.py:135
  0.0 47.4 %collective-permute-start.5 = (bf16[2048,128]{1,0:T(8,128)(2,1)}, bf16[2048,128]{1,0:T(8,128)(2,1)}, u32[]{:S(2)}, u32[]{:S(2)}) collective-permute-start(bf16[2048,128]{1,0:T(8,128)(2,1)} %param.7), channel_id=1, source_target_pairs={{0,2},{1,3},{2,0},{3,1},{4,6},{5,7},{6,4},{7,5},{8,10},{9,11},{10,... | collective-permute-start | bytes 1572872 | tf_op jit(solution)/shard_map/ppermute | solution.py:135
  0.6 53.9 %collective-permute-start.4 = (bf16[2048,128]{1,0:T(8,128)(2,1)}, bf16[2048,128]{1,0:T(8,128)(2,1)S(1)}, u32[]{:S(2)}, u32[]{:S(2)}) collective-permute-start(bf16[2048,128]{1,0:T(8,128)(2,1)} %param.7), channel_id=1, source_target_pairs={{0,3},{1,0},{2,1},{3,2},{4,7},{5,4},{6,5},{7,6},{8,11},{9,8},{10,9... | collective-permute-start | bytes 1572872 | tf_op jit(solution)/shard_map/ppermute | solution.py:135
  2.7 22.4 %collective-permute-start = (bf16[4,2,128]{2,1,0:T(2,128)(2,1)S(1)}, bf16[4,2,128]{2,1,0:T(2,128)(2,1)S(1)}, u32[]{:S(2)}, u32[]{:S(2)}) collective-permute-start(bf16[4,2,128]{2,1,0:T(2,128)(2,1)S(1)} %get-tuple-element.31), channel_id=1, source_target_pairs={{0,1},{1,2},{2,3},{4,5},{5,6},{6,7},{8,9},{9,10},{10,11},{12,13},{... | collective-permute-start | bytes 6152 | tf_op jit(solution)/shard_map/ppermute | solution.py:19
  4.6 20.5 %collective-permute-start.1 = (bf16[4,2,128]{2,1,0:T(2,128)(2,1)S(1)}, bf16[4,2,128]{2,1,0:T(2,128)(2,1)S(1)}, u32[]{:S(2)}, u32[]{:S(2)}) collective-permute-start(bf16[4,2,128]{2,1,0:T(2,128)(2,1)S(1)} %get-tuple-element.32), channel_id=1, source_target_pairs={{1,0},{2,1},{3,2},{5,4},{6,5},{7,6},{9,8},{10,9},{11,10},{13,12},{... | collective-permute-start | bytes 6152 | tf_op jit(solution)/shard_map/ppermute | solution.py:22
  9.5 1.2 %copy-start.3 = (f32[2,128]{1,0:T(2,128)S(1)}, f32[2,128]{1,0:T(2,128)}, u32[]{:S(2)}) copy-start(f32[2,128]{1,0:T(2,128)} %param.9) | copy-start | bytes 3076
  9.5 15.6 %copy-start.2 = (bf16[4,64,128]{2,1,0:T(8,128)(2,1)S(1)}, bf16[4,64,128]{2,1,0:T(8,128)(2,1)}, u32[]{:S(2)}) copy-start(bf16[4,64,128]{2,1,0:T(8,128)(2,1)} %param.6) | copy-start | bytes 196612
  25.2 7.3 %collective-permute-start.2 = (bf16[2,68,128]{2,1,0:T(8,128)(2,1)S(1)}, bf16[2,68,128]{2,1,0:T(8,128)(2,1)S(1)}, u32[]{:S(2)}, u32[]{:S(2)}) collective-permute-start(bf16[2,68,128]{2,1,0:T(8,128)(2,1)S(1)} %get-tuple-element.29), channel_id=1, source_target_pairs={{0,4},{4,8},{8,12},{12,16},{16,20},{20,24},{24,28},{1,5},{5,9},{9,... | collective-permute-start | bytes 104456 | tf_op jit(solution)/shard_map/ppermute | solution.py:19
  28.6 6.8 %collective-permute-start.3 = (bf16[2,68,128]{2,1,0:T(8,128)(2,1)S(1)}, bf16[2,68,128]{2,1,0:T(8,128)(2,1)S(1)}, u32[]{:S(2)}, u32[]{:S(2)}) collective-permute-start(bf16[2,68,128]{2,1,0:T(8,128)(2,1)S(1)} %get-tuple-element.30), channel_id=1, source_target_pairs={{4,0},{8,4},{12,8},{16,12},{20,16},{24,20},{28,24},{5,1},{9,5},{13... | collective-permute-start | bytes 104456 | tf_op jit(solution)/shard_map/ppermute | solution.py:22
  64.0 0.7 copy-start.7
  64.2 1.8 %copy-start.4 = (f32[128]{0:T(128)S(1)}, f32[128]{0:T(128)}, u32[]{:S(2)}) copy-start(f32[128]{0:T(128)} %param.10) | copy-start | bytes 1540
  65.7 0.7 %copy-start.5 = (bf16[2,3,3,128]{3,0,2,1:T(2,128)(2,1)S(1)}, bf16[2,3,3,128]{3,0,2,1:T(2,128)(2,1)}, u32[]{:S(2)}) copy-start(bf16[2,3,3,128]{3,0,2,1:T(2,128)(2,1)} %param.11) | copy-start | bytes 13828
  65.7 0.7 copy-start.6

commit v3 on v2

--- a/solution.py
+++ b/solution.py
@@ -26,13 +26,13 @@
 
 def shard_kernel(*refs, scale, chans, first, last):
     if first:
-        q_ref, km_ref = refs[:2]
-        outs = refs[2:]
+        q_ref, k_ref, pos_ref = refs[:3]
+        outs = refs[3:]
     else:
-        q_ref, km_ref, m_ref, acc_ref, st_ref = refs[:5]
-        outs = refs[5:]
+        q_ref, k_ref, pos_ref, m_ref, acc_ref, st_ref = refs[:6]
+        outs = refs[6:]
     s = lax.dot_general(
-        q_ref[...], km_ref[:, 0:chans], (((1,), (1,)), ((), ())),
+        q_ref[...], k_ref[...], (((1,), (1,)), ((), ())),
         preferred_element_type=jnp.float32,
     ) * scale
     peak = jnp.max(s, axis=1, keepdims=True)
@@ -42,10 +42,9 @@
     w = jnp.exp(s - peak)
     hi = w.astype(jnp.bfloat16)
     lo = (w - hi.astype(jnp.float32)).astype(jnp.bfloat16)
-    both = jnp.dot(hi, km_ref[...], preferred_element_type=jnp.float32)
-    acc = both[:, 0:chans]
-    st = both[:, chans:] + jnp.dot(
-        lo, km_ref[:, chans:], preferred_element_type=jnp.float32
+    acc = jnp.dot(hi, k_ref[...], preferred_element_type=jnp.float32)
+    st = jnp.dot(hi, pos_ref[...], preferred_element_type=jnp.float32) + jnp.dot(
+        lo, pos_ref[...], preferred_element_type=jnp.float32
     )
     if not first:
         alpha = jnp.exp(old - peak)
@@ -71,28 +70,30 @@
     return hi, (x - hi.astype(jnp.float32)).astype(jnp.bfloat16)
 
 
-def with_positions(keys, offset, width):
-    count = keys.shape[0]
+def positions(count, offset, width):
     index = offset + jnp.arange(count, dtype=jnp.int32)
     col_hi, col_lo = split_bf16((index % width).astype(jnp.float32) / width)
     row_hi, row_lo = split_bf16((index // width).astype(jnp.float32) / width)
     cols = jnp.stack(
         [jnp.ones((count,), jnp.bfloat16), col_hi, col_lo, row_hi, row_lo], axis=1
     )
-    cols = jnp.pad(cols, ((0, 0), (0, 128 - cols.shape[1])))
-    return jnp.concatenate([keys, cols], axis=1)
+    return jnp.pad(cols, ((0, 0), (0, 128 - cols.shape[1])))
 
 
-def match_step(queries, km, state, tq, first, last):
+def match_step(queries, keys, pos, state, tq, first, last):
     padded, chans = queries.shape
     nq = padded // tq
-    tk = km.shape[0]
+    tk = keys.shape[0]
     kernel = functools.partial(
         shard_kernel, scale=1.0 / math.sqrt(chans), chans=chans, first=first, last=last
     )
     row_spec = lambda width: pl.BlockSpec((tq, width), lambda i: (i, 0))
-    in_specs = [row_spec(chans), pl.BlockSpec((tk, km.shape[1]), lambda i: (0, 0))]
-    args = [queries, km]
+    in_specs = [
+        row_spec(chans),
+        pl.BlockSpec((tk, chans), lambda i: (0, 0)),
+        pl.BlockSpec((tk, 128), lambda i: (0, 0)),
+    ]
+    args = [queries, keys, pos]
     if not first:
         in_specs += [row_spec(128), row_spec(chans), row_spec(128)]
         args += list(state)
@@ -136,8 +137,8 @@
         shards.append((moved, (me - shift) % n))
     state = None
     for step, (keys, owner) in enumerate(shards):
-        km = with_positions(keys, owner * tk, width)
-        state = match_step(queries, km, state, tq, step == 0, step == n - 1)
+        pos = positions(tk, owner * tk, width)
+        state = match_step(queries, keys, pos, state, tq, step == 0, step == n - 1)
     warped, flow = state
     return warped[:count], flow[:count, 0], flow[:count, 1]
 
@@ -148,7 +149,9 @@
     width = cols * lax.axis_size("match")
     row_first = lax.axis_index("space") * rows
     col_first = lax.axis_index("match") * cols
-    ext = extended(source, (("match", 1), ("space", 0)), HALO)
+    ext = extended(source, (("match", 1),), HALO)
+    targets, ext = lax.optimization_barrier((targets, ext))
+    ext = extended(ext, (("space", 0),), HALO)
     erows, ecols = rows + 2 * HALO, cols + 2 * HALO
     warped, sum_x, sum_y = match(ext.reshape(erows * ecols, chans), targets, width)
     warped = warped.reshape(erows, ecols, chans)

time: 69.4 us -> 58.2 us (0.84)
  the two profiles are of different devices: /device:TPU:14 before, /device:TPU:0 now
where the time goes in v3:
time: 58.2 us; the launch traced here: 57.2 us
  Pallas kernels  23 us (40%)
  local copies, waits for them, and re-layouts  14.5 us (25%)
  starting transfers between devices  12.5 us (21%)
  matrix products  2.64 us (5%)
  waiting for transfers between devices  2.29 us (4%)
  other arithmetic  1.94 us (3%)
    pallas_call x4, Pallas kernels, match_step(): pl.pallas_call(kernel, grid=(nq,), in_specs=in_specs, out_specs=out_specs...  23 us
    ppermute x2, starting transfers between devices, extended(): lax.ppermute(lax.slice_in_dim(block, block.shape[dim] - width, None, axis...  5.77 us
    unnamed x23, local copies, waits for them, and re-layouts  5.1 us
    ppermute x3, starting transfers between devices, match(): lax.ppermute(targets, 'match', [(j, (j + shift) % n) for j in range(n)])  4.11 us
    pad x4, local copies, waits for them, and re-layouts, positions(): return jnp.pad(cols, ((0, 0), (0, 128 - cols.shape[1])))  3.64 us
    ppermute x2, starting transfers between devices, extended(): lax.ppermute(lax.slice_in_dim(block, 0, width, axis=dim), axis, backward)  2.58 us
    ppermute x2, waiting for transfers between devices, extended(): lax.ppermute(lax.slice_in_dim(block, 0, width, axis=dim), axis, backward)  2.27 us
    conv_general_dilated x1, matrix products, local(): lax.conv_general_dilated(hidden[None], jnp.transpose(conv_out, (1, 2, 3,...  1.7 us
  transfers between devices with their start and end apart: 7, of which 1 were waited for; matrix products, arithmetic and copies ran while one was open for 12% of the time, Pallas kernels for 29%

profile of v3, /device:TPU:0, one launch (start us, length us, event | category | flops | bytes accessed | tf_op | source)
XLA Modules:
  0.0 57.2 jit_solution(8182434993709098134)
XLA Ops:
  0.0 0.8 %fusion.41 = (bf16[4,2,128]{2,1,0:T(2,128)(2,1)S(1)}, bf16[4,2,128]{2,1,0:T(2,128)(2,1)S(1)}) fusion(bf16[4,64,128]{2,1,0:T(8,128)(2,1)} %param.6), kind=kLoop, calls=%fused_computation.102 | loop fusion | bytes 8192 | tf_op jit(solution)/shard_map/slice | solution.py:20
  0.8 2.3 %collective-permute-start = (bf16[4,2,128]{2,1,0:T(2,128)(2,1)S(1)}, bf16[4,2,128]{2,1,0:T(2,128)(2,1)S(1)}, u32[]{:S(2)}, u32[]{:S(2)}) collective-permute-start(bf16[4,2,128]{2,1,0:T(2,128)(2,1)S(1)} %get-tuple-element.35), channel_id=1, source_target_pairs={{0,1},{1,2},{2,3},{4,5},{5,6},{6,7},{8,9},{9,10},{10,11},{12,13},{... | collective-permute-start | bytes 6152 | tf_op jit(solution)/shard_map/ppermute | solution.py:19
  3.1 1.3 %collective-permute-start.1 = (bf16[4,2,128]{2,1,0:T(2,128)(2,1)S(1)}, bf16[4,2,128]{2,1,0:T(2,128)(2,1)S(1)}, u32[]{:S(2)}, u32[]{:S(2)}) collective-permute-start(bf16[4,2,128]{2,1,0:T(2,128)(2,1)S(1)} %get-tuple-element.36), channel_id=1, source_target_pairs={{1,0},{2,1},{3,2},{5,4},{6,5},{7,6},{9,8},{10,9},{11,10},{13,12},{... | collective-permute-start | bytes 6152 | tf_op jit(solution)/shard_map/ppermute | solution.py:22
  4.4 0.1 subtract_convert_fusion.2
  4.5 0.1 fusion.27
  4.6 0.1 subtract_convert_fusion
  4.7 0.1 fusion.28
  4.8 0.1 subtract_convert_fusion.4
  4.9 0.1 fusion.26
  5.0 0.1 subtract_convert_fusion.6
  5.1 0.1 fusion.32
  5.3 0.7 %copy-done.6 = f32[2,128]{1,0:T(2,128)S(1)} copy-done((f32[2,128]{1,0:T(2,128)S(1)}, f32[2,128]{1,0:T(2,128)}, u32[]{:S(2)}) %copy-start.6) | copy-done | bytes 1048
  6.0 2.3 %collective-permute-done.1 = bf16[4,2,128]{2,1,0:T(2,128)(2,1)S(1)} collective-permute-done((bf16[4,2,128]{2,1,0:T(2,128)(2,1)S(1)}, bf16[4,2,128]{2,1,0:T(2,128)(2,1)S(1)}, u32[]{:S(2)}, u32[]{:S(2)}) %collective-permute-start.1) | collective-permute-done | bytes 2080 | tf_op jit(solution)/shard_map/ppermute | solution.py:22
  8.3 2.4 %collective-permute-start.6 = (bf16[2048,128]{1,0:T(8,128)(2,1)}, bf16[2048,128]{1,0:T(8,128)(2,1)S(1)}, u32[]{:S(2)}, u32[]{:S(2)}) collective-permute-start(bf16[2048,128]{1,0:T(8,128)(2,1)} %refs_1_), channel_id=1, source_target_pairs={{0,1},{1,2},{2,3},{3,0},{4,5},{5,6},{6,7},{7,4},{8,9},{9,10},{10,1... | collective-permute-start | bytes 1572872 | tf_op jit(solution)/shard_map/ppermute | solution.py:136
  10.7 0.3 collective-permute-start.5
  11.0 1.4 %collective-permute-start.4 = (bf16[2048,128]{1,0:T(8,128)(2,1)}, bf16[2048,128]{1,0:T(8,128)(2,1)S(1)}, u32[]{:S(2)}, u32[]{:S(2)}) collective-permute-start(bf16[2048,128]{1,0:T(8,128)(2,1)} %refs_1_), channel_id=1, source_target_pairs={{0,3},{1,0},{2,1},{3,2},{4,7},{5,4},{6,5},{7,6},{8,11},{9,8},{10,9... | collective-permute-start | bytes 1572872 | tf_op jit(solution)/shard_map/ppermute | solution.py:136
  12.4 3.4 %collective-permute-start.2 = (bf16[2,68,128]{2,1,0:T(8,128)(2,1)S(1)}, bf16[2,68,128]{2,1,0:T(8,128)(2,1)S(1)}, u32[]{:S(2)}, u32[]{:S(2)}) collective-permute-start(bf16[2,68,128]{2,1,0:T(8,128)(2,1)S(1)} %get-tuple-element.33), channel_id=1, source_target_pairs={{0,4},{4,8},{8,12},{12,16},{16,20},{20,24},{24,28},{1,5},{5,9},{9,... | collective-permute-start | bytes 104456 | tf_op jit(solution)/shard_map/ppermute | solution.py:19
  15.9 1.3 %collective-permute-start.3 = (bf16[2,68,128]{2,1,0:T(8,128)(2,1)S(1)}, bf16[2,68,128]{2,1,0:T(8,128)(2,1)S(1)}, u32[]{:S(2)}, u32[]{:S(2)}) collective-permute-start(bf16[2,68,128]{2,1,0:T(8,128)(2,1)S(1)} %get-tuple-element.34), channel_id=1, source_target_pairs={{4,0},{8,4},{12,8},{16,12},{20,16},{24,20},{28,24},{5,1},{9,5},{13... | collective-permute-start | bytes 104456 | tf_op jit(solution)/shard_map/ppermute | solution.py:22
  17.3 0.3 copy.20
  17.7 0.3 copy.21
  18.0 0.9 %pad.15.refs_2_ = bf16[2048,128]{1,0:T(8,128)(2,1)} pad(bf16[2048,5]{1,0:T(8,128)(2,1)S(1)} %copy.20, bf16[]{:T(256)} %constant.129.clone.1), padding=0_0x0_123 | pad | bytes 544770 | tf_op jit(solution)/shard_map/jit(_pad)/pad | solution.py:80
  18.9 0.9 %pad.16.refs_2_ = bf16[2048,128]{1,0:T(8,128)(2,1)} pad(bf16[2048,5]{1,0:T(8,128)(2,1)S(1)} %copy.21, bf16[]{:T(256)} %constant.129.clone.1), padding=0_0x0_123 | pad | bytes 544770 | tf_op jit(solution)/shard_map/jit(_pad)/pad | solution.py:80
  19.8 0.3 copy.19
  20.2 0.9 %pad.14.refs_2_ = bf16[2048,128]{1,0:T(8,128)(2,1)} pad(bf16[2048,5]{1,0:T(8,128)(2,1)S(1)} %copy.19, bf16[]{:T(256)} %constant.129.clone.1), padding=0_0x0_123 | pad | bytes 544770 | tf_op jit(solution)/shard_map/jit(_pad)/pad | solution.py:80
  21.2 0.3 copy.18
  21.5 0.9 %pad.13.refs_2_ = bf16[2048,128]{1,0:T(8,128)(2,1)} pad(bf16[2048,5]{1,0:T(8,128)(2,1)S(1)} %copy.18, bf16[]{:T(256)} %constant.129.clone.1), padding=0_0x0_123 | pad | bytes 544770 | tf_op jit(solution)/shard_map/jit(_pad)/pad | solution.py:80
  22.5 0.1 copy.22
  22.6 0.7 %reshape.517.refs_0_ = bf16[544,128]{1,0:T(8,128)(2,1)} reshape(bf16[8,68,128]{2,1,0:T(8,128)(2,1)S(1)} %pad_maximum_fusion) | data formatting | bytes 278528 | tf_op jit(solution)/shard_map/reshape | solution.py:156
  23.3 5.7 %shard_map.64 = (f32[544,128]{1,0:T(8,128)}, f32[544,128]{1,0:T(8,128)}, f32[544,128]{1,0:T(8,128)}) custom-call(bf16[544,128]{1,0:T(8,128)(2,1)} %reshape.517.refs_0_, bf16[2048,128]{1,0:T(8,128)(2,1)} %refs_1_, bf16[2048,128]{1,0:T(8,128)(2,1)} %pad.16.refs_2_), custom_call_target="tpu_custom_call" | custom-call | tf_op jit(solution)/shard_map/pallas_call | solution.py:113
  29.1 0.8 %copy-done.3 = bf16[2048,128]{1,0:T(8,128)(2,1)} copy-done((bf16[2048,128]{1,0:T(8,128)(2,1)}, bf16[2048,128]{1,0:T(8,128)(2,1)S(1)}, u32[]{:S(2)}) %copy-start.3) | copy-done | bytes 524312
  29.9 5.6 %shard_map.65 = (f32[544,128]{1,0:T(8,128)}, f32[544,128]{1,0:T(8,128)}, f32[544,128]{1,0:T(8,128)}) custom-call(bf16[544,128]{1,0:T(8,128)(2,1)} %reshape.517.refs_0_, bf16[2048,128]{1,0:T(8,128)(2,1)} %copy-done.3, bf16[2048,128]{1,0:T(8,128)(2,1)} %pad.15.refs_2_, f32[544,128]{1,0:T(8,128)} %get-tuple-element.20.refs_3_, ...), custom_call_target="tpu_custom_call" | custom-call | tf_op jit(solution)/shard_map/pallas_call | solution.py:113
  35.4 0.8 %copy-done.2 = bf16[2048,128]{1,0:T(8,128)(2,1)} copy-done((bf16[2048,128]{1,0:T(8,128)(2,1)}, bf16[2048,128]{1,0:T(8,128)(2,1)S(1)}, u32[]{:S(2)}) %copy-start.2) | copy-done | bytes 524312
  36.2 5.5 %shard_map.66 = (f32[544,128]{1,0:T(8,128)}, f32[544,128]{1,0:T(8,128)}, f32[544,128]{1,0:T(8,128)}) custom-call(bf16[544,128]{1,0:T(8,128)(2,1)} %reshape.517.refs_0_, bf16[2048,128]{1,0:T(8,128)(2,1)} %copy-done.2, bf16[2048,128]{1,0:T(8,128)(2,1)} %pad.14.refs_2_, f32[544,128]{1,0:T(8,128)} %get-tuple-element.23.refs_3_, ...), custom_call_target="tpu_custom_call" | custom-call | tf_op jit(solution)/shard_map/pallas_call | solution.py:113
  41.7 0.8 %copy-done.1 = bf16[2048,128]{1,0:T(8,128)(2,1)} copy-done((bf16[2048,128]{1,0:T(8,128)(2,1)}, bf16[2048,128]{1,0:T(8,128)(2,1)S(1)}, u32[]{:S(2)}) %copy-start.1) | copy-done | bytes 524312
  42.6 6.2 %shard_map.67 = (f32[544,128]{1,0:T(8,128)}, f32[544,128]{1,0:T(8,128)}) custom-call(bf16[544,128]{1,0:T(8,128)(2,1)} %reshape.517.refs_0_, bf16[2048,128]{1,0:T(8,128)(2,1)} %copy-done.1, bf16[2048,128]{1,0:T(8,128)(2,1)} %pad.13.refs_2_, f32[544,128]{1,0:T(8,128)} %get-tuple-element.26.refs_3_, f32[544,128]{1,0:T(8,128)} %get-tuple-element.27.refs_4_, ...), custom_call_target="tpu_custom_call" | custom-call | tf_op jit(solution)/shard_map/pallas_call | solution.py:113
  48.7 1.4 %slice_reduce_fusion.1 = (f32[544]{0:T(1024)S(1)}, f32[544]{0:T(1024)S(1)}) fusion(f32[544,128]{1,0:T(8,128)} %get-tuple-element.29), kind=kLoop, calls=%fused_computation.9 | loop fusion | bytes 8704 | tf_op jit(solution)/shard_map/slice | solution.py:143
  50.7 0.1 select_bitcast_fusion
  51.1 0.6 %copy-done.10 = pred[8,9]{0,1:T(8,128)(4,1)S(1)} copy-done((pred[8,9]{0,1:T(8,128)(4,1)S(1)}, pred[8,9]{0,1:T(8,128)(4,1)}, u32[]{:S(2)}) %copy-start.10) | copy-done | bytes 96
  51.7 0.9 %convolution_select_fusion = f32[6,8,9,128]{3,1,2,0:T(8,128)S(1)} fusion(bf16[3,3,128,128]{3,2,1,0:T(8,128)(2,1)S(1)} %copy-done, f32[8,1,7,2,128]{4,2,3,0,1:T(8,128)S(1)} %slice.56, f32[8,1,8,9,128]{4,2,3,0,1:T(8,128)S(1)} %copy.25, pred[8,9]{0,1:T(8,128)(4,1)S(1)} %copy-done.10), kind=kOutput, calls=%fused_computation | convolution fusion | flops 764737536 | bytes 868424 | tf_op jit(solution)/shard_map/conv_general_dilated | solution.py:167
  52.7 0.1 copy.27
  52.8 0.1 copy.28
  52.9 0.7 %copy-done.7 = f32[128]{0:T(128)S(1)} copy-done((f32[128]{0:T(128)S(1)}, f32[128]{0:T(128)}, u32[]{:S(2)}) %copy-start.7) | copy-done | bytes 536
  53.6 0.3 select_bitcast_fusion.1
  54.0 0.6 %copy-done.8 = bf16[2,3,3,128]{3,0,2,1:T(2,128)(2,1)S(1)} copy-done((bf16[2,3,3,128]{3,0,2,1:T(2,128)(2,1)S(1)}, bf16[2,3,3,128]{3,0,2,1:T(2,128)(2,1)}, u32[]{:S(2)}) %copy-start.8) | copy-done | bytes 4632
  54.6 1.7 %convolution_select_fusion.1 = f32[4,8,9,2]{1,3,2,0:T(2,128)S(1)} fusion(bf16[2,3,3,128]{3,0,2,1:T(2,128)(2,1)S(1)} %copy-done.8, bf16[6,1,7,2,128]{4,2,3,0,1:T(8,128)(2,1)S(1)} %slice.58, bf16[6,1,8,9,128]{4,2,3,0,1:T(8,128)(2,1)S(1)} %copy.30, pred[8,9]{0,1:T(8,128)(4,1)S(1)} %copy-done.9), kind=kOutput, calls=%fused_computation.1 | convolution fusion | flops 1733184 | bytes 139080 | tf_op jit(solution)/shard_map/conv_general_dilated | solution.py:178
  56.3 0.1 copy.33
  56.5 0.1 reshape.544
  56.6 0.6 %fusion.25 = f32[2,4,64]{2,1,0:T(4,128)} fusion(f32[4,1,72,2]{2,0,3,1:T(4,128)S(1)} %reshape.544, f32[1,4,64]{2,1,0:T(4,128)S(1)} %slice_bitcast_fusion.2, f32[1,4,64]{2,1,0:T(4,128)S(1)} %slice_bitcast_fusion.3), kind=kLoop, calls=%fused_computation.73 | loop fusion | flops 1024 | bytes 6144 | tf_op jit(solution)/shard_map/add | solution.py:184
  (53 shorter events, 1.4 us)
Async XLA Ops:
  0.0 51.1 %copy-start = (bf16[3,3,128,128]{3,2,1,0:T(8,128)(2,1)S(1)}, bf16[3,3,128,128]{3,2,1,0:T(8,128)(2,1)}, u32[]{:S(2)}) copy-start(bf16[3,3,128,128]{3,2,1,0:T(8,128)(2,1)} %param.8) | copy-start | bytes 884740
  0.8 5.2 %collective-permute-start = (bf16[4,2,128]{2,1,0:T(2,128)(2,1)S(1)}, bf16[4,2,128]{2,1,0:T(2,128)(2,1)S(1)}, u32[]{:S(2)}, u32[]{:S(2)}) collective-permute-start(bf16[4,2,128]{2,1,0:T(2,128)(2,1)S(1)} %get-tuple-element.35), channel_id=1, source_target_pairs={{0,1},{1,2},{2,3},{4,5},{5,6},{6,7},{8,9},{9,10},{10,11},{12,13},{... | collective-permute-start | bytes 6152 | tf_op jit(solution)/shard_map/ppermute | solution.py:19
  3.1 5.2 %collective-permute-start.1 = (bf16[4,2,128]{2,1,0:T(2,128)(2,1)S(1)}, bf16[4,2,128]{2,1,0:T(2,128)(2,1)S(1)}, u32[]{:S(2)}, u32[]{:S(2)}) collective-permute-start(bf16[4,2,128]{2,1,0:T(2,128)(2,1)S(1)} %get-tuple-element.36), channel_id=1, source_target_pairs={{1,0},{2,1},{3,2},{5,4},{6,5},{7,6},{9,8},{10,9},{11,10},{13,12},{... | collective-permute-start | bytes 6152 | tf_op jit(solution)/shard_map/ppermute | solution.py:22
  4.8 3.5 %copy-start.5 = (bf16[4,64,128]{2,1,0:T(8,128)(2,1)S(1)}, bf16[4,64,128]{2,1,0:T(8,128)(2,1)}, u32[]{:S(2)}) copy-start(bf16[4,64,128]{2,1,0:T(8,128)(2,1)} %param.6) | copy-start | bytes 196612
  5.2 0.7 %copy-start.6 = (f32[2,128]{1,0:T(2,128)S(1)}, f32[2,128]{1,0:T(2,128)}, u32[]{:S(2)}) copy-start(f32[2,128]{1,0:T(2,128)} %param.9) | copy-start | bytes 3076
  8.3 20.8 %collective-permute-start.6 = (bf16[2048,128]{1,0:T(8,128)(2,1)}, bf16[2048,128]{1,0:T(8,128)(2,1)S(1)}, u32[]{:S(2)}, u32[]{:S(2)}) collective-permute-start(bf16[2048,128]{1,0:T(8,128)(2,1)} %refs_1_), channel_id=1, source_target_pairs={{0,1},{1,2},{2,3},{3,0},{4,5},{5,6},{6,7},{7,4},{8,9},{9,10},{10,1... | collective-permute-start | bytes 1572872 | tf_op jit(solution)/shard_map/ppermute | solution.py:136
  10.7 24.7 %collective-permute-start.5 = (bf16[2048,128]{1,0:T(8,128)(2,1)}, bf16[2048,128]{1,0:T(8,128)(2,1)S(1)}, u32[]{:S(2)}, u32[]{:S(2)}) collective-permute-start(bf16[2048,128]{1,0:T(8,128)(2,1)} %refs_1_), channel_id=1, source_target_pairs={{0,2},{1,3},{2,0},{3,1},{4,6},{5,7},{6,4},{7,5},{8,10},{9,11},{10,... | collective-permute-start | bytes 1572872 | tf_op jit(solution)/shard_map/ppermute | solution.py:136
  11.0 30.7 %collective-permute-start.4 = (bf16[2048,128]{1,0:T(8,128)(2,1)}, bf16[2048,128]{1,0:T(8,128)(2,1)S(1)}, u32[]{:S(2)}, u32[]{:S(2)}) collective-permute-start(bf16[2048,128]{1,0:T(8,128)(2,1)} %refs_1_), channel_id=1, source_target_pairs={{0,3},{1,0},{2,1},{3,2},{4,7},{5,4},{6,5},{7,6},{8,11},{9,8},{10,9... | collective-permute-start | bytes 1572872 | tf_op jit(solution)/shard_map/ppermute | solution.py:136
  12.4 10.2 %collective-permute-start.2 = (bf16[2,68,128]{2,1,0:T(8,128)(2,1)S(1)}, bf16[2,68,128]{2,1,0:T(8,128)(2,1)S(1)}, u32[]{:S(2)}, u32[]{:S(2)}) collective-permute-start(bf16[2,68,128]{2,1,0:T(8,128)(2,1)S(1)} %get-tuple-element.33), channel_id=1, source_target_pairs={{0,4},{4,8},{8,12},{12,16},{16,20},{20,24},{24,28},{1,5},{5,9},{9,... | collective-permute-start | bytes 104456 | tf_op jit(solution)/shard_map/ppermute | solution.py:19
  15.9 6.7 %collective-permute-start.3 = (bf16[2,68,128]{2,1,0:T(8,128)(2,1)S(1)}, bf16[2,68,128]{2,1,0:T(8,128)(2,1)S(1)}, u32[]{:S(2)}, u32[]{:S(2)}) collective-permute-start(bf16[2,68,128]{2,1,0:T(8,128)(2,1)S(1)} %get-tuple-element.34), channel_id=1, source_target_pairs={{4,0},{8,4},{12,8},{16,12},{20,16},{24,20},{28,24},{5,1},{9,5},{13... | collective-permute-start | bytes 104456 | tf_op jit(solution)/shard_map/ppermute | solution.py:22
  29.1 0.8 %copy-start.3 = (bf16[2048,128]{1,0:T(8,128)(2,1)}, bf16[2048,128]{1,0:T(8,128)(2,1)S(1)}, u32[]{:S(2)}) copy-start(bf16[2048,128]{1,0:T(8,128)(2,1)S(1)} %collective-permute-done.6.refs_1_) | copy-start | bytes 1572868
  35.4 0.8 %copy-start.2 = (bf16[2048,128]{1,0:T(8,128)(2,1)}, bf16[2048,128]{1,0:T(8,128)(2,1)S(1)}, u32[]{:S(2)}) copy-start(bf16[2048,128]{1,0:T(8,128)(2,1)S(1)} %collective-permute-done.5.refs_1_) | copy-start | bytes 1572868
  41.7 0.8 %copy-start.1 = (bf16[2048,128]{1,0:T(8,128)(2,1)}, bf16[2048,128]{1,0:T(8,128)(2,1)S(1)}, u32[]{:S(2)}) copy-start(bf16[2048,128]{1,0:T(8,128)(2,1)S(1)} %collective-permute-done.4.refs_1_) | copy-start | bytes 1572868
  48.7 1.9 %copy-start.4 = (f32[544,128]{1,0:T(8,128)S(1)}, f32[544,128]{1,0:T(8,128)}, u32[]{:S(2)}) copy-start(f32[544,128]{1,0:T(8,128)} %get-tuple-element.30) | copy-start | bytes 835588
  51.0 0.7 %copy-start.10 = (pred[8,9]{0,1:T(8,128)(4,1)S(1)}, pred[8,9]{0,1:T(8,128)(4,1)}, u32[]{:S(2)}) copy-start(pred[8,9]{0,1:T(8,128)(4,1)} %constant.155) | copy-start | bytes 220
  52.9 0.7 %copy-start.7 = (f32[128]{0:T(128)S(1)}, f32[128]{0:T(128)}, u32[]{:S(2)}) copy-start(f32[128]{0:T(128)} %param.10) | copy-start | bytes 1540
  53.9 0.7 %copy-start.8 = (bf16[2,3,3,128]{3,0,2,1:T(2,128)(2,1)S(1)}, bf16[2,3,3,128]{3,0,2,1:T(2,128)(2,1)}, u32[]{:S(2)}) copy-start(bf16[2,3,3,128]{3,0,2,1:T(2,128)(2,1)} %param.11) | copy-start | bytes 13828
  54.0 0.7 %copy-start.9 = (pred[8,9]{0,1:T(8,128)(4,1)S(1)}, pred[8,9]{0,1:T(8,128)(4,1)}, u32[]{:S(2)}) copy-start(pred[8,9]{0,1:T(8,128)(4,1)} %constant.154) | copy-start | bytes 220

commit v4 on v3

--- a/solution.py
+++ b/solution.py
@@ -51,13 +51,13 @@
         acc = acc_ref[...] * alpha + acc
         st = st_ref[...] * alpha + st
     if last:
-        warped_ref, flow_ref = outs
+        (out_ref,) = outs
         total = st[:, 0:1]
-        warped_ref[...] = acc / total
+        out_ref[:, 0:chans] = acc / total
         fx = (st[:, 1:2] + st[:, 2:3]) / total
         fy = (st[:, 3:4] + st[:, 4:5]) / total
-        lane = lax.broadcasted_iota(jnp.int32, flow_ref.shape, 1)
-        flow_ref[...] = jnp.where(lane == 0, fx, jnp.where(lane == 1, fy, 0.0))
+        lane = lax.broadcasted_iota(jnp.int32, (st.shape[0], 128), 1)
+        out_ref[:, chans:] = jnp.where(lane == 0, fx, jnp.where(lane == 1, fy, 0.0))
     else:
         m_out, acc_out, st_out = outs
         m_out[...] = jnp.broadcast_to(peak, m_out.shape)
@@ -71,13 +71,16 @@
 
 
 def positions(count, offset, width):
-    index = offset + jnp.arange(count, dtype=jnp.int32)
+    index = offset + jnp.arange(count, dtype=jnp.int32)[:, None]
     col_hi, col_lo = split_bf16((index % width).astype(jnp.float32) / width)
     row_hi, row_lo = split_bf16((index // width).astype(jnp.float32) / width)
-    cols = jnp.stack(
-        [jnp.ones((count,), jnp.bfloat16), col_hi, col_lo, row_hi, row_lo], axis=1
-    )
-    return jnp.pad(cols, ((0, 0), (0, 128 - cols.shape[1])))
+    lane = jnp.arange(128, dtype=jnp.int32)[None, :]
+    zero = jnp.zeros((), jnp.bfloat16)
+    pos = jnp.where(lane == 4, row_lo, zero)
+    pos = jnp.where(lane == 3, row_hi, pos)
+    pos = jnp.where(lane == 2, col_lo, pos)
+    pos = jnp.where(lane == 1, col_hi, pos)
+    return jnp.where(lane == 0, jnp.ones((), jnp.bfloat16), pos)
 
 
 def match_step(queries, keys, pos, state, tq, first, last):
@@ -98,11 +101,8 @@
         in_specs += [row_spec(128), row_spec(chans), row_spec(128)]
         args += list(state)
     if last:
-        out_specs = [row_spec(chans), row_spec(128)]
-        out_shape = [
-            jax.ShapeDtypeStruct((padded, chans), jnp.float32),
-            jax.ShapeDtypeStruct((padded, 128), jnp.float32),
-        ]
+        out_specs = [row_spec(chans + 128)]
+        out_shape = [jax.ShapeDtypeStruct((padded, chans + 128), jnp.float32)]
     else:
         out_specs = [row_spec(128), row_spec(chans), row_spec(128)]
         out_shape = [
@@ -139,8 +139,8 @@
     for step, (keys, owner) in enumerate(shards):
         pos = positions(tk, owner * tk, width)
         state = match_step(queries, keys, pos, state, tq, step == 0, step == n - 1)
-    warped, flow = state
-    return warped[:count], flow[:count, 0], flow[:count, 1]
+    (out,) = state
+    return out[:count]
 
 
 def local(source, targets, conv_in, flow_proj, in_bias, conv_out):
@@ -149,20 +149,17 @@
     width = cols * lax.axis_size("match")
     row_first = lax.axis_index("space") * rows
     col_first = lax.axis_index("match") * cols
-    ext = extended(source, (("match", 1),), HALO)
-    targets, ext = lax.optimization_barrier((targets, ext))
-    ext = extended(ext, (("space", 0),), HALO)
+    out = match(source.reshape(rows * cols, chans), targets, width)
+    ext = extended(out.reshape(rows, cols, out.shape[1]), (("match", 1), ("space", 0)), HALO)
     erows, ecols = rows + 2 * HALO, cols + 2 * HALO
-    warped, sum_x, sum_y = match(ext.reshape(erows * ecols, chans), targets, width)
-    warped = warped.reshape(erows, ecols, chans)
     grow = row_first - HALO + jnp.arange(erows, dtype=jnp.int32)
     gcol = col_first - HALO + jnp.arange(ecols, dtype=jnp.int32)
     inside = ((grow >= 0) & (grow < all_rows))[:, None] & ((gcol >= 0) & (gcol < width))[None, :]
-    warped = jnp.where(inside[:, :, None], warped, 0.0)
+    warped = jnp.where(inside[:, :, None], ext[:, :, 0:chans], 0.0)
     col_pos = gcol.astype(jnp.float32) / width
     row_pos = grow.astype(jnp.float32) / width
-    flow_x = sum_x.reshape(erows, ecols) - col_pos[None, :]
-    flow_y = sum_y.reshape(erows, ecols) - row_pos[:, None]
+    flow_x = ext[:, :, chans] - col_pos[None, :]
+    flow_y = ext[:, :, chans + 1] - row_pos[:, None]
 
     pre = lax.conv_general_dilated(
         warped[None], conv_in.astype(jnp.float32), (1, 1), "VALID",

time: 58.2 us -> 68.2 us (1.17)
  the two profiles are of different devices: /device:TPU:0 before, /device:TPU:1 now
where the time goes in v4:
time: 68.2 us; the launch traced here: 67.8 us
  waiting for transfers between devices  19.5 us (29%)
  Pallas kernels  14.6 us (21%)
  starting transfers between devices  12.5 us (18%)
  other arithmetic  10 us (15%)
  local copies, waits for them, and re-layouts  8.17 us (12%)
  matrix products  2.64 us (4%)
    pallas_call x4, Pallas kernels, match_step(): pl.pallas_call(kernel, grid=(nq,), in_specs=in_specs, out_specs=out_specs...  14.6 us
    select_n x2, other arithmetic, positions(): return jnp.where(lane == 0, jnp.ones((), jnp.bfloat16), pos)  7.75 us
    ppermute x2, waiting for transfers between devices, extended(): lax.ppermute(lax.slice_in_dim(block, 0, width, axis=dim), axis, backward)  7.55 us
    ppermute x2, waiting for transfers between devices, extended(): lax.ppermute(lax.slice_in_dim(block, block.shape[dim] - width, None, axis...  6.3 us
    ppermute x3, waiting for transfers between devices, match(): lax.ppermute(targets, 'match', [(j, (j + shift) % n) for j in range(n)])  5.61 us
    ppermute x2, starting transfers between devices, extended(): lax.ppermute(lax.slice_in_dim(block, block.shape[dim] - width, None, axis...  5.51 us
    unnamed x19, local copies, waits for them, and re-layouts  5.3 us
    ppermute x2, starting transfers between devices, extended(): lax.ppermute(lax.slice_in_dim(block, 0, width, axis=dim), axis, backward)  3.91 us
  transfers between devices with their start and end apart: 7, of which 5 were waited for; matrix products, arithmetic and copies ran while one was open for 12% of the time, Pallas kernels for 16%

profile of v4, /device:TPU:1, one launch (start us, length us, event | category | flops | bytes accessed | tf_op | source)
XLA Modules:
  0.0 67.8 jit_solution(15930711367979369257)
XLA Ops:
  0.0 2.6 %collective-permute-start.2 = (bf16[2048,128]{1,0:T(8,128)(2,1)}, bf16[2048,128]{1,0:T(8,128)(2,1)S(1)}, u32[]{:S(2)}, u32[]{:S(2)}) collective-permute-start(bf16[2048,128]{1,0:T(8,128)(2,1)} %refs_1_.1), channel_id=1, source_target_pairs={{0,1},{1,2},{2,3},{3,0},{4,5},{5,6},{6,7},{7,4},{8,9},{9,10},{10,1... | collective-permute-start | bytes 1572872 | tf_op jit(solution)/shard_map/ppermute | solution.py:136
  2.6 0.5 collective-permute-start
  3.4 0.7 copy-done.4
  4.1 5.2 %select_select_fusion = (bf16[2048,128]{1,0:T(8,128)(2,1)}, bf16[2048,128]{1,0:T(8,128)(2,1)}, bf16[2048,128]{1,0:T(8,128)(2,1)}) fusion(pred[128]{0:T(512)(128)(4,1)S(1)} %get-tuple-element.38, pred[128]{0:T(512)(128)(4,1)S(1)} %get-tuple-element.39, pred[128]{0:T(512)(128)(4,1)S(1)} %get-tuple-element.40, pred[128]{0:T(512)(128)(4,1)S(1)} %get-tuple-element.41, ...), kind=kLoop, calls=%fused_computation.9 | loop fusion | flops 3932160 | bytes 1622656 | tf_op jit(solution)/shard_map/jit(_where)/select_n | solution.py:83
  9.2 3.4 %shard_map.64 = (f32[256,128]{1,0:T(8,128)}, f32[256,128]{1,0:T(8,128)}, f32[256,128]{1,0:T(8,128)}) custom-call(bf16[256,128]{1,0:T(8,128)(2,1)} %bitcast.57, bf16[2048,128]{1,0:T(8,128)(2,1)} %refs_1_.1, bf16[2048,128]{1,0:T(8,128)(2,1)} %get-tuple-element.29.refs_2_), custom_call_target="tpu_custom_call" | custom-call | tf_op jit(solution)/shard_map/pallas_call | solution.py:113
  12.7 2.6 %select_select_fusion.3.refs_2_ = bf16[2048,128]{1,0:T(8,128)(2,1)} fusion(pred[128]{0:T(512)(128)(4,1)S(1)} %get-tuple-element.38, pred[128]{0:T(512)(128)(4,1)S(1)} %get-tuple-element.39, pred[128]{0:T(512)(128)(4,1)S(1)} %get-tuple-element.40, pred[128]{0:T(512)(128)(4,1)S(1)} %get-tuple-element.41, pred[128]{0:T(512)(128)(4,1)S(1)} %iota_compare_fusion.7, ...), kind=kLoop, calls=%fused_computation.12 | loop fusion | flops 1310720 | bytes 541312 | tf_op jit(solution)/shard_map/jit(_where)/select_n | solution.py:83
  15.2 0.8 %copy-done.3 = bf16[2048,128]{1,0:T(8,128)(2,1)} copy-done((bf16[2048,128]{1,0:T(8,128)(2,1)}, bf16[2048,128]{1,0:T(8,128)(2,1)S(1)}, u32[]{:S(2)}) %copy-start.3) | copy-done | bytes 524312
  16.0 3.7 %shard_map.65 = (f32[256,128]{1,0:T(8,128)}, f32[256,128]{1,0:T(8,128)}, f32[256,128]{1,0:T(8,128)}) custom-call(bf16[256,128]{1,0:T(8,128)(2,1)} %bitcast.58, bf16[2048,128]{1,0:T(8,128)(2,1)} %copy-done.3, bf16[2048,128]{1,0:T(8,128)(2,1)} %get-tuple-element.31.refs_2_, f32[256,128]{1,0:T(8,128)} %get-tuple-element.14.refs_3_, ...), custom_call_target="tpu_custom_call" | custom-call | tf_op jit(solution)/shard_map/pallas_call | solution.py:113
  19.7 5.6 %collective-permute-done.1.refs_1_ = bf16[2048,128]{1,0:T(8,128)(2,1)S(1)} collective-permute-done((bf16[2048,128]{1,0:T(8,128)(2,1)}, bf16[2048,128]{1,0:T(8,128)(2,1)S(1)}, u32[]{:S(2)}, u32[]{:S(2)}) %collective-permute-start.1) | collective-permute-done | bytes 524320 | tf_op jit(solution)/shard_map/ppermute | solution.py:136
  25.3 0.8 %copy-done.2 = bf16[2048,128]{1,0:T(8,128)(2,1)} copy-done((bf16[2048,128]{1,0:T(8,128)(2,1)}, bf16[2048,128]{1,0:T(8,128)(2,1)S(1)}, u32[]{:S(2)}) %copy-start.2) | copy-done | bytes 524312
  26.1 3.7 %shard_map.66 = (f32[256,128]{1,0:T(8,128)}, f32[256,128]{1,0:T(8,128)}, f32[256,128]{1,0:T(8,128)}) custom-call(bf16[256,128]{1,0:T(8,128)(2,1)} %bitcast.59, bf16[2048,128]{1,0:T(8,128)(2,1)} %copy-done.2, bf16[2048,128]{1,0:T(8,128)(2,1)} %get-tuple-element.30.refs_2_, f32[256,128]{1,0:T(8,128)} %get-tuple-element.17.refs_3_, ...), custom_call_target="tpu_custom_call" | custom-call | tf_op jit(solution)/shard_map/pallas_call | solution.py:113
  29.8 0.8 %copy-done.1 = bf16[2048,128]{1,0:T(8,128)(2,1)} copy-done((bf16[2048,128]{1,0:T(8,128)(2,1)}, bf16[2048,128]{1,0:T(8,128)(2,1)S(1)}, u32[]{:S(2)}) %copy-start.1) | copy-done | bytes 524312
  30.6 3.9 %shard_map.67 = f32[256,256]{1,0:T(8,128)} custom-call(bf16[256,128]{1,0:T(8,128)(2,1)} %bitcast.60, bf16[2048,128]{1,0:T(8,128)(2,1)} %copy-done.1, bf16[2048,128]{1,0:T(8,128)(2,1)} %select_select_fusion.3.refs_2_, f32[256,128]{1,0:T(8,128)} %get-tuple-element.20.refs_3_, f32[256,128]{1,0:T(8,128)} %get-tuple-element.21.refs_4_, ...), custom_call_target="tpu_custom_call" | custom-call | tf_op jit(solution)/shard_map/pallas_call | solution.py:113
  34.5 1.2 %copy.22 = f32[4,64,256]{1,0,2:T(4,128)S(1)} copy(f32[4,64,256]{2,1,0:T(8,128)} %bitcast.61) | data formatting | bytes 524288 | tf_op jit(solution)/shard_map/reshape | solution.py:153
  35.7 0.3 fusion.73
  36.0 1.9 %collective-permute-start.3 = (f32[4,2,256]{1,0,2:T(4,128)S(1)}, f32[4,2,256]{1,0,2:T(4,128)S(1)}, u32[]{:S(2)}, u32[]{:S(2)}) collective-permute-start(f32[4,2,256]{1,0,2:T(4,128)S(1)} %get-tuple-element.27), channel_id=1, source_target_pairs={{0,1},{1,2},{2,3},{4,5},{5,6},{6,7},{8,9},{9,10},{10,11},{12,13},{... | collective-permute-start | bytes 24584 | tf_op jit(solution)/shard_map/ppermute | solution.py:19
  37.9 2.4 %collective-permute-start.4 = (f32[4,2,256]{1,0,2:T(4,128)S(1)}, f32[4,2,256]{1,0,2:T(4,128)S(1)}, u32[]{:S(2)}, u32[]{:S(2)}) collective-permute-start(f32[4,2,256]{1,0,2:T(4,128)S(1)} %get-tuple-element.28), channel_id=1, source_target_pairs={{1,0},{2,1},{3,2},{5,4},{6,5},{7,6},{9,8},{10,9},{11,10},{13,12},{... | collective-permute-start | bytes 24584 | tf_op jit(solution)/shard_map/ppermute | solution.py:22
  40.4 0.1 broadcast_and_fusion
  40.5 3.6 %collective-permute-done.3 = f32[4,2,256]{1,0,2:T(4,128)S(1)} collective-permute-done((f32[4,2,256]{1,0,2:T(4,128)S(1)}, f32[4,2,256]{1,0,2:T(4,128)S(1)}, u32[]{:S(2)}, u32[]{:S(2)}) %collective-permute-start.3) | collective-permute-done | bytes 8224 | tf_op jit(solution)/shard_map/ppermute | solution.py:19
  44.0 4.9 %collective-permute-done.4 = f32[4,2,256]{1,0,2:T(4,128)S(1)} collective-permute-done((f32[4,2,256]{1,0,2:T(4,128)S(1)}, f32[4,2,256]{1,0,2:T(4,128)S(1)}, u32[]{:S(2)}, u32[]{:S(2)}) %collective-permute-start.4) | collective-permute-done | bytes 8224 | tf_op jit(solution)/shard_map/ppermute | solution.py:22
  48.9 0.6 pad_maximum_fusion.4
  49.5 0.2 fusion.72
  49.7 3.6 %collective-permute-start.5 = (f32[2,68,256]{1,0,2:T(2,128)S(1)}, f32[2,68,256]{1,0,2:T(2,128)S(1)}, u32[]{:S(2)}, u32[]{:S(2)}) collective-permute-start(f32[2,68,256]{1,0,2:T(2,128)S(1)} %get-tuple-element.25), channel_id=1, source_target_pairs={{0,4},{4,8},{8,12},{12,16},{16,20},{20,24},{24,28},{1,5},{5,9},{9,... | collective-permute-start | bytes 417800 | tf_op jit(solution)/shard_map/ppermute | solution.py:19
  53.3 1.5 %collective-permute-start.6 = (f32[2,68,256]{1,0,2:T(2,128)S(1)}, f32[2,68,256]{1,0,2:T(2,128)S(1)}, u32[]{:S(2)}, u32[]{:S(2)}) collective-permute-start(f32[2,68,256]{1,0,2:T(2,128)S(1)} %get-tuple-element.26), channel_id=1, source_target_pairs={{4,0},{8,4},{12,8},{16,12},{20,16},{24,20},{28,24},{5,1},{9,5},{13... | collective-permute-start | bytes 417800 | tf_op jit(solution)/shard_map/ppermute | solution.py:22
  54.8 0.1 slice.50
  54.9 0.1 copy.25
  55.0 2.7 %collective-permute-done.5 = f32[2,68,256]{1,0,2:T(2,128)S(1)} collective-permute-done((f32[2,68,256]{1,0,2:T(2,128)S(1)}, f32[2,68,256]{1,0,2:T(2,128)S(1)}, u32[]{:S(2)}, u32[]{:S(2)}) %collective-permute-start.5) | collective-permute-done | bytes 139296 | tf_op jit(solution)/shard_map/ppermute | solution.py:19
  57.7 2.7 %collective-permute-done.6 = f32[2,68,256]{1,0,2:T(2,128)S(1)} collective-permute-done((f32[2,68,256]{1,0,2:T(2,128)S(1)}, f32[2,68,256]{1,0,2:T(2,128)S(1)}, u32[]{:S(2)}, u32[]{:S(2)}) %collective-permute-start.6) | collective-permute-done | bytes 139296 | tf_op jit(solution)/shard_map/ppermute | solution.py:22
  60.4 0.1 fusion.57
  60.5 0.1 slice.54
  60.6 0.1 slice_bitcast_fusion.2
  60.7 0.1 slice.52
  60.7 0.1 slice_bitcast_fusion.3
  60.8 0.4 fusion.1
  61.3 0.3 copy.38
  61.5 0.1 copy.28
  61.6 0.6 copy-done.8
  62.3 0.9 %convolution_select_fusion = f32[6,8,9,128]{3,1,2,0:T(8,128)S(1)} fusion(bf16[3,3,128,128]{3,2,1,0:T(8,128)(2,1)S(1)} %copy-done, f32[8,1,7,2,128]{4,2,3,0,1:T(8,128)S(1)} %slice.64, f32[8,1,8,9,128]{4,2,3,0,1:T(8,128)S(1)} %copy.28, pred[8,9]{0,1:T(8,128)(4,1)S(1)} %copy-done.8), kind=kOutput, calls=%fused_computation | convolution fusion | flops 764737536 | bytes 868424 | tf_op jit(solution)/shard_map/conv_general_dilated | solution.py:164
  63.2 0.1 copy.29
  63.3 0.1 copy.30
  63.4 0.1 copy.31
  63.5 0.7 copy-done.5
  64.2 0.3 select_bitcast_fusion
  64.6 0.6 copy-done.6
  65.2 1.7 %convolution_select_fusion.1 = f32[4,8,9,2]{1,3,2,0:T(2,128)S(1)} fusion(bf16[2,3,3,128]{3,0,2,1:T(2,128)(2,1)S(1)} %copy-done.6, bf16[6,1,7,2,128]{4,2,3,0,1:T(8,128)(2,1)S(1)} %slice.66, bf16[6,1,8,9,128]{4,2,3,0,1:T(8,128)(2,1)S(1)} %copy.33, pred[8,9]{0,1:T(8,128)(4,1)S(1)} %copy-done.7), kind=kOutput, calls=%fused_computation.1 | convolution fusion | flops 1733184 | bytes 139080 | tf_op jit(solution)/shard_map/conv_general_dilated | solution.py:175
  66.9 0.1 copy.36
  67.1 0.1 reshape.448
  67.2 0.6 fusion.55
  (35 shorter events, 0.3 us)
Async XLA Ops:
  0.0 61.6 %copy-start = (bf16[3,3,128,128]{3,2,1,0:T(8,128)(2,1)S(1)}, bf16[3,3,128,128]{3,2,1,0:T(8,128)(2,1)}, u32[]{:S(2)}) copy-start(bf16[3,3,128,128]{3,2,1,0:T(8,128)(2,1)} %param.8) | copy-start | bytes 884740
  0.0 15.2 %collective-permute-start.2 = (bf16[2048,128]{1,0:T(8,128)(2,1)}, bf16[2048,128]{1,0:T(8,128)(2,1)S(1)}, u32[]{:S(2)}, u32[]{:S(2)}) collective-permute-start(bf16[2048,128]{1,0:T(8,128)(2,1)} %refs_1_.1), channel_id=1, source_target_pairs={{0,1},{1,2},{2,3},{3,0},{4,5},{5,6},{6,7},{7,4},{8,9},{9,10},{10,1... | collective-permute-start | bytes 1572872 | tf_op jit(solution)/shard_map/ppermute | solution.py:136
  2.6 22.7 %collective-permute-start.1 = (bf16[2048,128]{1,0:T(8,128)(2,1)}, bf16[2048,128]{1,0:T(8,128)(2,1)S(1)}, u32[]{:S(2)}, u32[]{:S(2)}) collective-permute-start(bf16[2048,128]{1,0:T(8,128)(2,1)} %refs_1_.1), channel_id=1, source_target_pairs={{0,2},{1,3},{2,0},{3,1},{4,6},{5,7},{6,4},{7,5},{8,10},{9,11},{10,... | collective-permute-start | bytes 1572872 | tf_op jit(solution)/shard_map/ppermute | solution.py:136
  2.6 27.2 %collective-permute-start = (bf16[2048,128]{1,0:T(8,128)(2,1)}, bf16[2048,128]{1,0:T(8,128)(2,1)S(1)}, u32[]{:S(2)}, u32[]{:S(2)}) collective-permute-start(bf16[2048,128]{1,0:T(8,128)(2,1)} %refs_1_.1), channel_id=1, source_target_pairs={{0,3},{1,0},{2,1},{3,2},{4,7},{5,4},{6,5},{7,6},{8,11},{9,8},{10,9... | collective-permute-start | bytes 1572872 | tf_op jit(solution)/shard_map/ppermute | solution.py:136
  3.4 0.7 %copy-start.4 = (f32[2,128]{1,0:T(2,128)S(1)}, f32[2,128]{1,0:T(2,128)}, u32[]{:S(2)}) copy-start(f32[2,128]{1,0:T(2,128)} %param.9) | copy-start | bytes 3076
  15.2 0.8 %copy-start.3 = (bf16[2048,128]{1,0:T(8,128)(2,1)}, bf16[2048,128]{1,0:T(8,128)(2,1)S(1)}, u32[]{:S(2)}) copy-start(bf16[2048,128]{1,0:T(8,128)(2,1)S(1)} %collective-permute-done.2.refs_1_) | copy-start | bytes 1572868
  25.3 0.8 %copy-start.2 = (bf16[2048,128]{1,0:T(8,128)(2,1)}, bf16[2048,128]{1,0:T(8,128)(2,1)S(1)}, u32[]{:S(2)}) copy-start(bf16[2048,128]{1,0:T(8,128)(2,1)S(1)} %collective-permute-done.1.refs_1_) | copy-start | bytes 1572868
  29.8 0.8 %copy-start.1 = (bf16[2048,128]{1,0:T(8,128)(2,1)}, bf16[2048,128]{1,0:T(8,128)(2,1)S(1)}, u32[]{:S(2)}) copy-start(bf16[2048,128]{1,0:T(8,128)(2,1)S(1)} %collective-permute-done.refs_1_) | copy-start | bytes 1572868
  36.0 8.0 %collective-permute-start.3 = (f32[4,2,256]{1,0,2:T(4,128)S(1)}, f32[4,2,256]{1,0,2:T(4,128)S(1)}, u32[]{:S(2)}, u32[]{:S(2)}) collective-permute-start(f32[4,2,256]{1,0,2:T(4,128)S(1)} %get-tuple-element.27), channel_id=1, source_target_pairs={{0,1},{1,2},{2,3},{4,5},{5,6},{6,7},{8,9},{9,10},{10,11},{12,13},{... | collective-permute-start | bytes 24584 | tf_op jit(solution)/shard_map/ppermute | solution.py:19
  37.9 11.0 %collective-permute-start.4 = (f32[4,2,256]{1,0,2:T(4,128)S(1)}, f32[4,2,256]{1,0,2:T(4,128)S(1)}, u32[]{:S(2)}, u32[]{:S(2)}) collective-permute-start(f32[4,2,256]{1,0,2:T(4,128)S(1)} %get-tuple-element.28), channel_id=1, source_target_pairs={{1,0},{2,1},{3,2},{5,4},{6,5},{7,6},{9,8},{10,9},{11,10},{13,12},{... | collective-permute-start | bytes 24584 | tf_op jit(solution)/shard_map/ppermute | solution.py:22
  49.7 8.0 %collective-permute-start.5 = (f32[2,68,256]{1,0,2:T(2,128)S(1)}, f32[2,68,256]{1,0,2:T(2,128)S(1)}, u32[]{:S(2)}, u32[]{:S(2)}) collective-permute-start(f32[2,68,256]{1,0,2:T(2,128)S(1)} %get-tuple-element.25), channel_id=1, source_target_pairs={{0,4},{4,8},{8,12},{12,16},{16,20},{20,24},{24,28},{1,5},{5,9},{9,... | collective-permute-start | bytes 417800 | tf_op jit(solution)/shard_map/ppermute | solution.py:19
  53.3 7.1 %collective-permute-start.6 = (f32[2,68,256]{1,0,2:T(2,128)S(1)}, f32[2,68,256]{1,0,2:T(2,128)S(1)}, u32[]{:S(2)}, u32[]{:S(2)}) collective-permute-start(f32[2,68,256]{1,0,2:T(2,128)S(1)} %get-tuple-element.26), channel_id=1, source_target_pairs={{4,0},{8,4},{12,8},{16,12},{20,16},{24,20},{28,24},{5,1},{9,5},{13... | collective-permute-start | bytes 417800 | tf_op jit(solution)/shard_map/ppermute | solution.py:22
  61.6 0.7 %copy-start.8 = (pred[8,9]{0,1:T(8,128)(4,1)S(1)}, pred[8,9]{0,1:T(8,128)(4,1)}, u32[]{:S(2)}) copy-start(pred[8,9]{0,1:T(8,128)(4,1)} %constant.151) | copy-start | bytes 220
  63.5 0.7 copy-start.5
  64.5 0.7 %copy-start.6 = (bf16[2,3,3,128]{3,0,2,1:T(2,128)(2,1)S(1)}, bf16[2,3,3,128]{3,0,2,1:T(2,128)(2,1)}, u32[]{:S(2)}) copy-start(bf16[2,3,3,128]{3,0,2,1:T(2,128)(2,1)} %param.11) | copy-start | bytes 13828
  64.5 0.7 %copy-start.7 = (pred[8,9]{0,1:T(8,128)(4,1)S(1)}, pred[8,9]{0,1:T(8,128)(4,1)}, u32[]{:S(2)}) copy-start(pred[8,9]{0,1:T(8,128)(4,1)} %constant.150) | copy-start | bytes 220

commit v5 on v3

--- a/solution.py
+++ b/solution.py
@@ -43,9 +43,10 @@
     hi = w.astype(jnp.bfloat16)
     lo = (w - hi.astype(jnp.float32)).astype(jnp.bfloat16)
     acc = jnp.dot(hi, k_ref[...], preferred_element_type=jnp.float32)
-    st = jnp.dot(hi, pos_ref[...], preferred_element_type=jnp.float32) + jnp.dot(
-        lo, pos_ref[...], preferred_element_type=jnp.float32
-    )
+    lanes = (((1,), (1,)), ((), ()))
+    st = lax.dot_general(
+        hi, pos_ref[...], lanes, preferred_element_type=jnp.float32
+    ) + lax.dot_general(lo, pos_ref[...], lanes, preferred_element_type=jnp.float32)
     if not first:
         alpha = jnp.exp(old - peak)
         acc = acc_ref[...] * alpha + acc
@@ -74,10 +75,9 @@
     index = offset + jnp.arange(count, dtype=jnp.int32)
     col_hi, col_lo = split_bf16((index % width).astype(jnp.float32) / width)
     row_hi, row_lo = split_bf16((index // width).astype(jnp.float32) / width)
-    cols = jnp.stack(
-        [jnp.ones((count,), jnp.bfloat16), col_hi, col_lo, row_hi, row_lo], axis=1
-    )
-    return jnp.pad(cols, ((0, 0), (0, 128 - cols.shape[1])))
+    zero = jnp.zeros((count,), jnp.bfloat16)
+    one = jnp.ones((count,), jnp.bfloat16)
+    return jnp.stack([one, col_hi, col_lo, row_hi, row_lo, zero, zero, zero])
 
 
 def match_step(queries, keys, pos, state, tq, first, last):
@@ -91,11 +91,11 @@
     in_specs = [
         row_spec(chans),
         pl.BlockSpec((tk, chans), lambda i: (0, 0)),
-        pl.BlockSpec((tk, 128), lambda i: (0, 0)),
+        pl.BlockSpec((8, tk), lambda i: (0, 0)),
     ]
     args = [queries, keys, pos]
     if not first:
-        in_specs += [row_spec(128), row_spec(chans), row_spec(128)]
+        in_specs += [row_spec(128), row_spec(chans), row_spec(8)]
         args += list(state)
     if last:
         out_specs = [row_spec(chans), row_spec(128)]
@@ -104,11 +104,11 @@
             jax.ShapeDtypeStruct((padded, 128), jnp.float32),
         ]
     else:
-        out_specs = [row_spec(128), row_spec(chans), row_spec(128)]
+        out_specs = [row_spec(128), row_spec(chans), row_spec(8)]
         out_shape = [
             jax.ShapeDtypeStruct((padded, 128), jnp.float32),
             jax.ShapeDtypeStruct((padded, chans), jnp.float32),
-            jax.ShapeDtypeStruct((padded, 128), jnp.float32),
+            jax.ShapeDtypeStruct((padded, 8), jnp.float32),
         ]
     return pl.pallas_call(
         kernel,

time: 58.2 us -> 56.1 us (0.964); the launches traced: 57.2 us -> 55.7 us
  local copies, waits for them, and re-layouts: 14.5 us -> 12.1 us
  waiting for transfers between devices: 2.29 us -> 3.79 us
  Pallas kernels: 23 us -> 22.4 us
    pad x4 -> x0, local copies, waits for them, and re-layouts: 3.64 us -> none  [positions(): return jnp.pad(cols, ((0, 0), (0, 128 - cols.shape[1])))]
    ppermute x2, waiting for transfers between devices: 2.27 us -> 3.77 us  [extended(): lax.ppermute(lax.slice_in_dim(block, 0, width, axis=dim), axis, backward)]
    another operation x9 -> x7, local copies, waits for them, and re-layouts: 1.55 us -> 2.81 us  [the longest x4 2.79 us: positions(): return jnp.stack([one, col_hi, col_lo, row_hi, row_lo, zero, zero, zero])]
    pallas_call x4, Pallas kernels: 23 us -> 22.4 us  [match_step(): pl.pallas_call(kernel, grid=(nq,), in_specs=in_specs, out_specs=out_specs...]
  transfers between devices with their start and end apart: 7 -> 7, of which waited for: 1 -> 2; matrix products, arithmetic and copies ran while one was open for 12% -> 8% of each run, Pallas kernels for 29% -> 29%
where the time goes in v5:
time: 56.1 us; the launch traced here: 55.7 us
  Pallas kernels  22.4 us (40%)
  starting transfers between devices  12.5 us (22%)
  local copies, waits for them, and re-layouts  12.1 us (22%)
  waiting for transfers between devices  3.79 us (7%)
  matrix products  2.64 us (5%)
  other arithmetic  1.94 us (3%)
    pallas_call x4, Pallas kernels, match_step(): pl.pallas_call(kernel, grid=(nq,), in_specs=in_specs, out_specs=out_specs...  22.4 us
    ppermute x2, starting transfers between devices, extended(): lax.ppermute(lax.slice_in_dim(block, block.shape[dim] - width, None, axis...  5.77 us
    unnamed x23, local copies, waits for them, and re-layouts  5.14 us
    ppermute x3, starting transfers between devices, match(): lax.ppermute(targets, 'match', [(j, (j + shift) % n) for j in range(n)])  4.11 us
    ppermute x2, waiting for transfers between devices, extended(): lax.ppermute(lax.slice_in_dim(block, 0, width, axis=dim), axis, backward)  3.77 us
    another operation x4, local copies, waits for them, and re-layouts, positions(): return jnp.stack([one, col_hi, col_lo, row_hi, row_lo, zero, zero, zero])  2.79 us
    ppermute x2, starting transfers between devices, extended(): lax.ppermute(lax.slice_in_dim(block, 0, width, axis=dim), axis, backward)  2.58 us
    conv_general_dilated x1, matrix products, local(): lax.conv_general_dilated(hidden[None], jnp.transpose(conv_out, (1, 2, 3,...  1.7 us
  transfers between devices with their start and end apart: 7, of which 2 were waited for; matrix products, arithmetic and copies ran while one was open for 8% of the time, Pallas kernels for 29%

profile of v5, /device:TPU:0, one launch (start us, length us, event | category | flops | bytes accessed | tf_op | source)
XLA Modules:
  0.0 55.7 jit_solution(1612027475044359987)
XLA Ops:
  0.0 0.8 %fusion.41 = (bf16[4,2,128]{2,1,0:T(2,128)(2,1)S(1)}, bf16[4,2,128]{2,1,0:T(2,128)(2,1)S(1)}) fusion(bf16[4,64,128]{2,1,0:T(8,128)(2,1)} %param.6), kind=kLoop, calls=%fused_computation.102 | loop fusion | bytes 8192 | tf_op jit(solution)/shard_map/slice | solution.py:20
  0.8 2.3 %collective-permute-start = (bf16[4,2,128]{2,1,0:T(2,128)(2,1)S(1)}, bf16[4,2,128]{2,1,0:T(2,128)(2,1)S(1)}, u32[]{:S(2)}, u32[]{:S(2)}) collective-permute-start(bf16[4,2,128]{2,1,0:T(2,128)(2,1)S(1)} %get-tuple-element.35), channel_id=1, source_target_pairs={{0,1},{1,2},{2,3},{4,5},{5,6},{6,7},{8,9},{9,10},{10,11},{12,13},{... | collective-permute-start | bytes 6152 | tf_op jit(solution)/shard_map/ppermute | solution.py:19
  3.1 1.3 %collective-permute-start.1 = (bf16[4,2,128]{2,1,0:T(2,128)(2,1)S(1)}, bf16[4,2,128]{2,1,0:T(2,128)(2,1)S(1)}, u32[]{:S(2)}, u32[]{:S(2)}) collective-permute-start(bf16[4,2,128]{2,1,0:T(2,128)(2,1)S(1)} %get-tuple-element.36), channel_id=1, source_target_pairs={{1,0},{2,1},{3,2},{5,4},{6,5},{7,6},{9,8},{10,9},{11,10},{13,12},{... | collective-permute-start | bytes 6152 | tf_op jit(solution)/shard_map/ppermute | solution.py:22
  4.4 0.1 subtract_convert_fusion.2
  4.5 0.1 fusion.27
  4.6 0.1 subtract_convert_fusion
  4.7 0.1 fusion.28
  4.8 0.1 subtract_convert_fusion.4
  4.9 0.1 fusion.26
  5.0 0.1 subtract_convert_fusion.6
  5.1 0.1 fusion.32
  5.3 0.7 %copy-done.6 = f32[2,128]{1,0:T(2,128)S(1)} copy-done((f32[2,128]{1,0:T(2,128)S(1)}, f32[2,128]{1,0:T(2,128)}, u32[]{:S(2)}) %copy-start.6) | copy-done | bytes 1048
  6.0 2.3 %collective-permute-done.1 = bf16[4,2,128]{2,1,0:T(2,128)(2,1)S(1)} collective-permute-done((bf16[4,2,128]{2,1,0:T(2,128)(2,1)S(1)}, bf16[4,2,128]{2,1,0:T(2,128)(2,1)S(1)}, u32[]{:S(2)}, u32[]{:S(2)}) %collective-permute-start.1) | collective-permute-done | bytes 2080 | tf_op jit(solution)/shard_map/ppermute | solution.py:22
  8.3 2.4 %collective-permute-start.6 = (bf16[2048,128]{1,0:T(8,128)(2,1)}, bf16[2048,128]{1,0:T(8,128)(2,1)S(1)}, u32[]{:S(2)}, u32[]{:S(2)}) collective-permute-start(bf16[2048,128]{1,0:T(8,128)(2,1)} %refs_1_), channel_id=1, source_target_pairs={{0,1},{1,2},{2,3},{3,0},{4,5},{5,6},{6,7},{7,4},{8,9},{9,10},{10,1... | collective-permute-start | bytes 1572872 | tf_op jit(solution)/shard_map/ppermute | solution.py:136
  10.7 0.3 collective-permute-start.5
  11.0 1.4 %collective-permute-start.4 = (bf16[2048,128]{1,0:T(8,128)(2,1)}, bf16[2048,128]{1,0:T(8,128)(2,1)S(1)}, u32[]{:S(2)}, u32[]{:S(2)}) collective-permute-start(bf16[2048,128]{1,0:T(8,128)(2,1)} %refs_1_), channel_id=1, source_target_pairs={{0,3},{1,0},{2,1},{3,2},{4,7},{5,4},{6,5},{7,6},{8,11},{9,8},{10,9... | collective-permute-start | bytes 1572872 | tf_op jit(solution)/shard_map/ppermute | solution.py:136
  12.4 3.4 %collective-permute-start.2 = (bf16[2,68,128]{2,1,0:T(8,128)(2,1)S(1)}, bf16[2,68,128]{2,1,0:T(8,128)(2,1)S(1)}, u32[]{:S(2)}, u32[]{:S(2)}) collective-permute-start(bf16[2,68,128]{2,1,0:T(8,128)(2,1)S(1)} %get-tuple-element.33), channel_id=1, source_target_pairs={{0,4},{4,8},{8,12},{12,16},{16,20},{20,24},{24,28},{1,5},{5,9},{9,... | collective-permute-start | bytes 104456 | tf_op jit(solution)/shard_map/ppermute | solution.py:19
  15.9 1.3 %collective-permute-start.3 = (bf16[2,68,128]{2,1,0:T(8,128)(2,1)S(1)}, bf16[2,68,128]{2,1,0:T(8,128)(2,1)S(1)}, u32[]{:S(2)}, u32[]{:S(2)}) collective-permute-start(bf16[2,68,128]{2,1,0:T(8,128)(2,1)S(1)} %get-tuple-element.34), channel_id=1, source_target_pairs={{4,0},{8,4},{12,8},{16,12},{20,16},{24,20},{28,24},{5,1},{9,5},{13... | collective-permute-start | bytes 104456 | tf_op jit(solution)/shard_map/ppermute | solution.py:22
  17.2 0.1 slice.47
  17.3 0.1 copy.7
  17.4 0.7 %stack.16.refs_2_ = bf16[8,2048]{1,0:T(8,128)(2,1)} concatenate(bf16[1,2048]{1,0:T(2,128)(2,1)S(1)} %broadcast.804, bf16[1,2048]{1,0:T(2,128)(2,1)S(1)} %get-tuple-element.50, bf16[1,2048]{1,0:T(2,128)(2,1)S(1)} %get-tuple-element.48, bf16[1,2048]{1,0:T(2,128)(2,1)S(1)} %get-tuple-element.49, bf16[1,2048]{1,0:T(2,128)(2,1)S(1)} %get-tuple-element.47, ...), dimensions={0} | concatenate | bytes 65536 | tf_op jit(solution)/shard_map/stack | solution.py:80
  18.1 0.7 %stack.17.refs_2_ = bf16[8,2048]{1,0:T(8,128)(2,1)} concatenate(bf16[1,2048]{1,0:T(2,128)(2,1)S(1)} %broadcast.804, bf16[1,2048]{1,0:T(2,128)(2,1)S(1)} %get-tuple-element.54, bf16[1,2048]{1,0:T(2,128)(2,1)S(1)} %get-tuple-element.52, bf16[1,2048]{1,0:T(2,128)(2,1)S(1)} %get-tuple-element.53, bf16[1,2048]{1,0:T(2,128)(2,1)S(1)} %get-tuple-element.51, ...), dimensions={0} | concatenate | bytes 65536 | tf_op jit(solution)/shard_map/stack | solution.py:80
  18.8 0.7 %stack.15.refs_2_ = bf16[8,2048]{1,0:T(8,128)(2,1)} concatenate(bf16[1,2048]{1,0:T(2,128)(2,1)S(1)} %broadcast.804, bf16[1,2048]{1,0:T(2,128)(2,1)S(1)} %get-tuple-element.46, bf16[1,2048]{1,0:T(2,128)(2,1)S(1)} %get-tuple-element.44, bf16[1,2048]{1,0:T(2,128)(2,1)S(1)} %get-tuple-element.45, bf16[1,2048]{1,0:T(2,128)(2,1)S(1)} %get-tuple-element.43, ...), dimensions={0} | concatenate | bytes 65536 | tf_op jit(solution)/shard_map/stack | solution.py:80
  19.5 0.7 %stack.14.refs_2_ = bf16[8,2048]{1,0:T(8,128)(2,1)} concatenate(bf16[1,2048]{1,0:T(2,128)(2,1)S(1)} %broadcast.804, bf16[1,2048]{1,0:T(2,128)(2,1)S(1)} %get-tuple-element.42, bf16[1,2048]{1,0:T(2,128)(2,1)S(1)} %get-tuple-element.40, bf16[1,2048]{1,0:T(2,128)(2,1)S(1)} %get-tuple-element.41, bf16[1,2048]{1,0:T(2,128)(2,1)S(1)} %get-tuple-element.39, ...), dimensions={0} | concatenate | bytes 65536 | tf_op jit(solution)/shard_map/stack | solution.py:80
  20.2 1.5 %collective-permute-done.3 = bf16[2,68,128]{2,1,0:T(8,128)(2,1)S(1)} collective-permute-done((bf16[2,68,128]{2,1,0:T(8,128)(2,1)S(1)}, bf16[2,68,128]{2,1,0:T(8,128)(2,1)S(1)}, u32[]{:S(2)}, u32[]{:S(2)}) %collective-permute-start.3) | collective-permute-done | bytes 34848 | tf_op jit(solution)/shard_map/ppermute | solution.py:22
  21.7 0.7 %reshape.517.refs_0_ = bf16[544,128]{1,0:T(8,128)(2,1)} reshape(bf16[8,68,128]{2,1,0:T(8,128)(2,1)S(1)} %pad_maximum_fusion) | data formatting | bytes 278528 | tf_op jit(solution)/shard_map/reshape | solution.py:156
  22.4 5.6 %shard_map.64 = (f32[544,128]{1,0:T(8,128)}, f32[544,128]{1,0:T(8,128)}, f32[544,8]{1,0:T(8,128)}) custom-call(bf16[544,128]{1,0:T(8,128)(2,1)} %reshape.517.refs_0_, bf16[2048,128]{1,0:T(8,128)(2,1)} %refs_1_, bf16[8,2048]{1,0:T(8,128)(2,1)} %stack.17.refs_2_), custom_call_target="tpu_custom_call" | custom-call | tf_op jit(solution)/shard_map/pallas_call | solution.py:113
  28.0 0.8 %copy-done.3 = bf16[2048,128]{1,0:T(8,128)(2,1)} copy-done((bf16[2048,128]{1,0:T(8,128)(2,1)}, bf16[2048,128]{1,0:T(8,128)(2,1)S(1)}, u32[]{:S(2)}) %copy-start.3) | copy-done | bytes 524312
  28.8 5.4 %shard_map.65 = (f32[544,128]{1,0:T(8,128)}, f32[544,128]{1,0:T(8,128)}, f32[544,8]{1,0:T(8,128)}) custom-call(bf16[544,128]{1,0:T(8,128)(2,1)} %reshape.517.refs_0_, bf16[2048,128]{1,0:T(8,128)(2,1)} %copy-done.3, bf16[8,2048]{1,0:T(8,128)(2,1)} %stack.16.refs_2_, f32[544,128]{1,0:T(8,128)} %get-tuple-element.20.refs_3_, ...), custom_call_target="tpu_custom_call" | custom-call | tf_op jit(solution)/shard_map/pallas_call | solution.py:113
  34.2 0.8 %copy-done.2 = bf16[2048,128]{1,0:T(8,128)(2,1)} copy-done((bf16[2048,128]{1,0:T(8,128)(2,1)}, bf16[2048,128]{1,0:T(8,128)(2,1)S(1)}, u32[]{:S(2)}) %copy-start.2) | copy-done | bytes 524312
  35.0 5.4 %shard_map.66 = (f32[544,128]{1,0:T(8,128)}, f32[544,128]{1,0:T(8,128)}, f32[544,8]{1,0:T(8,128)}) custom-call(bf16[544,128]{1,0:T(8,128)(2,1)} %reshape.517.refs_0_, bf16[2048,128]{1,0:T(8,128)(2,1)} %copy-done.2, bf16[8,2048]{1,0:T(8,128)(2,1)} %stack.15.refs_2_, f32[544,128]{1,0:T(8,128)} %get-tuple-element.23.refs_3_, ...), custom_call_target="tpu_custom_call" | custom-call | tf_op jit(solution)/shard_map/pallas_call | solution.py:113
  40.4 0.8 %copy-done.1 = bf16[2048,128]{1,0:T(8,128)(2,1)} copy-done((bf16[2048,128]{1,0:T(8,128)(2,1)}, bf16[2048,128]{1,0:T(8,128)(2,1)S(1)}, u32[]{:S(2)}) %copy-start.1) | copy-done | bytes 524312
  41.2 6.1 %shard_map.67 = (f32[544,128]{1,0:T(8,128)}, f32[544,128]{1,0:T(8,128)}) custom-call(bf16[544,128]{1,0:T(8,128)(2,1)} %reshape.517.refs_0_, bf16[2048,128]{1,0:T(8,128)(2,1)} %copy-done.1, bf16[8,2048]{1,0:T(8,128)(2,1)} %stack.14.refs_2_, f32[544,128]{1,0:T(8,128)} %get-tuple-element.26.refs_3_, f32[544,128]{1,0:T(8,128)} %get-tuple-element.27.refs_4_, ...), custom_call_target="tpu_custom_call" | custom-call | tf_op jit(solution)/shard_map/pallas_call | solution.py:113
  47.3 1.4 %slice_reduce_fusion.1 = (f32[544]{0:T(1024)S(1)}, f32[544]{0:T(1024)S(1)}) fusion(f32[544,128]{1,0:T(8,128)} %get-tuple-element.29), kind=kLoop, calls=%fused_computation.9 | loop fusion | bytes 8704 | tf_op jit(solution)/shard_map/slice | solution.py:143
  48.8 0.1 slice.48
  49.1 0.1 slice.50
  49.3 0.1 select_bitcast_fusion
  49.6 0.6 %copy-done.10 = pred[8,9]{0,1:T(8,128)(4,1)S(1)} copy-done((pred[8,9]{0,1:T(8,128)(4,1)S(1)}, pred[8,9]{0,1:T(8,128)(4,1)}, u32[]{:S(2)}) %copy-start.10) | copy-done | bytes 96
  50.3 0.9 %convolution_select_fusion = f32[6,8,9,128]{3,1,2,0:T(8,128)S(1)} fusion(bf16[3,3,128,128]{3,2,1,0:T(8,128)(2,1)S(1)} %copy-done, f32[8,1,7,2,128]{4,2,3,0,1:T(8,128)S(1)} %slice.56, f32[8,1,8,9,128]{4,2,3,0,1:T(8,128)S(1)} %copy.10, pred[8,9]{0,1:T(8,128)(4,1)S(1)} %copy-done.10), kind=kOutput, calls=%fused_computation | convolution fusion | flops 764737536 | bytes 868424 | tf_op jit(solution)/shard_map/conv_general_dilated | solution.py:167
  51.3 0.1 copy.12
  51.4 0.1 copy.13
  51.5 0.7 %copy-done.7 = f32[128]{0:T(128)S(1)} copy-done((f32[128]{0:T(128)S(1)}, f32[128]{0:T(128)}, u32[]{:S(2)}) %copy-start.7) | copy-done | bytes 536
  52.1 0.3 select_bitcast_fusion.1
  52.5 0.6 %copy-done.8 = bf16[2,3,3,128]{3,0,2,1:T(2,128)(2,1)S(1)} copy-done((bf16[2,3,3,128]{3,0,2,1:T(2,128)(2,1)S(1)}, bf16[2,3,3,128]{3,0,2,1:T(2,128)(2,1)}, u32[]{:S(2)}) %copy-start.8) | copy-done | bytes 4632
  53.2 1.7 %convolution_select_fusion.1 = f32[4,8,9,2]{1,3,2,0:T(2,128)S(1)} fusion(bf16[2,3,3,128]{3,0,2,1:T(2,128)(2,1)S(1)} %copy-done.8, bf16[6,1,7,2,128]{4,2,3,0,1:T(8,128)(2,1)S(1)} %slice.58, bf16[6,1,8,9,128]{4,2,3,0,1:T(8,128)(2,1)S(1)} %copy.15, pred[8,9]{0,1:T(8,128)(4,1)S(1)} %copy-done.9), kind=kOutput, calls=%fused_computation.1 | convolution fusion | flops 1733184 | bytes 139080 | tf_op jit(solution)/shard_map/conv_general_dilated | solution.py:178
  54.9 0.1 copy.18
  55.0 0.1 reshape.544
  55.1 0.6 %fusion.25 = f32[2,4,64]{2,1,0:T(4,128)} fusion(f32[4,1,72,2]{2,0,3,1:T(4,128)S(1)} %reshape.544, f32[1,4,64]{2,1,0:T(4,128)S(1)} %slice_bitcast_fusion.2, f32[1,4,64]{2,1,0:T(4,128)S(1)} %slice_bitcast_fusion.3), kind=kLoop, calls=%fused_computation.73 | loop fusion | flops 1024 | bytes 6144 | tf_op jit(solution)/shard_map/add | solution.py:184
  (47 shorter events, 0.9 us)
Async XLA Ops:
  0.0 49.6 %copy-start = (bf16[3,3,128,128]{3,2,1,0:T(8,128)(2,1)S(1)}, bf16[3,3,128,128]{3,2,1,0:T(8,128)(2,1)}, u32[]{:S(2)}) copy-start(bf16[3,3,128,128]{3,2,1,0:T(8,128)(2,1)} %param.8) | copy-start | bytes 884740
  0.8 5.2 %collective-permute-start = (bf16[4,2,128]{2,1,0:T(2,128)(2,1)S(1)}, bf16[4,2,128]{2,1,0:T(2,128)(2,1)S(1)}, u32[]{:S(2)}, u32[]{:S(2)}) collective-permute-start(bf16[4,2,128]{2,1,0:T(2,128)(2,1)S(1)} %get-tuple-element.35), channel_id=1, source_target_pairs={{0,1},{1,2},{2,3},{4,5},{5,6},{6,7},{8,9},{9,10},{10,11},{12,13},{... | collective-permute-start | bytes 6152 | tf_op jit(solution)/shard_map/ppermute | solution.py:19
  3.1 5.2 %collective-permute-start.1 = (bf16[4,2,128]{2,1,0:T(2,128)(2,1)S(1)}, bf16[4,2,128]{2,1,0:T(2,128)(2,1)S(1)}, u32[]{:S(2)}, u32[]{:S(2)}) collective-permute-start(bf16[4,2,128]{2,1,0:T(2,128)(2,1)S(1)} %get-tuple-element.36), channel_id=1, source_target_pairs={{1,0},{2,1},{3,2},{5,4},{6,5},{7,6},{9,8},{10,9},{11,10},{13,12},{... | collective-permute-start | bytes 6152 | tf_op jit(solution)/shard_map/ppermute | solution.py:22
  4.8 3.5 %copy-start.5 = (bf16[4,64,128]{2,1,0:T(8,128)(2,1)S(1)}, bf16[4,64,128]{2,1,0:T(8,128)(2,1)}, u32[]{:S(2)}) copy-start(bf16[4,64,128]{2,1,0:T(8,128)(2,1)} %param.6) | copy-start | bytes 196612
  5.2 0.7 %copy-start.6 = (f32[2,128]{1,0:T(2,128)S(1)}, f32[2,128]{1,0:T(2,128)}, u32[]{:S(2)}) copy-start(f32[2,128]{1,0:T(2,128)} %param.9) | copy-start | bytes 3076
  8.3 19.7 %collective-permute-start.6 = (bf16[2048,128]{1,0:T(8,128)(2,1)}, bf16[2048,128]{1,0:T(8,128)(2,1)S(1)}, u32[]{:S(2)}, u32[]{:S(2)}) collective-permute-start(bf16[2048,128]{1,0:T(8,128)(2,1)} %refs_1_), channel_id=1, source_target_pairs={{0,1},{1,2},{2,3},{3,0},{4,5},{5,6},{6,7},{7,4},{8,9},{9,10},{10,1... | collective-permute-start | bytes 1572872 | tf_op jit(solution)/shard_map/ppermute | solution.py:136
  10.7 23.5 %collective-permute-start.5 = (bf16[2048,128]{1,0:T(8,128)(2,1)}, bf16[2048,128]{1,0:T(8,128)(2,1)S(1)}, u32[]{:S(2)}, u32[]{:S(2)}) collective-permute-start(bf16[2048,128]{1,0:T(8,128)(2,1)} %refs_1_), channel_id=1, source_target_pairs={{0,2},{1,3},{2,0},{3,1},{4,6},{5,7},{6,4},{7,5},{8,10},{9,11},{10,... | collective-permute-start | bytes 1572872 | tf_op jit(solution)/shard_map/ppermute | solution.py:136
  11.0 29.4 %collective-permute-start.4 = (bf16[2048,128]{1,0:T(8,128)(2,1)}, bf16[2048,128]{1,0:T(8,128)(2,1)S(1)}, u32[]{:S(2)}, u32[]{:S(2)}) collective-permute-start(bf16[2048,128]{1,0:T(8,128)(2,1)} %refs_1_), channel_id=1, source_target_pairs={{0,3},{1,0},{2,1},{3,2},{4,7},{5,4},{6,5},{7,6},{8,11},{9,8},{10,9... | collective-permute-start | bytes 1572872 | tf_op jit(solution)/shard_map/ppermute | solution.py:136
  12.4 7.8 %collective-permute-start.2 = (bf16[2,68,128]{2,1,0:T(8,128)(2,1)S(1)}, bf16[2,68,128]{2,1,0:T(8,128)(2,1)S(1)}, u32[]{:S(2)}, u32[]{:S(2)}) collective-permute-start(bf16[2,68,128]{2,1,0:T(8,128)(2,1)S(1)} %get-tuple-element.33), channel_id=1, source_target_pairs={{0,4},{4,8},{8,12},{12,16},{16,20},{20,24},{24,28},{1,5},{5,9},{9,... | collective-permute-start | bytes 104456 | tf_op jit(solution)/shard_map/ppermute | solution.py:19
  15.9 5.9 %collective-permute-start.3 = (bf16[2,68,128]{2,1,0:T(8,128)(2,1)S(1)}, bf16[2,68,128]{2,1,0:T(8,128)(2,1)S(1)}, u32[]{:S(2)}, u32[]{:S(2)}) collective-permute-start(bf16[2,68,128]{2,1,0:T(8,128)(2,1)S(1)} %get-tuple-element.34), channel_id=1, source_target_pairs={{4,0},{8,4},{12,8},{16,12},{20,16},{24,20},{28,24},{5,1},{9,5},{13... | collective-permute-start | bytes 104456 | tf_op jit(solution)/shard_map/ppermute | solution.py:22
  28.0 0.8 %copy-start.3 = (bf16[2048,128]{1,0:T(8,128)(2,1)}, bf16[2048,128]{1,0:T(8,128)(2,1)S(1)}, u32[]{:S(2)}) copy-start(bf16[2048,128]{1,0:T(8,128)(2,1)S(1)} %collective-permute-done.6.refs_1_) | copy-start | bytes 1572868
  34.2 0.8 %copy-start.2 = (bf16[2048,128]{1,0:T(8,128)(2,1)}, bf16[2048,128]{1,0:T(8,128)(2,1)S(1)}, u32[]{:S(2)}) copy-start(bf16[2048,128]{1,0:T(8,128)(2,1)S(1)} %collective-permute-done.5.refs_1_) | copy-start | bytes 1572868
  40.4 0.8 %copy-start.1 = (bf16[2048,128]{1,0:T(8,128)(2,1)}, bf16[2048,128]{1,0:T(8,128)(2,1)S(1)}, u32[]{:S(2)}) copy-start(bf16[2048,128]{1,0:T(8,128)(2,1)S(1)} %collective-permute-done.4.refs_1_) | copy-start | bytes 1572868
  47.3 1.9 %copy-start.4 = (f32[544,128]{1,0:T(8,128)S(1)}, f32[544,128]{1,0:T(8,128)}, u32[]{:S(2)}) copy-start(f32[544,128]{1,0:T(8,128)} %get-tuple-element.30) | copy-start | bytes 835588
  49.6 0.7 %copy-start.10 = (pred[8,9]{0,1:T(8,128)(4,1)S(1)}, pred[8,9]{0,1:T(8,128)(4,1)}, u32[]{:S(2)}) copy-start(pred[8,9]{0,1:T(8,128)(4,1)} %constant.147) | copy-start | bytes 220
  51.5 0.7 %copy-start.7 = (f32[128]{0:T(128)S(1)}, f32[128]{0:T(128)}, u32[]{:S(2)}) copy-start(f32[128]{0:T(128)} %param.10) | copy-start | bytes 1540
  52.5 0.7 %copy-start.8 = (bf16[2,3,3,128]{3,0,2,1:T(2,128)(2,1)S(1)}, bf16[2,3,3,128]{3,0,2,1:T(2,128)(2,1)}, u32[]{:S(2)}) copy-start(bf16[2,3,3,128]{3,0,2,1:T(2,128)(2,1)} %param.11) | copy-start | bytes 13828
  52.5 0.7 %copy-start.9 = (pred[8,9]{0,1:T(8,128)(4,1)S(1)}, pred[8,9]{0,1:T(8,128)(4,1)}, u32[]{:S(2)}) copy-start(pred[8,9]{0,1:T(8,128)(4,1)} %constant.146) | copy-start | bytes 220

commit v6 on v5

--- a/solution.py
+++ b/solution.py
@@ -24,7 +24,25 @@
     return block
 
 
-def shard_kernel(*refs, scale, chans, first, last):
+def row_sums(w, base_ref, width):
+    area = w[:, 0:width]
+    weighted = None
+    for g in range(1, w.shape[1] // width):
+        part = w[:, g * width:(g + 1) * width]
+        area = area + part
+        weighted = part * float(g) if weighted is None else weighted + part * float(g)
+    lane = lax.broadcasted_iota(jnp.int32, (1, width), 1)
+    col = lane.astype(jnp.float32) / width
+    total = jnp.sum(area, axis=1, keepdims=True)
+    sum_x = jnp.sum(area * col, axis=1, keepdims=True)
+    local = jnp.zeros_like(total) if weighted is None else jnp.sum(weighted, axis=1, keepdims=True)
+    sum_y = (base_ref[0:1, 0:1] * total + local) / width
+    lane8 = lax.broadcasted_iota(jnp.int32, (w.shape[0], 8), 1)
+    zero = jnp.zeros((), jnp.float32)
+    return jnp.where(lane8 == 0, total, jnp.where(lane8 == 1, sum_x, jnp.where(lane8 == 3, sum_y, zero)))
+
+
+def shard_kernel(*refs, scale, chans, first, last, width):
     if first:
         q_ref, k_ref, pos_ref = refs[:3]
         outs = refs[3:]
@@ -41,12 +59,16 @@
         peak = jnp.maximum(old, peak)
     w = jnp.exp(s - peak)
     hi = w.astype(jnp.bfloat16)
-    lo = (w - hi.astype(jnp.float32)).astype(jnp.bfloat16)
+    if not width:
+        lo = (w - hi.astype(jnp.float32)).astype(jnp.bfloat16)
     acc = jnp.dot(hi, k_ref[...], preferred_element_type=jnp.float32)
-    lanes = (((1,), (1,)), ((), ()))
-    st = lax.dot_general(
-        hi, pos_ref[...], lanes, preferred_element_type=jnp.float32
-    ) + lax.dot_general(lo, pos_ref[...], lanes, preferred_element_type=jnp.float32)
+    if width:
+        st = row_sums(w, pos_ref, width)
+    else:
+        lanes = (((1,), (1,)), ((), ()))
+        st = lax.dot_general(
+            hi, pos_ref[...], lanes, preferred_element_type=jnp.float32
+        ) + lax.dot_general(lo, pos_ref[...], lanes, preferred_element_type=jnp.float32)
     if not first:
         alpha = jnp.exp(old - peak)
         acc = acc_ref[...] * alpha + acc
@@ -80,18 +102,19 @@
     return jnp.stack([one, col_hi, col_lo, row_hi, row_lo, zero, zero, zero])
 
 
-def match_step(queries, keys, pos, state, tq, first, last):
+def match_step(queries, keys, pos, state, tq, first, last, width):
     padded, chans = queries.shape
     nq = padded // tq
     tk = keys.shape[0]
     kernel = functools.partial(
-        shard_kernel, scale=1.0 / math.sqrt(chans), chans=chans, first=first, last=last
+        shard_kernel, scale=1.0 / math.sqrt(chans), chans=chans, first=first, last=last,
+        width=width,
     )
     row_spec = lambda width: pl.BlockSpec((tq, width), lambda i: (i, 0))
     in_specs = [
         row_spec(chans),
         pl.BlockSpec((tk, chans), lambda i: (0, 0)),
-        pl.BlockSpec((8, tk), lambda i: (0, 0)),
+        pl.BlockSpec(pos.shape, lambda i: (0, 0)),
     ]
     args = [queries, keys, pos]
     if not first:
@@ -137,8 +160,14 @@
         shards.append((moved, (me - shift) % n))
     state = None
     for step, (keys, owner) in enumerate(shards):
-        pos = positions(tk, owner * tk, width)
-        state = match_step(queries, keys, pos, state, tq, step == 0, step == n - 1)
+        if tk % width == 0:
+            base = (owner * (tk // width)).astype(jnp.float32)
+            pos = jnp.full((8, 128), base, jnp.float32)
+            seg = width
+        else:
+            pos = positions(tk, owner * tk, width)
+            seg = 0
+        state = match_step(queries, keys, pos, state, tq, step == 0, step == n - 1, seg)
     warped, flow = state
     return warped[:count], flow[:count, 0], flow[:count, 1]
 

time: 56.1 us -> 54.8 us (0.977)
  waiting for transfers between devices: 3.79 us -> 7.35 us
  Pallas kernels: 22.4 us -> 20 us
  local copies, waits for them, and re-layouts: 12.1 us -> 9.78 us
    ppermute x2, waiting for transfers between devices: 3.77 us -> 7.31 us  [extended(): lax.ppermute(lax.slice_in_dim(block, 0, width, axis=dim), axis, backward)]
    another operation x7 -> x0, local copies, waits for them, and re-layouts: 2.81 us -> none  [the longest x4 2.79 us: positions(): return jnp.stack([one, col_hi, col_lo, row_hi, row_lo, zero, zero, zero])]
    broadcast_in_dim x0 -> x4, local copies, waits for them, and re-layouts: none -> 2.47 us  [match(): pos = jnp.full((8, 128), base, jnp.float32)]
    pallas_call x4, Pallas kernels: 22.4 us -> 20 us  [match_step(): pl.pallas_call(kernel, grid=(nq,), in_specs=in_specs, out_specs=out_specs...]
    unnamed x23 -> x21, local copies, waits for them, and re-layouts: 5.14 us -> 3.2 us
    concatenate x2, other arithmetic: 0.05 us -> 0.89 us  [extended(): block = jnp.concatenate([low, block, high], axis=dim)]
    convert_element_type x8 -> x0, other arithmetic: 0.68 us -> none  [the longest x4 0.35 us: split_bf16(): return (hi, (x - hi.astype(jnp.float32)).astype(jnp.bfloat16))]
  transfers between devices with their start and end apart: 7 -> 7, of which waited for: 2 -> 2; matrix products, arithmetic and copies ran while one was open for 8% -> 5% of each run, Pallas kernels for 29% -> 27%
where the time goes in v6:
time: 54.8 us; the launch traced here: 54.4 us
  Pallas kernels  20 us (36%)
  starting transfers between devices  12.2 us (22%)
  local copies, waits for them, and re-layouts  9.78 us (18%)
  waiting for transfers between devices  7.35 us (13%)
  matrix products  2.64 us (5%)
  other arithmetic  2.1 us (4%)
    pallas_call x4, Pallas kernels, match_step(): pl.pallas_call(kernel, grid=(nq,), in_specs=in_specs, out_specs=out_specs...  20 us
    ppermute x2, waiting for transfers between devices, extended(): lax.ppermute(lax.slice_in_dim(block, 0, width, axis=dim), axis, backward)  7.31 us
    ppermute x2, starting transfers between devices, extended(): lax.ppermute(lax.slice_in_dim(block, block.shape[dim] - width, None, axis...  5.77 us
    ppermute x3, starting transfers between devices, match(): lax.ppermute(targets, 'match', [(j, (j + shift) % n) for j in range(n)])  3.83 us
    unnamed x21, local copies, waits for them, and re-layouts  3.2 us
    ppermute x2, starting transfers between devices, extended(): lax.ppermute(lax.slice_in_dim(block, 0, width, axis=dim), axis, backward)  2.58 us
    broadcast_in_dim x4, local copies, waits for them, and re-layouts, match(): pos = jnp.full((8, 128), base, jnp.float32)  2.47 us
    conv_general_dilated x1, matrix products, local(): lax.conv_general_dilated(hidden[None], jnp.transpose(conv_out, (1, 2, 3,...  1.7 us
  transfers between devices with their start and end apart: 7, of which 2 were waited for; matrix products, arithmetic and copies ran while one was open for 5% of the time, Pallas kernels for 27%

profile of v6, /device:TPU:0, one launch (start us, length us, event | category | flops | bytes accessed | tf_op | source)
XLA Modules:
  0.0 54.4 jit_solution(11188768648485757251)
XLA Ops:
  0.0 0.8 %fusion.25 = (bf16[4,2,128]{2,1,0:T(2,128)(2,1)S(1)}, bf16[4,2,128]{2,1,0:T(2,128)(2,1)S(1)}) fusion(bf16[4,64,128]{2,1,0:T(8,128)(2,1)} %param.6), kind=kLoop, calls=%fused_computation.50 | loop fusion | bytes 8192 | tf_op jit(solution)/shard_map/slice | solution.py:20
  0.8 2.3 %collective-permute-start = (bf16[4,2,128]{2,1,0:T(2,128)(2,1)S(1)}, bf16[4,2,128]{2,1,0:T(2,128)(2,1)S(1)}, u32[]{:S(2)}, u32[]{:S(2)}) collective-permute-start(bf16[4,2,128]{2,1,0:T(2,128)(2,1)S(1)} %get-tuple-element.35), channel_id=1, source_target_pairs={{0,1},{1,2},{2,3},{4,5},{5,6},{6,7},{8,9},{9,10},{10,11},{12,13},{... | collective-permute-start | bytes 6152 | tf_op jit(solution)/shard_map/ppermute | solution.py:19
  3.1 1.3 %collective-permute-start.1 = (bf16[4,2,128]{2,1,0:T(2,128)(2,1)S(1)}, bf16[4,2,128]{2,1,0:T(2,128)(2,1)S(1)}, u32[]{:S(2)}, u32[]{:S(2)}) collective-permute-start(bf16[4,2,128]{2,1,0:T(2,128)(2,1)S(1)} %get-tuple-element.36), channel_id=1, source_target_pairs={{1,0},{2,1},{3,2},{5,4},{6,5},{7,6},{9,8},{10,9},{11,10},{13,12},{... | collective-permute-start | bytes 6152 | tf_op jit(solution)/shard_map/ppermute | solution.py:22
  4.5 0.7 %copy-done.5 = f32[2,128]{1,0:T(2,128)S(1)} copy-done((f32[2,128]{1,0:T(2,128)S(1)}, f32[2,128]{1,0:T(2,128)}, u32[]{:S(2)}) %copy-start.5) | copy-done | bytes 1048
  5.1 0.1 broadcast_and_fusion
  5.2 3.1 %collective-permute-done.1 = bf16[4,2,128]{2,1,0:T(2,128)(2,1)S(1)} collective-permute-done((bf16[4,2,128]{2,1,0:T(2,128)(2,1)S(1)}, bf16[4,2,128]{2,1,0:T(2,128)(2,1)S(1)}, u32[]{:S(2)}, u32[]{:S(2)}) %collective-permute-start.1) | collective-permute-done | bytes 2080 | tf_op jit(solution)/shard_map/ppermute | solution.py:22
  8.3 0.9 %pad_maximum_fusion.1 = bf16[4,68,128]{2,1,0:T(8,128)(2,1)S(1)} fusion(bf16[4,2,128]{2,1,0:T(2,128)(2,1)S(1)} %collective-permute-done.1, bf16[4,64,128]{2,1,0:T(8,128)(2,1)} %param.6, bf16[4,2,128]{2,1,0:T(2,128)(2,1)S(1)} %collective-permute-done), kind=kLoop, calls=%fused_computation.26 | loop fusion | flops 208896 | bytes 139264 | tf_op jit(solution)/shard_map/concatenate | solution.py:23
  9.1 2.4 %collective-permute-start.6 = (bf16[2048,128]{1,0:T(8,128)(2,1)}, bf16[2048,128]{1,0:T(8,128)(2,1)S(1)}, u32[]{:S(2)}, u32[]{:S(2)}) collective-permute-start(bf16[2048,128]{1,0:T(8,128)(2,1)} %refs_1_), channel_id=1, source_target_pairs={{0,1},{1,2},{2,3},{3,0},{4,5},{5,6},{6,7},{7,4},{8,9},{9,10},{10,1... | collective-permute-start | bytes 1572872 | tf_op jit(solution)/shard_map/ppermute | solution.py:159
  11.6 1.4 %collective-permute-start.4 = (bf16[2048,128]{1,0:T(8,128)(2,1)}, bf16[2048,128]{1,0:T(8,128)(2,1)S(1)}, u32[]{:S(2)}, u32[]{:S(2)}) collective-permute-start(bf16[2048,128]{1,0:T(8,128)(2,1)} %refs_1_), channel_id=1, source_target_pairs={{0,3},{1,0},{2,1},{3,2},{4,7},{5,4},{6,5},{7,6},{8,11},{9,8},{10,9... | collective-permute-start | bytes 1572872 | tf_op jit(solution)/shard_map/ppermute | solution.py:159
  13.0 3.4 %collective-permute-start.2 = (bf16[2,68,128]{2,1,0:T(8,128)(2,1)S(1)}, bf16[2,68,128]{2,1,0:T(8,128)(2,1)S(1)}, u32[]{:S(2)}, u32[]{:S(2)}) collective-permute-start(bf16[2,68,128]{2,1,0:T(8,128)(2,1)S(1)} %get-tuple-element.33), channel_id=1, source_target_pairs={{0,4},{4,8},{8,12},{12,16},{16,20},{20,24},{24,28},{1,5},{5,9},{9,... | collective-permute-start | bytes 104456 | tf_op jit(solution)/shard_map/ppermute | solution.py:19
  16.4 1.3 %collective-permute-start.3 = (bf16[2,68,128]{2,1,0:T(8,128)(2,1)S(1)}, bf16[2,68,128]{2,1,0:T(8,128)(2,1)S(1)}, u32[]{:S(2)}, u32[]{:S(2)}) collective-permute-start(bf16[2,68,128]{2,1,0:T(8,128)(2,1)S(1)} %get-tuple-element.34), channel_id=1, source_target_pairs={{4,0},{8,4},{12,8},{16,12},{20,16},{24,20},{28,24},{5,1},{9,5},{13... | collective-permute-start | bytes 104456 | tf_op jit(solution)/shard_map/ppermute | solution.py:22
  17.8 0.1 slice.47
  17.9 0.1 copy.7
  18.0 4.2 %collective-permute-done.3 = bf16[2,68,128]{2,1,0:T(8,128)(2,1)S(1)} collective-permute-done((bf16[2,68,128]{2,1,0:T(8,128)(2,1)S(1)}, bf16[2,68,128]{2,1,0:T(8,128)(2,1)S(1)}, u32[]{:S(2)}, u32[]{:S(2)}) %collective-permute-start.3) | collective-permute-done | bytes 34848 | tf_op jit(solution)/shard_map/ppermute | solution.py:22
  22.3 0.7 %reshape.77.refs_0_ = bf16[544,128]{1,0:T(8,128)(2,1)} reshape(bf16[8,68,128]{2,1,0:T(8,128)(2,1)S(1)} %pad_maximum_fusion) | data formatting | bytes 278528 | tf_op jit(solution)/shard_map/reshape | solution.py:185
  23.0 0.6 %broadcast_in_dim.50.refs_2_ = f32[8,128]{1,0:T(8,128)} broadcast(f32[]{:T(128)S(6)} %convert_element_type.34), dimensions={} | broadcast | bytes 4100 | tf_op jit(solution)/shard_map/broadcast_in_dim | solution.py:165
  23.6 5.0 %shard_map.64 = (f32[544,128]{1,0:T(8,128)}, f32[544,128]{1,0:T(8,128)}, f32[544,8]{1,0:T(8,128)}) custom-call(bf16[544,128]{1,0:T(8,128)(2,1)} %reshape.77.refs_0_, bf16[2048,128]{1,0:T(8,128)(2,1)} %refs_1_, f32[8,128]{1,0:T(8,128)} %broadcast_in_dim.50.refs_2_), custom_call_target="tpu_custom_call" | custom-call | tf_op jit(solution)/shard_map/pallas_call | solution.py:136
  28.6 0.6 %broadcast_in_dim.49.refs_2_ = f32[8,128]{1,0:T(8,128)} broadcast(f32[]{:T(128)S(6)} %convert_element_type.33), dimensions={} | broadcast | bytes 4100 | tf_op jit(solution)/shard_map/broadcast_in_dim | solution.py:165
  29.2 0.2 copy-done.3
  29.3 4.9 %shard_map.65 = (f32[544,128]{1,0:T(8,128)}, f32[544,128]{1,0:T(8,128)}, f32[544,8]{1,0:T(8,128)}) custom-call(bf16[544,128]{1,0:T(8,128)(2,1)} %reshape.77.refs_0_, bf16[2048,128]{1,0:T(8,128)(2,1)} %copy-done.3, f32[8,128]{1,0:T(8,128)} %broadcast_in_dim.49.refs_2_, f32[544,128]{1,0:T(8,128)} %get-tuple-element.20.refs_3_, ...), custom_call_target="tpu_custom_call" | custom-call | tf_op jit(solution)/shard_map/pallas_call | solution.py:136
  34.3 0.6 %broadcast_in_dim.48.refs_2_ = f32[8,128]{1,0:T(8,128)} broadcast(f32[]{:T(128)S(6)} %convert_element_type.32), dimensions={} | broadcast | bytes 4100 | tf_op jit(solution)/shard_map/broadcast_in_dim | solution.py:165
  34.9 0.2 copy-done.2
  35.1 4.9 %shard_map.66 = (f32[544,128]{1,0:T(8,128)}, f32[544,128]{1,0:T(8,128)}, f32[544,8]{1,0:T(8,128)}) custom-call(bf16[544,128]{1,0:T(8,128)(2,1)} %reshape.77.refs_0_, bf16[2048,128]{1,0:T(8,128)(2,1)} %copy-done.2, f32[8,128]{1,0:T(8,128)} %broadcast_in_dim.48.refs_2_, f32[544,128]{1,0:T(8,128)} %get-tuple-element.23.refs_3_, ...), custom_call_target="tpu_custom_call" | custom-call | tf_op jit(solution)/shard_map/pallas_call | solution.py:136
  40.0 0.6 %broadcast_in_dim.47.refs_2_ = f32[8,128]{1,0:T(8,128)} broadcast(f32[]{:T(128)S(6)} %convert_element_type.31), dimensions={} | broadcast | bytes 4100 | tf_op jit(solution)/shard_map/broadcast_in_dim | solution.py:165
  40.6 0.2 copy-done.1
  40.8 5.2 %shard_map.67 = (f32[544,128]{1,0:T(8,128)}, f32[544,128]{1,0:T(8,128)}) custom-call(bf16[544,128]{1,0:T(8,128)(2,1)} %reshape.77.refs_0_, bf16[2048,128]{1,0:T(8,128)(2,1)} %copy-done.1, f32[8,128]{1,0:T(8,128)} %broadcast_in_dim.47.refs_2_, f32[544,128]{1,0:T(8,128)} %get-tuple-element.26.refs_3_, f32[544,128]{1,0:T(8,128)} %get-tuple-element.27.refs_4_, ...), custom_call_target="tpu_custom_call" | custom-call | tf_op jit(solution)/shard_map/pallas_call | solution.py:136
  46.0 1.4 %slice_reduce_fusion.1 = (f32[544]{0:T(1024)S(1)}, f32[544]{0:T(1024)S(1)}) fusion(f32[544,128]{1,0:T(8,128)} %get-tuple-element.29), kind=kLoop, calls=%fused_computation.9 | loop fusion | bytes 8704 | tf_op jit(solution)/shard_map/slice | solution.py:172
  47.4 0.1 reshape_squeeze.6
  47.5 0.1 reshape_squeeze.7
  47.6 0.1 slice.48
  47.7 0.1 broadcast_subtract_fusion
  47.7 0.1 slice_bitcast_fusion.2
  47.8 0.1 slice.50
  47.9 0.1 select_bitcast_fusion
  48.1 0.1 copy.20
  48.2 0.1 copy.10
  48.3 0.6 %copy-done.9 = pred[8,9]{0,1:T(8,128)(4,1)S(1)} copy-done((pred[8,9]{0,1:T(8,128)(4,1)S(1)}, pred[8,9]{0,1:T(8,128)(4,1)}, u32[]{:S(2)}) %copy-start.9) | copy-done | bytes 96
  48.9 0.9 %convolution_select_fusion = f32[6,8,9,128]{3,1,2,0:T(8,128)S(1)} fusion(bf16[3,3,128,128]{3,2,1,0:T(8,128)(2,1)S(1)} %copy-done, f32[8,1,7,2,128]{4,2,3,0,1:T(8,128)S(1)} %slice.56, f32[8,1,8,9,128]{4,2,3,0,1:T(8,128)S(1)} %copy.10, pred[8,9]{0,1:T(8,128)(4,1)S(1)} %copy-done.9), kind=kOutput, calls=%fused_computation | convolution fusion | flops 764737536 | bytes 868424 | tf_op jit(solution)/shard_map/conv_general_dilated | solution.py:196
  49.9 0.1 copy.11
  49.9 0.1 copy.12
  50.0 0.1 copy.13
  50.1 0.7 %copy-done.6 = f32[128]{0:T(128)S(1)} copy-done((f32[128]{0:T(128)S(1)}, f32[128]{0:T(128)}, u32[]{:S(2)}) %copy-start.6) | copy-done | bytes 536
  50.8 0.3 select_bitcast_fusion.1
  51.2 0.6 %copy-done.7 = bf16[2,3,3,128]{3,0,2,1:T(2,128)(2,1)S(1)} copy-done((bf16[2,3,3,128]{3,0,2,1:T(2,128)(2,1)S(1)}, bf16[2,3,3,128]{3,0,2,1:T(2,128)(2,1)}, u32[]{:S(2)}) %copy-start.7) | copy-done | bytes 4632
  51.8 1.7 %convolution_select_fusion.1 = f32[4,8,9,2]{1,3,2,0:T(2,128)S(1)} fusion(bf16[2,3,3,128]{3,0,2,1:T(2,128)(2,1)S(1)} %copy-done.7, bf16[6,1,7,2,128]{4,2,3,0,1:T(8,128)(2,1)S(1)} %slice.58, bf16[6,1,8,9,128]{4,2,3,0,1:T(8,128)(2,1)S(1)} %copy.15, pred[8,9]{0,1:T(8,128)(4,1)S(1)} %copy-done.8), kind=kOutput, calls=%fused_computation.1 | convolution fusion | flops 1733184 | bytes 139080 | tf_op jit(solution)/shard_map/conv_general_dilated | solution.py:207
  53.5 0.1 copy.18
  53.7 0.1 reshape.104
  53.8 0.6 %fusion.17 = f32[2,4,64]{2,1,0:T(4,128)} fusion(f32[4,1,72,2]{2,0,3,1:T(4,128)S(1)} %reshape.104, f32[1,4,64]{2,1,0:T(4,128)S(1)} %get-tuple-element.39, f32[1,4,64]{2,1,0:T(4,128)S(1)} %get-tuple-element.40), kind=kLoop, calls=%fused_computation.29 | loop fusion | flops 1024 | bytes 6144 | tf_op jit(solution)/shard_map/add | solution.py:213
  (33 shorter events, 0.3 us)
Async XLA Ops:
  0.0 48.3 %copy-start = (bf16[3,3,128,128]{3,2,1,0:T(8,128)(2,1)S(1)}, bf16[3,3,128,128]{3,2,1,0:T(8,128)(2,1)}, u32[]{:S(2)}) copy-start(bf16[3,3,128,128]{3,2,1,0:T(8,128)(2,1)} %param.8) | copy-start | bytes 884740
  0.8 4.4 %collective-permute-start = (bf16[4,2,128]{2,1,0:T(2,128)(2,1)S(1)}, bf16[4,2,128]{2,1,0:T(2,128)(2,1)S(1)}, u32[]{:S(2)}, u32[]{:S(2)}) collective-permute-start(bf16[4,2,128]{2,1,0:T(2,128)(2,1)S(1)} %get-tuple-element.35), channel_id=1, source_target_pairs={{0,1},{1,2},{2,3},{4,5},{5,6},{6,7},{8,9},{9,10},{10,11},{12,13},{... | collective-permute-start | bytes 6152 | tf_op jit(solution)/shard_map/ppermute | solution.py:19
  3.1 5.2 %collective-permute-start.1 = (bf16[4,2,128]{2,1,0:T(2,128)(2,1)S(1)}, bf16[4,2,128]{2,1,0:T(2,128)(2,1)S(1)}, u32[]{:S(2)}, u32[]{:S(2)}) collective-permute-start(bf16[4,2,128]{2,1,0:T(2,128)(2,1)S(1)} %get-tuple-element.36), channel_id=1, source_target_pairs={{1,0},{2,1},{3,2},{5,4},{6,5},{7,6},{9,8},{10,9},{11,10},{13,12},{... | collective-permute-start | bytes 6152 | tf_op jit(solution)/shard_map/ppermute | solution.py:22
  4.4 0.7 %copy-start.5 = (f32[2,128]{1,0:T(2,128)S(1)}, f32[2,128]{1,0:T(2,128)}, u32[]{:S(2)}) copy-start(f32[2,128]{1,0:T(2,128)} %param.9) | copy-start | bytes 3076
  9.1 19.4 %collective-permute-start.6 = (bf16[2048,128]{1,0:T(8,128)(2,1)}, bf16[2048,128]{1,0:T(8,128)(2,1)S(1)}, u32[]{:S(2)}, u32[]{:S(2)}) collective-permute-start(bf16[2048,128]{1,0:T(8,128)(2,1)} %refs_1_), channel_id=1, source_target_pairs={{0,1},{1,2},{2,3},{3,0},{4,5},{5,6},{6,7},{7,4},{8,9},{9,10},{10,1... | collective-permute-start | bytes 1572872 | tf_op jit(solution)/shard_map/ppermute | solution.py:159
  11.6 22.7 %collective-permute-start.5 = (bf16[2048,128]{1,0:T(8,128)(2,1)}, bf16[2048,128]{1,0:T(8,128)(2,1)S(1)}, u32[]{:S(2)}, u32[]{:S(2)}) collective-permute-start(bf16[2048,128]{1,0:T(8,128)(2,1)} %refs_1_), channel_id=1, source_target_pairs={{0,2},{1,3},{2,0},{3,1},{4,6},{5,7},{6,4},{7,5},{8,10},{9,11},{10,... | collective-permute-start | bytes 1572872 | tf_op jit(solution)/shard_map/ppermute | solution.py:159
  11.6 28.4 %collective-permute-start.4 = (bf16[2048,128]{1,0:T(8,128)(2,1)}, bf16[2048,128]{1,0:T(8,128)(2,1)S(1)}, u32[]{:S(2)}, u32[]{:S(2)}) collective-permute-start(bf16[2048,128]{1,0:T(8,128)(2,1)} %refs_1_), channel_id=1, source_target_pairs={{0,3},{1,0},{2,1},{3,2},{4,7},{5,4},{6,5},{7,6},{8,11},{9,8},{10,9... | collective-permute-start | bytes 1572872 | tf_op jit(solution)/shard_map/ppermute | solution.py:159
  13.0 5.0 %collective-permute-start.2 = (bf16[2,68,128]{2,1,0:T(8,128)(2,1)S(1)}, bf16[2,68,128]{2,1,0:T(8,128)(2,1)S(1)}, u32[]{:S(2)}, u32[]{:S(2)}) collective-permute-start(bf16[2,68,128]{2,1,0:T(8,128)(2,1)S(1)} %get-tuple-element.33), channel_id=1, source_target_pairs={{0,4},{4,8},{8,12},{12,16},{16,20},{20,24},{24,28},{1,5},{5,9},{9,... | collective-permute-start | bytes 104456 | tf_op jit(solution)/shard_map/ppermute | solution.py:19
  16.4 5.9 %collective-permute-start.3 = (bf16[2,68,128]{2,1,0:T(8,128)(2,1)S(1)}, bf16[2,68,128]{2,1,0:T(8,128)(2,1)S(1)}, u32[]{:S(2)}, u32[]{:S(2)}) collective-permute-start(bf16[2,68,128]{2,1,0:T(8,128)(2,1)S(1)} %get-tuple-element.34), channel_id=1, source_target_pairs={{4,0},{8,4},{12,8},{16,12},{20,16},{24,20},{28,24},{5,1},{9,5},{13... | collective-permute-start | bytes 104456 | tf_op jit(solution)/shard_map/ppermute | solution.py:22
  28.6 0.8 %copy-start.3 = (bf16[2048,128]{1,0:T(8,128)(2,1)}, bf16[2048,128]{1,0:T(8,128)(2,1)S(1)}, u32[]{:S(2)}) copy-start(bf16[2048,128]{1,0:T(8,128)(2,1)S(1)} %collective-permute-done.6.refs_1_) | copy-start | bytes 1572868
  34.3 0.8 %copy-start.2 = (bf16[2048,128]{1,0:T(8,128)(2,1)}, bf16[2048,128]{1,0:T(8,128)(2,1)S(1)}, u32[]{:S(2)}) copy-start(bf16[2048,128]{1,0:T(8,128)(2,1)S(1)} %collective-permute-done.5.refs_1_) | copy-start | bytes 1572868
  40.0 0.8 %copy-start.1 = (bf16[2048,128]{1,0:T(8,128)(2,1)}, bf16[2048,128]{1,0:T(8,128)(2,1)S(1)}, u32[]{:S(2)}) copy-start(bf16[2048,128]{1,0:T(8,128)(2,1)S(1)} %collective-permute-done.4.refs_1_) | copy-start | bytes 1572868
  46.0 1.9 %copy-start.4 = (f32[544,128]{1,0:T(8,128)S(1)}, f32[544,128]{1,0:T(8,128)}, u32[]{:S(2)}) copy-start(f32[544,128]{1,0:T(8,128)} %get-tuple-element.30) | copy-start | bytes 835588
  48.2 0.7 %copy-start.9 = (pred[8,9]{0,1:T(8,128)(4,1)S(1)}, pred[8,9]{0,1:T(8,128)(4,1)}, u32[]{:S(2)}) copy-start(pred[8,9]{0,1:T(8,128)(4,1)} %constant.73) | copy-start | bytes 220
  50.1 0.7 %copy-start.6 = (f32[128]{0:T(128)S(1)}, f32[128]{0:T(128)}, u32[]{:S(2)}) copy-start(f32[128]{0:T(128)} %param.10) | copy-start | bytes 1540
  51.1 0.7 %copy-start.7 = (bf16[2,3,3,128]{3,0,2,1:T(2,128)(2,1)S(1)}, bf16[2,3,3,128]{3,0,2,1:T(2,128)(2,1)}, u32[]{:S(2)}) copy-start(bf16[2,3,3,128]{3,0,2,1:T(2,128)(2,1)} %param.11) | copy-start | bytes 13828
  51.2 0.7 %copy-start.8 = (pred[8,9]{0,1:T(8,128)(4,1)S(1)}, pred[8,9]{0,1:T(8,128)(4,1)}, u32[]{:S(2)}) copy-start(pred[8,9]{0,1:T(8,128)(4,1)} %constant.72) | copy-start | bytes 220

commit v7 on v6

--- a/solution.py
+++ b/solution.py
@@ -24,7 +24,7 @@
     return block
 
 
-def row_sums(w, base_ref, width):
+def row_sums(w, base_ref, width, slot):
     area = w[:, 0:width]
     weighted = None
     for g in range(1, w.shape[1] // width):
@@ -36,13 +36,13 @@
     total = jnp.sum(area, axis=1, keepdims=True)
     sum_x = jnp.sum(area * col, axis=1, keepdims=True)
     local = jnp.zeros_like(total) if weighted is None else jnp.sum(weighted, axis=1, keepdims=True)
-    sum_y = (base_ref[0:1, 0:1] * total + local) / width
+    sum_y = (base_ref[0:1, slot:slot + 1] * total + local) / width
     lane8 = lax.broadcasted_iota(jnp.int32, (w.shape[0], 8), 1)
     zero = jnp.zeros((), jnp.float32)
     return jnp.where(lane8 == 0, total, jnp.where(lane8 == 1, sum_x, jnp.where(lane8 == 3, sum_y, zero)))
 
 
-def shard_kernel(*refs, scale, chans, first, last, width):
+def shard_kernel(*refs, scale, chans, first, last, width, slot):
     if first:
         q_ref, k_ref, pos_ref = refs[:3]
         outs = refs[3:]
@@ -63,7 +63,7 @@
         lo = (w - hi.astype(jnp.float32)).astype(jnp.bfloat16)
     acc = jnp.dot(hi, k_ref[...], preferred_element_type=jnp.float32)
     if width:
-        st = row_sums(w, pos_ref, width)
+        st = row_sums(w, pos_ref, width, slot)
     else:
         lanes = (((1,), (1,)), ((), ()))
         st = lax.dot_general(
@@ -102,13 +102,13 @@
     return jnp.stack([one, col_hi, col_lo, row_hi, row_lo, zero, zero, zero])
 
 
-def match_step(queries, keys, pos, state, tq, first, last, width):
+def match_step(queries, keys, pos, state, tq, first, last, width, slot):
     padded, chans = queries.shape
     nq = padded // tq
     tk = keys.shape[0]
     kernel = functools.partial(
         shard_kernel, scale=1.0 / math.sqrt(chans), chans=chans, first=first, last=last,
-        width=width,
+        width=width, slot=slot,
     )
     row_spec = lambda width: pl.BlockSpec((tq, width), lambda i: (i, 0))
     in_specs = [
@@ -159,15 +159,20 @@
         moved = lax.ppermute(targets, "match", [(j, (j + shift) % n) for j in range(n)])
         shards.append((moved, (me - shift) % n))
     state = None
+    if tk % width == 0:
+        lane = jnp.arange(128, dtype=jnp.int32)
+        bases = ((me - lane) % n) * (tk // width)
+        table = jnp.broadcast_to(bases.astype(jnp.float32)[None, :], (8, 128))
     for step, (keys, owner) in enumerate(shards):
         if tk % width == 0:
-            base = (owner * (tk // width)).astype(jnp.float32)
-            pos = jnp.full((8, 128), base, jnp.float32)
+            pos = table
             seg = width
         else:
             pos = positions(tk, owner * tk, width)
             seg = 0
-        state = match_step(queries, keys, pos, state, tq, step == 0, step == n - 1, seg)
+        state = match_step(
+            queries, keys, pos, state, tq, step == 0, step == n - 1, seg, step % 128
+        )
     warped, flow = state
     return warped[:count], flow[:count, 0], flow[:count, 1]
 

time: 54.8 us -> 55.3 us (level)
    broadcast_in_dim x4 -> x1, local copies, waits for them, and re-layouts: 2.47 us -> 0.59 us  [match(): table = jnp.broadcast_to(bases.astype(jnp.float32)[None, :], (8, 128))]
    unnamed x21, local copies, waits for them, and re-layouts: 3.2 us -> 5.07 us
  transfers between devices with their start and end apart: 7 -> 7, of which waited for: 2 -> 3; matrix products, arithmetic and copies ran while one was open for 5% -> 3% of each run, Pallas kernels for 27% -> 27%
where the time goes in v7:
time: 55.3 us; the launch traced here: 54.8 us
  Pallas kernels  20.5 us (37%)
  starting transfers between devices  12.2 us (22%)
  local copies, waits for them, and re-layouts  9.78 us (18%)
  waiting for transfers between devices  7.39 us (13%)
  matrix products  2.64 us (5%)
  other arithmetic  2.11 us (4%)
    pallas_call x4, Pallas kernels, match_step(): pl.pallas_call(kernel, grid=(nq,), in_specs=in_specs, out_specs=out_specs...  20.5 us
    ppermute x2, waiting for transfers between devices, extended(): lax.ppermute(lax.slice_in_dim(block, 0, width, axis=dim), axis, backward)  7.29 us
    ppermute x2, starting transfers between devices, extended(): lax.ppermute(lax.slice_in_dim(block, block.shape[dim] - width, None, axis...  5.77 us
    unnamed x21, local copies, waits for them, and re-layouts  5.07 us
    ppermute x3, starting transfers between devices, match(): lax.ppermute(targets, 'match', [(j, (j + shift) % n) for j in range(n)])  3.83 us
    ppermute x2, starting transfers between devices, extended(): lax.ppermute(lax.slice_in_dim(block, 0, width, axis=dim), axis, backward)  2.58 us
    conv_general_dilated x1, matrix products, local(): lax.conv_general_dilated(hidden[None], jnp.transpose(conv_out, (1, 2, 3,...  1.7 us
    slice x1, local copies, waits for them, and re-layouts, match(): return (warped[:count], flow[:count, 0], flow[:count, 1])  1.42 us
  transfers between devices with their start and end apart: 7, of which 3 were waited for; matrix products, arithmetic and copies ran while one was open for 3% of the time, Pallas kernels for 27%

profile of v7, /device:TPU:0, one launch (start us, length us, event | category | flops | bytes accessed | tf_op | source)
XLA Modules:
  0.0 54.8 jit_solution(13228758089570047594)
XLA Ops:
  0.0 0.8 %fusion.28 = (bf16[4,2,128]{2,1,0:T(2,128)(2,1)S(1)}, bf16[4,2,128]{2,1,0:T(2,128)(2,1)S(1)}) fusion(bf16[4,64,128]{2,1,0:T(8,128)(2,1)} %param.6), kind=kLoop, calls=%fused_computation.56 | loop fusion | bytes 8192 | tf_op jit(solution)/shard_map/slice | solution.py:20
  0.8 2.3 %collective-permute-start = (bf16[4,2,128]{2,1,0:T(2,128)(2,1)S(1)}, bf16[4,2,128]{2,1,0:T(2,128)(2,1)S(1)}, u32[]{:S(2)}, u32[]{:S(2)}) collective-permute-start(bf16[4,2,128]{2,1,0:T(2,128)(2,1)S(1)} %get-tuple-element.35), channel_id=1, source_target_pairs={{0,1},{1,2},{2,3},{4,5},{5,6},{6,7},{8,9},{9,10},{10,11},{12,13},{... | collective-permute-start | bytes 6152 | tf_op jit(solution)/shard_map/ppermute | solution.py:19
  3.1 1.3 %collective-permute-start.1 = (bf16[4,2,128]{2,1,0:T(2,128)(2,1)S(1)}, bf16[4,2,128]{2,1,0:T(2,128)(2,1)S(1)}, u32[]{:S(2)}, u32[]{:S(2)}) collective-permute-start(bf16[4,2,128]{2,1,0:T(2,128)(2,1)S(1)} %get-tuple-element.36), channel_id=1, source_target_pairs={{1,0},{2,1},{3,2},{5,4},{6,5},{7,6},{9,8},{10,9},{11,10},{13,12},{... | collective-permute-start | bytes 6152 | tf_op jit(solution)/shard_map/ppermute | solution.py:22
  4.5 0.7 %copy-done.5 = f32[2,128]{1,0:T(2,128)S(1)} copy-done((f32[2,128]{1,0:T(2,128)S(1)}, f32[2,128]{1,0:T(2,128)}, u32[]{:S(2)}) %copy-start.5) | copy-done | bytes 1048
  5.1 0.1 broadcast_and_fusion
  5.2 3.1 %collective-permute-done.1 = bf16[4,2,128]{2,1,0:T(2,128)(2,1)S(1)} collective-permute-done((bf16[4,2,128]{2,1,0:T(2,128)(2,1)S(1)}, bf16[4,2,128]{2,1,0:T(2,128)(2,1)S(1)}, u32[]{:S(2)}, u32[]{:S(2)}) %collective-permute-start.1) | collective-permute-done | bytes 2080 | tf_op jit(solution)/shard_map/ppermute | solution.py:22
  8.3 0.9 %pad_maximum_fusion.1 = bf16[4,68,128]{2,1,0:T(8,128)(2,1)S(1)} fusion(bf16[4,2,128]{2,1,0:T(2,128)(2,1)S(1)} %collective-permute-done.1, bf16[4,64,128]{2,1,0:T(8,128)(2,1)} %param.6, bf16[4,2,128]{2,1,0:T(2,128)(2,1)S(1)} %collective-permute-done), kind=kLoop, calls=%fused_computation.26 | loop fusion | flops 208896 | bytes 139264 | tf_op jit(solution)/shard_map/concatenate | solution.py:23
  9.1 2.4 %collective-permute-start.6 = (bf16[2048,128]{1,0:T(8,128)(2,1)}, bf16[2048,128]{1,0:T(8,128)(2,1)S(1)}, u32[]{:S(2)}, u32[]{:S(2)}) collective-permute-start(bf16[2048,128]{1,0:T(8,128)(2,1)} %refs_1_), channel_id=1, source_target_pairs={{0,1},{1,2},{2,3},{3,0},{4,5},{5,6},{6,7},{7,4},{8,9},{9,10},{10,1... | collective-permute-start | bytes 1572872 | tf_op jit(solution)/shard_map/ppermute | solution.py:159
  11.6 0.0 collective-permute-start.5
  11.6 1.4 %collective-permute-start.4 = (bf16[2048,128]{1,0:T(8,128)(2,1)}, bf16[2048,128]{1,0:T(8,128)(2,1)S(1)}, u32[]{:S(2)}, u32[]{:S(2)}) collective-permute-start(bf16[2048,128]{1,0:T(8,128)(2,1)} %refs_1_), channel_id=1, source_target_pairs={{0,3},{1,0},{2,1},{3,2},{4,7},{5,4},{6,5},{7,6},{8,11},{9,8},{10,9... | collective-permute-start | bytes 1572872 | tf_op jit(solution)/shard_map/ppermute | solution.py:159
  13.0 3.4 %collective-permute-start.2 = (bf16[2,68,128]{2,1,0:T(8,128)(2,1)S(1)}, bf16[2,68,128]{2,1,0:T(8,128)(2,1)S(1)}, u32[]{:S(2)}, u32[]{:S(2)}) collective-permute-start(bf16[2,68,128]{2,1,0:T(8,128)(2,1)S(1)} %get-tuple-element.33), channel_id=1, source_target_pairs={{0,4},{4,8},{8,12},{12,16},{16,20},{20,24},{24,28},{1,5},{5,9},{9,... | collective-permute-start | bytes 104456 | tf_op jit(solution)/shard_map/ppermute | solution.py:19
  16.4 1.3 %collective-permute-start.3 = (bf16[2,68,128]{2,1,0:T(8,128)(2,1)S(1)}, bf16[2,68,128]{2,1,0:T(8,128)(2,1)S(1)}, u32[]{:S(2)}, u32[]{:S(2)}) collective-permute-start(bf16[2,68,128]{2,1,0:T(8,128)(2,1)S(1)} %get-tuple-element.34), channel_id=1, source_target_pairs={{4,0},{8,4},{12,8},{16,12},{20,16},{24,20},{28,24},{5,1},{9,5},{13... | collective-permute-start | bytes 104456 | tf_op jit(solution)/shard_map/ppermute | solution.py:22
  17.7 0.1 slice.47
  17.8 0.1 copy.7
  18.0 0.1 collective-permute-done.2
  18.0 4.2 %collective-permute-done.3 = bf16[2,68,128]{2,1,0:T(8,128)(2,1)S(1)} collective-permute-done((bf16[2,68,128]{2,1,0:T(8,128)(2,1)S(1)}, bf16[2,68,128]{2,1,0:T(8,128)(2,1)S(1)}, u32[]{:S(2)}, u32[]{:S(2)}) %collective-permute-start.3) | collective-permute-done | bytes 34848 | tf_op jit(solution)/shard_map/ppermute | solution.py:22
  22.3 0.7 %reshape.94.refs_0_ = bf16[544,128]{1,0:T(8,128)(2,1)} reshape(bf16[8,68,128]{2,1,0:T(8,128)(2,1)S(1)} %pad_maximum_fusion) | data formatting | bytes 278528 | tf_op jit(solution)/shard_map/reshape | solution.py:190
  23.0 0.6 %broadcast_in_dim.22.refs_2_ = f32[8,128]{1,0:T(8,128)} broadcast(f32[128]{0:T(128)S(1)} %fusion.19), dimensions={1} | broadcast | bytes 4608 | tf_op jit(solution)/shard_map/broadcast_in_dim | solution.py:165
  23.6 5.0 %shard_map.64 = (f32[544,128]{1,0:T(8,128)}, f32[544,128]{1,0:T(8,128)}, f32[544,8]{1,0:T(8,128)}) custom-call(bf16[544,128]{1,0:T(8,128)(2,1)} %reshape.94.refs_0_, bf16[2048,128]{1,0:T(8,128)(2,1)} %refs_1_, f32[8,128]{1,0:T(8,128)} %broadcast_in_dim.22.refs_2_), custom_call_target="tpu_custom_call" | custom-call | tf_op jit(solution)/shard_map/pallas_call | solution.py:136
  28.6 0.8 %copy-done.3 = bf16[2048,128]{1,0:T(8,128)(2,1)} copy-done((bf16[2048,128]{1,0:T(8,128)(2,1)}, bf16[2048,128]{1,0:T(8,128)(2,1)S(1)}, u32[]{:S(2)}) %copy-start.3) | copy-done | bytes 524312
  29.3 5.0 %shard_map.65 = (f32[544,128]{1,0:T(8,128)}, f32[544,128]{1,0:T(8,128)}, f32[544,8]{1,0:T(8,128)}) custom-call(bf16[544,128]{1,0:T(8,128)(2,1)} %reshape.94.refs_0_, bf16[2048,128]{1,0:T(8,128)(2,1)} %copy-done.3, f32[8,128]{1,0:T(8,128)} %broadcast_in_dim.22.refs_2_, f32[544,128]{1,0:T(8,128)} %get-tuple-element.20.refs_3_, ...), custom_call_target="tpu_custom_call" | custom-call | tf_op jit(solution)/shard_map/pallas_call | solution.py:136
  34.3 0.8 %copy-done.2 = bf16[2048,128]{1,0:T(8,128)(2,1)} copy-done((bf16[2048,128]{1,0:T(8,128)(2,1)}, bf16[2048,128]{1,0:T(8,128)(2,1)S(1)}, u32[]{:S(2)}) %copy-start.2) | copy-done | bytes 524312
  35.1 4.9 %shard_map.66 = (f32[544,128]{1,0:T(8,128)}, f32[544,128]{1,0:T(8,128)}, f32[544,8]{1,0:T(8,128)}) custom-call(bf16[544,128]{1,0:T(8,128)(2,1)} %reshape.94.refs_0_, bf16[2048,128]{1,0:T(8,128)(2,1)} %copy-done.2, f32[8,128]{1,0:T(8,128)} %broadcast_in_dim.22.refs_2_, f32[544,128]{1,0:T(8,128)} %get-tuple-element.23.refs_3_, ...), custom_call_target="tpu_custom_call" | custom-call | tf_op jit(solution)/shard_map/pallas_call | solution.py:136
  40.1 0.8 %copy-done.1 = bf16[2048,128]{1,0:T(8,128)(2,1)} copy-done((bf16[2048,128]{1,0:T(8,128)(2,1)}, bf16[2048,128]{1,0:T(8,128)(2,1)S(1)}, u32[]{:S(2)}) %copy-start.1) | copy-done | bytes 524312
  40.9 5.6 %shard_map.67 = (f32[544,128]{1,0:T(8,128)}, f32[544,128]{1,0:T(8,128)}) custom-call(bf16[544,128]{1,0:T(8,128)(2,1)} %reshape.94.refs_0_, bf16[2048,128]{1,0:T(8,128)(2,1)} %copy-done.1, f32[8,128]{1,0:T(8,128)} %broadcast_in_dim.22.refs_2_, f32[544,128]{1,0:T(8,128)} %get-tuple-element.26.refs_3_, f32[544,128]{1,0:T(8,128)} %get-tuple-element.27.refs_4_, ...), custom_call_target="tpu_custom_call" | custom-call | tf_op jit(solution)/shard_map/pallas_call | solution.py:136
  46.4 1.4 %slice_reduce_fusion.1 = (f32[544]{0:T(1024)S(1)}, f32[544]{0:T(1024)S(1)}) fusion(f32[544,128]{1,0:T(8,128)} %get-tuple-element.29), kind=kLoop, calls=%fused_computation.9 | loop fusion | bytes 8704 | tf_op jit(solution)/shard_map/slice | solution.py:177
  47.9 0.1 reshape_squeeze.6
  47.9 0.1 reshape_squeeze.7
  48.0 0.1 slice.48
  48.1 0.1 broadcast_subtract_fusion
  48.2 0.1 slice_bitcast_fusion.2
  48.2 0.1 slice.50
  48.3 0.1 select_bitcast_fusion
  48.5 0.1 copy.20
  48.6 0.1 copy.10
  48.7 0.6 %copy-done.9 = pred[8,9]{0,1:T(8,128)(4,1)S(1)} copy-done((pred[8,9]{0,1:T(8,128)(4,1)S(1)}, pred[8,9]{0,1:T(8,128)(4,1)}, u32[]{:S(2)}) %copy-start.9) | copy-done | bytes 96
  49.3 0.9 %convolution_select_fusion = f32[6,8,9,128]{3,1,2,0:T(8,128)S(1)} fusion(bf16[3,3,128,128]{3,2,1,0:T(8,128)(2,1)S(1)} %copy-done, f32[8,1,7,2,128]{4,2,3,0,1:T(8,128)S(1)} %slice.56, f32[8,1,8,9,128]{4,2,3,0,1:T(8,128)S(1)} %copy.10, pred[8,9]{0,1:T(8,128)(4,1)S(1)} %copy-done.9), kind=kOutput, calls=%fused_computation | convolution fusion | flops 764737536 | bytes 868424 | tf_op jit(solution)/shard_map/conv_general_dilated | solution.py:201
  50.3 0.1 copy.11
  50.4 0.1 copy.12
  50.5 0.1 copy.13
  50.6 0.7 %copy-done.6 = f32[128]{0:T(128)S(1)} copy-done((f32[128]{0:T(128)S(1)}, f32[128]{0:T(128)}, u32[]{:S(2)}) %copy-start.6) | copy-done | bytes 536
  51.2 0.3 select_bitcast_fusion.1
  51.6 0.6 %copy-done.7 = bf16[2,3,3,128]{3,0,2,1:T(2,128)(2,1)S(1)} copy-done((bf16[2,3,3,128]{3,0,2,1:T(2,128)(2,1)S(1)}, bf16[2,3,3,128]{3,0,2,1:T(2,128)(2,1)}, u32[]{:S(2)}) %copy-start.7) | copy-done | bytes 4632
  52.3 0.0 copy-done.8
  52.3 1.7 %convolution_select_fusion.1 = f32[4,8,9,2]{1,3,2,0:T(2,128)S(1)} fusion(bf16[2,3,3,128]{3,0,2,1:T(2,128)(2,1)S(1)} %copy-done.7, bf16[6,1,7,2,128]{4,2,3,0,1:T(8,128)(2,1)S(1)} %slice.58, bf16[6,1,8,9,128]{4,2,3,0,1:T(8,128)(2,1)S(1)} %copy.15, pred[8,9]{0,1:T(8,128)(4,1)S(1)} %copy-done.8), kind=kOutput, calls=%fused_computation.1 | convolution fusion | flops 1733184 | bytes 139080 | tf_op jit(solution)/shard_map/conv_general_dilated | solution.py:212
  54.0 0.1 copy.18
  54.1 0.1 reshape.121
  54.2 0.6 %fusion.17 = f32[2,4,64]{2,1,0:T(4,128)} fusion(f32[4,1,72,2]{2,0,3,1:T(4,128)S(1)} %reshape.121, f32[1,4,64]{2,1,0:T(4,128)S(1)} %get-tuple-element.39, f32[1,4,64]{2,1,0:T(4,128)S(1)} %get-tuple-element.40), kind=kLoop, calls=%fused_computation.29 | loop fusion | flops 1024 | bytes 6144 | tf_op jit(solution)/shard_map/add | solution.py:218
  (31 shorter events, 0.2 us)
Async XLA Ops:
  0.0 48.7 %copy-start = (bf16[3,3,128,128]{3,2,1,0:T(8,128)(2,1)S(1)}, bf16[3,3,128,128]{3,2,1,0:T(8,128)(2,1)}, u32[]{:S(2)}) copy-start(bf16[3,3,128,128]{3,2,1,0:T(8,128)(2,1)} %param.8) | copy-start | bytes 884740
  0.8 4.5 %collective-permute-start = (bf16[4,2,128]{2,1,0:T(2,128)(2,1)S(1)}, bf16[4,2,128]{2,1,0:T(2,128)(2,1)S(1)}, u32[]{:S(2)}, u32[]{:S(2)}) collective-permute-start(bf16[4,2,128]{2,1,0:T(2,128)(2,1)S(1)} %get-tuple-element.35), channel_id=1, source_target_pairs={{0,1},{1,2},{2,3},{4,5},{5,6},{6,7},{8,9},{9,10},{10,11},{12,13},{... | collective-permute-start | bytes 6152 | tf_op jit(solution)/shard_map/ppermute | solution.py:19
  3.1 5.2 %collective-permute-start.1 = (bf16[4,2,128]{2,1,0:T(2,128)(2,1)S(1)}, bf16[4,2,128]{2,1,0:T(2,128)(2,1)S(1)}, u32[]{:S(2)}, u32[]{:S(2)}) collective-permute-start(bf16[4,2,128]{2,1,0:T(2,128)(2,1)S(1)} %get-tuple-element.36), channel_id=1, source_target_pairs={{1,0},{2,1},{3,2},{5,4},{6,5},{7,6},{9,8},{10,9},{11,10},{13,12},{... | collective-permute-start | bytes 6152 | tf_op jit(solution)/shard_map/ppermute | solution.py:22
  4.4 0.7 %copy-start.5 = (f32[2,128]{1,0:T(2,128)S(1)}, f32[2,128]{1,0:T(2,128)}, u32[]{:S(2)}) copy-start(f32[2,128]{1,0:T(2,128)} %param.9) | copy-start | bytes 3076
  9.1 19.4 %collective-permute-start.6 = (bf16[2048,128]{1,0:T(8,128)(2,1)}, bf16[2048,128]{1,0:T(8,128)(2,1)S(1)}, u32[]{:S(2)}, u32[]{:S(2)}) collective-permute-start(bf16[2048,128]{1,0:T(8,128)(2,1)} %refs_1_), channel_id=1, source_target_pairs={{0,1},{1,2},{2,3},{3,0},{4,5},{5,6},{6,7},{7,4},{8,9},{9,10},{10,1... | collective-permute-start | bytes 1572872 | tf_op jit(solution)/shard_map/ppermute | solution.py:159
  11.6 22.8 %collective-permute-start.5 = (bf16[2048,128]{1,0:T(8,128)(2,1)}, bf16[2048,128]{1,0:T(8,128)(2,1)S(1)}, u32[]{:S(2)}, u32[]{:S(2)}) collective-permute-start(bf16[2048,128]{1,0:T(8,128)(2,1)} %refs_1_), channel_id=1, source_target_pairs={{0,2},{1,3},{2,0},{3,1},{4,6},{5,7},{6,4},{7,5},{8,10},{9,11},{10,... | collective-permute-start | bytes 1572872 | tf_op jit(solution)/shard_map/ppermute | solution.py:159
  11.6 28.5 %collective-permute-start.4 = (bf16[2048,128]{1,0:T(8,128)(2,1)}, bf16[2048,128]{1,0:T(8,128)(2,1)S(1)}, u32[]{:S(2)}, u32[]{:S(2)}) collective-permute-start(bf16[2048,128]{1,0:T(8,128)(2,1)} %refs_1_), channel_id=1, source_target_pairs={{0,3},{1,0},{2,1},{3,2},{4,7},{5,4},{6,5},{7,6},{8,11},{9,8},{10,9... | collective-permute-start | bytes 1572872 | tf_op jit(solution)/shard_map/ppermute | solution.py:159
  13.0 5.0 %collective-permute-start.2 = (bf16[2,68,128]{2,1,0:T(8,128)(2,1)S(1)}, bf16[2,68,128]{2,1,0:T(8,128)(2,1)S(1)}, u32[]{:S(2)}, u32[]{:S(2)}) collective-permute-start(bf16[2,68,128]{2,1,0:T(8,128)(2,1)S(1)} %get-tuple-element.33), channel_id=1, source_target_pairs={{0,4},{4,8},{8,12},{12,16},{16,20},{20,24},{24,28},{1,5},{5,9},{9,... | collective-permute-start | bytes 104456 | tf_op jit(solution)/shard_map/ppermute | solution.py:19
  16.4 5.9 %collective-permute-start.3 = (bf16[2,68,128]{2,1,0:T(8,128)(2,1)S(1)}, bf16[2,68,128]{2,1,0:T(8,128)(2,1)S(1)}, u32[]{:S(2)}, u32[]{:S(2)}) collective-permute-start(bf16[2,68,128]{2,1,0:T(8,128)(2,1)S(1)} %get-tuple-element.34), channel_id=1, source_target_pairs={{4,0},{8,4},{12,8},{16,12},{20,16},{24,20},{28,24},{5,1},{9,5},{13... | collective-permute-start | bytes 104456 | tf_op jit(solution)/shard_map/ppermute | solution.py:22
  28.6 0.8 %copy-start.3 = (bf16[2048,128]{1,0:T(8,128)(2,1)}, bf16[2048,128]{1,0:T(8,128)(2,1)S(1)}, u32[]{:S(2)}) copy-start(bf16[2048,128]{1,0:T(8,128)(2,1)S(1)} %collective-permute-done.6.refs_1_) | copy-start | bytes 1572868
  34.3 0.8 %copy-start.2 = (bf16[2048,128]{1,0:T(8,128)(2,1)}, bf16[2048,128]{1,0:T(8,128)(2,1)S(1)}, u32[]{:S(2)}) copy-start(bf16[2048,128]{1,0:T(8,128)(2,1)S(1)} %collective-permute-done.5.refs_1_) | copy-start | bytes 1572868
  40.1 0.8 %copy-start.1 = (bf16[2048,128]{1,0:T(8,128)(2,1)}, bf16[2048,128]{1,0:T(8,128)(2,1)S(1)}, u32[]{:S(2)}) copy-start(bf16[2048,128]{1,0:T(8,128)(2,1)S(1)} %collective-permute-done.4.refs_1_) | copy-start | bytes 1572868
  46.4 1.9 %copy-start.4 = (f32[544,128]{1,0:T(8,128)S(1)}, f32[544,128]{1,0:T(8,128)}, u32[]{:S(2)}) copy-start(f32[544,128]{1,0:T(8,128)} %get-tuple-element.30) | copy-start | bytes 835588
  48.7 0.7 %copy-start.9 = (pred[8,9]{0,1:T(8,128)(4,1)S(1)}, pred[8,9]{0,1:T(8,128)(4,1)}, u32[]{:S(2)}) copy-start(pred[8,9]{0,1:T(8,128)(4,1)} %constant.60) | copy-start | bytes 220
  50.6 0.7 %copy-start.6 = (f32[128]{0:T(128)S(1)}, f32[128]{0:T(128)}, u32[]{:S(2)}) copy-start(f32[128]{0:T(128)} %param.10) | copy-start | bytes 1540
  51.6 0.7 %copy-start.7 = (bf16[2,3,3,128]{3,0,2,1:T(2,128)(2,1)S(1)}, bf16[2,3,3,128]{3,0,2,1:T(2,128)(2,1)}, u32[]{:S(2)}) copy-start(bf16[2,3,3,128]{3,0,2,1:T(2,128)(2,1)} %param.11) | copy-start | bytes 13828
  51.6 0.7 %copy-start.8 = (pred[8,9]{0,1:T(8,128)(4,1)S(1)}, pred[8,9]{0,1:T(8,128)(4,1)}, u32[]{:S(2)}) copy-start(pred[8,9]{0,1:T(8,128)(4,1)} %constant.59) | copy-start | bytes 220

commit v8 on v7

--- a/solution.py
+++ b/solution.py
@@ -155,14 +155,25 @@
     n = lax.axis_size("match")
     me = lax.axis_index("match")
     shards = [(targets, me)]
-    for shift in range(1, n):
-        moved = lax.ppermute(targets, "match", [(j, (j + shift) % n) for j in range(n)])
-        shards.append((moved, (me - shift) % n))
+    if n % 2 == 0:
+        chips = n // 2
+        sibling = [(j, j ^ 1) for j in range(n)]
+        shards.append((lax.ppermute(targets, "match", sibling), me ^ 1))
+        for shift in range(1, chips):
+            hop = [(j, ((j // 2 + shift) % chips) * 2 + j % 2) for j in range(n)]
+            moved = lax.ppermute(targets, "match", hop)
+            owner = ((me // 2 - shift) % chips) * 2 + me % 2
+            shards.append((moved, owner))
+            shards.append((lax.ppermute(moved, "match", sibling), owner ^ 1))
+    else:
+        for shift in range(1, n):
+            moved = lax.ppermute(targets, "match", [(j, (j + shift) % n) for j in range(n)])
+            shards.append((moved, (me - shift) % n))
     state = None
     if tk % width == 0:
-        lane = jnp.arange(128, dtype=jnp.int32)
-        bases = ((me - lane) % n) * (tk // width)
-        table = jnp.broadcast_to(bases.astype(jnp.float32)[None, :], (8, 128))
+        owners = jnp.stack([owner for _, owner in shards]) * (tk // width)
+        owners = jnp.pad(owners.astype(jnp.float32), (0, 128 - n))
+        table = jnp.broadcast_to(owners[None, :], (8, 128))
     for step, (keys, owner) in enumerate(shards):
         if tk % width == 0:
             pos = table

time: 55.3 us -> 65 us (1.18)
  waiting for transfers between devices: 7.39 us -> 19.3 us
  local copies, waits for them, and re-layouts: 9.78 us -> 8.38 us
  other arithmetic: 2.11 us -> 1.34 us
    ppermute x3, waiting for transfers between devices: 0.01 us -> 11.3 us  [the longest x1 11.3 us: match(): moved = lax.ppermute(targets, 'match', hop)]
    unnamed x21 -> x23, local copies, waits for them, and re-layouts: 5.07 us -> 3.64 us
    concatenate x2, other arithmetic: 0.89 us -> 0.05 us  [extended(): block = jnp.concatenate([low, block, high], axis=dim)]
    ppermute x2, waiting for transfers between devices: 7.29 us -> 8 us  [extended(): lax.ppermute(lax.slice_in_dim(block, 0, width, axis=dim), axis, backward)]
  transfers between devices with their start and end apart: 7 -> 7, of which waited for: 3 -> 3; matrix products, arithmetic and copies ran while one was open for 3% -> 3% of each run, Pallas kernels for 27% -> 23%
where the time goes in v8:
time: 65 us; the launch traced here: 64.6 us
  Pallas kernels  20.5 us (32%)
  waiting for transfers between devices  19.3 us (30%)
  starting transfers between devices  12.1 us (19%)
  local copies, waits for them, and re-layouts  8.38 us (13%)
  matrix products  2.64 us (4%)
  other arithmetic  1.34 us (2%)
    pallas_call x4, Pallas kernels, match_step(): pl.pallas_call(kernel, grid=(nq,), in_specs=in_specs, out_specs=out_specs...  20.5 us
    ppermute x1, waiting for transfers between devices, match(): moved = lax.ppermute(targets, 'match', hop)  11.3 us
    ppermute x2, waiting for transfers between devices, extended(): lax.ppermute(lax.slice_in_dim(block, 0, width, axis=dim), axis, backward)  8 us
    ppermute x2, starting transfers between devices, extended(): lax.ppermute(lax.slice_in_dim(block, block.shape[dim] - width, None, axis...  5.77 us
    unnamed x23, local copies, waits for them, and re-layouts  3.64 us
    ppermute x2, starting transfers between devices, extended(): lax.ppermute(lax.slice_in_dim(block, 0, width, axis=dim), axis, backward)  2.58 us
    ppermute x1, starting transfers between devices, match(): moved = lax.ppermute(targets, 'match', hop)  2.35 us
    conv_general_dilated x1, matrix products, local(): lax.conv_general_dilated(hidden[None], jnp.transpose(conv_out, (1, 2, 3,...  1.7 us
  transfers between devices with their start and end apart: 7, of which 3 were waited for; matrix products, arithmetic and copies ran while one was open for 3% of the time, Pallas kernels for 23%

profile of v8, /device:TPU:0, one launch (start us, length us, event | category | flops | bytes accessed | tf_op | source)
XLA Modules:
  0.0 64.6 jit_solution(2728117890400282147)
XLA Ops:
  0.0 0.8 %fusion.26 = (bf16[4,2,128]{2,1,0:T(2,128)(2,1)S(1)}, bf16[4,2,128]{2,1,0:T(2,128)(2,1)S(1)}) fusion(bf16[4,64,128]{2,1,0:T(8,128)(2,1)} %param.6), kind=kLoop, calls=%fused_computation.52 | loop fusion | bytes 8192 | tf_op jit(solution)/shard_map/slice | solution.py:20
  0.8 2.3 %collective-permute-start = (bf16[4,2,128]{2,1,0:T(2,128)(2,1)S(1)}, bf16[4,2,128]{2,1,0:T(2,128)(2,1)S(1)}, u32[]{:S(2)}, u32[]{:S(2)}) collective-permute-start(bf16[4,2,128]{2,1,0:T(2,128)(2,1)S(1)} %get-tuple-element.35), channel_id=1, source_target_pairs={{0,1},{1,2},{2,3},{4,5},{5,6},{6,7},{8,9},{9,10},{10,11},{12,13},{... | collective-permute-start | bytes 6152 | tf_op jit(solution)/shard_map/ppermute | solution.py:19
  3.1 1.3 %collective-permute-start.1 = (bf16[4,2,128]{2,1,0:T(2,128)(2,1)S(1)}, bf16[4,2,128]{2,1,0:T(2,128)(2,1)S(1)}, u32[]{:S(2)}, u32[]{:S(2)}) collective-permute-start(bf16[4,2,128]{2,1,0:T(2,128)(2,1)S(1)} %get-tuple-element.36), channel_id=1, source_target_pairs={{1,0},{2,1},{3,2},{5,4},{6,5},{7,6},{9,8},{10,9},{11,10},{13,12},{... | collective-permute-start | bytes 6152 | tf_op jit(solution)/shard_map/ppermute | solution.py:22
  4.5 3.8 %collective-permute-done.1 = bf16[4,2,128]{2,1,0:T(2,128)(2,1)S(1)} collective-permute-done((bf16[4,2,128]{2,1,0:T(2,128)(2,1)S(1)}, bf16[4,2,128]{2,1,0:T(2,128)(2,1)S(1)}, u32[]{:S(2)}, u32[]{:S(2)}) %collective-permute-start.1) | collective-permute-done | bytes 2080 | tf_op jit(solution)/shard_map/ppermute | solution.py:22
  8.3 2.3 %collective-permute-start.4 = (bf16[2048,128]{1,0:T(8,128)(2,1)}, bf16[2048,128]{1,0:T(8,128)(2,1)S(1)}, u32[]{:S(2)}, u32[]{:S(2)}) collective-permute-start(bf16[2048,128]{1,0:T(8,128)(2,1)} %refs_1_), channel_id=1, source_target_pairs={{0,2},{1,3},{2,0},{3,1},{4,6},{5,7},{6,4},{7,5},{8,10},{9,11},{10,... | collective-permute-start | bytes 1572872 | tf_op jit(solution)/shard_map/ppermute | solution.py:164
  10.7 0.1 broadcast_and_fusion
  10.8 0.7 %collective-permute-start.6 = (bf16[2048,128]{1,0:T(8,128)(2,1)}, bf16[2048,128]{1,0:T(8,128)(2,1)S(1)}, u32[]{:S(2)}, u32[]{:S(2)}) collective-permute-start(bf16[2048,128]{1,0:T(8,128)(2,1)} %refs_1_), channel_id=1, source_target_pairs={{0,1},{1,0},{2,3},{3,2},{4,5},{5,4},{6,7},{7,6},{8,9},{9,8},{10,11... | collective-permute-start | bytes 1572872 | tf_op jit(solution)/shard_map/ppermute | solution.py:161
  11.4 11.3 %collective-permute-done.4.refs_1_ = bf16[2048,128]{1,0:T(8,128)(2,1)S(1)} collective-permute-done((bf16[2048,128]{1,0:T(8,128)(2,1)}, bf16[2048,128]{1,0:T(8,128)(2,1)S(1)}, u32[]{:S(2)}, u32[]{:S(2)}) %collective-permute-start.4) | collective-permute-done | bytes 524320 | tf_op jit(solution)/shard_map/ppermute | solution.py:164
  22.7 0.8 %collective-permute-start.5 = (bf16[2048,128]{1,0:T(8,128)(2,1)S(1)}, bf16[2048,128]{1,0:T(8,128)(2,1)S(1)}, u32[]{:S(2)}, u32[]{:S(2)}) collective-permute-start(bf16[2048,128]{1,0:T(8,128)(2,1)S(1)} %collective-permute-done.4.refs_1_), channel_id=1, source_target_pairs={{0,1},{1,0},{2,3},{3,2},{4,5},{5,4},{6,7},{7,6},{8,9},{9,8},{10,11... | collective-permute-start | bytes 1572872 | tf_op jit(solution)/shard_map/ppermute | solution.py:167
  23.5 3.4 %collective-permute-start.2 = (bf16[2,68,128]{2,1,0:T(8,128)(2,1)S(1)}, bf16[2,68,128]{2,1,0:T(8,128)(2,1)S(1)}, u32[]{:S(2)}, u32[]{:S(2)}) collective-permute-start(bf16[2,68,128]{2,1,0:T(8,128)(2,1)S(1)} %get-tuple-element.33), channel_id=1, source_target_pairs={{0,4},{4,8},{8,12},{12,16},{16,20},{20,24},{24,28},{1,5},{5,9},{9,... | collective-permute-start | bytes 104456 | tf_op jit(solution)/shard_map/ppermute | solution.py:19
  26.9 1.3 %collective-permute-start.3 = (bf16[2,68,128]{2,1,0:T(8,128)(2,1)S(1)}, bf16[2,68,128]{2,1,0:T(8,128)(2,1)S(1)}, u32[]{:S(2)}, u32[]{:S(2)}) collective-permute-start(bf16[2,68,128]{2,1,0:T(8,128)(2,1)S(1)} %get-tuple-element.34), channel_id=1, source_target_pairs={{4,0},{8,4},{12,8},{16,12},{20,16},{24,20},{28,24},{5,1},{9,5},{13... | collective-permute-start | bytes 104456 | tf_op jit(solution)/shard_map/ppermute | solution.py:22
  28.2 0.1 fusion.18
  28.3 0.1 slice.47
  28.4 0.1 copy.7
  28.5 0.0 collective-permute-done.2
  28.6 4.2 %collective-permute-done.3 = bf16[2,68,128]{2,1,0:T(8,128)(2,1)S(1)} collective-permute-done((bf16[2,68,128]{2,1,0:T(8,128)(2,1)S(1)}, bf16[2,68,128]{2,1,0:T(8,128)(2,1)S(1)}, u32[]{:S(2)}, u32[]{:S(2)}) %collective-permute-start.3) | collective-permute-done | bytes 34848 | tf_op jit(solution)/shard_map/ppermute | solution.py:22
  32.8 0.7 %reshape.78.refs_0_ = bf16[544,128]{1,0:T(8,128)(2,1)} reshape(bf16[8,68,128]{2,1,0:T(8,128)(2,1)S(1)} %pad_maximum_fusion) | data formatting | bytes 278528 | tf_op jit(solution)/shard_map/reshape | solution.py:201
  33.5 0.6 broadcast_in_dim.22.refs_2_
  34.1 5.0 %shard_map.64 = (f32[544,128]{1,0:T(8,128)}, f32[544,128]{1,0:T(8,128)}, f32[544,8]{1,0:T(8,128)}) custom-call(bf16[544,128]{1,0:T(8,128)(2,1)} %reshape.78.refs_0_, bf16[2048,128]{1,0:T(8,128)(2,1)} %refs_1_, f32[8,128]{1,0:T(8,128)} %broadcast_in_dim.22.refs_2_), custom_call_target="tpu_custom_call" | custom-call | tf_op jit(solution)/shard_map/pallas_call | solution.py:136
  39.1 0.8 %copy-done.3 = bf16[2048,128]{1,0:T(8,128)(2,1)} copy-done((bf16[2048,128]{1,0:T(8,128)(2,1)}, bf16[2048,128]{1,0:T(8,128)(2,1)S(1)}, u32[]{:S(2)}) %copy-start.3) | copy-done | bytes 524312
  39.9 4.9 %shard_map.65 = (f32[544,128]{1,0:T(8,128)}, f32[544,128]{1,0:T(8,128)}, f32[544,8]{1,0:T(8,128)}) custom-call(bf16[544,128]{1,0:T(8,128)(2,1)} %reshape.78.refs_0_, bf16[2048,128]{1,0:T(8,128)(2,1)} %copy-done.3, f32[8,128]{1,0:T(8,128)} %broadcast_in_dim.22.refs_2_, f32[544,128]{1,0:T(8,128)} %get-tuple-element.20.refs_3_, ...), custom_call_target="tpu_custom_call" | custom-call | tf_op jit(solution)/shard_map/pallas_call | solution.py:136
  44.8 5.0 %shard_map.66 = (f32[544,128]{1,0:T(8,128)}, f32[544,128]{1,0:T(8,128)}, f32[544,8]{1,0:T(8,128)}) custom-call(bf16[544,128]{1,0:T(8,128)(2,1)} %reshape.78.refs_0_, bf16[2048,128]{1,0:T(8,128)(2,1)} %copy-done.1, f32[8,128]{1,0:T(8,128)} %broadcast_in_dim.22.refs_2_, f32[544,128]{1,0:T(8,128)} %get-tuple-element.23.refs_3_, ...), custom_call_target="tpu_custom_call" | custom-call | tf_op jit(solution)/shard_map/pallas_call | solution.py:136
  49.8 0.8 %copy-done.2 = bf16[2048,128]{1,0:T(8,128)(2,1)} copy-done((bf16[2048,128]{1,0:T(8,128)(2,1)}, bf16[2048,128]{1,0:T(8,128)(2,1)S(1)}, u32[]{:S(2)}) %copy-start.2) | copy-done | bytes 524312
  50.6 5.6 %shard_map.67 = (f32[544,128]{1,0:T(8,128)}, f32[544,128]{1,0:T(8,128)}) custom-call(bf16[544,128]{1,0:T(8,128)(2,1)} %reshape.78.refs_0_, bf16[2048,128]{1,0:T(8,128)(2,1)} %copy-done.2, f32[8,128]{1,0:T(8,128)} %broadcast_in_dim.22.refs_2_, f32[544,128]{1,0:T(8,128)} %get-tuple-element.26.refs_3_, f32[544,128]{1,0:T(8,128)} %get-tuple-element.27.refs_4_, ...), custom_call_target="tpu_custom_call" | custom-call | tf_op jit(solution)/shard_map/pallas_call | solution.py:136
  56.2 1.4 %slice_reduce_fusion.1 = (f32[544]{0:T(1024)S(1)}, f32[544]{0:T(1024)S(1)}) fusion(f32[544,128]{1,0:T(8,128)} %get-tuple-element.29), kind=kLoop, calls=%fused_computation.9 | loop fusion | bytes 8704 | tf_op jit(solution)/shard_map/slice | solution.py:188
  57.6 0.1 reshape_squeeze.6
  57.7 0.1 reshape_squeeze.7
  57.8 0.1 slice.48
  57.8 0.1 broadcast_subtract_fusion
  57.9 0.1 slice_bitcast_fusion.2
  58.0 0.1 slice.50
  58.1 0.1 select_bitcast_fusion
  58.3 0.1 copy.20
  58.3 0.1 copy.10
  58.5 0.6 %copy-done.10 = pred[8,9]{0,1:T(8,128)(4,1)S(1)} copy-done((pred[8,9]{0,1:T(8,128)(4,1)S(1)}, pred[8,9]{0,1:T(8,128)(4,1)}, u32[]{:S(2)}) %copy-start.10) | copy-done | bytes 96
  59.1 0.9 %convolution_select_fusion = f32[6,8,9,128]{3,1,2,0:T(8,128)S(1)} fusion(bf16[3,3,128,128]{3,2,1,0:T(8,128)(2,1)S(1)} %copy-done, f32[8,1,7,2,128]{4,2,3,0,1:T(8,128)S(1)} %slice.56, f32[8,1,8,9,128]{4,2,3,0,1:T(8,128)S(1)} %copy.10, pred[8,9]{0,1:T(8,128)(4,1)S(1)} %copy-done.10), kind=kOutput, calls=%fused_computation | convolution fusion | flops 764737536 | bytes 868424 | tf_op jit(solution)/shard_map/conv_general_dilated | solution.py:212
  60.0 0.1 copy.11
  60.1 0.1 copy.12
  60.2 0.1 copy.13
  60.3 0.7 %copy-done.7 = f32[128]{0:T(128)S(1)} copy-done((f32[128]{0:T(128)S(1)}, f32[128]{0:T(128)}, u32[]{:S(2)}) %copy-start.7) | copy-done | bytes 536
  61.0 0.3 select_bitcast_fusion.1
  61.3 0.0 copy-start.9
  61.4 0.6 %copy-done.8 = bf16[2,3,3,128]{3,0,2,1:T(2,128)(2,1)S(1)} copy-done((bf16[2,3,3,128]{3,0,2,1:T(2,128)(2,1)S(1)}, bf16[2,3,3,128]{3,0,2,1:T(2,128)(2,1)}, u32[]{:S(2)}) %copy-start.8) | copy-done | bytes 4632
  62.0 0.0 copy-done.9
  62.0 1.7 %convolution_select_fusion.1 = f32[4,8,9,2]{1,3,2,0:T(2,128)S(1)} fusion(bf16[2,3,3,128]{3,0,2,1:T(2,128)(2,1)S(1)} %copy-done.8, bf16[6,1,7,2,128]{4,2,3,0,1:T(8,128)(2,1)S(1)} %slice.58, bf16[6,1,8,9,128]{4,2,3,0,1:T(8,128)(2,1)S(1)} %copy.15, pred[8,9]{0,1:T(8,128)(4,1)S(1)} %copy-done.9), kind=kOutput, calls=%fused_computation.1 | convolution fusion | flops 1733184 | bytes 139080 | tf_op jit(solution)/shard_map/conv_general_dilated | solution.py:223
  63.7 0.1 copy.18
  63.9 0.1 reshape.105
  64.0 0.6 fusion.17
  (34 shorter events, 0.3 us)
Async XLA Ops:
  0.0 58.4 %copy-start = (bf16[3,3,128,128]{3,2,1,0:T(8,128)(2,1)S(1)}, bf16[3,3,128,128]{3,2,1,0:T(8,128)(2,1)}, u32[]{:S(2)}) copy-start(bf16[3,3,128,128]{3,2,1,0:T(8,128)(2,1)} %param.8) | copy-start | bytes 884740
  0.0 8.3 %copy-start.5 = (bf16[4,64,128]{2,1,0:T(8,128)(2,1)S(1)}, bf16[4,64,128]{2,1,0:T(8,128)(2,1)}, u32[]{:S(2)}) copy-start(bf16[4,64,128]{2,1,0:T(8,128)(2,1)} %param.6) | copy-start | bytes 196612
  0.8 3.7 %collective-permute-start = (bf16[4,2,128]{2,1,0:T(2,128)(2,1)S(1)}, bf16[4,2,128]{2,1,0:T(2,128)(2,1)S(1)}, u32[]{:S(2)}, u32[]{:S(2)}) collective-permute-start(bf16[4,2,128]{2,1,0:T(2,128)(2,1)S(1)} %get-tuple-element.35), channel_id=1, source_target_pairs={{0,1},{1,2},{2,3},{4,5},{5,6},{6,7},{8,9},{9,10},{10,11},{12,13},{... | collective-permute-start | bytes 6152 | tf_op jit(solution)/shard_map/ppermute | solution.py:19
  3.1 5.2 %collective-permute-start.1 = (bf16[4,2,128]{2,1,0:T(2,128)(2,1)S(1)}, bf16[4,2,128]{2,1,0:T(2,128)(2,1)S(1)}, u32[]{:S(2)}, u32[]{:S(2)}) collective-permute-start(bf16[4,2,128]{2,1,0:T(2,128)(2,1)S(1)} %get-tuple-element.36), channel_id=1, source_target_pairs={{1,0},{2,1},{3,2},{5,4},{6,5},{7,6},{9,8},{10,9},{11,10},{13,12},{... | collective-permute-start | bytes 6152 | tf_op jit(solution)/shard_map/ppermute | solution.py:22
  8.3 2.4 %copy-start.6 = (f32[2,128]{1,0:T(2,128)S(1)}, f32[2,128]{1,0:T(2,128)}, u32[]{:S(2)}) copy-start(f32[2,128]{1,0:T(2,128)} %param.9) | copy-start | bytes 3076
  8.3 14.4 %collective-permute-start.4 = (bf16[2048,128]{1,0:T(8,128)(2,1)}, bf16[2048,128]{1,0:T(8,128)(2,1)S(1)}, u32[]{:S(2)}, u32[]{:S(2)}) collective-permute-start(bf16[2048,128]{1,0:T(8,128)(2,1)} %refs_1_), channel_id=1, source_target_pairs={{0,2},{1,3},{2,0},{3,1},{4,6},{5,7},{6,4},{7,5},{8,10},{9,11},{10,... | collective-permute-start | bytes 1572872 | tf_op jit(solution)/shard_map/ppermute | solution.py:164
  10.8 28.3 %collective-permute-start.6 = (bf16[2048,128]{1,0:T(8,128)(2,1)}, bf16[2048,128]{1,0:T(8,128)(2,1)S(1)}, u32[]{:S(2)}, u32[]{:S(2)}) collective-permute-start(bf16[2048,128]{1,0:T(8,128)(2,1)} %refs_1_), channel_id=1, source_target_pairs={{0,1},{1,0},{2,3},{3,2},{4,5},{5,4},{6,7},{7,6},{8,9},{9,8},{10,11... | collective-permute-start | bytes 1572872 | tf_op jit(solution)/shard_map/ppermute | solution.py:161
  22.7 16.4 %copy-start.1 = (bf16[2048,128]{1,0:T(8,128)(2,1)}, bf16[2048,128]{1,0:T(8,128)(2,1)S(1)}, u32[]{:S(2)}) copy-start(bf16[2048,128]{1,0:T(8,128)(2,1)S(1)} %collective-permute-done.4.refs_1_) | copy-start | bytes 1572868
  22.7 27.1 %collective-permute-start.5 = (bf16[2048,128]{1,0:T(8,128)(2,1)S(1)}, bf16[2048,128]{1,0:T(8,128)(2,1)S(1)}, u32[]{:S(2)}, u32[]{:S(2)}) collective-permute-start(bf16[2048,128]{1,0:T(8,128)(2,1)S(1)} %collective-permute-done.4.refs_1_), channel_id=1, source_target_pairs={{0,1},{1,0},{2,3},{3,2},{4,5},{5,4},{6,7},{7,6},{8,9},{9,8},{10,11... | collective-permute-start | bytes 1572872 | tf_op jit(solution)/shard_map/ppermute | solution.py:167
  23.5 5.0 %collective-permute-start.2 = (bf16[2,68,128]{2,1,0:T(8,128)(2,1)S(1)}, bf16[2,68,128]{2,1,0:T(8,128)(2,1)S(1)}, u32[]{:S(2)}, u32[]{:S(2)}) collective-permute-start(bf16[2,68,128]{2,1,0:T(8,128)(2,1)S(1)} %get-tuple-element.33), channel_id=1, source_target_pairs={{0,4},{4,8},{8,12},{12,16},{16,20},{20,24},{24,28},{1,5},{5,9},{9,... | collective-permute-start | bytes 104456 | tf_op jit(solution)/shard_map/ppermute | solution.py:19
  26.9 5.9 %collective-permute-start.3 = (bf16[2,68,128]{2,1,0:T(8,128)(2,1)S(1)}, bf16[2,68,128]{2,1,0:T(8,128)(2,1)S(1)}, u32[]{:S(2)}, u32[]{:S(2)}) collective-permute-start(bf16[2,68,128]{2,1,0:T(8,128)(2,1)S(1)} %get-tuple-element.34), channel_id=1, source_target_pairs={{4,0},{8,4},{12,8},{16,12},{20,16},{24,20},{28,24},{5,1},{9,5},{13... | collective-permute-start | bytes 104456 | tf_op jit(solution)/shard_map/ppermute | solution.py:22
  39.1 0.8 %copy-start.3 = (bf16[2048,128]{1,0:T(8,128)(2,1)}, bf16[2048,128]{1,0:T(8,128)(2,1)S(1)}, u32[]{:S(2)}) copy-start(bf16[2048,128]{1,0:T(8,128)(2,1)S(1)} %collective-permute-done.6.refs_1_) | copy-start | bytes 1572868
  49.8 0.8 %copy-start.2 = (bf16[2048,128]{1,0:T(8,128)(2,1)}, bf16[2048,128]{1,0:T(8,128)(2,1)S(1)}, u32[]{:S(2)}) copy-start(bf16[2048,128]{1,0:T(8,128)(2,1)S(1)} %collective-permute-done.5.refs_1_) | copy-start | bytes 1572868
  56.2 1.9 %copy-start.4 = (f32[544,128]{1,0:T(8,128)S(1)}, f32[544,128]{1,0:T(8,128)}, u32[]{:S(2)}) copy-start(f32[544,128]{1,0:T(8,128)} %get-tuple-element.30) | copy-start | bytes 835588
  58.4 0.7 %copy-start.10 = (pred[8,9]{0,1:T(8,128)(4,1)S(1)}, pred[8,9]{0,1:T(8,128)(4,1)}, u32[]{:S(2)}) copy-start(pred[8,9]{0,1:T(8,128)(4,1)} %constant.80) | copy-start | bytes 220
  60.3 0.7 %copy-start.7 = (f32[128]{0:T(128)S(1)}, f32[128]{0:T(128)}, u32[]{:S(2)}) copy-start(f32[128]{0:T(128)} %param.10) | copy-start | bytes 1540
  61.3 0.7 %copy-start.8 = (bf16[2,3,3,128]{3,0,2,1:T(2,128)(2,1)S(1)}, bf16[2,3,3,128]{3,0,2,1:T(2,128)(2,1)}, u32[]{:S(2)}) copy-start(bf16[2,3,3,128]{3,0,2,1:T(2,128)(2,1)} %param.11) | copy-start | bytes 13828
  61.3 0.7 %copy-start.9 = (pred[8,9]{0,1:T(8,128)(4,1)S(1)}, pred[8,9]{0,1:T(8,128)(4,1)}, u32[]{:S(2)}) copy-start(pred[8,9]{0,1:T(8,128)(4,1)} %constant.79) | copy-start | bytes 220

commit v9 on v8

--- a/solution.py
+++ b/solution.py
@@ -154,27 +154,33 @@
         queries = jnp.pad(queries, ((0, padded - count), (0, 0)))
     n = lax.axis_size("match")
     me = lax.axis_index("match")
-    shards = [(targets, me)]
+    shards = [(targets, me, None)]
     if n % 2 == 0:
         chips = n // 2
         sibling = [(j, j ^ 1) for j in range(n)]
-        shards.append((lax.ppermute(targets, "match", sibling), me ^ 1))
+        shards.append((lax.ppermute(targets, "match", sibling), me ^ 1, None))
         for shift in range(1, chips):
             hop = [(j, ((j // 2 + shift) % chips) * 2 + j % 2) for j in range(n)]
             moved = lax.ppermute(targets, "match", hop)
             owner = ((me // 2 - shift) % chips) * 2 + me % 2
-            shards.append((moved, owner))
-            shards.append((lax.ppermute(moved, "match", sibling), owner ^ 1))
+            shards.append((moved, owner, sibling))
+            shards.append((None, owner ^ 1, None))
     else:
         for shift in range(1, n):
             moved = lax.ppermute(targets, "match", [(j, (j + shift) % n) for j in range(n)])
-            shards.append((moved, (me - shift) % n))
+            shards.append((moved, (me - shift) % n, None))
     state = None
     if tk % width == 0:
-        owners = jnp.stack([owner for _, owner in shards]) * (tk // width)
+        owners = jnp.stack([owner for _, owner, _ in shards]) * (tk // width)
         owners = jnp.pad(owners.astype(jnp.float32), (0, 128 - n))
         table = jnp.broadcast_to(owners[None, :], (8, 128))
-    for step, (keys, owner) in enumerate(shards):
+    pending = None
+    for step, (keys, owner, forward) in enumerate(shards):
+        if keys is None:
+            keys = pending
+        if forward:
+            keys, state = lax.optimization_barrier((keys, state))
+            pending = lax.ppermute(keys, "match", forward)
         if tk % width == 0:
             pos = table
             seg = width

time: 65 us -> 53.9 us (0.83)
  waiting for transfers between devices: 19.3 us -> 8.25 us
  starting transfers between devices: 12.1 us -> 10.8 us
  local copies, waits for them, and re-layouts: 8.38 us -> 9.04 us
    ppermute x1, waiting for transfers between devices: 11.3 us -> 0.01 us  [match(): moved = lax.ppermute(targets, 'match', hop)]
    ppermute x1, starting transfers between devices: 2.35 us -> 0.01 us  [match(): moved = lax.ppermute(targets, 'match', hop)]
    ppermute x2, starting transfers between devices: 1.45 us -> 2.48 us  [the longest x1 2.42 us: match(): shards.append((lax.ppermute(targets, 'match', sibling), me ^ 1, None))]
    unnamed x23, local copies, waits for them, and re-layouts: 3.64 us -> 4.32 us
  transfers between devices with their start and end apart: 7 -> 7, of which waited for: 3 -> 3; matrix products, arithmetic and copies ran while one was open for 3% -> 3% of each run, Pallas kernels for 23% -> 28%
where the time goes in v9:
time: 53.9 us; the launch traced here: 52.9 us
  Pallas kernels  20.5 us (38%)
  starting transfers between devices  10.8 us (20%)
  local copies, waits for them, and re-layouts  9.04 us (17%)
  waiting for transfers between devices  8.25 us (15%)
  matrix products  2.64 us (5%)
  other arithmetic  1.34 us (2%)
    pallas_call x4, Pallas kernels, match_step(): pl.pallas_call(kernel, grid=(nq,), in_specs=in_specs, out_specs=out_specs...  20.5 us
    ppermute x2, waiting for transfers between devices, extended(): lax.ppermute(lax.slice_in_dim(block, 0, width, axis=dim), axis, backward)  8.02 us
    ppermute x2, starting transfers between devices, extended(): lax.ppermute(lax.slice_in_dim(block, block.shape[dim] - width, None, axis...  5.77 us
    unnamed x23, local copies, waits for them, and re-layouts  4.32 us
    ppermute x2, starting transfers between devices, extended(): lax.ppermute(lax.slice_in_dim(block, 0, width, axis=dim), axis, backward)  2.58 us
    ppermute x1, starting transfers between devices, match(): shards.append((lax.ppermute(targets, 'match', sibling), me ^ 1, None))  2.42 us
    conv_general_dilated x1, matrix products, local(): lax.conv_general_dilated(hidden[None], jnp.transpose(conv_out, (1, 2, 3,...  1.7 us
    slice x1, local copies, waits for them, and re-layouts, match(): return (warped[:count], flow[:count, 0], flow[:count, 1])  1.42 us
  transfers between devices with their start and end apart: 7, of which 3 were waited for; matrix products, arithmetic and copies ran while one was open for 3% of the time, Pallas kernels for 28%

profile of v9, /device:TPU:0, one launch (start us, length us, event | category | flops | bytes accessed | tf_op | source)
XLA Modules:
  0.0 52.9 jit_solution(5155490492065387437)
XLA Ops:
  0.0 0.8 %fusion.26 = (bf16[4,2,128]{2,1,0:T(2,128)(2,1)S(1)}, bf16[4,2,128]{2,1,0:T(2,128)(2,1)S(1)}) fusion(bf16[4,64,128]{2,1,0:T(8,128)(2,1)} %param.6), kind=kLoop, calls=%fused_computation.52 | loop fusion | bytes 8192 | tf_op jit(solution)/shard_map/slice | solution.py:20
  0.8 2.3 %collective-permute-start = (bf16[4,2,128]{2,1,0:T(2,128)(2,1)S(1)}, bf16[4,2,128]{2,1,0:T(2,128)(2,1)S(1)}, u32[]{:S(2)}, u32[]{:S(2)}) collective-permute-start(bf16[4,2,128]{2,1,0:T(2,128)(2,1)S(1)} %get-tuple-element.43), channel_id=1, source_target_pairs={{0,1},{1,2},{2,3},{4,5},{5,6},{6,7},{8,9},{9,10},{10,11},{12,13},{... | collective-permute-start | bytes 6152 | tf_op jit(solution)/shard_map/ppermute | solution.py:19
  3.1 1.3 %collective-permute-start.1 = (bf16[4,2,128]{2,1,0:T(2,128)(2,1)S(1)}, bf16[4,2,128]{2,1,0:T(2,128)(2,1)S(1)}, u32[]{:S(2)}, u32[]{:S(2)}) collective-permute-start(bf16[4,2,128]{2,1,0:T(2,128)(2,1)S(1)} %get-tuple-element.44), channel_id=1, source_target_pairs={{1,0},{2,1},{3,2},{5,4},{6,5},{7,6},{9,8},{10,9},{11,10},{13,12},{... | collective-permute-start | bytes 6152 | tf_op jit(solution)/shard_map/ppermute | solution.py:22
  4.5 3.8 %collective-permute-done.1 = bf16[4,2,128]{2,1,0:T(2,128)(2,1)S(1)} collective-permute-done((bf16[4,2,128]{2,1,0:T(2,128)(2,1)S(1)}, bf16[4,2,128]{2,1,0:T(2,128)(2,1)S(1)}, u32[]{:S(2)}, u32[]{:S(2)}) %collective-permute-start.1) | collective-permute-done | bytes 2080 | tf_op jit(solution)/shard_map/ppermute | solution.py:22
  8.3 2.4 %collective-permute-start.5 = (bf16[2048,128]{1,0:T(8,128)(2,1)}, bf16[2048,128]{1,0:T(8,128)(2,1)S(1)}, u32[]{:S(2)}, u32[]{:S(2)}) collective-permute-start(bf16[2048,128]{1,0:T(8,128)(2,1)} %refs_1_), channel_id=1, source_target_pairs={{0,1},{1,0},{2,3},{3,2},{4,5},{5,4},{6,7},{7,6},{8,9},{9,8},{10,11... | collective-permute-start | bytes 1572872 | tf_op jit(solution)/shard_map/ppermute | solution.py:161
  10.7 0.0 collective-permute-start.4
  10.8 3.4 %collective-permute-start.2 = (bf16[2,68,128]{2,1,0:T(8,128)(2,1)S(1)}, bf16[2,68,128]{2,1,0:T(8,128)(2,1)S(1)}, u32[]{:S(2)}, u32[]{:S(2)}) collective-permute-start(bf16[2,68,128]{2,1,0:T(8,128)(2,1)S(1)} %get-tuple-element.41), channel_id=1, source_target_pairs={{0,4},{4,8},{8,12},{12,16},{16,20},{20,24},{24,28},{1,5},{5,9},{9,... | collective-permute-start | bytes 104456 | tf_op jit(solution)/shard_map/ppermute | solution.py:19
  14.2 1.3 %collective-permute-start.3 = (bf16[2,68,128]{2,1,0:T(8,128)(2,1)S(1)}, bf16[2,68,128]{2,1,0:T(8,128)(2,1)S(1)}, u32[]{:S(2)}, u32[]{:S(2)}) collective-permute-start(bf16[2,68,128]{2,1,0:T(8,128)(2,1)S(1)} %get-tuple-element.42), channel_id=1, source_target_pairs={{4,0},{8,4},{12,8},{16,12},{20,16},{24,20},{28,24},{5,1},{9,5},{13... | collective-permute-start | bytes 104456 | tf_op jit(solution)/shard_map/ppermute | solution.py:22
  15.5 0.1 fusion.18
  15.6 0.2 collective-permute-done.2
  15.8 4.2 %collective-permute-done.3 = bf16[2,68,128]{2,1,0:T(8,128)(2,1)S(1)} collective-permute-done((bf16[2,68,128]{2,1,0:T(8,128)(2,1)S(1)}, bf16[2,68,128]{2,1,0:T(8,128)(2,1)S(1)}, u32[]{:S(2)}, u32[]{:S(2)}) %collective-permute-start.3) | collective-permute-done | bytes 34848 | tf_op jit(solution)/shard_map/ppermute | solution.py:22
  20.1 0.7 %reshape.78.refs_0_ = bf16[544,128]{1,0:T(8,128)(2,1)} reshape(bf16[8,68,128]{2,1,0:T(8,128)(2,1)S(1)} %pad_maximum_fusion) | data formatting | bytes 278528 | tf_op jit(solution)/shard_map/reshape | solution.py:207
  20.8 0.6 %broadcast_in_dim.22.refs_2_ = f32[8,128]{1,0:T(8,128)} broadcast(f32[128]{0:T(128)S(1)} %pad.4), dimensions={1} | broadcast | bytes 4608 | tf_op jit(solution)/shard_map/broadcast_in_dim | solution.py:176
  21.3 5.0 %shard_map.64 = (f32[544,128]{1,0:T(8,128)}, f32[544,128]{1,0:T(8,128)}, f32[544,8]{1,0:T(8,128)}) custom-call(bf16[544,128]{1,0:T(8,128)(2,1)} %reshape.78.refs_0_, bf16[2048,128]{1,0:T(8,128)(2,1)} %refs_1_, f32[8,128]{1,0:T(8,128)} %broadcast_in_dim.22.refs_2_), custom_call_target="tpu_custom_call" | custom-call | tf_op jit(solution)/shard_map/pallas_call | solution.py:136
  26.3 0.8 %copy-done.2 = bf16[2048,128]{1,0:T(8,128)(2,1)} copy-done((bf16[2048,128]{1,0:T(8,128)(2,1)}, bf16[2048,128]{1,0:T(8,128)(2,1)S(1)}, u32[]{:S(2)}) %copy-start.2) | copy-done | bytes 524312
  27.1 5.0 %shard_map.65 = (f32[544,128]{1,0:T(8,128)}, f32[544,128]{1,0:T(8,128)}, f32[544,8]{1,0:T(8,128)}) custom-call(bf16[544,128]{1,0:T(8,128)(2,1)} %reshape.78.refs_0_, bf16[2048,128]{1,0:T(8,128)(2,1)} %copy-done.2, f32[8,128]{1,0:T(8,128)} %broadcast_in_dim.22.refs_2_, f32[544,128]{1,0:T(8,128)} %get-tuple-element.24.refs_3_, ...), custom_call_target="tpu_custom_call" | custom-call | tf_op jit(solution)/shard_map/pallas_call | solution.py:136
  32.1 0.1 collective-permute-start.6
  32.2 0.1 broadcast_and_fusion
  32.2 0.1 slice.47
  32.3 0.1 copy.7
  32.5 0.7 %copy-done.6 = f32[2,128]{1,0:T(2,128)S(1)} copy-done((f32[2,128]{1,0:T(2,128)S(1)}, f32[2,128]{1,0:T(2,128)}, u32[]{:S(2)}) %copy-start.6) | copy-done | bytes 1048
  33.1 4.9 %shard_map.66 = (f32[544,128]{1,0:T(8,128)}, f32[544,128]{1,0:T(8,128)}, f32[544,8]{1,0:T(8,128)}) custom-call(bf16[544,128]{1,0:T(8,128)(2,1)} %reshape.78.refs_0_, bf16[2048,128]{1,0:T(8,128)(2,1)} %copy-done.1, f32[8,128]{1,0:T(8,128)} %broadcast_in_dim.22.refs_2_, f32[544,128]{1,0:T(8,128)} %get-tuple-element.31.refs_3_, ...), custom_call_target="tpu_custom_call" | custom-call | tf_op jit(solution)/shard_map/pallas_call | solution.py:136
  38.1 0.8 %copy-done.3 = bf16[2048,128]{1,0:T(8,128)(2,1)} copy-done((bf16[2048,128]{1,0:T(8,128)(2,1)}, bf16[2048,128]{1,0:T(8,128)(2,1)S(1)}, u32[]{:S(2)}) %copy-start.3) | copy-done | bytes 524312
  38.9 5.6 %shard_map.67 = (f32[544,128]{1,0:T(8,128)}, f32[544,128]{1,0:T(8,128)}) custom-call(bf16[544,128]{1,0:T(8,128)(2,1)} %reshape.78.refs_0_, bf16[2048,128]{1,0:T(8,128)(2,1)} %copy-done.3, f32[8,128]{1,0:T(8,128)} %broadcast_in_dim.22.refs_2_, f32[544,128]{1,0:T(8,128)} %get-tuple-element.34.refs_3_, f32[544,128]{1,0:T(8,128)} %get-tuple-element.35.refs_4_, ...), custom_call_target="tpu_custom_call" | custom-call | tf_op jit(solution)/shard_map/pallas_call | solution.py:136
  44.5 1.4 %slice_reduce_fusion.1 = (f32[544]{0:T(1024)S(1)}, f32[544]{0:T(1024)S(1)}) fusion(f32[544,128]{1,0:T(8,128)} %get-tuple-element.37), kind=kLoop, calls=%fused_computation.9 | loop fusion | bytes 8704 | tf_op jit(solution)/shard_map/slice | solution.py:194
  45.9 0.1 reshape_squeeze.6
  46.0 0.1 reshape_squeeze.7
  46.1 0.1 slice.48
  46.1 0.1 broadcast_subtract_fusion
  46.2 0.1 slice_bitcast_fusion.2
  46.3 0.1 slice.50
  46.4 0.1 select_bitcast_fusion
  46.5 0.1 copy.20
  46.6 0.1 copy.10
  46.7 0.0 copy-start.10
  46.7 0.6 %copy-done.10 = pred[8,9]{0,1:T(8,128)(4,1)S(1)} copy-done((pred[8,9]{0,1:T(8,128)(4,1)S(1)}, pred[8,9]{0,1:T(8,128)(4,1)}, u32[]{:S(2)}) %copy-start.10) | copy-done | bytes 96
  47.4 0.9 %convolution_select_fusion = f32[6,8,9,128]{3,1,2,0:T(8,128)S(1)} fusion(bf16[3,3,128,128]{3,2,1,0:T(8,128)(2,1)S(1)} %copy-done, f32[8,1,7,2,128]{4,2,3,0,1:T(8,128)S(1)} %slice.56, f32[8,1,8,9,128]{4,2,3,0,1:T(8,128)S(1)} %copy.10, pred[8,9]{0,1:T(8,128)(4,1)S(1)} %copy-done.10), kind=kOutput, calls=%fused_computation | convolution fusion | flops 764737536 | bytes 868424 | tf_op jit(solution)/shard_map/conv_general_dilated | solution.py:218
  48.3 0.1 copy.11
  48.4 0.1 copy.12
  48.5 0.1 copy.13
  48.6 0.7 %copy-done.7 = f32[128]{0:T(128)S(1)} copy-done((f32[128]{0:T(128)S(1)}, f32[128]{0:T(128)}, u32[]{:S(2)}) %copy-start.7) | copy-done | bytes 536
  49.3 0.3 select_bitcast_fusion.1
  49.7 0.6 %copy-done.8 = bf16[2,3,3,128]{3,0,2,1:T(2,128)(2,1)S(1)} copy-done((bf16[2,3,3,128]{3,0,2,1:T(2,128)(2,1)S(1)}, bf16[2,3,3,128]{3,0,2,1:T(2,128)(2,1)}, u32[]{:S(2)}) %copy-start.8) | copy-done | bytes 4632
  50.3 0.0 copy-done.9
  50.3 1.7 %convolution_select_fusion.1 = f32[4,8,9,2]{1,3,2,0:T(2,128)S(1)} fusion(bf16[2,3,3,128]{3,0,2,1:T(2,128)(2,1)S(1)} %copy-done.8, bf16[6,1,7,2,128]{4,2,3,0,1:T(8,128)(2,1)S(1)} %slice.58, bf16[6,1,8,9,128]{4,2,3,0,1:T(8,128)(2,1)S(1)} %copy.15, pred[8,9]{0,1:T(8,128)(4,1)S(1)} %copy-done.9), kind=kOutput, calls=%fused_computation.1 | convolution fusion | flops 1733184 | bytes 139080 | tf_op jit(solution)/shard_map/conv_general_dilated | solution.py:229
  52.0 0.1 copy.18
  52.2 0.1 reshape.105
  52.2 0.6 %fusion.17 = f32[2,4,64]{2,1,0:T(4,128)} fusion(f32[4,1,72,2]{2,0,3,1:T(4,128)S(1)} %reshape.105, f32[1,4,64]{2,1,0:T(4,128)S(1)} %get-tuple-element.47, f32[1,4,64]{2,1,0:T(4,128)S(1)} %get-tuple-element.48), kind=kLoop, calls=%fused_computation.29 | loop fusion | flops 1024 | bytes 6144 | tf_op jit(solution)/shard_map/add | solution.py:235
  (34 shorter events, 0.3 us)
Async XLA Ops:
  0.0 46.7 %copy-start = (bf16[3,3,128,128]{3,2,1,0:T(8,128)(2,1)S(1)}, bf16[3,3,128,128]{3,2,1,0:T(8,128)(2,1)}, u32[]{:S(2)}) copy-start(bf16[3,3,128,128]{3,2,1,0:T(8,128)(2,1)} %param.8) | copy-start | bytes 884740
  0.0 8.3 %copy-start.5 = (bf16[4,64,128]{2,1,0:T(8,128)(2,1)S(1)}, bf16[4,64,128]{2,1,0:T(8,128)(2,1)}, u32[]{:S(2)}) copy-start(bf16[4,64,128]{2,1,0:T(8,128)(2,1)} %param.6) | copy-start | bytes 196612
  0.8 3.7 %collective-permute-start = (bf16[4,2,128]{2,1,0:T(2,128)(2,1)S(1)}, bf16[4,2,128]{2,1,0:T(2,128)(2,1)S(1)}, u32[]{:S(2)}, u32[]{:S(2)}) collective-permute-start(bf16[4,2,128]{2,1,0:T(2,128)(2,1)S(1)} %get-tuple-element.43), channel_id=1, source_target_pairs={{0,1},{1,2},{2,3},{4,5},{5,6},{6,7},{8,9},{9,10},{10,11},{12,13},{... | collective-permute-start | bytes 6152 | tf_op jit(solution)/shard_map/ppermute | solution.py:19
  3.1 5.2 %collective-permute-start.1 = (bf16[4,2,128]{2,1,0:T(2,128)(2,1)S(1)}, bf16[4,2,128]{2,1,0:T(2,128)(2,1)S(1)}, u32[]{:S(2)}, u32[]{:S(2)}) collective-permute-start(bf16[4,2,128]{2,1,0:T(2,128)(2,1)S(1)} %get-tuple-element.44), channel_id=1, source_target_pairs={{1,0},{2,1},{3,2},{5,4},{6,5},{7,6},{9,8},{10,9},{11,10},{13,12},{... | collective-permute-start | bytes 6152 | tf_op jit(solution)/shard_map/ppermute | solution.py:22
  8.3 18.0 %collective-permute-start.5 = (bf16[2048,128]{1,0:T(8,128)(2,1)}, bf16[2048,128]{1,0:T(8,128)(2,1)S(1)}, u32[]{:S(2)}, u32[]{:S(2)}) collective-permute-start(bf16[2048,128]{1,0:T(8,128)(2,1)} %refs_1_), channel_id=1, source_target_pairs={{0,1},{1,0},{2,3},{3,2},{4,5},{5,4},{6,7},{7,6},{8,9},{9,8},{10,11... | collective-permute-start | bytes 1572872 | tf_op jit(solution)/shard_map/ppermute | solution.py:161
  10.7 21.3 %collective-permute-start.4 = (bf16[2048,128]{1,0:T(8,128)(2,1)}, bf16[2048,128]{1,0:T(8,128)(2,1)S(1)}, u32[]{:S(2)}, u32[]{:S(2)}) collective-permute-start(bf16[2048,128]{1,0:T(8,128)(2,1)} %refs_1_), channel_id=1, source_target_pairs={{0,2},{1,3},{2,0},{3,1},{4,6},{5,7},{6,4},{7,5},{8,10},{9,11},{10,... | collective-permute-start | bytes 1572872 | tf_op jit(solution)/shard_map/ppermute | solution.py:164
  10.8 5.0 %collective-permute-start.2 = (bf16[2,68,128]{2,1,0:T(8,128)(2,1)S(1)}, bf16[2,68,128]{2,1,0:T(8,128)(2,1)S(1)}, u32[]{:S(2)}, u32[]{:S(2)}) collective-permute-start(bf16[2,68,128]{2,1,0:T(8,128)(2,1)S(1)} %get-tuple-element.41), channel_id=1, source_target_pairs={{0,4},{4,8},{8,12},{12,16},{16,20},{20,24},{24,28},{1,5},{5,9},{9,... | collective-permute-start | bytes 104456 | tf_op jit(solution)/shard_map/ppermute | solution.py:19
  14.2 5.9 %collective-permute-start.3 = (bf16[2,68,128]{2,1,0:T(8,128)(2,1)S(1)}, bf16[2,68,128]{2,1,0:T(8,128)(2,1)S(1)}, u32[]{:S(2)}, u32[]{:S(2)}) collective-permute-start(bf16[2,68,128]{2,1,0:T(8,128)(2,1)S(1)} %get-tuple-element.42), channel_id=1, source_target_pairs={{4,0},{8,4},{12,8},{16,12},{20,16},{24,20},{28,24},{5,1},{9,5},{13... | collective-permute-start | bytes 104456 | tf_op jit(solution)/shard_map/ppermute | solution.py:22
  26.3 0.8 %copy-start.2 = (bf16[2048,128]{1,0:T(8,128)(2,1)}, bf16[2048,128]{1,0:T(8,128)(2,1)S(1)}, u32[]{:S(2)}) copy-start(bf16[2048,128]{1,0:T(8,128)(2,1)S(1)} %collective-permute-done.5.refs_1_) | copy-start | bytes 1572868
  32.1 1.1 %copy-start.1 = (bf16[2048,128]{1,0:T(8,128)(2,1)}, bf16[2048,128]{1,0:T(8,128)(2,1)S(1)}, u32[]{:S(2)}) copy-start(bf16[2048,128]{1,0:T(8,128)(2,1)S(1)} %collective-permute-done.4.refs_1_) | copy-start | bytes 1572868
  32.1 6.0 %collective-permute-start.6 = (bf16[2048,128]{1,0:T(8,128)(2,1)S(1)}, bf16[2048,128]{1,0:T(8,128)(2,1)S(1)}, u32[]{:S(2)}, u32[]{:S(2)}) collective-permute-start(bf16[2048,128]{1,0:T(8,128)(2,1)S(1)} %collective-permute-done.4.refs_1_), channel_id=1, source_target_pairs={{0,1},{1,0},{2,3},{3,2},{4,5},{5,4},{6,7},{7,6},{8,9},{9,8},{10,11... | collective-permute-start | bytes 1572872 | tf_op jit(solution)/shard_map/ppermute | solution.py:183
  32.5 0.7 %copy-start.6 = (f32[2,128]{1,0:T(2,128)S(1)}, f32[2,128]{1,0:T(2,128)}, u32[]{:S(2)}) copy-start(f32[2,128]{1,0:T(2,128)} %param.9) | copy-start | bytes 3076
  38.1 0.8 %copy-start.3 = (bf16[2048,128]{1,0:T(8,128)(2,1)}, bf16[2048,128]{1,0:T(8,128)(2,1)S(1)}, u32[]{:S(2)}) copy-start(bf16[2048,128]{1,0:T(8,128)(2,1)S(1)} %collective-permute-done.6.refs_1_) | copy-start | bytes 1572868
  44.5 1.9 %copy-start.4 = (f32[544,128]{1,0:T(8,128)S(1)}, f32[544,128]{1,0:T(8,128)}, u32[]{:S(2)}) copy-start(f32[544,128]{1,0:T(8,128)} %get-tuple-element.38) | copy-start | bytes 835588
  46.7 0.7 %copy-start.10 = (pred[8,9]{0,1:T(8,128)(4,1)S(1)}, pred[8,9]{0,1:T(8,128)(4,1)}, u32[]{:S(2)}) copy-start(pred[8,9]{0,1:T(8,128)(4,1)} %constant.80) | copy-start | bytes 220
  48.6 0.7 %copy-start.7 = (f32[128]{0:T(128)S(1)}, f32[128]{0:T(128)}, u32[]{:S(2)}) copy-start(f32[128]{0:T(128)} %param.10) | copy-start | bytes 1540
  49.6 0.7 %copy-start.8 = (bf16[2,3,3,128]{3,0,2,1:T(2,128)(2,1)S(1)}, bf16[2,3,3,128]{3,0,2,1:T(2,128)(2,1)}, u32[]{:S(2)}) copy-start(bf16[2,3,3,128]{3,0,2,1:T(2,128)(2,1)} %param.11) | copy-start | bytes 13828
  49.6 0.7 %copy-start.9 = (pred[8,9]{0,1:T(8,128)(4,1)S(1)}, pred[8,9]{0,1:T(8,128)(4,1)}, u32[]{:S(2)}) copy-start(pred[8,9]{0,1:T(8,128)(4,1)} %constant.79) | copy-start | bytes 220

commit v10 on v9

--- a/solution.py
+++ b/solution.py
@@ -25,12 +25,16 @@
 
 
 def row_sums(w, base_ref, width, slot):
-    area = w[:, 0:width]
+    count = w.shape[1] // width
+    parts = [w[:, g * width:(g + 1) * width] for g in range(count)]
     weighted = None
-    for g in range(1, w.shape[1] // width):
-        part = w[:, g * width:(g + 1) * width]
-        area = area + part
-        weighted = part * float(g) if weighted is None else weighted + part * float(g)
+    area = parts[-1]
+    for g in range(count - 1, 0, -1):
+        if g < count - 1:
+            area = area + parts[g]
+        weighted = area if weighted is None else weighted + area
+    if count > 1:
+        area = area + parts[0]
     lane = lax.broadcasted_iota(jnp.int32, (1, width), 1)
     col = lane.astype(jnp.float32) / width
     total = jnp.sum(area, axis=1, keepdims=True)
@@ -52,12 +56,13 @@
     s = lax.dot_general(
         q_ref[...], k_ref[...], (((1,), (1,)), ((), ())),
         preferred_element_type=jnp.float32,
-    ) * scale
+    )
     peak = jnp.max(s, axis=1, keepdims=True)
     if not first:
         old = m_ref[:, 0:1]
         peak = jnp.maximum(old, peak)
-    w = jnp.exp(s - peak)
+    rate = scale * math.log2(math.e)
+    w = jnp.exp2((s - peak) * rate)
     hi = w.astype(jnp.bfloat16)
     if not width:
         lo = (w - hi.astype(jnp.float32)).astype(jnp.bfloat16)
@@ -70,7 +75,7 @@
             hi, pos_ref[...], lanes, preferred_element_type=jnp.float32
         ) + lax.dot_general(lo, pos_ref[...], lanes, preferred_element_type=jnp.float32)
     if not first:
-        alpha = jnp.exp(old - peak)
+        alpha = jnp.exp2((old - peak) * rate)
         acc = acc_ref[...] * alpha + acc
         st = st_ref[...] * alpha + st
     if last:

time: 53.9 us -> 53.2 us (0.987)
  Pallas kernels: 20.5 us -> 19.7 us
    pallas_call x4, Pallas kernels: 20.5 us -> 19.7 us  [match_step(): pl.pallas_call(kernel, grid=(nq,), in_specs=in_specs, out_specs=out_specs...]
  transfers between devices with their start and end apart: 7 -> 7, of which waited for: 3 -> 3; matrix products, arithmetic and copies ran while one was open for 3% -> 3% of each run, Pallas kernels for 28% -> 27%
where the time goes in v10:
time: 53.2 us; the launch traced here: 52.1 us
  Pallas kernels  19.7 us (37%)
  starting transfers between devices  10.8 us (20%)
  local copies, waits for them, and re-layouts  9.04 us (17%)
  waiting for transfers between devices  8.25 us (16%)
  matrix products  2.64 us (5%)
  other arithmetic  1.34 us (3%)
    pallas_call x4, Pallas kernels, match_step(): pl.pallas_call(kernel, grid=(nq,), in_specs=in_specs, out_specs=out_specs...  19.7 us
    ppermute x2, waiting for transfers between devices, extended(): lax.ppermute(lax.slice_in_dim(block, 0, width, axis=dim), axis, backward)  8.02 us
    ppermute x2, starting transfers between devices, extended(): lax.ppermute(lax.slice_in_dim(block, block.shape[dim] - width, None, axis...  5.77 us
    unnamed x23, local copies, waits for them, and re-layouts  4.32 us
    ppermute x2, starting transfers between devices, extended(): lax.ppermute(lax.slice_in_dim(block, 0, width, axis=dim), axis, backward)  2.58 us
    ppermute x1, starting transfers between devices, match(): shards.append((lax.ppermute(targets, 'match', sibling), me ^ 1, None))  2.42 us
    conv_general_dilated x1, matrix products, local(): lax.conv_general_dilated(hidden[None], jnp.transpose(conv_out, (1, 2, 3,...  1.7 us
    slice x1, local copies, waits for them, and re-layouts, match(): return (warped[:count], flow[:count, 0], flow[:count, 1])  1.42 us
  transfers between devices with their start and end apart: 7, of which 3 were waited for; matrix products, arithmetic and copies ran while one was open for 3% of the time, Pallas kernels for 27%

profile of v10, /device:TPU:0, one launch (start us, length us, event | category | flops | bytes accessed | tf_op | source)
XLA Modules:
  0.0 52.1 jit_solution(3758425064574396912)
XLA Ops:
  0.0 0.8 %fusion.26 = (bf16[4,2,128]{2,1,0:T(2,128)(2,1)S(1)}, bf16[4,2,128]{2,1,0:T(2,128)(2,1)S(1)}) fusion(bf16[4,64,128]{2,1,0:T(8,128)(2,1)} %param.6), kind=kLoop, calls=%fused_computation.52 | loop fusion | bytes 8192 | tf_op jit(solution)/shard_map/slice | solution.py:20
  0.8 2.3 %collective-permute-start = (bf16[4,2,128]{2,1,0:T(2,128)(2,1)S(1)}, bf16[4,2,128]{2,1,0:T(2,128)(2,1)S(1)}, u32[]{:S(2)}, u32[]{:S(2)}) collective-permute-start(bf16[4,2,128]{2,1,0:T(2,128)(2,1)S(1)} %get-tuple-element.43), channel_id=1, source_target_pairs={{0,1},{1,2},{2,3},{4,5},{5,6},{6,7},{8,9},{9,10},{10,11},{12,13},{... | collective-permute-start | bytes 6152 | tf_op jit(solution)/shard_map/ppermute | solution.py:19
  3.1 1.3 %collective-permute-start.1 = (bf16[4,2,128]{2,1,0:T(2,128)(2,1)S(1)}, bf16[4,2,128]{2,1,0:T(2,128)(2,1)S(1)}, u32[]{:S(2)}, u32[]{:S(2)}) collective-permute-start(bf16[4,2,128]{2,1,0:T(2,128)(2,1)S(1)} %get-tuple-element.44), channel_id=1, source_target_pairs={{1,0},{2,1},{3,2},{5,4},{6,5},{7,6},{9,8},{10,9},{11,10},{13,12},{... | collective-permute-start | bytes 6152 | tf_op jit(solution)/shard_map/ppermute | solution.py:22
  4.5 3.8 %collective-permute-done.1 = bf16[4,2,128]{2,1,0:T(2,128)(2,1)S(1)} collective-permute-done((bf16[4,2,128]{2,1,0:T(2,128)(2,1)S(1)}, bf16[4,2,128]{2,1,0:T(2,128)(2,1)S(1)}, u32[]{:S(2)}, u32[]{:S(2)}) %collective-permute-start.1) | collective-permute-done | bytes 2080 | tf_op jit(solution)/shard_map/ppermute | solution.py:22
  8.3 2.4 %collective-permute-start.5 = (bf16[2048,128]{1,0:T(8,128)(2,1)}, bf16[2048,128]{1,0:T(8,128)(2,1)S(1)}, u32[]{:S(2)}, u32[]{:S(2)}) collective-permute-start(bf16[2048,128]{1,0:T(8,128)(2,1)} %refs_1_), channel_id=1, source_target_pairs={{0,1},{1,0},{2,3},{3,2},{4,5},{5,4},{6,7},{7,6},{8,9},{9,8},{10,11... | collective-permute-start | bytes 1572872 | tf_op jit(solution)/shard_map/ppermute | solution.py:166
  10.7 0.0 collective-permute-start.4
  10.8 3.4 %collective-permute-start.2 = (bf16[2,68,128]{2,1,0:T(8,128)(2,1)S(1)}, bf16[2,68,128]{2,1,0:T(8,128)(2,1)S(1)}, u32[]{:S(2)}, u32[]{:S(2)}) collective-permute-start(bf16[2,68,128]{2,1,0:T(8,128)(2,1)S(1)} %get-tuple-element.41), channel_id=1, source_target_pairs={{0,4},{4,8},{8,12},{12,16},{16,20},{20,24},{24,28},{1,5},{5,9},{9,... | collective-permute-start | bytes 104456 | tf_op jit(solution)/shard_map/ppermute | solution.py:19
  14.2 1.3 %collective-permute-start.3 = (bf16[2,68,128]{2,1,0:T(8,128)(2,1)S(1)}, bf16[2,68,128]{2,1,0:T(8,128)(2,1)S(1)}, u32[]{:S(2)}, u32[]{:S(2)}) collective-permute-start(bf16[2,68,128]{2,1,0:T(8,128)(2,1)S(1)} %get-tuple-element.42), channel_id=1, source_target_pairs={{4,0},{8,4},{12,8},{16,12},{20,16},{24,20},{28,24},{5,1},{9,5},{13... | collective-permute-start | bytes 104456 | tf_op jit(solution)/shard_map/ppermute | solution.py:22
  15.5 0.1 fusion.18
  15.6 0.2 collective-permute-done.2
  15.8 4.2 %collective-permute-done.3 = bf16[2,68,128]{2,1,0:T(8,128)(2,1)S(1)} collective-permute-done((bf16[2,68,128]{2,1,0:T(8,128)(2,1)S(1)}, bf16[2,68,128]{2,1,0:T(8,128)(2,1)S(1)}, u32[]{:S(2)}, u32[]{:S(2)}) %collective-permute-start.3) | collective-permute-done | bytes 34848 | tf_op jit(solution)/shard_map/ppermute | solution.py:22
  20.1 0.7 %reshape.78.refs_0_ = bf16[544,128]{1,0:T(8,128)(2,1)} reshape(bf16[8,68,128]{2,1,0:T(8,128)(2,1)S(1)} %pad_maximum_fusion) | data formatting | bytes 278528 | tf_op jit(solution)/shard_map/reshape | solution.py:212
  20.8 0.6 %broadcast_in_dim.22.refs_2_ = f32[8,128]{1,0:T(8,128)} broadcast(f32[128]{0:T(128)S(1)} %pad.4), dimensions={1} | broadcast | bytes 4608 | tf_op jit(solution)/shard_map/broadcast_in_dim | solution.py:181
  21.3 4.7 %shard_map.64 = (f32[544,128]{1,0:T(8,128)}, f32[544,128]{1,0:T(8,128)}, f32[544,8]{1,0:T(8,128)}) custom-call(bf16[544,128]{1,0:T(8,128)(2,1)} %reshape.78.refs_0_, bf16[2048,128]{1,0:T(8,128)(2,1)} %refs_1_, f32[8,128]{1,0:T(8,128)} %broadcast_in_dim.22.refs_2_), custom_call_target="tpu_custom_call" | custom-call | tf_op jit(solution)/shard_map/pallas_call | solution.py:141
  26.1 0.8 %copy-done.2 = bf16[2048,128]{1,0:T(8,128)(2,1)} copy-done((bf16[2048,128]{1,0:T(8,128)(2,1)}, bf16[2048,128]{1,0:T(8,128)(2,1)S(1)}, u32[]{:S(2)}) %copy-start.2) | copy-done | bytes 524312
  26.9 4.8 %shard_map.65 = (f32[544,128]{1,0:T(8,128)}, f32[544,128]{1,0:T(8,128)}, f32[544,8]{1,0:T(8,128)}) custom-call(bf16[544,128]{1,0:T(8,128)(2,1)} %reshape.78.refs_0_, bf16[2048,128]{1,0:T(8,128)(2,1)} %copy-done.2, f32[8,128]{1,0:T(8,128)} %broadcast_in_dim.22.refs_2_, f32[544,128]{1,0:T(8,128)} %get-tuple-element.24.refs_3_, ...), custom_call_target="tpu_custom_call" | custom-call | tf_op jit(solution)/shard_map/pallas_call | solution.py:141
  31.7 0.1 collective-permute-start.6
  31.8 0.1 broadcast_and_fusion
  31.8 0.1 slice.47
  31.9 0.1 copy.7
  32.1 0.7 %copy-done.6 = f32[2,128]{1,0:T(2,128)S(1)} copy-done((f32[2,128]{1,0:T(2,128)S(1)}, f32[2,128]{1,0:T(2,128)}, u32[]{:S(2)}) %copy-start.6) | copy-done | bytes 1048
  32.7 4.8 %shard_map.66 = (f32[544,128]{1,0:T(8,128)}, f32[544,128]{1,0:T(8,128)}, f32[544,8]{1,0:T(8,128)}) custom-call(bf16[544,128]{1,0:T(8,128)(2,1)} %reshape.78.refs_0_, bf16[2048,128]{1,0:T(8,128)(2,1)} %copy-done.1, f32[8,128]{1,0:T(8,128)} %broadcast_in_dim.22.refs_2_, f32[544,128]{1,0:T(8,128)} %get-tuple-element.31.refs_3_, ...), custom_call_target="tpu_custom_call" | custom-call | tf_op jit(solution)/shard_map/pallas_call | solution.py:141
  37.5 0.8 %copy-done.3 = bf16[2048,128]{1,0:T(8,128)(2,1)} copy-done((bf16[2048,128]{1,0:T(8,128)(2,1)}, bf16[2048,128]{1,0:T(8,128)(2,1)S(1)}, u32[]{:S(2)}) %copy-start.3) | copy-done | bytes 524312
  38.3 5.4 %shard_map.67 = (f32[544,128]{1,0:T(8,128)}, f32[544,128]{1,0:T(8,128)}) custom-call(bf16[544,128]{1,0:T(8,128)(2,1)} %reshape.78.refs_0_, bf16[2048,128]{1,0:T(8,128)(2,1)} %copy-done.3, f32[8,128]{1,0:T(8,128)} %broadcast_in_dim.22.refs_2_, f32[544,128]{1,0:T(8,128)} %get-tuple-element.34.refs_3_, f32[544,128]{1,0:T(8,128)} %get-tuple-element.35.refs_4_, ...), custom_call_target="tpu_custom_call" | custom-call | tf_op jit(solution)/shard_map/pallas_call | solution.py:141
  43.7 1.4 %slice_reduce_fusion.1 = (f32[544]{0:T(1024)S(1)}, f32[544]{0:T(1024)S(1)}) fusion(f32[544,128]{1,0:T(8,128)} %get-tuple-element.37), kind=kLoop, calls=%fused_computation.9 | loop fusion | bytes 8704 | tf_op jit(solution)/shard_map/slice | solution.py:199
  45.2 0.1 reshape_squeeze.6
  45.2 0.1 reshape_squeeze.7
  45.3 0.1 slice.48
  45.4 0.1 broadcast_subtract_fusion
  45.5 0.1 slice_bitcast_fusion.2
  45.5 0.1 slice.50
  45.6 0.1 select_bitcast_fusion
  45.8 0.1 copy.20
  45.9 0.1 copy.10
  46.0 0.0 copy-start.10
  46.0 0.6 %copy-done.10 = pred[8,9]{0,1:T(8,128)(4,1)S(1)} copy-done((pred[8,9]{0,1:T(8,128)(4,1)S(1)}, pred[8,9]{0,1:T(8,128)(4,1)}, u32[]{:S(2)}) %copy-start.10) | copy-done | bytes 96
  46.6 0.9 %convolution_select_fusion = f32[6,8,9,128]{3,1,2,0:T(8,128)S(1)} fusion(bf16[3,3,128,128]{3,2,1,0:T(8,128)(2,1)S(1)} %copy-done, f32[8,1,7,2,128]{4,2,3,0,1:T(8,128)S(1)} %slice.56, f32[8,1,8,9,128]{4,2,3,0,1:T(8,128)S(1)} %copy.10, pred[8,9]{0,1:T(8,128)(4,1)S(1)} %copy-done.10), kind=kOutput, calls=%fused_computation | convolution fusion | flops 764737536 | bytes 868424 | tf_op jit(solution)/shard_map/conv_general_dilated | solution.py:223
  47.6 0.1 copy.11
  47.7 0.1 copy.12
  47.8 0.1 copy.13
  47.9 0.7 %copy-done.7 = f32[128]{0:T(128)S(1)} copy-done((f32[128]{0:T(128)S(1)}, f32[128]{0:T(128)}, u32[]{:S(2)}) %copy-start.7) | copy-done | bytes 536
  48.5 0.3 select_bitcast_fusion.1
  48.9 0.6 %copy-done.8 = bf16[2,3,3,128]{3,0,2,1:T(2,128)(2,1)S(1)} copy-done((bf16[2,3,3,128]{3,0,2,1:T(2,128)(2,1)S(1)}, bf16[2,3,3,128]{3,0,2,1:T(2,128)(2,1)}, u32[]{:S(2)}) %copy-start.8) | copy-done | bytes 4632
  49.6 0.0 copy-done.9
  49.6 1.7 %convolution_select_fusion.1 = f32[4,8,9,2]{1,3,2,0:T(2,128)S(1)} fusion(bf16[2,3,3,128]{3,0,2,1:T(2,128)(2,1)S(1)} %copy-done.8, bf16[6,1,7,2,128]{4,2,3,0,1:T(8,128)(2,1)S(1)} %slice.58, bf16[6,1,8,9,128]{4,2,3,0,1:T(8,128)(2,1)S(1)} %copy.15, pred[8,9]{0,1:T(8,128)(4,1)S(1)} %copy-done.9), kind=kOutput, calls=%fused_computation.1 | convolution fusion | flops 1733184 | bytes 139080 | tf_op jit(solution)/shard_map/conv_general_dilated | solution.py:234
  51.3 0.1 copy.18
  51.4 0.1 reshape.105
  51.5 0.6 %fusion.17 = f32[2,4,64]{2,1,0:T(4,128)} fusion(f32[4,1,72,2]{2,0,3,1:T(4,128)S(1)} %reshape.105, f32[1,4,64]{2,1,0:T(4,128)S(1)} %get-tuple-element.47, f32[1,4,64]{2,1,0:T(4,128)S(1)} %get-tuple-element.48), kind=kLoop, calls=%fused_computation.29 | loop fusion | flops 1024 | bytes 6144 | tf_op jit(solution)/shard_map/add | solution.py:240
  (34 shorter events, 0.3 us)
Async XLA Ops:
  0.0 46.0 %copy-start = (bf16[3,3,128,128]{3,2,1,0:T(8,128)(2,1)S(1)}, bf16[3,3,128,128]{3,2,1,0:T(8,128)(2,1)}, u32[]{:S(2)}) copy-start(bf16[3,3,128,128]{3,2,1,0:T(8,128)(2,1)} %param.8) | copy-start | bytes 884740
  0.0 8.3 %copy-start.5 = (bf16[4,64,128]{2,1,0:T(8,128)(2,1)S(1)}, bf16[4,64,128]{2,1,0:T(8,128)(2,1)}, u32[]{:S(2)}) copy-start(bf16[4,64,128]{2,1,0:T(8,128)(2,1)} %param.6) | copy-start | bytes 196612
  0.8 3.7 %collective-permute-start = (bf16[4,2,128]{2,1,0:T(2,128)(2,1)S(1)}, bf16[4,2,128]{2,1,0:T(2,128)(2,1)S(1)}, u32[]{:S(2)}, u32[]{:S(2)}) collective-permute-start(bf16[4,2,128]{2,1,0:T(2,128)(2,1)S(1)} %get-tuple-element.43), channel_id=1, source_target_pairs={{0,1},{1,2},{2,3},{4,5},{5,6},{6,7},{8,9},{9,10},{10,11},{12,13},{... | collective-permute-start | bytes 6152 | tf_op jit(solution)/shard_map/ppermute | solution.py:19
  3.1 5.2 %collective-permute-start.1 = (bf16[4,2,128]{2,1,0:T(2,128)(2,1)S(1)}, bf16[4,2,128]{2,1,0:T(2,128)(2,1)S(1)}, u32[]{:S(2)}, u32[]{:S(2)}) collective-permute-start(bf16[4,2,128]{2,1,0:T(2,128)(2,1)S(1)} %get-tuple-element.44), channel_id=1, source_target_pairs={{1,0},{2,1},{3,2},{5,4},{6,5},{7,6},{9,8},{10,9},{11,10},{13,12},{... | collective-permute-start | bytes 6152 | tf_op jit(solution)/shard_map/ppermute | solution.py:22
  8.3 17.7 %collective-permute-start.5 = (bf16[2048,128]{1,0:T(8,128)(2,1)}, bf16[2048,128]{1,0:T(8,128)(2,1)S(1)}, u32[]{:S(2)}, u32[]{:S(2)}) collective-permute-start(bf16[2048,128]{1,0:T(8,128)(2,1)} %refs_1_), channel_id=1, source_target_pairs={{0,1},{1,0},{2,3},{3,2},{4,5},{5,4},{6,7},{7,6},{8,9},{9,8},{10,11... | collective-permute-start | bytes 1572872 | tf_op jit(solution)/shard_map/ppermute | solution.py:166
  10.7 20.9 %collective-permute-start.4 = (bf16[2048,128]{1,0:T(8,128)(2,1)}, bf16[2048,128]{1,0:T(8,128)(2,1)S(1)}, u32[]{:S(2)}, u32[]{:S(2)}) collective-permute-start(bf16[2048,128]{1,0:T(8,128)(2,1)} %refs_1_), channel_id=1, source_target_pairs={{0,2},{1,3},{2,0},{3,1},{4,6},{5,7},{6,4},{7,5},{8,10},{9,11},{10,... | collective-permute-start | bytes 1572872 | tf_op jit(solution)/shard_map/ppermute | solution.py:169
  10.8 5.0 %collective-permute-start.2 = (bf16[2,68,128]{2,1,0:T(8,128)(2,1)S(1)}, bf16[2,68,128]{2,1,0:T(8,128)(2,1)S(1)}, u32[]{:S(2)}, u32[]{:S(2)}) collective-permute-start(bf16[2,68,128]{2,1,0:T(8,128)(2,1)S(1)} %get-tuple-element.41), channel_id=1, source_target_pairs={{0,4},{4,8},{8,12},{12,16},{16,20},{20,24},{24,28},{1,5},{5,9},{9,... | collective-permute-start | bytes 104456 | tf_op jit(solution)/shard_map/ppermute | solution.py:19
  14.2 5.9 %collective-permute-start.3 = (bf16[2,68,128]{2,1,0:T(8,128)(2,1)S(1)}, bf16[2,68,128]{2,1,0:T(8,128)(2,1)S(1)}, u32[]{:S(2)}, u32[]{:S(2)}) collective-permute-start(bf16[2,68,128]{2,1,0:T(8,128)(2,1)S(1)} %get-tuple-element.42), channel_id=1, source_target_pairs={{4,0},{8,4},{12,8},{16,12},{20,16},{24,20},{28,24},{5,1},{9,5},{13... | collective-permute-start | bytes 104456 | tf_op jit(solution)/shard_map/ppermute | solution.py:22
  26.1 0.8 %copy-start.2 = (bf16[2048,128]{1,0:T(8,128)(2,1)}, bf16[2048,128]{1,0:T(8,128)(2,1)S(1)}, u32[]{:S(2)}) copy-start(bf16[2048,128]{1,0:T(8,128)(2,1)S(1)} %collective-permute-done.5.refs_1_) | copy-start | bytes 1572868
  31.7 1.1 %copy-start.1 = (bf16[2048,128]{1,0:T(8,128)(2,1)}, bf16[2048,128]{1,0:T(8,128)(2,1)S(1)}, u32[]{:S(2)}) copy-start(bf16[2048,128]{1,0:T(8,128)(2,1)S(1)} %collective-permute-done.4.refs_1_) | copy-start | bytes 1572868
  31.7 5.8 %collective-permute-start.6 = (bf16[2048,128]{1,0:T(8,128)(2,1)S(1)}, bf16[2048,128]{1,0:T(8,128)(2,1)S(1)}, u32[]{:S(2)}, u32[]{:S(2)}) collective-permute-start(bf16[2048,128]{1,0:T(8,128)(2,1)S(1)} %collective-permute-done.4.refs_1_), channel_id=1, source_target_pairs={{0,1},{1,0},{2,3},{3,2},{4,5},{5,4},{6,7},{7,6},{8,9},{9,8},{10,11... | collective-permute-start | bytes 1572872 | tf_op jit(solution)/shard_map/ppermute | solution.py:188
  32.0 0.7 %copy-start.6 = (f32[2,128]{1,0:T(2,128)S(1)}, f32[2,128]{1,0:T(2,128)}, u32[]{:S(2)}) copy-start(f32[2,128]{1,0:T(2,128)} %param.9) | copy-start | bytes 3076
  37.5 0.8 %copy-start.3 = (bf16[2048,128]{1,0:T(8,128)(2,1)}, bf16[2048,128]{1,0:T(8,128)(2,1)S(1)}, u32[]{:S(2)}) copy-start(bf16[2048,128]{1,0:T(8,128)(2,1)S(1)} %collective-permute-done.6.refs_1_) | copy-start | bytes 1572868
  43.7 1.9 %copy-start.4 = (f32[544,128]{1,0:T(8,128)S(1)}, f32[544,128]{1,0:T(8,128)}, u32[]{:S(2)}) copy-start(f32[544,128]{1,0:T(8,128)} %get-tuple-element.38) | copy-start | bytes 835588
  46.0 0.7 %copy-start.10 = (pred[8,9]{0,1:T(8,128)(4,1)S(1)}, pred[8,9]{0,1:T(8,128)(4,1)}, u32[]{:S(2)}) copy-start(pred[8,9]{0,1:T(8,128)(4,1)} %constant.80) | copy-start | bytes 220
  47.9 0.7 %copy-start.7 = (f32[128]{0:T(128)S(1)}, f32[128]{0:T(128)}, u32[]{:S(2)}) copy-start(f32[128]{0:T(128)} %param.10) | copy-start | bytes 1540
  48.9 0.7 %copy-start.8 = (bf16[2,3,3,128]{3,0,2,1:T(2,128)(2,1)S(1)}, bf16[2,3,3,128]{3,0,2,1:T(2,128)(2,1)}, u32[]{:S(2)}) copy-start(bf16[2,3,3,128]{3,0,2,1:T(2,128)(2,1)} %param.11) | copy-start | bytes 13828
  48.9 0.7 %copy-start.9 = (pred[8,9]{0,1:T(8,128)(4,1)S(1)}, pred[8,9]{0,1:T(8,128)(4,1)}, u32[]{:S(2)}) copy-start(pred[8,9]{0,1:T(8,128)(4,1)} %constant.79) | copy-start | bytes 220

commit v11 on v10

--- a/solution.py
+++ b/solution.py
@@ -1,4 +1,5 @@
 import functools
+import itertools
 import math
 
 import jax
@@ -44,6 +45,37 @@
     lane8 = lax.broadcasted_iota(jnp.int32, (w.shape[0], 8), 1)
     zero = jnp.zeros((), jnp.float32)
     return jnp.where(lane8 == 0, total, jnp.where(lane8 == 1, sum_x, jnp.where(lane8 == 3, sum_y, zero)))
+
+
+def halo_ring(block, width):
+    rows, cols = block.shape[:2]
+    counts = (lax.axis_size("space"), lax.axis_size("match"))
+    pieces = {}
+    for dr in (-1, 0, 1):
+        for dc in (-1, 0, 1):
+            if dr == 0 and dc == 0:
+                continue
+            part = block
+            if dr:
+                part = lax.slice_in_dim(part, 0 if dr > 0 else rows - width, width if dr > 0 else rows, axis=0)
+            if dc:
+                part = lax.slice_in_dim(part, 0 if dc > 0 else cols - width, width if dc > 0 else cols, axis=1)
+            axes = [(name, step, size) for name, step, size in
+                    (("space", dr, counts[0]), ("match", dc, counts[1])) if step]
+            names = tuple(name for name, _, _ in axes)
+            pairs = []
+            grid = [range(size) for _, _, size in axes]
+            for place in itertools.product(*grid):
+                target = tuple(p - step for p, (_, step, _) in zip(place, axes))
+                if all(0 <= t < size for t, (_, _, size) in zip(target, axes)):
+                    flat = lambda idx: functools.reduce(
+                        lambda acc, pair: acc * pair[1][2] + pair[0], zip(idx, axes), 0)
+                    pairs.append((flat(place), flat(target)))
+            name = names[0] if len(names) == 1 else names
+            pieces[(dr, dc)] = lax.ppermute(part, name, pairs)
+    band = lambda dr: jnp.concatenate(
+        [pieces[(dr, -1)], pieces[(dr, 0)] if dr else block, pieces[(dr, 1)]], axis=1)
+    return jnp.concatenate([band(-1), band(0), band(1)], axis=0)
 
 
 def shard_kernel(*refs, scale, chans, first, last, width, slot):
@@ -205,9 +237,8 @@
     width = cols * lax.axis_size("match")
     row_first = lax.axis_index("space") * rows
     col_first = lax.axis_index("match") * cols
-    ext = extended(source, (("match", 1),), HALO)
+    ext = halo_ring(source, HALO)
     targets, ext = lax.optimization_barrier((targets, ext))
-    ext = extended(ext, (("space", 0),), HALO)
     erows, ecols = rows + 2 * HALO, cols + 2 * HALO
     warped, sum_x, sum_y = match(ext.reshape(erows * ecols, chans), targets, width)
     warped = warped.reshape(erows, ecols, chans)

time: 53.2 us -> 65.9 us (1.24)
  the two profiles are of different devices: /device:TPU:0 before, /device:TPU:25 now
where the time goes in v11:
time: 65.9 us; the launch traced here: 65.3 us
  starting transfers between devices  26.3 us (40%)
  Pallas kernels  19.8 us (30%)
  local copies, waits for them, and re-layouts  9.83 us (15%)
  waiting for transfers between devices  5.02 us (8%)
  matrix products  2.64 us (4%)
  other arithmetic  1.34 us (2%)
    ppermute x8, starting transfers between devices, halo_ring(): pieces[dr, dc] = lax.ppermute(part, name, pairs)  24.5 us
    pallas_call x4, Pallas kernels, match_step(): pl.pallas_call(kernel, grid=(nq,), in_specs=in_specs, out_specs=out_specs...  19.8 us
    unnamed x23, local copies, waits for them, and re-layouts  4.3 us
    ppermute x8, waiting for transfers between devices, halo_ring(): pieces[dr, dc] = lax.ppermute(part, name, pairs)  3.88 us
    conv_general_dilated x1, matrix products, local(): lax.conv_general_dilated(hidden[None], jnp.transpose(conv_out, (1, 2, 3,...  1.7 us
    slice x1, local copies, waits for them, and re-layouts, match(): return (warped[:count], flow[:count, 0], flow[:count, 1])  1.42 us
  transfers between devices with their start and end apart: 11, of which 2 were waited for; matrix products, arithmetic and copies ran while one was open for 4% of the time, Pallas kernels for 22%

profile of v11, /device:TPU:25, one launch (start us, length us, event | category | flops | bytes accessed | tf_op | source)
XLA Modules:
  0.0 65.3 jit_solution(4079372568950266253)
XLA Ops:
  0.0 0.8 %fusion.25 = (bf16[2,2,128]{2,1,0:T(2,128)(2,1)S(1)}, bf16[2,2,128]{2,1,0:T(2,128)(2,1)S(1)}, bf16[2,2,128]{2,1,0:T(2,128)(2,1)S(1)}, bf16[2,2,128]{2,1,0:T(2,128)(2,1)S(1)}) fusion(bf16[4,64,128]{2,1,0:T(8,128)(2,1)} %param.6), kind=kLoop, calls=%fused_computation.50 | loop fusion | bytes 8192 | tf_op jit(solution)/shard_map/slice | solution.py:62
  0.8 4.6 %collective-permute-start = (bf16[2,2,128]{2,1,0:T(2,128)(2,1)S(1)}, bf16[2,2,128]{2,1,0:T(2,128)(2,1)S(1)}, u32[]{:S(2)}, u32[]{:S(2)}) collective-permute-start(bf16[2,2,128]{2,1,0:T(2,128)(2,1)S(1)} %get-tuple-element.41), channel_id=1, source_target_pairs={{0,5},{1,6},{2,7},{4,9},{5,10},{6,11},{8,13},{9,14},{10,15},{12,17... | collective-permute-start | bytes 3080 | tf_op jit(solution)/shard_map/ppermute | solution.py:75
  5.4 1.9 %collective-permute-start.2 = (bf16[2,2,128]{2,1,0:T(2,128)(2,1)S(1)}, bf16[2,2,128]{2,1,0:T(2,128)(2,1)S(1)}, u32[]{:S(2)}, u32[]{:S(2)}) collective-permute-start(bf16[2,2,128]{2,1,0:T(2,128)(2,1)S(1)} %get-tuple-element.43), channel_id=1, source_target_pairs={{1,4},{2,5},{3,6},{5,8},{6,9},{7,10},{9,12},{10,13},{11,14},{13,16... | collective-permute-start | bytes 3080 | tf_op jit(solution)/shard_map/ppermute | solution.py:75
  7.4 5.6 %collective-permute-start.5 = (bf16[2,2,128]{2,1,0:T(2,128)(2,1)S(1)}, bf16[2,2,128]{2,1,0:T(2,128)(2,1)S(1)}, u32[]{:S(2)}, u32[]{:S(2)}) collective-permute-start(bf16[2,2,128]{2,1,0:T(2,128)(2,1)S(1)} %get-tuple-element.42), channel_id=1, source_target_pairs={{4,1},{5,2},{6,3},{8,5},{9,6},{10,7},{12,9},{13,10},{14,11},{16,13... | collective-permute-start | bytes 3080 | tf_op jit(solution)/shard_map/ppermute | solution.py:75
  12.9 0.8 %fusion.26 = (bf16[2,64,128]{2,1,0:T(8,128)(2,1)S(1)}, bf16[2,64,128]{2,1,0:T(8,128)(2,1)S(1)}) fusion(bf16[4,64,128]{2,1,0:T(8,128)(2,1)} %param.6), kind=kLoop, calls=%fused_computation.51 | loop fusion | bytes 131072 | tf_op jit(solution)/shard_map/slice | solution.py:60
  13.7 1.9 %collective-permute-start.1 = (bf16[2,64,128]{2,1,0:T(8,128)(2,1)S(1)}, bf16[2,64,128]{2,1,0:T(8,128)(2,1)S(1)}, u32[]{:S(2)}, u32[]{:S(2)}) collective-permute-start(bf16[2,64,128]{2,1,0:T(8,128)(2,1)S(1)} %get-tuple-element.45), channel_id=1, source_target_pairs={{0,4},{4,8},{8,12},{12,16},{16,20},{20,24},{24,28},{1,5},{5,9},{9,... | collective-permute-start | bytes 98312 | tf_op jit(solution)/shard_map/ppermute | solution.py:75
  15.6 4.3 %collective-permute-start.6 = (bf16[2,64,128]{2,1,0:T(8,128)(2,1)S(1)}, bf16[2,64,128]{2,1,0:T(8,128)(2,1)S(1)}, u32[]{:S(2)}, u32[]{:S(2)}) collective-permute-start(bf16[2,64,128]{2,1,0:T(8,128)(2,1)S(1)} %get-tuple-element.46), channel_id=1, source_target_pairs={{4,0},{8,4},{12,8},{16,12},{20,16},{24,20},{28,24},{5,1},{9,5},{13... | collective-permute-start | bytes 98312 | tf_op jit(solution)/shard_map/ppermute | solution.py:75
  19.9 1.9 %collective-permute-start.3 = (bf16[4,2,128]{2,1,0:T(2,128)(2,1)S(1)}, bf16[4,2,128]{2,1,0:T(2,128)(2,1)S(1)}, u32[]{:S(2)}, u32[]{:S(2)}) collective-permute-start(bf16[4,2,128]{2,1,0:T(2,128)(2,1)S(1)} %get-tuple-element.47), channel_id=1, source_target_pairs={{0,1},{1,2},{2,3},{4,5},{5,6},{6,7},{8,9},{9,10},{10,11},{12,13},{... | collective-permute-start | bytes 6152 | tf_op jit(solution)/shard_map/ppermute | solution.py:75
  21.9 2.4 %collective-permute-start.4 = (bf16[4,2,128]{2,1,0:T(2,128)(2,1)S(1)}, bf16[4,2,128]{2,1,0:T(2,128)(2,1)S(1)}, u32[]{:S(2)}, u32[]{:S(2)}) collective-permute-start(bf16[4,2,128]{2,1,0:T(2,128)(2,1)S(1)} %get-tuple-element.48), channel_id=1, source_target_pairs={{1,0},{2,1},{3,2},{5,4},{6,5},{7,6},{9,8},{10,9},{11,10},{13,12},{... | collective-permute-start | bytes 6152 | tf_op jit(solution)/shard_map/ppermute | solution.py:75
  24.3 1.9 %collective-permute-start.7 = (bf16[2,2,128]{2,1,0:T(2,128)(2,1)S(1)}, bf16[2,2,128]{2,1,0:T(2,128)(2,1)S(1)}, u32[]{:S(2)}, u32[]{:S(2)}) collective-permute-start(bf16[2,2,128]{2,1,0:T(2,128)(2,1)S(1)} %get-tuple-element.44), channel_id=1, source_target_pairs={{5,0},{6,1},{7,2},{9,4},{10,5},{11,6},{13,8},{14,9},{15,10},{17,12... | collective-permute-start | bytes 3080 | tf_op jit(solution)/shard_map/ppermute | solution.py:75
  26.2 3.9 %collective-permute-done.7 = bf16[2,2,128]{2,1,0:T(2,128)(2,1)S(1)} collective-permute-done((bf16[2,2,128]{2,1,0:T(2,128)(2,1)S(1)}, bf16[2,2,128]{2,1,0:T(2,128)(2,1)S(1)}, u32[]{:S(2)}, u32[]{:S(2)}) %collective-permute-start.7) | collective-permute-done | bytes 1056 | tf_op jit(solution)/shard_map/ppermute | solution.py:75
  30.2 0.1 collective-permute-start.9
  30.3 0.5 collective-permute-start.8
  30.7 0.1 fusion.18
  30.8 0.7 %reshape.78.refs_0_ = bf16[544,128]{1,0:T(8,128)(2,1)} reshape(bf16[8,68,128]{2,1,0:T(8,128)(2,1)S(1)} %maximum_maximum_fusion) | data formatting | bytes 278528 | tf_op jit(solution)/shard_map/reshape | solution.py:243
  31.5 0.6 broadcast_in_dim.22.refs_2_
  32.1 4.7 %shard_map.64 = (f32[544,128]{1,0:T(8,128)}, f32[544,128]{1,0:T(8,128)}, f32[544,8]{1,0:T(8,128)}) custom-call(bf16[544,128]{1,0:T(8,128)(2,1)} %reshape.78.refs_0_, bf16[2048,128]{1,0:T(8,128)(2,1)} %refs_1_, f32[8,128]{1,0:T(8,128)} %broadcast_in_dim.22.refs_2_), custom_call_target="tpu_custom_call" | custom-call | tf_op jit(solution)/shard_map/pallas_call | solution.py:173
  36.8 0.8 %copy-done.2 = bf16[2048,128]{1,0:T(8,128)(2,1)} copy-done((bf16[2048,128]{1,0:T(8,128)(2,1)}, bf16[2048,128]{1,0:T(8,128)(2,1)S(1)}, u32[]{:S(2)}) %copy-start.2) | copy-done | bytes 524312
  37.6 4.8 %shard_map.65 = (f32[544,128]{1,0:T(8,128)}, f32[544,128]{1,0:T(8,128)}, f32[544,8]{1,0:T(8,128)}) custom-call(bf16[544,128]{1,0:T(8,128)(2,1)} %reshape.78.refs_0_, bf16[2048,128]{1,0:T(8,128)(2,1)} %copy-done.2, f32[8,128]{1,0:T(8,128)} %broadcast_in_dim.22.refs_2_, f32[544,128]{1,0:T(8,128)} %get-tuple-element.24.refs_3_, ...), custom_call_target="tpu_custom_call" | custom-call | tf_op jit(solution)/shard_map/pallas_call | solution.py:173
  42.5 1.1 %collective-permute-done.8.refs_1_ = bf16[2048,128]{1,0:T(8,128)(2,1)S(1)} collective-permute-done((bf16[2048,128]{1,0:T(8,128)(2,1)}, bf16[2048,128]{1,0:T(8,128)(2,1)S(1)}, u32[]{:S(2)}, u32[]{:S(2)}) %collective-permute-start.8) | collective-permute-done | bytes 524320 | tf_op jit(solution)/shard_map/ppermute | solution.py:201
  43.6 1.3 %collective-permute-start.10 = (bf16[2048,128]{1,0:T(8,128)(2,1)S(1)}, bf16[2048,128]{1,0:T(8,128)(2,1)S(1)}, u32[]{:S(2)}, u32[]{:S(2)}) collective-permute-start(bf16[2048,128]{1,0:T(8,128)(2,1)S(1)} %collective-permute-done.8.refs_1_), channel_id=1, source_target_pairs={{0,1},{1,0},{2,3},{3,2},{4,5},{5,4},{6,7},{7,6},{8,9},{9,8},{10,11... | collective-permute-start | bytes 1572872 | tf_op jit(solution)/shard_map/ppermute | solution.py:220
  44.9 0.1 broadcast_and_fusion
  45.0 0.1 slice.71
  45.0 0.1 copy.7
  45.2 0.7 %copy-done.6 = f32[2,128]{1,0:T(2,128)S(1)} copy-done((f32[2,128]{1,0:T(2,128)S(1)}, f32[2,128]{1,0:T(2,128)}, u32[]{:S(2)}) %copy-start.6) | copy-done | bytes 1048
  45.9 4.8 %shard_map.66 = (f32[544,128]{1,0:T(8,128)}, f32[544,128]{1,0:T(8,128)}, f32[544,8]{1,0:T(8,128)}) custom-call(bf16[544,128]{1,0:T(8,128)(2,1)} %reshape.78.refs_0_, bf16[2048,128]{1,0:T(8,128)(2,1)} %copy-done.1, f32[8,128]{1,0:T(8,128)} %broadcast_in_dim.22.refs_2_, f32[544,128]{1,0:T(8,128)} %get-tuple-element.31.refs_3_, ...), custom_call_target="tpu_custom_call" | custom-call | tf_op jit(solution)/shard_map/pallas_call | solution.py:173
  50.7 0.8 %copy-done.3 = bf16[2048,128]{1,0:T(8,128)(2,1)} copy-done((bf16[2048,128]{1,0:T(8,128)(2,1)}, bf16[2048,128]{1,0:T(8,128)(2,1)S(1)}, u32[]{:S(2)}) %copy-start.3) | copy-done | bytes 524312
  51.5 5.5 %shard_map.67 = (f32[544,128]{1,0:T(8,128)}, f32[544,128]{1,0:T(8,128)}) custom-call(bf16[544,128]{1,0:T(8,128)(2,1)} %reshape.78.refs_0_, bf16[2048,128]{1,0:T(8,128)(2,1)} %copy-done.3, f32[8,128]{1,0:T(8,128)} %broadcast_in_dim.22.refs_2_, f32[544,128]{1,0:T(8,128)} %get-tuple-element.34.refs_3_, f32[544,128]{1,0:T(8,128)} %get-tuple-element.35.refs_4_, ...), custom_call_target="tpu_custom_call" | custom-call | tf_op jit(solution)/shard_map/pallas_call | solution.py:173
  56.9 1.4 %slice_reduce_fusion.1 = (f32[544]{0:T(1024)S(1)}, f32[544]{0:T(1024)S(1)}) fusion(f32[544,128]{1,0:T(8,128)} %get-tuple-element.37), kind=kLoop, calls=%fused_computation.9 | loop fusion | bytes 8704 | tf_op jit(solution)/shard_map/slice | solution.py:231
  58.3 0.1 reshape_squeeze.6
  58.4 0.1 reshape_squeeze.7
  58.5 0.1 slice.72
  58.6 0.1 broadcast_subtract_fusion
  58.6 0.1 slice_bitcast_fusion.2
  58.7 0.1 slice.74
  58.8 0.1 select_bitcast_fusion
  59.2 0.6 copy-done.10
  59.8 0.9 %convolution_select_fusion = f32[6,8,9,128]{3,1,2,0:T(8,128)S(1)} fusion(bf16[3,3,128,128]{3,2,1,0:T(8,128)(2,1)S(1)} %copy-done, f32[8,1,7,2,128]{4,2,3,0,1:T(8,128)S(1)} %slice.80, f32[8,1,8,9,128]{4,2,3,0,1:T(8,128)S(1)} %copy.10, pred[8,9]{0,1:T(8,128)(4,1)S(1)} %copy-done.10), kind=kOutput, calls=%fused_computation | convolution fusion | flops 764737536 | bytes 868424 | tf_op jit(solution)/shard_map/conv_general_dilated | solution.py:254
  60.8 0.1 copy.11
  60.8 0.1 copy.12
  60.9 0.1 copy.13
  61.0 0.7 %copy-done.7 = f32[128]{0:T(128)S(1)} copy-done((f32[128]{0:T(128)S(1)}, f32[128]{0:T(128)}, u32[]{:S(2)}) %copy-start.7) | copy-done | bytes 536
  61.7 0.3 select_bitcast_fusion.1
  62.1 0.6 copy-done.8
  62.7 1.7 %convolution_select_fusion.1 = f32[4,8,9,2]{1,3,2,0:T(2,128)S(1)} fusion(bf16[2,3,3,128]{3,0,2,1:T(2,128)(2,1)S(1)} %copy-done.8, bf16[6,1,7,2,128]{4,2,3,0,1:T(8,128)(2,1)S(1)} %slice.82, bf16[6,1,8,9,128]{4,2,3,0,1:T(8,128)(2,1)S(1)} %copy.15, pred[8,9]{0,1:T(8,128)(4,1)S(1)} %copy-done.9), kind=kOutput, calls=%fused_computation.1 | convolution fusion | flops 1733184 | bytes 139080 | tf_op jit(solution)/shard_map/conv_general_dilated | solution.py:265
  64.4 0.1 copy.18
  64.6 0.1 reshape.105
  64.7 0.6 fusion.17
  (42 shorter events, 0.4 us)
Async XLA Ops:
  0.0 59.2 %copy-start = (bf16[3,3,128,128]{3,2,1,0:T(8,128)(2,1)S(1)}, bf16[3,3,128,128]{3,2,1,0:T(8,128)(2,1)}, u32[]{:S(2)}) copy-start(bf16[3,3,128,128]{3,2,1,0:T(8,128)(2,1)} %param.8) | copy-start | bytes 884740
  0.8 19.2 %collective-permute-start = (bf16[2,2,128]{2,1,0:T(2,128)(2,1)S(1)}, bf16[2,2,128]{2,1,0:T(2,128)(2,1)S(1)}, u32[]{:S(2)}, u32[]{:S(2)}) collective-permute-start(bf16[2,2,128]{2,1,0:T(2,128)(2,1)S(1)} %get-tuple-element.41), channel_id=1, source_target_pairs={{0,5},{1,6},{2,7},{4,9},{5,10},{6,11},{8,13},{9,14},{10,15},{12,17... | collective-permute-start | bytes 3080 | tf_op jit(solution)/shard_map/ppermute | solution.py:75
  5.4 16.5 %collective-permute-start.2 = (bf16[2,2,128]{2,1,0:T(2,128)(2,1)S(1)}, bf16[2,2,128]{2,1,0:T(2,128)(2,1)S(1)}, u32[]{:S(2)}, u32[]{:S(2)}) collective-permute-start(bf16[2,2,128]{2,1,0:T(2,128)(2,1)S(1)} %get-tuple-element.43), channel_id=1, source_target_pairs={{1,4},{2,5},{3,6},{5,8},{6,9},{7,10},{9,12},{10,13},{11,14},{13,16... | collective-permute-start | bytes 3080 | tf_op jit(solution)/shard_map/ppermute | solution.py:75
  7.3 12.6 %copy-start.4 = (bf16[4,64,128]{2,1,0:T(8,128)(2,1)S(1)}, bf16[4,64,128]{2,1,0:T(8,128)(2,1)}, u32[]{:S(2)}) copy-start(bf16[4,64,128]{2,1,0:T(8,128)(2,1)} %param.6) | copy-start | bytes 196612
  7.4 16.9 %collective-permute-start.5 = (bf16[2,2,128]{2,1,0:T(2,128)(2,1)S(1)}, bf16[2,2,128]{2,1,0:T(2,128)(2,1)S(1)}, u32[]{:S(2)}, u32[]{:S(2)}) collective-permute-start(bf16[2,2,128]{2,1,0:T(2,128)(2,1)S(1)} %get-tuple-element.42), channel_id=1, source_target_pairs={{4,1},{5,2},{6,3},{8,5},{9,6},{10,7},{12,9},{13,10},{14,11},{16,13... | collective-permute-start | bytes 3080 | tf_op jit(solution)/shard_map/ppermute | solution.py:75
  13.7 16.4 %collective-permute-start.1 = (bf16[2,64,128]{2,1,0:T(8,128)(2,1)S(1)}, bf16[2,64,128]{2,1,0:T(8,128)(2,1)S(1)}, u32[]{:S(2)}, u32[]{:S(2)}) collective-permute-start(bf16[2,64,128]{2,1,0:T(8,128)(2,1)S(1)} %get-tuple-element.45), channel_id=1, source_target_pairs={{0,4},{4,8},{8,12},{12,16},{16,20},{20,24},{24,28},{1,5},{5,9},{9,... | collective-permute-start | bytes 98312 | tf_op jit(solution)/shard_map/ppermute | solution.py:75
  15.6 14.5 %collective-permute-start.6 = (bf16[2,64,128]{2,1,0:T(8,128)(2,1)S(1)}, bf16[2,64,128]{2,1,0:T(8,128)(2,1)S(1)}, u32[]{:S(2)}, u32[]{:S(2)}) collective-permute-start(bf16[2,64,128]{2,1,0:T(8,128)(2,1)S(1)} %get-tuple-element.46), channel_id=1, source_target_pairs={{4,0},{8,4},{12,8},{16,12},{20,16},{24,20},{28,24},{5,1},{9,5},{13... | collective-permute-start | bytes 98312 | tf_op jit(solution)/shard_map/ppermute | solution.py:75
  19.9 10.1 %collective-permute-start.3 = (bf16[4,2,128]{2,1,0:T(2,128)(2,1)S(1)}, bf16[4,2,128]{2,1,0:T(2,128)(2,1)S(1)}, u32[]{:S(2)}, u32[]{:S(2)}) collective-permute-start(bf16[4,2,128]{2,1,0:T(2,128)(2,1)S(1)} %get-tuple-element.47), channel_id=1, source_target_pairs={{0,1},{1,2},{2,3},{4,5},{5,6},{6,7},{8,9},{9,10},{10,11},{12,13},{... | collective-permute-start | bytes 6152 | tf_op jit(solution)/shard_map/ppermute | solution.py:75
  21.9 8.2 %collective-permute-start.4 = (bf16[4,2,128]{2,1,0:T(2,128)(2,1)S(1)}, bf16[4,2,128]{2,1,0:T(2,128)(2,1)S(1)}, u32[]{:S(2)}, u32[]{:S(2)}) collective-permute-start(bf16[4,2,128]{2,1,0:T(2,128)(2,1)S(1)} %get-tuple-element.48), channel_id=1, source_target_pairs={{1,0},{2,1},{3,2},{5,4},{6,5},{7,6},{9,8},{10,9},{11,10},{13,12},{... | collective-permute-start | bytes 6152 | tf_op jit(solution)/shard_map/ppermute | solution.py:75
  24.3 5.8 %collective-permute-start.7 = (bf16[2,2,128]{2,1,0:T(2,128)(2,1)S(1)}, bf16[2,2,128]{2,1,0:T(2,128)(2,1)S(1)}, u32[]{:S(2)}, u32[]{:S(2)}) collective-permute-start(bf16[2,2,128]{2,1,0:T(2,128)(2,1)S(1)} %get-tuple-element.44), channel_id=1, source_target_pairs={{5,0},{6,1},{7,2},{9,4},{10,5},{11,6},{13,8},{14,9},{15,10},{17,12... | collective-permute-start | bytes 3080 | tf_op jit(solution)/shard_map/ppermute | solution.py:75
  30.2 6.7 %collective-permute-start.9 = (bf16[2048,128]{1,0:T(8,128)(2,1)}, bf16[2048,128]{1,0:T(8,128)(2,1)S(1)}, u32[]{:S(2)}, u32[]{:S(2)}) collective-permute-start(bf16[2048,128]{1,0:T(8,128)(2,1)} %refs_1_), channel_id=1, source_target_pairs={{0,1},{1,0},{2,3},{3,2},{4,5},{5,4},{6,7},{7,6},{8,9},{9,8},{10,11... | collective-permute-start | bytes 1572872 | tf_op jit(solution)/shard_map/ppermute | solution.py:198
  30.3 13.3 %collective-permute-start.8 = (bf16[2048,128]{1,0:T(8,128)(2,1)}, bf16[2048,128]{1,0:T(8,128)(2,1)S(1)}, u32[]{:S(2)}, u32[]{:S(2)}) collective-permute-start(bf16[2048,128]{1,0:T(8,128)(2,1)} %refs_1_), channel_id=1, source_target_pairs={{0,2},{1,3},{2,0},{3,1},{4,6},{5,7},{6,4},{7,5},{8,10},{9,11},{10,... | collective-permute-start | bytes 1572872 | tf_op jit(solution)/shard_map/ppermute | solution.py:201
  36.8 0.8 %copy-start.2 = (bf16[2048,128]{1,0:T(8,128)(2,1)}, bf16[2048,128]{1,0:T(8,128)(2,1)S(1)}, u32[]{:S(2)}) copy-start(bf16[2048,128]{1,0:T(8,128)(2,1)S(1)} %collective-permute-done.9.refs_1_) | copy-start | bytes 1572868
  43.6 2.3 %copy-start.1 = (bf16[2048,128]{1,0:T(8,128)(2,1)}, bf16[2048,128]{1,0:T(8,128)(2,1)S(1)}, u32[]{:S(2)}) copy-start(bf16[2048,128]{1,0:T(8,128)(2,1)S(1)} %collective-permute-done.8.refs_1_) | copy-start | bytes 1572868
  43.6 7.0 %collective-permute-start.10 = (bf16[2048,128]{1,0:T(8,128)(2,1)S(1)}, bf16[2048,128]{1,0:T(8,128)(2,1)S(1)}, u32[]{:S(2)}, u32[]{:S(2)}) collective-permute-start(bf16[2048,128]{1,0:T(8,128)(2,1)S(1)} %collective-permute-done.8.refs_1_), channel_id=1, source_target_pairs={{0,1},{1,0},{2,3},{3,2},{4,5},{5,4},{6,7},{7,6},{8,9},{9,8},{10,11... | collective-permute-start | bytes 1572872 | tf_op jit(solution)/shard_map/ppermute | solution.py:220
  45.2 0.7 %copy-start.6 = (f32[2,128]{1,0:T(2,128)S(1)}, f32[2,128]{1,0:T(2,128)}, u32[]{:S(2)}) copy-start(f32[2,128]{1,0:T(2,128)} %param.9) | copy-start | bytes 3076
  50.7 0.8 %copy-start.3 = (bf16[2048,128]{1,0:T(8,128)(2,1)}, bf16[2048,128]{1,0:T(8,128)(2,1)S(1)}, u32[]{:S(2)}) copy-start(bf16[2048,128]{1,0:T(8,128)(2,1)S(1)} %collective-permute-done.10.refs_1_) | copy-start | bytes 1572868
  56.9 1.9 %copy-start.5 = (f32[544,128]{1,0:T(8,128)S(1)}, f32[544,128]{1,0:T(8,128)}, u32[]{:S(2)}) copy-start(f32[544,128]{1,0:T(8,128)} %get-tuple-element.38) | copy-start | bytes 835588
  59.1 0.7 %copy-start.10 = (pred[8,9]{0,1:T(8,128)(4,1)S(1)}, pred[8,9]{0,1:T(8,128)(4,1)}, u32[]{:S(2)}) copy-start(pred[8,9]{0,1:T(8,128)(4,1)} %constant.80) | copy-start | bytes 220
  61.0 0.7 %copy-start.7 = (f32[128]{0:T(128)S(1)}, f32[128]{0:T(128)}, u32[]{:S(2)}) copy-start(f32[128]{0:T(128)} %param.10) | copy-start | bytes 1540
  62.0 0.7 %copy-start.8 = (bf16[2,3,3,128]{3,0,2,1:T(2,128)(2,1)S(1)}, bf16[2,3,3,128]{3,0,2,1:T(2,128)(2,1)}, u32[]{:S(2)}) copy-start(bf16[2,3,3,128]{3,0,2,1:T(2,128)(2,1)} %param.11) | copy-start | bytes 13828
  62.1 0.7 %copy-start.9 = (pred[8,9]{0,1:T(8,128)(4,1)S(1)}, pred[8,9]{0,1:T(8,128)(4,1)}, u32[]{:S(2)}) copy-start(pred[8,9]{0,1:T(8,128)(4,1)} %constant.79) | copy-start | bytes 220

commit v12 on v10

--- a/solution.py
+++ b/solution.py
@@ -46,34 +46,46 @@
     return jnp.where(lane8 == 0, total, jnp.where(lane8 == 1, sum_x, jnp.where(lane8 == 3, sum_y, zero)))
 
 
-def shard_kernel(*refs, scale, chans, first, last, width, slot):
-    if first:
-        q_ref, k_ref, pos_ref = refs[:3]
-        outs = refs[3:]
-    else:
-        q_ref, k_ref, pos_ref, m_ref, acc_ref, st_ref = refs[:6]
-        outs = refs[6:]
-    s = lax.dot_general(
-        q_ref[...], k_ref[...], (((1,), (1,)), ((), ())),
-        preferred_element_type=jnp.float32,
-    )
-    peak = jnp.max(s, axis=1, keepdims=True)
+def shard_kernel(*refs, scale, chans, first, last, width, slots):
+    parts = len(slots)
+    q_ref = refs[0]
+    k_refs = refs[1:1 + parts]
+    pos_ref = refs[1 + parts]
+    rest = refs[2 + parts:]
+    if not first:
+        m_ref, acc_ref, st_ref = rest[:3]
+        rest = rest[3:]
+    outs = rest
+    scores = [
+        lax.dot_general(
+            q_ref[...], k_ref[...], (((1,), (1,)), ((), ())),
+            preferred_element_type=jnp.float32,
+        )
+        for k_ref in k_refs
+    ]
+    peak = jnp.max(scores[0], axis=1, keepdims=True)
+    for s in scores[1:]:
+        peak = jnp.maximum(peak, jnp.max(s, axis=1, keepdims=True))
     if not first:
         old = m_ref[:, 0:1]
         peak = jnp.maximum(old, peak)
     rate = scale * math.log2(math.e)
-    w = jnp.exp2((s - peak) * rate)
-    hi = w.astype(jnp.bfloat16)
-    if not width:
-        lo = (w - hi.astype(jnp.float32)).astype(jnp.bfloat16)
-    acc = jnp.dot(hi, k_ref[...], preferred_element_type=jnp.float32)
-    if width:
-        st = row_sums(w, pos_ref, width, slot)
-    else:
-        lanes = (((1,), (1,)), ((), ()))
-        st = lax.dot_general(
-            hi, pos_ref[...], lanes, preferred_element_type=jnp.float32
-        ) + lax.dot_general(lo, pos_ref[...], lanes, preferred_element_type=jnp.float32)
+    acc = None
+    st = None
+    for s, k_ref, slot in zip(scores, k_refs, slots):
+        w = jnp.exp2((s - peak) * rate)
+        hi = w.astype(jnp.bfloat16)
+        part_acc = jnp.dot(hi, k_ref[...], preferred_element_type=jnp.float32)
+        if width:
+            part_st = row_sums(w, pos_ref, width, slot)
+        else:
+            lo = (w - hi.astype(jnp.float32)).astype(jnp.bfloat16)
+            lanes = (((1,), (1,)), ((), ()))
+            part_st = lax.dot_general(
+                hi, pos_ref[...], lanes, preferred_element_type=jnp.float32
+            ) + lax.dot_general(lo, pos_ref[...], lanes, preferred_element_type=jnp.float32)
+        acc = part_acc if acc is None else acc + part_acc
+        st = part_st if st is None else st + part_st
     if not first:
         alpha = jnp.exp2((old - peak) * rate)
         acc = acc_ref[...] * alpha + acc
@@ -107,21 +119,19 @@
     return jnp.stack([one, col_hi, col_lo, row_hi, row_lo, zero, zero, zero])
 
 
-def match_step(queries, keys, pos, state, tq, first, last, width, slot):
+def match_step(queries, keys, pos, state, tq, first, last, width, slots):
     padded, chans = queries.shape
     nq = padded // tq
-    tk = keys.shape[0]
+    tk = keys[0].shape[0]
     kernel = functools.partial(
         shard_kernel, scale=1.0 / math.sqrt(chans), chans=chans, first=first, last=last,
-        width=width, slot=slot,
+        width=width, slots=slots,
     )
     row_spec = lambda width: pl.BlockSpec((tq, width), lambda i: (i, 0))
-    in_specs = [
-        row_spec(chans),
-        pl.BlockSpec((tk, chans), lambda i: (0, 0)),
-        pl.BlockSpec(pos.shape, lambda i: (0, 0)),
-    ]
-    args = [queries, keys, pos]
+    in_specs = [row_spec(chans)]
+    in_specs += [pl.BlockSpec((tk, chans), lambda i: (0, 0)) for _ in keys]
+    in_specs += [pl.BlockSpec(pos.shape, lambda i: (0, 0))]
+    args = [queries, *keys, pos]
     if not first:
         in_specs += [row_spec(128), row_spec(chans), row_spec(8)]
         args += list(state)
@@ -180,20 +190,30 @@
         owners = jnp.pad(owners.astype(jnp.float32), (0, 128 - n))
         table = jnp.broadcast_to(owners[None, :], (8, 128))
     pending = None
-    for step, (keys, owner, forward) in enumerate(shards):
-        if keys is None:
-            keys = pending
-        if forward:
-            keys, state = lax.optimization_barrier((keys, state))
-            pending = lax.ppermute(keys, "match", forward)
+    whole_rows = tk % width == 0
+    if whole_rows and n > 1:
+        groups = [[0, 1]] + [[i] for i in range(2, n)]
+    else:
+        groups = [[i] for i in range(n)]
+    for group in groups:
+        keys = []
+        for step in group:
+            key, owner, forward = shards[step]
+            if key is None:
+                key = pending
+            if forward:
+                key, state = lax.optimization_barrier((key, state))
+                pending = lax.ppermute(key, "match", forward)
+            keys.append(key)
         if tk % width == 0:
             pos = table
             seg = width
         else:
-            pos = positions(tk, owner * tk, width)
+            pos = positions(tk, shards[group[0]][1] * tk, width)
             seg = 0
         state = match_step(
-            queries, keys, pos, state, tq, step == 0, step == n - 1, seg, step % 128
+            queries, keys, pos, state, tq, group[0] == 0, group[-1] == n - 1, seg,
+            tuple(step % 128 for step in group),
         )
     warped, flow = state
     return warped[:count], flow[:count, 0], flow[:count, 1]

time: 53.2 us -> 51 us (0.959)
  the two profiles are of different devices: /device:TPU:0 before, /device:TPU:23 now
where the time goes in v12:
time: 51 us; the launch traced here: 50.6 us
  Pallas kernels  18.3 us (36%)
  starting transfers between devices  15.6 us (31%)
  local copies, waits for them, and re-layouts  8.43 us (17%)
  waiting for transfers between devices  4.11 us (8%)
  matrix products  2.64 us (5%)
  other arithmetic  1.33 us (3%)
    pallas_call x3, Pallas kernels, match_step(): pl.pallas_call(kernel, grid=(nq,), in_specs=in_specs, out_specs=out_specs...  18.3 us
    ppermute x2, starting transfers between devices, extended(): lax.ppermute(lax.slice_in_dim(block, 0, width, axis=dim), axis, backward)  5.34 us
    ppermute x2, starting transfers between devices, extended(): lax.ppermute(lax.slice_in_dim(block, block.shape[dim] - width, None, axis...  4.43 us
    ppermute x2, waiting for transfers between devices, extended(): lax.ppermute(lax.slice_in_dim(block, 0, width, axis=dim), axis, backward)  4.09 us
    unnamed x23, local copies, waits for them, and re-layouts  3.67 us
    ppermute x1, starting transfers between devices, match(): shards.append((lax.ppermute(targets, 'match', sibling), me ^ 1, None))  2.29 us
    ppermute x1, starting transfers between devices, match(): pending = lax.ppermute(key, 'match', forward)  2.14 us
    conv_general_dilated x1, matrix products, local(): lax.conv_general_dilated(hidden[None], jnp.transpose(conv_out, (1, 2, 3,...  1.7 us
  transfers between devices with their start and end apart: 7, of which 2 were waited for; matrix products, arithmetic and copies ran while one was open for 3% of the time, Pallas kernels for 25%

profile of v12, /device:TPU:23, one launch (start us, length us, event | category | flops | bytes accessed | tf_op | source)
XLA Modules:
  0.0 50.6 jit_solution(16464847609050446029)
XLA Ops:
  0.0 0.8 %fusion.26 = (bf16[4,2,128]{2,1,0:T(2,128)(2,1)S(1)}, bf16[4,2,128]{2,1,0:T(2,128)(2,1)S(1)}) fusion(bf16[4,64,128]{2,1,0:T(8,128)(2,1)} %param.6), kind=kLoop, calls=%fused_computation.52 | loop fusion | bytes 8192 | tf_op jit(solution)/shard_map/slice | solution.py:20
  0.8 1.3 %collective-permute-start = (bf16[4,2,128]{2,1,0:T(2,128)(2,1)S(1)}, bf16[4,2,128]{2,1,0:T(2,128)(2,1)S(1)}, u32[]{:S(2)}, u32[]{:S(2)}) collective-permute-start(bf16[4,2,128]{2,1,0:T(2,128)(2,1)S(1)} %get-tuple-element.37), channel_id=1, source_target_pairs={{0,1},{1,2},{2,3},{4,5},{5,6},{6,7},{8,9},{9,10},{10,11},{12,13},{... | collective-permute-start | bytes 6152 | tf_op jit(solution)/shard_map/ppermute | solution.py:19
  2.1 3.2 %collective-permute-start.1 = (bf16[4,2,128]{2,1,0:T(2,128)(2,1)S(1)}, bf16[4,2,128]{2,1,0:T(2,128)(2,1)S(1)}, u32[]{:S(2)}, u32[]{:S(2)}) collective-permute-start(bf16[4,2,128]{2,1,0:T(2,128)(2,1)S(1)} %get-tuple-element.38), channel_id=1, source_target_pairs={{1,0},{2,1},{3,2},{5,4},{6,5},{7,6},{9,8},{10,9},{11,10},{13,12},{... | collective-permute-start | bytes 6152 | tf_op jit(solution)/shard_map/ppermute | solution.py:22
  5.4 0.7 %collective-permute-done.1 = bf16[4,2,128]{2,1,0:T(2,128)(2,1)S(1)} collective-permute-done((bf16[4,2,128]{2,1,0:T(2,128)(2,1)S(1)}, bf16[4,2,128]{2,1,0:T(2,128)(2,1)S(1)}, u32[]{:S(2)}, u32[]{:S(2)}) %collective-permute-start.1) | collective-permute-done | bytes 2080 | tf_op jit(solution)/shard_map/ppermute | solution.py:22
  6.1 2.3 %collective-permute-start.5 = (bf16[2048,128]{1,0:T(8,128)(2,1)}, bf16[2048,128]{1,0:T(8,128)(2,1)S(1)}, u32[]{:S(2)}, u32[]{:S(2)}) collective-permute-start(bf16[2048,128]{1,0:T(8,128)(2,1)} %refs_1_), channel_id=1, source_target_pairs={{0,1},{1,0},{2,3},{3,2},{4,5},{5,4},{6,7},{7,6},{8,9},{9,8},{10,11... | collective-permute-start | bytes 1572872 | tf_op jit(solution)/shard_map/ppermute | solution.py:176
  8.4 1.4 %collective-permute-start.4 = (bf16[2048,128]{1,0:T(8,128)(2,1)}, bf16[2048,128]{1,0:T(8,128)(2,1)S(1)}, u32[]{:S(2)}, u32[]{:S(2)}) collective-permute-start(bf16[2048,128]{1,0:T(8,128)(2,1)} %refs_1_), channel_id=1, source_target_pairs={{0,2},{1,3},{2,0},{3,1},{4,6},{5,7},{6,4},{7,5},{8,10},{9,11},{10,... | collective-permute-start | bytes 1572872 | tf_op jit(solution)/shard_map/ppermute | solution.py:179
  9.8 3.1 %collective-permute-start.2 = (bf16[2,68,128]{2,1,0:T(8,128)(2,1)S(1)}, bf16[2,68,128]{2,1,0:T(8,128)(2,1)S(1)}, u32[]{:S(2)}, u32[]{:S(2)}) collective-permute-start(bf16[2,68,128]{2,1,0:T(8,128)(2,1)S(1)} %get-tuple-element.35), channel_id=1, source_target_pairs={{0,4},{4,8},{8,12},{12,16},{16,20},{20,24},{24,28},{1,5},{5,9},{9,... | collective-permute-start | bytes 104456 | tf_op jit(solution)/shard_map/ppermute | solution.py:19
  13.0 2.1 %collective-permute-start.3 = (bf16[2,68,128]{2,1,0:T(8,128)(2,1)S(1)}, bf16[2,68,128]{2,1,0:T(8,128)(2,1)S(1)}, u32[]{:S(2)}, u32[]{:S(2)}) collective-permute-start(bf16[2,68,128]{2,1,0:T(8,128)(2,1)S(1)} %get-tuple-element.36), channel_id=1, source_target_pairs={{4,0},{8,4},{12,8},{16,12},{20,16},{24,20},{28,24},{5,1},{9,5},{13... | collective-permute-start | bytes 104456 | tf_op jit(solution)/shard_map/ppermute | solution.py:22
  15.1 0.1 fusion.18
  15.2 3.4 %collective-permute-done.3 = bf16[2,68,128]{2,1,0:T(8,128)(2,1)S(1)} collective-permute-done((bf16[2,68,128]{2,1,0:T(8,128)(2,1)S(1)}, bf16[2,68,128]{2,1,0:T(8,128)(2,1)S(1)}, u32[]{:S(2)}, u32[]{:S(2)}) %collective-permute-start.3) | collective-permute-done | bytes 34848 | tf_op jit(solution)/shard_map/ppermute | solution.py:22
  18.6 0.7 %reshape.78.refs_0_ = bf16[544,128]{1,0:T(8,128)(2,1)} reshape(bf16[8,68,128]{2,1,0:T(8,128)(2,1)S(1)} %pad_maximum_fusion) | data formatting | bytes 278528 | tf_op jit(solution)/shard_map/reshape | solution.py:232
  19.3 0.6 %broadcast_in_dim.22.refs_3_.refs_2_ = f32[8,128]{1,0:T(8,128)} broadcast(f32[128]{0:T(128)S(1)} %pad.4), dimensions={1} | broadcast | bytes 4608 | tf_op jit(solution)/shard_map/broadcast_in_dim | solution.py:191
  19.9 0.2 copy-done.3
  20.1 8.0 %shard_map.64 = (f32[544,128]{1,0:T(8,128)}, f32[544,128]{1,0:T(8,128)}, f32[544,8]{1,0:T(8,128)}) custom-call(bf16[544,128]{1,0:T(8,128)(2,1)} %reshape.78.refs_0_, bf16[2048,128]{1,0:T(8,128)(2,1)} %refs_1_, bf16[2048,128]{1,0:T(8,128)(2,1)} %copy-done.3, f32[8,128]{1,0:T(8,128)} %broadcast_in_dim.22.refs_3_.refs_2_), custom_call_target="tpu_custom_call" | custom-call | tf_op jit(solution)/shard_map/pallas_call | solution.py:151
  28.1 2.1 %collective-permute-start.6 = (bf16[2048,128]{1,0:T(8,128)(2,1)S(1)}, bf16[2048,128]{1,0:T(8,128)(2,1)S(1)}, u32[]{:S(2)}, u32[]{:S(2)}) collective-permute-start(bf16[2048,128]{1,0:T(8,128)(2,1)S(1)} %collective-permute-done.4.refs_1_), channel_id=1, source_target_pairs={{0,1},{1,0},{2,3},{3,2},{4,5},{5,4},{6,7},{7,6},{8,9},{9,8},{10,11... | collective-permute-start | bytes 1572872 | tf_op jit(solution)/shard_map/ppermute | solution.py:206
  30.3 0.1 broadcast_and_fusion
  30.3 0.1 slice.47
  30.4 0.1 copy.7
  30.6 0.7 %copy-done.6 = f32[2,128]{1,0:T(2,128)S(1)} copy-done((f32[2,128]{1,0:T(2,128)S(1)}, f32[2,128]{1,0:T(2,128)}, u32[]{:S(2)}) %copy-start.6) | copy-done | bytes 1048
  31.2 4.8 %shard_map.65 = (f32[544,128]{1,0:T(8,128)}, f32[544,128]{1,0:T(8,128)}, f32[544,8]{1,0:T(8,128)}) custom-call(bf16[544,128]{1,0:T(8,128)(2,1)} %reshape.78.refs_0_, bf16[2048,128]{1,0:T(8,128)(2,1)} %copy-done.1, f32[8,128]{1,0:T(8,128)} %broadcast_in_dim.22.refs_3_.refs_2_, f32[544,128]{1,0:T(8,128)} %get-tuple-element.25.refs_3_, ...), custom_call_target="tpu_custom_call" | custom-call | tf_op jit(solution)/shard_map/pallas_call | solution.py:151
  36.0 0.8 %copy-done.2 = bf16[2048,128]{1,0:T(8,128)(2,1)} copy-done((bf16[2048,128]{1,0:T(8,128)(2,1)}, bf16[2048,128]{1,0:T(8,128)(2,1)S(1)}, u32[]{:S(2)}) %copy-start.2) | copy-done | bytes 524312
  36.8 5.4 %shard_map.66 = (f32[544,128]{1,0:T(8,128)}, f32[544,128]{1,0:T(8,128)}) custom-call(bf16[544,128]{1,0:T(8,128)(2,1)} %reshape.78.refs_0_, bf16[2048,128]{1,0:T(8,128)(2,1)} %copy-done.2, f32[8,128]{1,0:T(8,128)} %broadcast_in_dim.22.refs_3_.refs_2_, f32[544,128]{1,0:T(8,128)} %get-tuple-element.28.refs_3_, f32[544,128]{1,0:T(8,128)} %get-tuple-element.29.refs_4_, ...), custom_call_target="tpu_custom_call" | custom-call | tf_op jit(solution)/shard_map/pallas_call | solution.py:151
  42.3 1.4 %slice_reduce_fusion.1 = (f32[544]{0:T(1024)S(1)}, f32[544]{0:T(1024)S(1)}) fusion(f32[544,128]{1,0:T(8,128)} %get-tuple-element.31), kind=kLoop, calls=%fused_computation.9 | loop fusion | bytes 8704 | tf_op jit(solution)/shard_map/slice | solution.py:219
  43.7 0.1 reshape_squeeze.6
  43.8 0.1 reshape_squeeze.7
  43.8 0.1 slice.48
  43.9 0.1 broadcast_subtract_fusion
  44.0 0.1 slice_bitcast_fusion.2
  44.1 0.1 slice.50
  44.2 0.1 select_bitcast_fusion
  44.3 0.1 copy.20
  44.4 0.1 copy.10
  44.5 0.0 copy-start.10
  44.5 0.6 %copy-done.10 = pred[8,9]{0,1:T(8,128)(4,1)S(1)} copy-done((pred[8,9]{0,1:T(8,128)(4,1)S(1)}, pred[8,9]{0,1:T(8,128)(4,1)}, u32[]{:S(2)}) %copy-start.10) | copy-done | bytes 96
  45.2 0.9 %convolution_select_fusion = f32[6,8,9,128]{3,1,2,0:T(8,128)S(1)} fusion(bf16[3,3,128,128]{3,2,1,0:T(8,128)(2,1)S(1)} %copy-done, f32[8,1,7,2,128]{4,2,3,0,1:T(8,128)S(1)} %slice.56, f32[8,1,8,9,128]{4,2,3,0,1:T(8,128)S(1)} %copy.10, pred[8,9]{0,1:T(8,128)(4,1)S(1)} %copy-done.10), kind=kOutput, calls=%fused_computation | convolution fusion | flops 764737536 | bytes 868424 | tf_op jit(solution)/shard_map/conv_general_dilated | solution.py:243
  46.1 0.1 copy.11
  46.2 0.1 copy.12
  46.3 0.1 copy.13
  46.4 0.7 %copy-done.7 = f32[128]{0:T(128)S(1)} copy-done((f32[128]{0:T(128)S(1)}, f32[128]{0:T(128)}, u32[]{:S(2)}) %copy-start.7) | copy-done | bytes 536
  47.1 0.3 select_bitcast_fusion.1
  47.4 0.0 copy-start.8
  47.4 0.0 copy-start.9
  47.4 0.6 %copy-done.8 = bf16[2,3,3,128]{3,0,2,1:T(2,128)(2,1)S(1)} copy-done((bf16[2,3,3,128]{3,0,2,1:T(2,128)(2,1)S(1)}, bf16[2,3,3,128]{3,0,2,1:T(2,128)(2,1)}, u32[]{:S(2)}) %copy-start.8) | copy-done | bytes 4632
  48.1 0.0 copy-done.9
  48.1 1.7 %convolution_select_fusion.1 = f32[4,8,9,2]{1,3,2,0:T(2,128)S(1)} fusion(bf16[2,3,3,128]{3,0,2,1:T(2,128)(2,1)S(1)} %copy-done.8, bf16[6,1,7,2,128]{4,2,3,0,1:T(8,128)(2,1)S(1)} %slice.58, bf16[6,1,8,9,128]{4,2,3,0,1:T(8,128)(2,1)S(1)} %copy.15, pred[8,9]{0,1:T(8,128)(4,1)S(1)} %copy-done.9), kind=kOutput, calls=%fused_computation.1 | convolution fusion | flops 1733184 | bytes 139080 | tf_op jit(solution)/shard_map/conv_general_dilated | solution.py:254
  49.8 0.1 copy.18
  49.9 0.1 reshape.105
  50.0 0.6 %fusion.17 = f32[2,4,64]{2,1,0:T(4,128)} fusion(f32[4,1,72,2]{2,0,3,1:T(4,128)S(1)} %reshape.105, f32[1,4,64]{2,1,0:T(4,128)S(1)} %get-tuple-element.41, f32[1,4,64]{2,1,0:T(4,128)S(1)} %get-tuple-element.42), kind=kLoop, calls=%fused_computation.29 | loop fusion | flops 1024 | bytes 6144 | tf_op jit(solution)/shard_map/add | solution.py:260
  (33 shorter events, 0.2 us)
Async XLA Ops:
  0.0 44.5 %copy-start = (bf16[3,3,128,128]{3,2,1,0:T(8,128)(2,1)S(1)}, bf16[3,3,128,128]{3,2,1,0:T(8,128)(2,1)}, u32[]{:S(2)}) copy-start(bf16[3,3,128,128]{3,2,1,0:T(8,128)(2,1)} %param.8) | copy-start | bytes 884740
  0.0 6.1 %copy-start.5 = (bf16[4,64,128]{2,1,0:T(8,128)(2,1)S(1)}, bf16[4,64,128]{2,1,0:T(8,128)(2,1)}, u32[]{:S(2)}) copy-start(bf16[4,64,128]{2,1,0:T(8,128)(2,1)} %param.6) | copy-start | bytes 196612
  0.8 4.6 %collective-permute-start = (bf16[4,2,128]{2,1,0:T(2,128)(2,1)S(1)}, bf16[4,2,128]{2,1,0:T(2,128)(2,1)S(1)}, u32[]{:S(2)}, u32[]{:S(2)}) collective-permute-start(bf16[4,2,128]{2,1,0:T(2,128)(2,1)S(1)} %get-tuple-element.37), channel_id=1, source_target_pairs={{0,1},{1,2},{2,3},{4,5},{5,6},{6,7},{8,9},{9,10},{10,11},{12,13},{... | collective-permute-start | bytes 6152 | tf_op jit(solution)/shard_map/ppermute | solution.py:19
  2.1 4.0 %collective-permute-start.1 = (bf16[4,2,128]{2,1,0:T(2,128)(2,1)S(1)}, bf16[4,2,128]{2,1,0:T(2,128)(2,1)S(1)}, u32[]{:S(2)}, u32[]{:S(2)}) collective-permute-start(bf16[4,2,128]{2,1,0:T(2,128)(2,1)S(1)} %get-tuple-element.38), channel_id=1, source_target_pairs={{1,0},{2,1},{3,2},{5,4},{6,5},{7,6},{9,8},{10,9},{11,10},{13,12},{... | collective-permute-start | bytes 6152 | tf_op jit(solution)/shard_map/ppermute | solution.py:22
  6.1 13.2 %collective-permute-start.5 = (bf16[2048,128]{1,0:T(8,128)(2,1)}, bf16[2048,128]{1,0:T(8,128)(2,1)S(1)}, u32[]{:S(2)}, u32[]{:S(2)}) collective-permute-start(bf16[2048,128]{1,0:T(8,128)(2,1)} %refs_1_), channel_id=1, source_target_pairs={{0,1},{1,0},{2,3},{3,2},{4,5},{5,4},{6,7},{7,6},{8,9},{9,8},{10,11... | collective-permute-start | bytes 1572872 | tf_op jit(solution)/shard_map/ppermute | solution.py:176
  8.4 19.7 %collective-permute-start.4 = (bf16[2048,128]{1,0:T(8,128)(2,1)}, bf16[2048,128]{1,0:T(8,128)(2,1)S(1)}, u32[]{:S(2)}, u32[]{:S(2)}) collective-permute-start(bf16[2048,128]{1,0:T(8,128)(2,1)} %refs_1_), channel_id=1, source_target_pairs={{0,2},{1,3},{2,0},{3,1},{4,6},{5,7},{6,4},{7,5},{8,10},{9,11},{10,... | collective-permute-start | bytes 1572872 | tf_op jit(solution)/shard_map/ppermute | solution.py:179
  9.8 5.4 %collective-permute-start.2 = (bf16[2,68,128]{2,1,0:T(8,128)(2,1)S(1)}, bf16[2,68,128]{2,1,0:T(8,128)(2,1)S(1)}, u32[]{:S(2)}, u32[]{:S(2)}) collective-permute-start(bf16[2,68,128]{2,1,0:T(8,128)(2,1)S(1)} %get-tuple-element.35), channel_id=1, source_target_pairs={{0,4},{4,8},{8,12},{12,16},{16,20},{20,24},{24,28},{1,5},{5,9},{9,... | collective-permute-start | bytes 104456 | tf_op jit(solution)/shard_map/ppermute | solution.py:19
  13.0 5.6 %collective-permute-start.3 = (bf16[2,68,128]{2,1,0:T(8,128)(2,1)S(1)}, bf16[2,68,128]{2,1,0:T(8,128)(2,1)S(1)}, u32[]{:S(2)}, u32[]{:S(2)}) collective-permute-start(bf16[2,68,128]{2,1,0:T(8,128)(2,1)S(1)} %get-tuple-element.36), channel_id=1, source_target_pairs={{4,0},{8,4},{12,8},{16,12},{20,16},{24,20},{28,24},{5,1},{9,5},{13... | collective-permute-start | bytes 104456 | tf_op jit(solution)/shard_map/ppermute | solution.py:22
  19.3 0.8 %copy-start.3 = (bf16[2048,128]{1,0:T(8,128)(2,1)}, bf16[2048,128]{1,0:T(8,128)(2,1)S(1)}, u32[]{:S(2)}) copy-start(bf16[2048,128]{1,0:T(8,128)(2,1)S(1)} %collective-permute-done.5.refs_2_) | copy-start | bytes 1572868
  28.1 3.1 %copy-start.1 = (bf16[2048,128]{1,0:T(8,128)(2,1)}, bf16[2048,128]{1,0:T(8,128)(2,1)S(1)}, u32[]{:S(2)}) copy-start(bf16[2048,128]{1,0:T(8,128)(2,1)S(1)} %collective-permute-done.4.refs_1_) | copy-start | bytes 1572868
  28.1 7.9 %collective-permute-start.6 = (bf16[2048,128]{1,0:T(8,128)(2,1)S(1)}, bf16[2048,128]{1,0:T(8,128)(2,1)S(1)}, u32[]{:S(2)}, u32[]{:S(2)}) collective-permute-start(bf16[2048,128]{1,0:T(8,128)(2,1)S(1)} %collective-permute-done.4.refs_1_), channel_id=1, source_target_pairs={{0,1},{1,0},{2,3},{3,2},{4,5},{5,4},{6,7},{7,6},{8,9},{9,8},{10,11... | collective-permute-start | bytes 1572872 | tf_op jit(solution)/shard_map/ppermute | solution.py:206
  30.5 0.7 %copy-start.6 = (f32[2,128]{1,0:T(2,128)S(1)}, f32[2,128]{1,0:T(2,128)}, u32[]{:S(2)}) copy-start(f32[2,128]{1,0:T(2,128)} %param.9) | copy-start | bytes 3076
  36.0 0.8 %copy-start.2 = (bf16[2048,128]{1,0:T(8,128)(2,1)}, bf16[2048,128]{1,0:T(8,128)(2,1)S(1)}, u32[]{:S(2)}) copy-start(bf16[2048,128]{1,0:T(8,128)(2,1)S(1)} %collective-permute-done.6.refs_1_) | copy-start | bytes 1572868
  42.3 1.9 %copy-start.4 = (f32[544,128]{1,0:T(8,128)S(1)}, f32[544,128]{1,0:T(8,128)}, u32[]{:S(2)}) copy-start(f32[544,128]{1,0:T(8,128)} %get-tuple-element.32) | copy-start | bytes 835588
  44.5 0.7 %copy-start.10 = (pred[8,9]{0,1:T(8,128)(4,1)S(1)}, pred[8,9]{0,1:T(8,128)(4,1)}, u32[]{:S(2)}) copy-start(pred[8,9]{0,1:T(8,128)(4,1)} %constant.80) | copy-start | bytes 220
  46.4 0.7 %copy-start.7 = (f32[128]{0:T(128)S(1)}, f32[128]{0:T(128)}, u32[]{:S(2)}) copy-start(f32[128]{0:T(128)} %param.10) | copy-start | bytes 1540
  47.4 0.7 %copy-start.8 = (bf16[2,3,3,128]{3,0,2,1:T(2,128)(2,1)S(1)}, bf16[2,3,3,128]{3,0,2,1:T(2,128)(2,1)}, u32[]{:S(2)}) copy-start(bf16[2,3,3,128]{3,0,2,1:T(2,128)(2,1)} %param.11) | copy-start | bytes 13828
  47.4 0.7 %copy-start.9 = (pred[8,9]{0,1:T(8,128)(4,1)S(1)}, pred[8,9]{0,1:T(8,128)(4,1)}, u32[]{:S(2)}) copy-start(pred[8,9]{0,1:T(8,128)(4,1)} %constant.79) | copy-start | bytes 220

commit v13 on v12

--- a/solution.py
+++ b/solution.py
@@ -192,7 +192,7 @@
     pending = None
     whole_rows = tk % width == 0
     if whole_rows and n > 1:
-        groups = [[0, 1]] + [[i] for i in range(2, n)]
+        groups = [[0]] + ([[1, 2]] if n > 2 else [[1]]) + [[i] for i in range(3, n)]
     else:
         groups = [[i] for i in range(n)]
     for group in groups:

time: 51 us -> 49.1 us (0.963)
  the two profiles are of different devices: /device:TPU:23 before, /device:TPU:0 now
where the time goes in v13:
time: 49.1 us; the launch traced here: 48.6 us
  Pallas kernels  16.4 us (33%)
  starting transfers between devices  10.7 us (22%)
  local copies, waits for them, and re-layouts  9.03 us (18%)
  waiting for transfers between devices  8.22 us (17%)
  matrix products  2.64 us (5%)
  other arithmetic  1.34 us (3%)
    pallas_call x3, Pallas kernels, match_step(): pl.pallas_call(kernel, grid=(nq,), in_specs=in_specs, out_specs=out_specs...  16.4 us
    ppermute x2, waiting for transfers between devices, extended(): lax.ppermute(lax.slice_in_dim(block, 0, width, axis=dim), axis, backward)  8.02 us
    ppermute x2, starting transfers between devices, extended(): lax.ppermute(lax.slice_in_dim(block, block.shape[dim] - width, None, axis...  5.77 us
    unnamed x23, local copies, waits for them, and re-layouts  4.28 us
    ppermute x2, starting transfers between devices, extended(): lax.ppermute(lax.slice_in_dim(block, 0, width, axis=dim), axis, backward)  2.58 us
    ppermute x1, starting transfers between devices, match(): moved = lax.ppermute(targets, 'match', hop)  2.35 us
    conv_general_dilated x1, matrix products, local(): lax.conv_general_dilated(hidden[None], jnp.transpose(conv_out, (1, 2, 3,...  1.7 us
    slice x1, local copies, waits for them, and re-layouts, match(): return (warped[:count], flow[:count, 0], flow[:count, 1])  1.42 us
  transfers between devices with their start and end apart: 7, of which 3 were waited for; matrix products, arithmetic and copies ran while one was open for 4% of the time, Pallas kernels for 22%

profile of v13, /device:TPU:0, one launch (start us, length us, event | category | flops | bytes accessed | tf_op | source)
XLA Modules:
  0.0 48.6 jit_solution(9385500110533096149)
XLA Ops:
  0.0 0.8 %fusion.26 = (bf16[4,2,128]{2,1,0:T(2,128)(2,1)S(1)}, bf16[4,2,128]{2,1,0:T(2,128)(2,1)S(1)}) fusion(bf16[4,64,128]{2,1,0:T(8,128)(2,1)} %param.6), kind=kLoop, calls=%fused_computation.52 | loop fusion | bytes 8192 | tf_op jit(solution)/shard_map/slice | solution.py:20
  0.8 2.3 %collective-permute-start = (bf16[4,2,128]{2,1,0:T(2,128)(2,1)S(1)}, bf16[4,2,128]{2,1,0:T(2,128)(2,1)S(1)}, u32[]{:S(2)}, u32[]{:S(2)}) collective-permute-start(bf16[4,2,128]{2,1,0:T(2,128)(2,1)S(1)} %get-tuple-element.37), channel_id=1, source_target_pairs={{0,1},{1,2},{2,3},{4,5},{5,6},{6,7},{8,9},{9,10},{10,11},{12,13},{... | collective-permute-start | bytes 6152 | tf_op jit(solution)/shard_map/ppermute | solution.py:19
  3.1 1.3 %collective-permute-start.1 = (bf16[4,2,128]{2,1,0:T(2,128)(2,1)S(1)}, bf16[4,2,128]{2,1,0:T(2,128)(2,1)S(1)}, u32[]{:S(2)}, u32[]{:S(2)}) collective-permute-start(bf16[4,2,128]{2,1,0:T(2,128)(2,1)S(1)} %get-tuple-element.38), channel_id=1, source_target_pairs={{1,0},{2,1},{3,2},{5,4},{6,5},{7,6},{9,8},{10,9},{11,10},{13,12},{... | collective-permute-start | bytes 6152 | tf_op jit(solution)/shard_map/ppermute | solution.py:22
  4.5 3.8 %collective-permute-done.1 = bf16[4,2,128]{2,1,0:T(2,128)(2,1)S(1)} collective-permute-done((bf16[4,2,128]{2,1,0:T(2,128)(2,1)S(1)}, bf16[4,2,128]{2,1,0:T(2,128)(2,1)S(1)}, u32[]{:S(2)}, u32[]{:S(2)}) %collective-permute-start.1) | collective-permute-done | bytes 2080 | tf_op jit(solution)/shard_map/ppermute | solution.py:22
  8.3 2.3 %collective-permute-start.4 = (bf16[2048,128]{1,0:T(8,128)(2,1)}, bf16[2048,128]{1,0:T(8,128)(2,1)S(1)}, u32[]{:S(2)}, u32[]{:S(2)}) collective-permute-start(bf16[2048,128]{1,0:T(8,128)(2,1)} %refs_1_), channel_id=1, source_target_pairs={{0,2},{1,3},{2,0},{3,1},{4,6},{5,7},{6,4},{7,5},{8,10},{9,11},{10,... | collective-permute-start | bytes 1572872 | tf_op jit(solution)/shard_map/ppermute | solution.py:179
  10.7 3.4 %collective-permute-start.2 = (bf16[2,68,128]{2,1,0:T(8,128)(2,1)S(1)}, bf16[2,68,128]{2,1,0:T(8,128)(2,1)S(1)}, u32[]{:S(2)}, u32[]{:S(2)}) collective-permute-start(bf16[2,68,128]{2,1,0:T(8,128)(2,1)S(1)} %get-tuple-element.35), channel_id=1, source_target_pairs={{0,4},{4,8},{8,12},{12,16},{16,20},{20,24},{24,28},{1,5},{5,9},{9,... | collective-permute-start | bytes 104456 | tf_op jit(solution)/shard_map/ppermute | solution.py:19
  14.1 1.3 %collective-permute-start.3 = (bf16[2,68,128]{2,1,0:T(8,128)(2,1)S(1)}, bf16[2,68,128]{2,1,0:T(8,128)(2,1)S(1)}, u32[]{:S(2)}, u32[]{:S(2)}) collective-permute-start(bf16[2,68,128]{2,1,0:T(8,128)(2,1)S(1)} %get-tuple-element.36), channel_id=1, source_target_pairs={{4,0},{8,4},{12,8},{16,12},{20,16},{24,20},{28,24},{5,1},{9,5},{13... | collective-permute-start | bytes 104456 | tf_op jit(solution)/shard_map/ppermute | solution.py:22
  15.4 0.1 fusion.18
  15.5 0.0 collective-permute-start.6
  15.6 0.2 collective-permute-done.2
  15.7 4.2 %collective-permute-done.3 = bf16[2,68,128]{2,1,0:T(8,128)(2,1)S(1)} collective-permute-done((bf16[2,68,128]{2,1,0:T(8,128)(2,1)S(1)}, bf16[2,68,128]{2,1,0:T(8,128)(2,1)S(1)}, u32[]{:S(2)}, u32[]{:S(2)}) %collective-permute-start.3) | collective-permute-done | bytes 34848 | tf_op jit(solution)/shard_map/ppermute | solution.py:22
  20.0 0.7 %reshape.78.refs_0_ = bf16[544,128]{1,0:T(8,128)(2,1)} reshape(bf16[8,68,128]{2,1,0:T(8,128)(2,1)S(1)} %pad_maximum_fusion) | data formatting | bytes 278528 | tf_op jit(solution)/shard_map/reshape | solution.py:232
  20.7 0.6 %broadcast_in_dim.22.refs_2_.refs_3_ = f32[8,128]{1,0:T(8,128)} broadcast(f32[128]{0:T(128)S(1)} %pad.4), dimensions={1} | broadcast | bytes 4608 | tf_op jit(solution)/shard_map/broadcast_in_dim | solution.py:191
  21.3 4.7 %shard_map.64 = (f32[544,128]{1,0:T(8,128)}, f32[544,128]{1,0:T(8,128)}, f32[544,8]{1,0:T(8,128)}) custom-call(bf16[544,128]{1,0:T(8,128)(2,1)} %reshape.78.refs_0_, bf16[2048,128]{1,0:T(8,128)(2,1)} %refs_1_, f32[8,128]{1,0:T(8,128)} %broadcast_in_dim.22.refs_2_.refs_3_), custom_call_target="tpu_custom_call" | custom-call | tf_op jit(solution)/shard_map/pallas_call | solution.py:151
  26.0 0.1 broadcast_and_fusion
  26.1 0.1 slice.47
  26.2 0.1 copy.7
  26.4 0.7 %copy-done.6 = f32[2,128]{1,0:T(2,128)S(1)} copy-done((f32[2,128]{1,0:T(2,128)S(1)}, f32[2,128]{1,0:T(2,128)}, u32[]{:S(2)}) %copy-start.6) | copy-done | bytes 1048
  27.0 0.8 %copy-done.3 = bf16[2048,128]{1,0:T(8,128)(2,1)} copy-done((bf16[2048,128]{1,0:T(8,128)(2,1)}, bf16[2048,128]{1,0:T(8,128)(2,1)S(1)}, u32[]{:S(2)}) %copy-start.3) | copy-done | bytes 524312
  27.8 6.2 %shard_map.65 = (f32[544,128]{1,0:T(8,128)}, f32[544,128]{1,0:T(8,128)}, f32[544,8]{1,0:T(8,128)}) custom-call(bf16[544,128]{1,0:T(8,128)(2,1)} %reshape.78.refs_0_, bf16[2048,128]{1,0:T(8,128)(2,1)} %copy-done.3, bf16[2048,128]{1,0:T(8,128)(2,1)} %copy-done.2, f32[8,128]{1,0:T(8,128)} %broadcast_in_dim.22.refs_2_.refs_3_, ...), custom_call_target="tpu_custom_call" | custom-call | tf_op jit(solution)/shard_map/pallas_call | solution.py:151
  34.0 0.8 %copy-done.1 = bf16[2048,128]{1,0:T(8,128)(2,1)} copy-done((bf16[2048,128]{1,0:T(8,128)(2,1)}, bf16[2048,128]{1,0:T(8,128)(2,1)S(1)}, u32[]{:S(2)}) %copy-start.1) | copy-done | bytes 524312
  34.8 5.4 %shard_map.66 = (f32[544,128]{1,0:T(8,128)}, f32[544,128]{1,0:T(8,128)}) custom-call(bf16[544,128]{1,0:T(8,128)(2,1)} %reshape.78.refs_0_, bf16[2048,128]{1,0:T(8,128)(2,1)} %copy-done.1, f32[8,128]{1,0:T(8,128)} %broadcast_in_dim.22.refs_2_.refs_3_, f32[544,128]{1,0:T(8,128)} %get-tuple-element.28.refs_3_, f32[544,128]{1,0:T(8,128)} %get-tuple-element.29.refs_4_, ...), custom_call_target="tpu_custom_call" | custom-call | tf_op jit(solution)/shard_map/pallas_call | solution.py:151
  40.2 1.4 %slice_reduce_fusion.1 = (f32[544]{0:T(1024)S(1)}, f32[544]{0:T(1024)S(1)}) fusion(f32[544,128]{1,0:T(8,128)} %get-tuple-element.31), kind=kLoop, calls=%fused_computation.9 | loop fusion | bytes 8704 | tf_op jit(solution)/shard_map/slice | solution.py:219
  41.7 0.1 reshape_squeeze.6
  41.7 0.1 reshape_squeeze.7
  41.8 0.1 slice.48
  41.9 0.1 broadcast_subtract_fusion
  42.0 0.1 slice_bitcast_fusion.2
  42.0 0.1 slice.50
  42.1 0.1 select_bitcast_fusion
  42.3 0.1 copy.20
  42.4 0.1 copy.10
  42.5 0.0 copy-start.10
  42.5 0.6 %copy-done.10 = pred[8,9]{0,1:T(8,128)(4,1)S(1)} copy-done((pred[8,9]{0,1:T(8,128)(4,1)S(1)}, pred[8,9]{0,1:T(8,128)(4,1)}, u32[]{:S(2)}) %copy-start.10) | copy-done | bytes 96
  43.1 0.9 %convolution_select_fusion = f32[6,8,9,128]{3,1,2,0:T(8,128)S(1)} fusion(bf16[3,3,128,128]{3,2,1,0:T(8,128)(2,1)S(1)} %copy-done, f32[8,1,7,2,128]{4,2,3,0,1:T(8,128)S(1)} %slice.56, f32[8,1,8,9,128]{4,2,3,0,1:T(8,128)S(1)} %copy.10, pred[8,9]{0,1:T(8,128)(4,1)S(1)} %copy-done.10), kind=kOutput, calls=%fused_computation | convolution fusion | flops 764737536 | bytes 868424 | tf_op jit(solution)/shard_map/conv_general_dilated | solution.py:243
  44.1 0.1 copy.11
  44.2 0.1 copy.12
  44.3 0.1 copy.13
  44.4 0.7 %copy-done.7 = f32[128]{0:T(128)S(1)} copy-done((f32[128]{0:T(128)S(1)}, f32[128]{0:T(128)}, u32[]{:S(2)}) %copy-start.7) | copy-done | bytes 536
  45.0 0.3 select_bitcast_fusion.1
  45.4 0.0 copy-start.8
  45.4 0.0 copy-start.9
  45.4 0.6 %copy-done.8 = bf16[2,3,3,128]{3,0,2,1:T(2,128)(2,1)S(1)} copy-done((bf16[2,3,3,128]{3,0,2,1:T(2,128)(2,1)S(1)}, bf16[2,3,3,128]{3,0,2,1:T(2,128)(2,1)}, u32[]{:S(2)}) %copy-start.8) | copy-done | bytes 4632
  46.1 0.0 copy-done.9
  46.1 1.7 %convolution_select_fusion.1 = f32[4,8,9,2]{1,3,2,0:T(2,128)S(1)} fusion(bf16[2,3,3,128]{3,0,2,1:T(2,128)(2,1)S(1)} %copy-done.8, bf16[6,1,7,2,128]{4,2,3,0,1:T(8,128)(2,1)S(1)} %slice.58, bf16[6,1,8,9,128]{4,2,3,0,1:T(8,128)(2,1)S(1)} %copy.15, pred[8,9]{0,1:T(8,128)(4,1)S(1)} %copy-done.9), kind=kOutput, calls=%fused_computation.1 | convolution fusion | flops 1733184 | bytes 139080 | tf_op jit(solution)/shard_map/conv_general_dilated | solution.py:254
  47.8 0.1 copy.18
  47.9 0.1 reshape.105
  48.0 0.6 %fusion.17 = f32[2,4,64]{2,1,0:T(4,128)} fusion(f32[4,1,72,2]{2,0,3,1:T(4,128)S(1)} %reshape.105, f32[1,4,64]{2,1,0:T(4,128)S(1)} %get-tuple-element.41, f32[1,4,64]{2,1,0:T(4,128)S(1)} %get-tuple-element.42), kind=kLoop, calls=%fused_computation.29 | loop fusion | flops 1024 | bytes 6144 | tf_op jit(solution)/shard_map/add | solution.py:260
  (33 shorter events, 0.2 us)
Async XLA Ops:
  0.0 42.5 %copy-start = (bf16[3,3,128,128]{3,2,1,0:T(8,128)(2,1)S(1)}, bf16[3,3,128,128]{3,2,1,0:T(8,128)(2,1)}, u32[]{:S(2)}) copy-start(bf16[3,3,128,128]{3,2,1,0:T(8,128)(2,1)} %param.8) | copy-start | bytes 884740
  0.0 8.3 %copy-start.5 = (bf16[4,64,128]{2,1,0:T(8,128)(2,1)S(1)}, bf16[4,64,128]{2,1,0:T(8,128)(2,1)}, u32[]{:S(2)}) copy-start(bf16[4,64,128]{2,1,0:T(8,128)(2,1)} %param.6) | copy-start | bytes 196612
  0.8 3.7 %collective-permute-start = (bf16[4,2,128]{2,1,0:T(2,128)(2,1)S(1)}, bf16[4,2,128]{2,1,0:T(2,128)(2,1)S(1)}, u32[]{:S(2)}, u32[]{:S(2)}) collective-permute-start(bf16[4,2,128]{2,1,0:T(2,128)(2,1)S(1)} %get-tuple-element.37), channel_id=1, source_target_pairs={{0,1},{1,2},{2,3},{4,5},{5,6},{6,7},{8,9},{9,10},{10,11},{12,13},{... | collective-permute-start | bytes 6152 | tf_op jit(solution)/shard_map/ppermute | solution.py:19
  3.1 5.2 %collective-permute-start.1 = (bf16[4,2,128]{2,1,0:T(2,128)(2,1)S(1)}, bf16[4,2,128]{2,1,0:T(2,128)(2,1)S(1)}, u32[]{:S(2)}, u32[]{:S(2)}) collective-permute-start(bf16[4,2,128]{2,1,0:T(2,128)(2,1)S(1)} %get-tuple-element.38), channel_id=1, source_target_pairs={{1,0},{2,1},{3,2},{5,4},{6,5},{7,6},{9,8},{10,9},{11,10},{13,12},{... | collective-permute-start | bytes 6152 | tf_op jit(solution)/shard_map/ppermute | solution.py:22
  8.3 17.7 %collective-permute-start.4 = (bf16[2048,128]{1,0:T(8,128)(2,1)}, bf16[2048,128]{1,0:T(8,128)(2,1)S(1)}, u32[]{:S(2)}, u32[]{:S(2)}) collective-permute-start(bf16[2048,128]{1,0:T(8,128)(2,1)} %refs_1_), channel_id=1, source_target_pairs={{0,2},{1,3},{2,0},{3,1},{4,6},{5,7},{6,4},{7,5},{8,10},{9,11},{10,... | collective-permute-start | bytes 1572872 | tf_op jit(solution)/shard_map/ppermute | solution.py:179
  10.7 5.0 %collective-permute-start.2 = (bf16[2,68,128]{2,1,0:T(8,128)(2,1)S(1)}, bf16[2,68,128]{2,1,0:T(8,128)(2,1)S(1)}, u32[]{:S(2)}, u32[]{:S(2)}) collective-permute-start(bf16[2,68,128]{2,1,0:T(8,128)(2,1)S(1)} %get-tuple-element.35), channel_id=1, source_target_pairs={{0,4},{4,8},{8,12},{12,16},{16,20},{20,24},{24,28},{1,5},{5,9},{9,... | collective-permute-start | bytes 104456 | tf_op jit(solution)/shard_map/ppermute | solution.py:19
  14.1 5.9 %collective-permute-start.3 = (bf16[2,68,128]{2,1,0:T(8,128)(2,1)S(1)}, bf16[2,68,128]{2,1,0:T(8,128)(2,1)S(1)}, u32[]{:S(2)}, u32[]{:S(2)}) collective-permute-start(bf16[2,68,128]{2,1,0:T(8,128)(2,1)S(1)} %get-tuple-element.36), channel_id=1, source_target_pairs={{4,0},{8,4},{12,8},{16,12},{20,16},{24,20},{28,24},{5,1},{9,5},{13... | collective-permute-start | bytes 104456 | tf_op jit(solution)/shard_map/ppermute | solution.py:22
  15.5 11.5 %collective-permute-start.6 = (bf16[2048,128]{1,0:T(8,128)(2,1)}, bf16[2048,128]{1,0:T(8,128)(2,1)S(1)}, u32[]{:S(2)}, u32[]{:S(2)}) collective-permute-start(bf16[2048,128]{1,0:T(8,128)(2,1)} %refs_1_), channel_id=1, source_target_pairs={{0,1},{1,0},{2,3},{3,2},{4,5},{5,4},{6,7},{7,6},{8,9},{9,8},{10,11... | collective-permute-start | bytes 1572872 | tf_op jit(solution)/shard_map/ppermute | solution.py:176
  26.0 1.0 %copy-start.2 = (bf16[2048,128]{1,0:T(8,128)(2,1)}, bf16[2048,128]{1,0:T(8,128)(2,1)S(1)}, u32[]{:S(2)}) copy-start(bf16[2048,128]{1,0:T(8,128)(2,1)S(1)} %collective-permute-done.4.refs_2_) | copy-start | bytes 1572868
  26.0 8.0 %collective-permute-start.5 = (bf16[2048,128]{1,0:T(8,128)(2,1)S(1)}, bf16[2048,128]{1,0:T(8,128)(2,1)S(1)}, u32[]{:S(2)}, u32[]{:S(2)}) collective-permute-start(bf16[2048,128]{1,0:T(8,128)(2,1)S(1)} %collective-permute-done.4.refs_2_), channel_id=1, source_target_pairs={{0,1},{1,0},{2,3},{3,2},{4,5},{5,4},{6,7},{7,6},{8,9},{9,8},{10,11... | collective-permute-start | bytes 1572872 | tf_op jit(solution)/shard_map/ppermute | solution.py:206
  26.3 0.7 %copy-start.6 = (f32[2,128]{1,0:T(2,128)S(1)}, f32[2,128]{1,0:T(2,128)}, u32[]{:S(2)}) copy-start(f32[2,128]{1,0:T(2,128)} %param.9) | copy-start | bytes 3076
  27.0 0.8 %copy-start.3 = (bf16[2048,128]{1,0:T(8,128)(2,1)}, bf16[2048,128]{1,0:T(8,128)(2,1)S(1)}, u32[]{:S(2)}) copy-start(bf16[2048,128]{1,0:T(8,128)(2,1)S(1)} %collective-permute-done.6.refs_1_) | copy-start | bytes 1572868
  34.0 0.8 %copy-start.1 = (bf16[2048,128]{1,0:T(8,128)(2,1)}, bf16[2048,128]{1,0:T(8,128)(2,1)S(1)}, u32[]{:S(2)}) copy-start(bf16[2048,128]{1,0:T(8,128)(2,1)S(1)} %collective-permute-done.5.refs_1_) | copy-start | bytes 1572868
  40.2 1.9 %copy-start.4 = (f32[544,128]{1,0:T(8,128)S(1)}, f32[544,128]{1,0:T(8,128)}, u32[]{:S(2)}) copy-start(f32[544,128]{1,0:T(8,128)} %get-tuple-element.32) | copy-start | bytes 835588
  42.5 0.7 %copy-start.10 = (pred[8,9]{0,1:T(8,128)(4,1)S(1)}, pred[8,9]{0,1:T(8,128)(4,1)}, u32[]{:S(2)}) copy-start(pred[8,9]{0,1:T(8,128)(4,1)} %constant.80) | copy-start | bytes 220
  44.4 0.7 %copy-start.7 = (f32[128]{0:T(128)S(1)}, f32[128]{0:T(128)}, u32[]{:S(2)}) copy-start(f32[128]{0:T(128)} %param.10) | copy-start | bytes 1540
  45.4 0.7 %copy-start.8 = (bf16[2,3,3,128]{3,0,2,1:T(2,128)(2,1)S(1)}, bf16[2,3,3,128]{3,0,2,1:T(2,128)(2,1)}, u32[]{:S(2)}) copy-start(bf16[2,3,3,128]{3,0,2,1:T(2,128)(2,1)} %param.11) | copy-start | bytes 13828
  45.4 0.7 %copy-start.9 = (pred[8,9]{0,1:T(8,128)(4,1)S(1)}, pred[8,9]{0,1:T(8,128)(4,1)}, u32[]{:S(2)}) copy-start(pred[8,9]{0,1:T(8,128)(4,1)} %constant.79) | copy-start | bytes 220

commit v14 on v13

--- a/solution.py
+++ b/solution.py
@@ -226,7 +226,9 @@
     row_first = lax.axis_index("space") * rows
     col_first = lax.axis_index("match") * cols
     ext = extended(source, (("match", 1),), HALO)
-    targets, ext = lax.optimization_barrier((targets, ext))
+    targets, ext, conv_in, flow_proj, in_bias, conv_out = lax.optimization_barrier(
+        (targets, ext, conv_in, flow_proj, in_bias, conv_out)
+    )
     ext = extended(ext, (("space", 0),), HALO)
     erows, ecols = rows + 2 * HALO, cols + 2 * HALO
     warped, sum_x, sum_y = match(ext.reshape(erows * ecols, chans), targets, width)
@@ -251,13 +253,16 @@
     pre = pre + fx1[:, :, None] * flow_proj[0] + fy1[:, :, None] * flow_proj[1] + in_bias
     hidden = jax.nn.silu(pre).astype(jnp.bfloat16)
     hidden = jnp.where(inside[1:-1, 1:-1, None], hidden, jnp.zeros((), jnp.bfloat16))
-    delta = lax.conv_general_dilated(
-        hidden[None], jnp.transpose(conv_out, (1, 2, 3, 0)), (1, 1), "VALID",
-        dimension_numbers=("NHWC", "HWIO", "NHWC"),
-        preferred_element_type=jnp.float32,
-    )[0]
+    taps = jnp.transpose(conv_out, (3, 0, 1, 2)).reshape(chans, -1)
+    proj = jnp.einsum("hwc,ck->hwk", hidden, taps, preferred_element_type=jnp.float32)
+    delta = None
+    for tap_a in range(3):
+        for tap_b in range(3):
+            part = proj[tap_a:tap_a + rows, tap_b:tap_b + cols]
+            part = jnp.stack([part[..., o * 9 + tap_a * 3 + tap_b] for o in range(2)])
+            delta = part if delta is None else delta + part
     flows = jnp.stack([flow_x[HALO:-HALO, HALO:-HALO], flow_y[HALO:-HALO, HALO:-HALO]])
-    return flows + jnp.transpose(delta, (2, 0, 1))
+    return flows + delta
 
 
 def solution(mesh):

time: 49.1 us -> 47.5 us (0.967)
  matrix products: 2.64 us -> 1.13 us
    conv_general_dilated x1 -> x0, matrix products: 1.7 us -> none  [local(): lax.conv_general_dilated(hidden[None], jnp.transpose(conv_out, (1, 2, 3,...]
    unnamed x23 -> x21, local copies, waits for them, and re-layouts: 4.28 us -> 4.28 us
  transfers between devices with their start and end apart: 7 -> 7, of which waited for: 3 -> 3; matrix products, arithmetic and copies ran while one was open for 4% -> 4% of each run, Pallas kernels for 22% -> 23%
where the time goes in v14:
time: 47.5 us; the launch traced here: 47 us
  Pallas kernels  16.4 us (35%)
  starting transfers between devices  10.7 us (23%)
  local copies, waits for them, and re-layouts  8.91 us (19%)
  waiting for transfers between devices  8.22 us (17%)
  other arithmetic  1.34 us (3%)
  matrix products  1.13 us (2%)
    pallas_call x3, Pallas kernels, match_step(): pl.pallas_call(kernel, grid=(nq,), in_specs=in_specs, out_specs=out_specs...  16.4 us
    ppermute x2, waiting for transfers between devices, extended(): lax.ppermute(lax.slice_in_dim(block, 0, width, axis=dim), axis, backward)  8.02 us
    ppermute x2, starting transfers between devices, extended(): lax.ppermute(lax.slice_in_dim(block, block.shape[dim] - width, None, axis...  5.77 us
    unnamed x21, local copies, waits for them, and re-layouts  4.28 us
    ppermute x2, starting transfers between devices, extended(): lax.ppermute(lax.slice_in_dim(block, 0, width, axis=dim), axis, backward)  2.58 us
    ppermute x1, starting transfers between devices, match(): moved = lax.ppermute(targets, 'match', hop)  2.35 us
    slice x1, local copies, waits for them, and re-layouts, match(): return (warped[:count], flow[:count, 0], flow[:count, 1])  1.42 us
  transfers between devices with their start and end apart: 7, of which 3 were waited for; matrix products, arithmetic and copies ran while one was open for 4% of the time, Pallas kernels for 23%

profile of v14, /device:TPU:0, one launch (start us, length us, event | category | flops | bytes accessed | tf_op | source)
XLA Modules:
  0.0 47.0 jit_solution(1360931887696875845)
XLA Ops:
  0.0 0.8 %fusion.24 = (bf16[4,2,128]{2,1,0:T(2,128)(2,1)S(1)}, bf16[4,2,128]{2,1,0:T(2,128)(2,1)S(1)}) fusion(bf16[4,64,128]{2,1,0:T(8,128)(2,1)} %param.6), kind=kLoop, calls=%fused_computation.50 | loop fusion | bytes 8192 | tf_op jit(solution)/shard_map/slice | solution.py:20
  0.8 2.3 %collective-permute-start = (bf16[4,2,128]{2,1,0:T(2,128)(2,1)S(1)}, bf16[4,2,128]{2,1,0:T(2,128)(2,1)S(1)}, u32[]{:S(2)}, u32[]{:S(2)}) collective-permute-start(bf16[4,2,128]{2,1,0:T(2,128)(2,1)S(1)} %get-tuple-element.63), channel_id=1, source_target_pairs={{0,1},{1,2},{2,3},{4,5},{5,6},{6,7},{8,9},{9,10},{10,11},{12,13},{... | collective-permute-start | bytes 6152 | tf_op jit(solution)/shard_map/ppermute | solution.py:19
  3.1 1.3 %collective-permute-start.1 = (bf16[4,2,128]{2,1,0:T(2,128)(2,1)S(1)}, bf16[4,2,128]{2,1,0:T(2,128)(2,1)S(1)}, u32[]{:S(2)}, u32[]{:S(2)}) collective-permute-start(bf16[4,2,128]{2,1,0:T(2,128)(2,1)S(1)} %get-tuple-element.64), channel_id=1, source_target_pairs={{1,0},{2,1},{3,2},{5,4},{6,5},{7,6},{9,8},{10,9},{11,10},{13,12},{... | collective-permute-start | bytes 6152 | tf_op jit(solution)/shard_map/ppermute | solution.py:22
  4.5 0.0 collective-permute-done
  4.5 3.8 %collective-permute-done.1 = bf16[4,2,128]{2,1,0:T(2,128)(2,1)S(1)} collective-permute-done((bf16[4,2,128]{2,1,0:T(2,128)(2,1)S(1)}, bf16[4,2,128]{2,1,0:T(2,128)(2,1)S(1)}, u32[]{:S(2)}, u32[]{:S(2)}) %collective-permute-start.1) | collective-permute-done | bytes 2080 | tf_op jit(solution)/shard_map/ppermute | solution.py:22
  8.3 2.3 %collective-permute-start.4 = (bf16[2048,128]{1,0:T(8,128)(2,1)}, bf16[2048,128]{1,0:T(8,128)(2,1)S(1)}, u32[]{:S(2)}, u32[]{:S(2)}) collective-permute-start(bf16[2048,128]{1,0:T(8,128)(2,1)} %refs_1_), channel_id=1, source_target_pairs={{0,2},{1,3},{2,0},{3,1},{4,6},{5,7},{6,4},{7,5},{8,10},{9,11},{10,... | collective-permute-start | bytes 1572872 | tf_op jit(solution)/shard_map/ppermute | solution.py:179
  10.7 3.4 %collective-permute-start.2 = (bf16[2,68,128]{2,1,0:T(8,128)(2,1)S(1)}, bf16[2,68,128]{2,1,0:T(8,128)(2,1)S(1)}, u32[]{:S(2)}, u32[]{:S(2)}) collective-permute-start(bf16[2,68,128]{2,1,0:T(8,128)(2,1)S(1)} %get-tuple-element.61), channel_id=1, source_target_pairs={{0,4},{4,8},{8,12},{12,16},{16,20},{20,24},{24,28},{1,5},{5,9},{9,... | collective-permute-start | bytes 104456 | tf_op jit(solution)/shard_map/ppermute | solution.py:19
  14.1 1.3 %collective-permute-start.3 = (bf16[2,68,128]{2,1,0:T(8,128)(2,1)S(1)}, bf16[2,68,128]{2,1,0:T(8,128)(2,1)S(1)}, u32[]{:S(2)}, u32[]{:S(2)}) collective-permute-start(bf16[2,68,128]{2,1,0:T(8,128)(2,1)S(1)} %get-tuple-element.62), channel_id=1, source_target_pairs={{4,0},{8,4},{12,8},{16,12},{20,16},{24,20},{28,24},{5,1},{9,5},{13... | collective-permute-start | bytes 104456 | tf_op jit(solution)/shard_map/ppermute | solution.py:22
  15.4 0.1 fusion.18
  15.5 0.0 collective-permute-start.6
  15.6 0.2 collective-permute-done.2
  15.7 4.2 %collective-permute-done.3 = bf16[2,68,128]{2,1,0:T(8,128)(2,1)S(1)} collective-permute-done((bf16[2,68,128]{2,1,0:T(8,128)(2,1)S(1)}, bf16[2,68,128]{2,1,0:T(8,128)(2,1)S(1)}, u32[]{:S(2)}, u32[]{:S(2)}) %collective-permute-start.3) | collective-permute-done | bytes 34848 | tf_op jit(solution)/shard_map/ppermute | solution.py:22
  20.0 0.7 %reshape.82.refs_0_ = bf16[544,128]{1,0:T(8,128)(2,1)} reshape(bf16[8,68,128]{2,1,0:T(8,128)(2,1)S(1)} %pad_maximum_fusion) | data formatting | bytes 278528 | tf_op jit(solution)/shard_map/reshape | solution.py:234
  20.7 0.6 %broadcast_in_dim.22.refs_2_.refs_3_ = f32[8,128]{1,0:T(8,128)} broadcast(f32[128]{0:T(128)S(1)} %pad.4), dimensions={1} | broadcast | bytes 4608 | tf_op jit(solution)/shard_map/broadcast_in_dim | solution.py:191
  21.3 4.7 %shard_map.64 = (f32[544,128]{1,0:T(8,128)}, f32[544,128]{1,0:T(8,128)}, f32[544,8]{1,0:T(8,128)}) custom-call(bf16[544,128]{1,0:T(8,128)(2,1)} %reshape.82.refs_0_, bf16[2048,128]{1,0:T(8,128)(2,1)} %refs_1_, f32[8,128]{1,0:T(8,128)} %broadcast_in_dim.22.refs_2_.refs_3_), custom_call_target="tpu_custom_call" | custom-call | tf_op jit(solution)/shard_map/pallas_call | solution.py:151
  26.0 0.0 collective-permute-done.4.refs_2_
  26.0 0.0 collective-permute-start.5
  26.0 0.1 broadcast_and_fusion
  26.1 0.1 slice.128
  26.2 0.1 copy.24
  26.4 0.7 %copy-done.6 = bf16[2,3,3,128]{3,0,2,1:T(2,128)(2,1)S(1)} copy-done((bf16[2,3,3,128]{3,0,2,1:T(2,128)(2,1)S(1)}, bf16[2,3,3,128]{3,0,2,1:T(2,128)(2,1)}, u32[]{:S(2)}) %copy-start.6) | copy-done | bytes 4632
  27.0 0.7 %copy-done.7 = f32[2,128]{1,0:T(2,128)S(1)} copy-done((f32[2,128]{1,0:T(2,128)S(1)}, f32[2,128]{1,0:T(2,128)}, u32[]{:S(2)}) %copy-start.7) | copy-done | bytes 1048
  27.7 0.0 collective-permute-done.6.refs_1_
  27.7 0.8 %copy-done.3 = bf16[2048,128]{1,0:T(8,128)(2,1)} copy-done((bf16[2048,128]{1,0:T(8,128)(2,1)}, bf16[2048,128]{1,0:T(8,128)(2,1)S(1)}, u32[]{:S(2)}) %copy-start.3) | copy-done | bytes 524312
  28.5 6.2 %shard_map.65 = (f32[544,128]{1,0:T(8,128)}, f32[544,128]{1,0:T(8,128)}, f32[544,8]{1,0:T(8,128)}) custom-call(bf16[544,128]{1,0:T(8,128)(2,1)} %reshape.82.refs_0_, bf16[2048,128]{1,0:T(8,128)(2,1)} %copy-done.3, bf16[2048,128]{1,0:T(8,128)(2,1)} %copy-done.2, f32[8,128]{1,0:T(8,128)} %broadcast_in_dim.22.refs_2_.refs_3_, ...), custom_call_target="tpu_custom_call" | custom-call | tf_op jit(solution)/shard_map/pallas_call | solution.py:151
  34.7 0.8 %copy-done.1 = bf16[2048,128]{1,0:T(8,128)(2,1)} copy-done((bf16[2048,128]{1,0:T(8,128)(2,1)}, bf16[2048,128]{1,0:T(8,128)(2,1)S(1)}, u32[]{:S(2)}) %copy-start.1) | copy-done | bytes 524312
  35.5 5.4 %shard_map.66 = (f32[544,128]{1,0:T(8,128)}, f32[544,128]{1,0:T(8,128)}) custom-call(bf16[544,128]{1,0:T(8,128)(2,1)} %reshape.82.refs_0_, bf16[2048,128]{1,0:T(8,128)(2,1)} %copy-done.1, f32[8,128]{1,0:T(8,128)} %broadcast_in_dim.22.refs_2_.refs_3_, f32[544,128]{1,0:T(8,128)} %get-tuple-element.32.refs_3_, f32[544,128]{1,0:T(8,128)} %get-tuple-element.33.refs_4_, ...), custom_call_target="tpu_custom_call" | custom-call | tf_op jit(solution)/shard_map/pallas_call | solution.py:151
  40.9 1.4 %slice_reduce_fusion.1 = (f32[544]{0:T(1024)S(1)}, f32[544]{0:T(1024)S(1)}) fusion(f32[544,128]{1,0:T(8,128)} %get-tuple-element.35), kind=kLoop, calls=%fused_computation.8 | loop fusion | bytes 8704 | tf_op jit(solution)/shard_map/slice | solution.py:219
  42.3 0.1 reshape_squeeze.6
  42.4 0.1 slice.129
  42.5 0.1 reshape_squeeze.7
  42.6 0.1 broadcast_subtract_fusion
  42.6 0.1 slice.131
  42.7 0.1 slice_bitcast_fusion.1
  42.8 0.1 select_bitcast_fusion
  43.0 0.1 copy.67
  43.1 0.1 copy.27
  43.1 0.0 copy-start.9
  43.2 0.6 %copy-done.9 = pred[8,9]{0,1:T(8,128)(4,1)S(1)} copy-done((pred[8,9]{0,1:T(8,128)(4,1)S(1)}, pred[8,9]{0,1:T(8,128)(4,1)}, u32[]{:S(2)}) %copy-start.9) | copy-done | bytes 96
  43.8 0.9 %convolution_select_fusion = f32[6,8,9,128]{3,1,2,0:T(8,128)S(1)} fusion(bf16[3,3,128,128]{3,2,1,0:T(8,128)(2,1)S(1)} %copy-done, f32[8,1,7,2,128]{4,2,3,0,1:T(8,128)S(1)} %slice.153, f32[8,1,8,9,128]{4,2,3,0,1:T(8,128)S(1)} %copy.27, pred[8,9]{0,1:T(8,128)(4,1)S(1)} %copy-done.9), kind=kOutput, calls=%fused_computation | convolution fusion | flops 764737536 | bytes 868424 | tf_op jit(solution)/shard_map/conv_general_dilated | solution.py:245
  44.8 0.1 copy.28
  44.8 0.1 copy.29
  44.9 0.1 copy.30
  45.1 0.7 %copy-done.8 = f32[128]{0:T(128)S(1)} copy-done((f32[128]{0:T(128)S(1)}, f32[128]{0:T(128)}, u32[]{:S(2)}) %copy-start.8) | copy-done | bytes 536
  45.7 0.3 select_bitcast_fusion.1
  46.0 0.2 fusion.9
  46.2 0.1 fusion.22
  46.3 0.6 %maximum_add_fusion = f32[2,4,64]{2,1,0:T(4,128)} fusion(f32[1,4,64]{2,1,0:T(4,128)S(1)} %get-tuple-element.67, f32[1,4,64]{2,1,0:T(4,128)S(1)} %get-tuple-element.68, f32[1,4,64]{2,1,0:T(4,128)S(1)} %bitcast.107, f32[1,4,64]{2,1,0:T(4,128)S(1)} %bitcast.108, f32[1,4,64]{2,1,0:T(4,128)S(1)} %bitcast.105, f32[1,4,64]{2,1,0:T(4,128)S(1)} %bitcast.106, ...), kind=kLoop, calls=%fused_computation.21 | loop fusion | flops 9728 | bytes 22528 | tf_op jit(solution)/shard_map/add | solution.py:265
  (29 shorter events, 0.2 us)
Async XLA Ops:
  0.0 43.2 %copy-start = (bf16[3,3,128,128]{3,2,1,0:T(8,128)(2,1)S(1)}, bf16[3,3,128,128]{3,2,1,0:T(8,128)(2,1)}, u32[]{:S(2)}) copy-start(bf16[3,3,128,128]{3,2,1,0:T(8,128)(2,1)} %param.8) | copy-start | bytes 884740
  0.0 8.3 %copy-start.5 = (bf16[4,64,128]{2,1,0:T(8,128)(2,1)S(1)}, bf16[4,64,128]{2,1,0:T(8,128)(2,1)}, u32[]{:S(2)}) copy-start(bf16[4,64,128]{2,1,0:T(8,128)(2,1)} %param.6) | copy-start | bytes 196612
  0.8 3.7 %collective-permute-start = (bf16[4,2,128]{2,1,0:T(2,128)(2,1)S(1)}, bf16[4,2,128]{2,1,0:T(2,128)(2,1)S(1)}, u32[]{:S(2)}, u32[]{:S(2)}) collective-permute-start(bf16[4,2,128]{2,1,0:T(2,128)(2,1)S(1)} %get-tuple-element.63), channel_id=1, source_target_pairs={{0,1},{1,2},{2,3},{4,5},{5,6},{6,7},{8,9},{9,10},{10,11},{12,13},{... | collective-permute-start | bytes 6152 | tf_op jit(solution)/shard_map/ppermute | solution.py:19
  3.1 5.2 %collective-permute-start.1 = (bf16[4,2,128]{2,1,0:T(2,128)(2,1)S(1)}, bf16[4,2,128]{2,1,0:T(2,128)(2,1)S(1)}, u32[]{:S(2)}, u32[]{:S(2)}) collective-permute-start(bf16[4,2,128]{2,1,0:T(2,128)(2,1)S(1)} %get-tuple-element.64), channel_id=1, source_target_pairs={{1,0},{2,1},{3,2},{5,4},{6,5},{7,6},{9,8},{10,9},{11,10},{13,12},{... | collective-permute-start | bytes 6152 | tf_op jit(solution)/shard_map/ppermute | solution.py:22
  8.3 17.7 %collective-permute-start.4 = (bf16[2048,128]{1,0:T(8,128)(2,1)}, bf16[2048,128]{1,0:T(8,128)(2,1)S(1)}, u32[]{:S(2)}, u32[]{:S(2)}) collective-permute-start(bf16[2048,128]{1,0:T(8,128)(2,1)} %refs_1_), channel_id=1, source_target_pairs={{0,2},{1,3},{2,0},{3,1},{4,6},{5,7},{6,4},{7,5},{8,10},{9,11},{10,... | collective-permute-start | bytes 1572872 | tf_op jit(solution)/shard_map/ppermute | solution.py:179
  10.7 5.0 %collective-permute-start.2 = (bf16[2,68,128]{2,1,0:T(8,128)(2,1)S(1)}, bf16[2,68,128]{2,1,0:T(8,128)(2,1)S(1)}, u32[]{:S(2)}, u32[]{:S(2)}) collective-permute-start(bf16[2,68,128]{2,1,0:T(8,128)(2,1)S(1)} %get-tuple-element.61), channel_id=1, source_target_pairs={{0,4},{4,8},{8,12},{12,16},{16,20},{20,24},{24,28},{1,5},{5,9},{9,... | collective-permute-start | bytes 104456 | tf_op jit(solution)/shard_map/ppermute | solution.py:19
  14.1 5.9 %collective-permute-start.3 = (bf16[2,68,128]{2,1,0:T(8,128)(2,1)S(1)}, bf16[2,68,128]{2,1,0:T(8,128)(2,1)S(1)}, u32[]{:S(2)}, u32[]{:S(2)}) collective-permute-start(bf16[2,68,128]{2,1,0:T(8,128)(2,1)S(1)} %get-tuple-element.62), channel_id=1, source_target_pairs={{4,0},{8,4},{12,8},{16,12},{20,16},{24,20},{28,24},{5,1},{9,5},{13... | collective-permute-start | bytes 104456 | tf_op jit(solution)/shard_map/ppermute | solution.py:22
  15.5 12.2 %collective-permute-start.6 = (bf16[2048,128]{1,0:T(8,128)(2,1)}, bf16[2048,128]{1,0:T(8,128)(2,1)S(1)}, u32[]{:S(2)}, u32[]{:S(2)}) collective-permute-start(bf16[2048,128]{1,0:T(8,128)(2,1)} %refs_1_), channel_id=1, source_target_pairs={{0,1},{1,0},{2,3},{3,2},{4,5},{5,4},{6,7},{7,6},{8,9},{9,8},{10,11... | collective-permute-start | bytes 1572872 | tf_op jit(solution)/shard_map/ppermute | solution.py:176
  26.0 1.7 %copy-start.2 = (bf16[2048,128]{1,0:T(8,128)(2,1)}, bf16[2048,128]{1,0:T(8,128)(2,1)S(1)}, u32[]{:S(2)}) copy-start(bf16[2048,128]{1,0:T(8,128)(2,1)S(1)} %collective-permute-done.4.refs_2_) | copy-start | bytes 1572868
  26.0 8.6 %collective-permute-start.5 = (bf16[2048,128]{1,0:T(8,128)(2,1)S(1)}, bf16[2048,128]{1,0:T(8,128)(2,1)S(1)}, u32[]{:S(2)}, u32[]{:S(2)}) collective-permute-start(bf16[2048,128]{1,0:T(8,128)(2,1)S(1)} %collective-permute-done.4.refs_2_), channel_id=1, source_target_pairs={{0,1},{1,0},{2,3},{3,2},{4,5},{5,4},{6,7},{7,6},{8,9},{9,8},{10,11... | collective-permute-start | bytes 1572872 | tf_op jit(solution)/shard_map/ppermute | solution.py:206
  26.3 0.7 %copy-start.6 = (bf16[2,3,3,128]{3,0,2,1:T(2,128)(2,1)S(1)}, bf16[2,3,3,128]{3,0,2,1:T(2,128)(2,1)}, u32[]{:S(2)}) copy-start(bf16[2,3,3,128]{3,0,2,1:T(2,128)(2,1)} %param.11) | copy-start | bytes 13828
  27.0 0.7 %copy-start.7 = (f32[2,128]{1,0:T(2,128)S(1)}, f32[2,128]{1,0:T(2,128)}, u32[]{:S(2)}) copy-start(f32[2,128]{1,0:T(2,128)} %param.9) | copy-start | bytes 3076
  27.7 0.8 %copy-start.3 = (bf16[2048,128]{1,0:T(8,128)(2,1)}, bf16[2048,128]{1,0:T(8,128)(2,1)S(1)}, u32[]{:S(2)}) copy-start(bf16[2048,128]{1,0:T(8,128)(2,1)S(1)} %collective-permute-done.6.refs_1_) | copy-start | bytes 1572868
  34.7 0.8 %copy-start.1 = (bf16[2048,128]{1,0:T(8,128)(2,1)}, bf16[2048,128]{1,0:T(8,128)(2,1)S(1)}, u32[]{:S(2)}) copy-start(bf16[2048,128]{1,0:T(8,128)(2,1)S(1)} %collective-permute-done.5.refs_1_) | copy-start | bytes 1572868
  40.9 1.9 %copy-start.4 = (f32[544,128]{1,0:T(8,128)S(1)}, f32[544,128]{1,0:T(8,128)}, u32[]{:S(2)}) copy-start(f32[544,128]{1,0:T(8,128)} %get-tuple-element.36) | copy-start | bytes 835588
  43.1 0.7 %copy-start.9 = (pred[8,9]{0,1:T(8,128)(4,1)S(1)}, pred[8,9]{0,1:T(8,128)(4,1)}, u32[]{:S(2)}) copy-start(pred[8,9]{0,1:T(8,128)(4,1)} %constant.75) | copy-start | bytes 220
  45.1 0.7 %copy-start.8 = (f32[128]{0:T(128)S(1)}, f32[128]{0:T(128)}, u32[]{:S(2)}) copy-start(f32[128]{0:T(128)} %param.10) | copy-start | bytes 1540

commit v15 on v14

--- a/solution.py
+++ b/solution.py
@@ -133,18 +133,18 @@
     in_specs += [pl.BlockSpec(pos.shape, lambda i: (0, 0))]
     args = [queries, *keys, pos]
     if not first:
-        in_specs += [row_spec(128), row_spec(chans), row_spec(8)]
+        in_specs += [row_spec(8), row_spec(chans), row_spec(8)]
         args += list(state)
     if last:
-        out_specs = [row_spec(chans), row_spec(128)]
+        out_specs = [row_spec(chans), row_spec(8)]
         out_shape = [
             jax.ShapeDtypeStruct((padded, chans), jnp.float32),
-            jax.ShapeDtypeStruct((padded, 128), jnp.float32),
+            jax.ShapeDtypeStruct((padded, 8), jnp.float32),
         ]
     else:
-        out_specs = [row_spec(128), row_spec(chans), row_spec(8)]
+        out_specs = [row_spec(8), row_spec(chans), row_spec(8)]
         out_shape = [
-            jax.ShapeDtypeStruct((padded, 128), jnp.float32),
+            jax.ShapeDtypeStruct((padded, 8), jnp.float32),
             jax.ShapeDtypeStruct((padded, chans), jnp.float32),
             jax.ShapeDtypeStruct((padded, 8), jnp.float32),
         ]

time: 47.5 us -> 47.5 us (level)
  no operation moved by 1% of the time
where the time goes in v15:
time: 47.5 us; the launch traced here: 47 us
  Pallas kernels  16.4 us (35%)
  starting transfers between devices  10.7 us (23%)
  local copies, waits for them, and re-layouts  8.91 us (19%)
  waiting for transfers between devices  8.22 us (17%)
  other arithmetic  1.34 us (3%)
  matrix products  1.13 us (2%)
    pallas_call x3, Pallas kernels, match_step(): pl.pallas_call(kernel, grid=(nq,), in_specs=in_specs, out_specs=out_specs...  16.4 us
    ppermute x2, waiting for transfers between devices, extended(): lax.ppermute(lax.slice_in_dim(block, 0, width, axis=dim), axis, backward)  8.02 us
    ppermute x2, starting transfers between devices, extended(): lax.ppermute(lax.slice_in_dim(block, block.shape[dim] - width, None, axis...  5.77 us
    unnamed x21, local copies, waits for them, and re-layouts  4.28 us
    ppermute x2, starting transfers between devices, extended(): lax.ppermute(lax.slice_in_dim(block, 0, width, axis=dim), axis, backward)  2.58 us
    ppermute x1, starting transfers between devices, match(): moved = lax.ppermute(targets, 'match', hop)  2.35 us
    slice x1, local copies, waits for them, and re-layouts, match(): return (warped[:count], flow[:count, 0], flow[:count, 1])  1.42 us
  transfers between devices with their start and end apart: 7, of which 3 were waited for; matrix products, arithmetic and copies ran while one was open for 4% of the time, Pallas kernels for 23%

profile of v15, /device:TPU:0, one launch (start us, length us, event | category | flops | bytes accessed | tf_op | source)
XLA Modules:
  0.0 47.0 jit_solution(3688446929300378317)
XLA Ops:
  0.0 0.8 %fusion.24 = (bf16[4,2,128]{2,1,0:T(2,128)(2,1)S(1)}, bf16[4,2,128]{2,1,0:T(2,128)(2,1)S(1)}) fusion(bf16[4,64,128]{2,1,0:T(8,128)(2,1)} %param.6), kind=kLoop, calls=%fused_computation.50 | loop fusion | bytes 8192 | tf_op jit(solution)/shard_map/slice | solution.py:20
  0.8 2.3 %collective-permute-start = (bf16[4,2,128]{2,1,0:T(2,128)(2,1)S(1)}, bf16[4,2,128]{2,1,0:T(2,128)(2,1)S(1)}, u32[]{:S(2)}, u32[]{:S(2)}) collective-permute-start(bf16[4,2,128]{2,1,0:T(2,128)(2,1)S(1)} %get-tuple-element.63), channel_id=1, source_target_pairs={{0,1},{1,2},{2,3},{4,5},{5,6},{6,7},{8,9},{9,10},{10,11},{12,13},{... | collective-permute-start | bytes 6152 | tf_op jit(solution)/shard_map/ppermute | solution.py:19
  3.1 1.3 %collective-permute-start.1 = (bf16[4,2,128]{2,1,0:T(2,128)(2,1)S(1)}, bf16[4,2,128]{2,1,0:T(2,128)(2,1)S(1)}, u32[]{:S(2)}, u32[]{:S(2)}) collective-permute-start(bf16[4,2,128]{2,1,0:T(2,128)(2,1)S(1)} %get-tuple-element.64), channel_id=1, source_target_pairs={{1,0},{2,1},{3,2},{5,4},{6,5},{7,6},{9,8},{10,9},{11,10},{13,12},{... | collective-permute-start | bytes 6152 | tf_op jit(solution)/shard_map/ppermute | solution.py:22
  4.5 0.0 collective-permute-done
  4.5 3.8 %collective-permute-done.1 = bf16[4,2,128]{2,1,0:T(2,128)(2,1)S(1)} collective-permute-done((bf16[4,2,128]{2,1,0:T(2,128)(2,1)S(1)}, bf16[4,2,128]{2,1,0:T(2,128)(2,1)S(1)}, u32[]{:S(2)}, u32[]{:S(2)}) %collective-permute-start.1) | collective-permute-done | bytes 2080 | tf_op jit(solution)/shard_map/ppermute | solution.py:22
  8.3 2.3 %collective-permute-start.4 = (bf16[2048,128]{1,0:T(8,128)(2,1)}, bf16[2048,128]{1,0:T(8,128)(2,1)S(1)}, u32[]{:S(2)}, u32[]{:S(2)}) collective-permute-start(bf16[2048,128]{1,0:T(8,128)(2,1)} %refs_1_), channel_id=1, source_target_pairs={{0,2},{1,3},{2,0},{3,1},{4,6},{5,7},{6,4},{7,5},{8,10},{9,11},{10,... | collective-permute-start | bytes 1572872 | tf_op jit(solution)/shard_map/ppermute | solution.py:179
  10.7 3.4 %collective-permute-start.2 = (bf16[2,68,128]{2,1,0:T(8,128)(2,1)S(1)}, bf16[2,68,128]{2,1,0:T(8,128)(2,1)S(1)}, u32[]{:S(2)}, u32[]{:S(2)}) collective-permute-start(bf16[2,68,128]{2,1,0:T(8,128)(2,1)S(1)} %get-tuple-element.61), channel_id=1, source_target_pairs={{0,4},{4,8},{8,12},{12,16},{16,20},{20,24},{24,28},{1,5},{5,9},{9,... | collective-permute-start | bytes 104456 | tf_op jit(solution)/shard_map/ppermute | solution.py:19
  14.1 1.3 %collective-permute-start.3 = (bf16[2,68,128]{2,1,0:T(8,128)(2,1)S(1)}, bf16[2,68,128]{2,1,0:T(8,128)(2,1)S(1)}, u32[]{:S(2)}, u32[]{:S(2)}) collective-permute-start(bf16[2,68,128]{2,1,0:T(8,128)(2,1)S(1)} %get-tuple-element.62), channel_id=1, source_target_pairs={{4,0},{8,4},{12,8},{16,12},{20,16},{24,20},{28,24},{5,1},{9,5},{13... | collective-permute-start | bytes 104456 | tf_op jit(solution)/shard_map/ppermute | solution.py:22
  15.4 0.1 fusion.18
  15.5 0.0 collective-permute-start.6
  15.6 0.2 collective-permute-done.2
  15.7 4.2 %collective-permute-done.3 = bf16[2,68,128]{2,1,0:T(8,128)(2,1)S(1)} collective-permute-done((bf16[2,68,128]{2,1,0:T(8,128)(2,1)S(1)}, bf16[2,68,128]{2,1,0:T(8,128)(2,1)S(1)}, u32[]{:S(2)}, u32[]{:S(2)}) %collective-permute-start.3) | collective-permute-done | bytes 34848 | tf_op jit(solution)/shard_map/ppermute | solution.py:22
  20.0 0.7 %reshape.82.refs_0_ = bf16[544,128]{1,0:T(8,128)(2,1)} reshape(bf16[8,68,128]{2,1,0:T(8,128)(2,1)S(1)} %pad_maximum_fusion) | data formatting | bytes 278528 | tf_op jit(solution)/shard_map/reshape | solution.py:234
  20.7 0.6 %broadcast_in_dim.22.refs_2_.refs_3_ = f32[8,128]{1,0:T(8,128)} broadcast(f32[128]{0:T(128)S(1)} %pad.4), dimensions={1} | broadcast | bytes 4608 | tf_op jit(solution)/shard_map/broadcast_in_dim | solution.py:191
  21.3 4.8 %shard_map.64 = (f32[544,8]{1,0:T(8,128)}, f32[544,128]{1,0:T(8,128)}, f32[544,8]{1,0:T(8,128)}) custom-call(bf16[544,128]{1,0:T(8,128)(2,1)} %reshape.82.refs_0_, bf16[2048,128]{1,0:T(8,128)(2,1)} %refs_1_, f32[8,128]{1,0:T(8,128)} %broadcast_in_dim.22.refs_2_.refs_3_), custom_call_target="tpu_custom_call" | custom-call | tf_op jit(solution)/shard_map/pallas_call | solution.py:151
  26.0 0.0 collective-permute-done.4.refs_2_
  26.0 0.0 collective-permute-start.5
  26.0 0.1 broadcast_and_fusion
  26.1 0.1 slice.128
  26.2 0.1 copy.24
  26.4 0.7 %copy-done.6 = bf16[2,3,3,128]{3,0,2,1:T(2,128)(2,1)S(1)} copy-done((bf16[2,3,3,128]{3,0,2,1:T(2,128)(2,1)S(1)}, bf16[2,3,3,128]{3,0,2,1:T(2,128)(2,1)}, u32[]{:S(2)}) %copy-start.6) | copy-done | bytes 4632
  27.1 0.7 %copy-done.7 = f32[2,128]{1,0:T(2,128)S(1)} copy-done((f32[2,128]{1,0:T(2,128)S(1)}, f32[2,128]{1,0:T(2,128)}, u32[]{:S(2)}) %copy-start.7) | copy-done | bytes 1048
  27.7 0.0 collective-permute-done.6.refs_1_
  27.7 0.8 %copy-done.3 = bf16[2048,128]{1,0:T(8,128)(2,1)} copy-done((bf16[2048,128]{1,0:T(8,128)(2,1)}, bf16[2048,128]{1,0:T(8,128)(2,1)S(1)}, u32[]{:S(2)}) %copy-start.3) | copy-done | bytes 524312
  28.5 6.2 %shard_map.65 = (f32[544,8]{1,0:T(8,128)}, f32[544,128]{1,0:T(8,128)}, f32[544,8]{1,0:T(8,128)}) custom-call(bf16[544,128]{1,0:T(8,128)(2,1)} %reshape.82.refs_0_, bf16[2048,128]{1,0:T(8,128)(2,1)} %copy-done.3, bf16[2048,128]{1,0:T(8,128)(2,1)} %copy-done.2, f32[8,128]{1,0:T(8,128)} %broadcast_in_dim.22.refs_2_.refs_3_, ...), custom_call_target="tpu_custom_call" | custom-call | tf_op jit(solution)/shard_map/pallas_call | solution.py:151
  34.7 0.8 %copy-done.1 = bf16[2048,128]{1,0:T(8,128)(2,1)} copy-done((bf16[2048,128]{1,0:T(8,128)(2,1)}, bf16[2048,128]{1,0:T(8,128)(2,1)S(1)}, u32[]{:S(2)}) %copy-start.1) | copy-done | bytes 524312
  35.5 5.4 %shard_map.66 = (f32[544,128]{1,0:T(8,128)}, f32[544,8]{1,0:T(8,128)}) custom-call(bf16[544,128]{1,0:T(8,128)(2,1)} %reshape.82.refs_0_, bf16[2048,128]{1,0:T(8,128)(2,1)} %copy-done.1, f32[8,128]{1,0:T(8,128)} %broadcast_in_dim.22.refs_2_.refs_3_, f32[544,8]{1,0:T(8,128)} %get-tuple-element.32.refs_3_, f32[544,128]{1,0:T(8,128)} %get-tuple-element.33.refs_4_, ...), custom_call_target="tpu_custom_call" | custom-call | tf_op jit(solution)/shard_map/pallas_call | solution.py:151
  41.0 1.4 %slice_reduce_fusion.1 = (f32[544]{0:T(1024)S(1)}, f32[544]{0:T(1024)S(1)}) fusion(f32[544,8]{1,0:T(8,128)} %get-tuple-element.35), kind=kLoop, calls=%fused_computation.8 | loop fusion | bytes 8704 | tf_op jit(solution)/shard_map/slice | solution.py:219
  42.4 0.1 reshape_squeeze.6
  42.5 0.1 slice.129
  42.5 0.1 reshape_squeeze.7
  42.6 0.1 broadcast_subtract_fusion
  42.7 0.1 slice.131
  42.8 0.1 slice_bitcast_fusion.1
  42.9 0.1 select_bitcast_fusion
  43.0 0.1 copy.67
  43.1 0.1 copy.27
  43.2 0.0 copy-start.9
  43.2 0.6 %copy-done.9 = pred[8,9]{0,1:T(8,128)(4,1)S(1)} copy-done((pred[8,9]{0,1:T(8,128)(4,1)S(1)}, pred[8,9]{0,1:T(8,128)(4,1)}, u32[]{:S(2)}) %copy-start.9) | copy-done | bytes 96
  43.9 0.9 %convolution_select_fusion = f32[6,8,9,128]{3,1,2,0:T(8,128)S(1)} fusion(bf16[3,3,128,128]{3,2,1,0:T(8,128)(2,1)S(1)} %copy-done, f32[8,1,7,2,128]{4,2,3,0,1:T(8,128)S(1)} %slice.153, f32[8,1,8,9,128]{4,2,3,0,1:T(8,128)S(1)} %copy.27, pred[8,9]{0,1:T(8,128)(4,1)S(1)} %copy-done.9), kind=kOutput, calls=%fused_computation | convolution fusion | flops 764737536 | bytes 868424 | tf_op jit(solution)/shard_map/conv_general_dilated | solution.py:245
  44.8 0.1 copy.28
  44.9 0.1 copy.29
  45.0 0.1 copy.30
  45.1 0.7 %copy-done.8 = f32[128]{0:T(128)S(1)} copy-done((f32[128]{0:T(128)S(1)}, f32[128]{0:T(128)}, u32[]{:S(2)}) %copy-start.8) | copy-done | bytes 536
  45.7 0.3 select_bitcast_fusion.1
  46.0 0.2 fusion.9
  46.2 0.1 fusion.22
  46.4 0.6 %maximum_add_fusion = f32[2,4,64]{2,1,0:T(4,128)} fusion(f32[1,4,64]{2,1,0:T(4,128)S(1)} %get-tuple-element.67, f32[1,4,64]{2,1,0:T(4,128)S(1)} %get-tuple-element.68, f32[1,4,64]{2,1,0:T(4,128)S(1)} %bitcast.107, f32[1,4,64]{2,1,0:T(4,128)S(1)} %bitcast.108, f32[1,4,64]{2,1,0:T(4,128)S(1)} %bitcast.105, f32[1,4,64]{2,1,0:T(4,128)S(1)} %bitcast.106, ...), kind=kLoop, calls=%fused_computation.21 | loop fusion | flops 9728 | bytes 22528 | tf_op jit(solution)/shard_map/add | solution.py:265
  (29 shorter events, 0.2 us)
Async XLA Ops:
  0.0 43.2 %copy-start = (bf16[3,3,128,128]{3,2,1,0:T(8,128)(2,1)S(1)}, bf16[3,3,128,128]{3,2,1,0:T(8,128)(2,1)}, u32[]{:S(2)}) copy-start(bf16[3,3,128,128]{3,2,1,0:T(8,128)(2,1)} %param.8) | copy-start | bytes 884740
  0.0 8.3 %copy-start.5 = (bf16[4,64,128]{2,1,0:T(8,128)(2,1)S(1)}, bf16[4,64,128]{2,1,0:T(8,128)(2,1)}, u32[]{:S(2)}) copy-start(bf16[4,64,128]{2,1,0:T(8,128)(2,1)} %param.6) | copy-start | bytes 196612
  0.8 3.7 %collective-permute-start = (bf16[4,2,128]{2,1,0:T(2,128)(2,1)S(1)}, bf16[4,2,128]{2,1,0:T(2,128)(2,1)S(1)}, u32[]{:S(2)}, u32[]{:S(2)}) collective-permute-start(bf16[4,2,128]{2,1,0:T(2,128)(2,1)S(1)} %get-tuple-element.63), channel_id=1, source_target_pairs={{0,1},{1,2},{2,3},{4,5},{5,6},{6,7},{8,9},{9,10},{10,11},{12,13},{... | collective-permute-start | bytes 6152 | tf_op jit(solution)/shard_map/ppermute | solution.py:19
  3.1 5.2 %collective-permute-start.1 = (bf16[4,2,128]{2,1,0:T(2,128)(2,1)S(1)}, bf16[4,2,128]{2,1,0:T(2,128)(2,1)S(1)}, u32[]{:S(2)}, u32[]{:S(2)}) collective-permute-start(bf16[4,2,128]{2,1,0:T(2,128)(2,1)S(1)} %get-tuple-element.64), channel_id=1, source_target_pairs={{1,0},{2,1},{3,2},{5,4},{6,5},{7,6},{9,8},{10,9},{11,10},{13,12},{... | collective-permute-start | bytes 6152 | tf_op jit(solution)/shard_map/ppermute | solution.py:22
  8.3 17.7 %collective-permute-start.4 = (bf16[2048,128]{1,0:T(8,128)(2,1)}, bf16[2048,128]{1,0:T(8,128)(2,1)S(1)}, u32[]{:S(2)}, u32[]{:S(2)}) collective-permute-start(bf16[2048,128]{1,0:T(8,128)(2,1)} %refs_1_), channel_id=1, source_target_pairs={{0,2},{1,3},{2,0},{3,1},{4,6},{5,7},{6,4},{7,5},{8,10},{9,11},{10,... | collective-permute-start | bytes 1572872 | tf_op jit(solution)/shard_map/ppermute | solution.py:179
  10.7 5.0 %collective-permute-start.2 = (bf16[2,68,128]{2,1,0:T(8,128)(2,1)S(1)}, bf16[2,68,128]{2,1,0:T(8,128)(2,1)S(1)}, u32[]{:S(2)}, u32[]{:S(2)}) collective-permute-start(bf16[2,68,128]{2,1,0:T(8,128)(2,1)S(1)} %get-tuple-element.61), channel_id=1, source_target_pairs={{0,4},{4,8},{8,12},{12,16},{16,20},{20,24},{24,28},{1,5},{5,9},{9,... | collective-permute-start | bytes 104456 | tf_op jit(solution)/shard_map/ppermute | solution.py:19
  14.1 5.9 %collective-permute-start.3 = (bf16[2,68,128]{2,1,0:T(8,128)(2,1)S(1)}, bf16[2,68,128]{2,1,0:T(8,128)(2,1)S(1)}, u32[]{:S(2)}, u32[]{:S(2)}) collective-permute-start(bf16[2,68,128]{2,1,0:T(8,128)(2,1)S(1)} %get-tuple-element.62), channel_id=1, source_target_pairs={{4,0},{8,4},{12,8},{16,12},{20,16},{24,20},{28,24},{5,1},{9,5},{13... | collective-permute-start | bytes 104456 | tf_op jit(solution)/shard_map/ppermute | solution.py:22
  15.5 12.2 %collective-permute-start.6 = (bf16[2048,128]{1,0:T(8,128)(2,1)}, bf16[2048,128]{1,0:T(8,128)(2,1)S(1)}, u32[]{:S(2)}, u32[]{:S(2)}) collective-permute-start(bf16[2048,128]{1,0:T(8,128)(2,1)} %refs_1_), channel_id=1, source_target_pairs={{0,1},{1,0},{2,3},{3,2},{4,5},{5,4},{6,7},{7,6},{8,9},{9,8},{10,11... | collective-permute-start | bytes 1572872 | tf_op jit(solution)/shard_map/ppermute | solution.py:176
  26.0 1.7 %copy-start.2 = (bf16[2048,128]{1,0:T(8,128)(2,1)}, bf16[2048,128]{1,0:T(8,128)(2,1)S(1)}, u32[]{:S(2)}) copy-start(bf16[2048,128]{1,0:T(8,128)(2,1)S(1)} %collective-permute-done.4.refs_2_) | copy-start | bytes 1572868
  26.0 8.7 %collective-permute-start.5 = (bf16[2048,128]{1,0:T(8,128)(2,1)S(1)}, bf16[2048,128]{1,0:T(8,128)(2,1)S(1)}, u32[]{:S(2)}, u32[]{:S(2)}) collective-permute-start(bf16[2048,128]{1,0:T(8,128)(2,1)S(1)} %collective-permute-done.4.refs_2_), channel_id=1, source_target_pairs={{0,1},{1,0},{2,3},{3,2},{4,5},{5,4},{6,7},{7,6},{8,9},{9,8},{10,11... | collective-permute-start | bytes 1572872 | tf_op jit(solution)/shard_map/ppermute | solution.py:206
  26.3 0.7 %copy-start.6 = (bf16[2,3,3,128]{3,0,2,1:T(2,128)(2,1)S(1)}, bf16[2,3,3,128]{3,0,2,1:T(2,128)(2,1)}, u32[]{:S(2)}) copy-start(bf16[2,3,3,128]{3,0,2,1:T(2,128)(2,1)} %param.11) | copy-start | bytes 13828
  27.0 0.7 %copy-start.7 = (f32[2,128]{1,0:T(2,128)S(1)}, f32[2,128]{1,0:T(2,128)}, u32[]{:S(2)}) copy-start(f32[2,128]{1,0:T(2,128)} %param.9) | copy-start | bytes 3076
  27.7 0.8 %copy-start.3 = (bf16[2048,128]{1,0:T(8,128)(2,1)}, bf16[2048,128]{1,0:T(8,128)(2,1)S(1)}, u32[]{:S(2)}) copy-start(bf16[2048,128]{1,0:T(8,128)(2,1)S(1)} %collective-permute-done.6.refs_1_) | copy-start | bytes 1572868
  34.7 0.8 %copy-start.1 = (bf16[2048,128]{1,0:T(8,128)(2,1)}, bf16[2048,128]{1,0:T(8,128)(2,1)S(1)}, u32[]{:S(2)}) copy-start(bf16[2048,128]{1,0:T(8,128)(2,1)S(1)} %collective-permute-done.5.refs_1_) | copy-start | bytes 1572868
  40.9 1.9 %copy-start.4 = (f32[544,128]{1,0:T(8,128)S(1)}, f32[544,128]{1,0:T(8,128)}, u32[]{:S(2)}) copy-start(f32[544,128]{1,0:T(8,128)} %get-tuple-element.36) | copy-start | bytes 835588
  43.2 0.7 %copy-start.9 = (pred[8,9]{0,1:T(8,128)(4,1)S(1)}, pred[8,9]{0,1:T(8,128)(4,1)}, u32[]{:S(2)}) copy-start(pred[8,9]{0,1:T(8,128)(4,1)} %constant.75) | copy-start | bytes 220
  45.1 0.7 %copy-start.8 = (f32[128]{0:T(128)S(1)}, f32[128]{0:T(128)}, u32[]{:S(2)}) copy-start(f32[128]{0:T(128)} %param.10) | copy-start | bytes 1540

commit v16 on v15

--- a/solution.py
+++ b/solution.py
@@ -24,7 +24,7 @@
     return block
 
 
-def row_sums(w, base_ref, width, slot):
+def row_sums(w, base, width):
     count = w.shape[1] // width
     parts = [w[:, g * width:(g + 1) * width] for g in range(count)]
     weighted = None
@@ -40,7 +40,7 @@
     total = jnp.sum(area, axis=1, keepdims=True)
     sum_x = jnp.sum(area * col, axis=1, keepdims=True)
     local = jnp.zeros_like(total) if weighted is None else jnp.sum(weighted, axis=1, keepdims=True)
-    sum_y = (base_ref[0:1, slot:slot + 1] * total + local) / width
+    sum_y = (base * total + local) / width
     lane8 = lax.broadcasted_iota(jnp.int32, (w.shape[0], 8), 1)
     zero = jnp.zeros((), jnp.float32)
     return jnp.where(lane8 == 0, total, jnp.where(lane8 == 1, sum_x, jnp.where(lane8 == 3, sum_y, zero)))
@@ -50,8 +50,13 @@
     parts = len(slots)
     q_ref = refs[0]
     k_refs = refs[1:1 + parts]
-    pos_ref = refs[1 + parts]
-    rest = refs[2 + parts:]
+    if width:
+        pos_ref = None
+        rest = refs[1 + parts:]
+        me = lax.axis_index("match")
+    else:
+        pos_ref = refs[1 + parts]
+        rest = refs[2 + parts:]
     if not first:
         m_ref, acc_ref, st_ref = rest[:3]
         rest = rest[3:]
@@ -77,7 +82,10 @@
         hi = w.astype(jnp.bfloat16)
         part_acc = jnp.dot(hi, k_ref[...], preferred_element_type=jnp.float32)
         if width:
-            part_st = row_sums(w, pos_ref, width, slot)
+            base = jnp.float32(0.0)
+            for device, rows_first in enumerate(slot):
+                base = jnp.where(me == device, jnp.float32(rows_first), base)
+            part_st = row_sums(w, base, width)
         else:
             lo = (w - hi.astype(jnp.float32)).astype(jnp.bfloat16)
             lanes = (((1,), (1,)), ((), ()))
@@ -130,8 +138,10 @@
     row_spec = lambda width: pl.BlockSpec((tq, width), lambda i: (i, 0))
     in_specs = [row_spec(chans)]
     in_specs += [pl.BlockSpec((tk, chans), lambda i: (0, 0)) for _ in keys]
-    in_specs += [pl.BlockSpec(pos.shape, lambda i: (0, 0))]
-    args = [queries, *keys, pos]
+    args = [queries, *keys]
+    if pos is not None:
+        in_specs += [pl.BlockSpec(pos.shape, lambda i: (0, 0))]
+        args.append(pos)
     if not first:
         in_specs += [row_spec(8), row_spec(chans), row_spec(8)]
         args += list(state)
@@ -169,6 +179,14 @@
         queries = jnp.pad(queries, ((0, padded - count), (0, 0)))
     n = lax.axis_size("match")
     me = lax.axis_index("match")
+    chips = n // 2
+    if n % 2 == 0:
+        rules = [lambda m: m, lambda m: m ^ 1]
+        for shift in range(1, chips):
+            rules.append(lambda m, s=shift: ((m // 2 - s) % chips) * 2 + m % 2)
+            rules.append(lambda m, s=shift: (((m // 2 - s) % chips) * 2 + m % 2) ^ 1)
+    else:
+        rules = [lambda m, s=shift: (m - s) % n for shift in range(n)]
     shards = [(targets, me, None)]
     if n % 2 == 0:
         chips = n // 2
@@ -185,10 +203,6 @@
             moved = lax.ppermute(targets, "match", [(j, (j + shift) % n) for j in range(n)])
             shards.append((moved, (me - shift) % n, None))
     state = None
-    if tk % width == 0:
-        owners = jnp.stack([owner for _, owner, _ in shards]) * (tk // width)
-        owners = jnp.pad(owners.astype(jnp.float32), (0, 128 - n))
-        table = jnp.broadcast_to(owners[None, :], (8, 128))
     pending = None
     whole_rows = tk % width == 0
     if whole_rows and n > 1:
@@ -206,14 +220,14 @@
                 pending = lax.ppermute(key, "match", forward)
             keys.append(key)
         if tk % width == 0:
-            pos = table
+            pos = None
             seg = width
         else:
             pos = positions(tk, shards[group[0]][1] * tk, width)
             seg = 0
         state = match_step(
             queries, keys, pos, state, tq, group[0] == 0, group[-1] == n - 1, seg,
-            tuple(step % 128 for step in group),
+            tuple(tuple(rules[step](m) * (tk // width) for m in range(n)) for step in group),
         )
     warped, flow = state
     return warped[:count], flow[:count, 0], flow[:count, 1]

time: 47.5 us -> 47.7 us (level)
  other arithmetic: 1.34 us -> 2.1 us
  local copies, waits for them, and re-layouts: 8.91 us -> 8.31 us
    concatenate x2, other arithmetic: 0.05 us -> 0.89 us  [extended(): block = jnp.concatenate([low, block, high], axis=dim)]
    broadcast_in_dim x1 -> x0, local copies, waits for them, and re-layouts: 0.59 us -> none  [match(): table = jnp.broadcast_to(owners[None, :], (8, 128))]
    unnamed x21 -> x19, local copies, waits for them, and re-layouts: 4.28 us -> 4.29 us
  transfers between devices with their start and end apart: 7 -> 7, of which waited for: 3 -> 3; matrix products, arithmetic and copies ran while one was open for 4% -> 2% of each run, Pallas kernels for 23% -> 24%
where the time goes in v16:
time: 47.7 us; the launch traced here: 47.1 us
  Pallas kernels  16.3 us (34%)
  starting transfers between devices  10.8 us (23%)
  local copies, waits for them, and re-layouts  8.31 us (17%)
  waiting for transfers between devices  8.31 us (17%)
  other arithmetic  2.1 us (4%)
  matrix products  1.13 us (2%)
    pallas_call x3, Pallas kernels, match_step(): pl.pallas_call(kernel, grid=(nq,), in_specs=in_specs, out_specs=out_specs...  16.3 us
    ppermute x2, waiting for transfers between devices, extended(): lax.ppermute(lax.slice_in_dim(block, 0, width, axis=dim), axis, backward)  8.08 us
    ppermute x2, starting transfers between devices, extended(): lax.ppermute(lax.slice_in_dim(block, block.shape[dim] - width, None, axis...  5.77 us
    unnamed x19, local copies, waits for them, and re-layouts  4.29 us
    ppermute x2, starting transfers between devices, extended(): lax.ppermute(lax.slice_in_dim(block, 0, width, axis=dim), axis, backward)  2.58 us
    ppermute x1, starting transfers between devices, match(): moved = lax.ppermute(targets, 'match', hop)  2.35 us
    slice x1, local copies, waits for them, and re-layouts, match(): return (warped[:count], flow[:count, 0], flow[:count, 1])  1.42 us
  transfers between devices with their start and end apart: 7, of which 3 were waited for; matrix products, arithmetic and copies ran while one was open for 2% of the time, Pallas kernels for 24%

profile of v16, /device:TPU:0, one launch (start us, length us, event | category | flops | bytes accessed | tf_op | source)
XLA Modules:
  0.0 47.1 jit_solution(10157019218853531522)
XLA Ops:
  0.0 0.8 %fusion.23 = (bf16[4,2,128]{2,1,0:T(2,128)(2,1)S(1)}, bf16[4,2,128]{2,1,0:T(2,128)(2,1)S(1)}) fusion(bf16[4,64,128]{2,1,0:T(8,128)(2,1)} %param.6), kind=kLoop, calls=%fused_computation.48 | loop fusion | bytes 8192 | tf_op jit(solution)/shard_map/slice | solution.py:20
  0.8 2.3 %collective-permute-start = (bf16[4,2,128]{2,1,0:T(2,128)(2,1)S(1)}, bf16[4,2,128]{2,1,0:T(2,128)(2,1)S(1)}, u32[]{:S(2)}, u32[]{:S(2)}) collective-permute-start(bf16[4,2,128]{2,1,0:T(2,128)(2,1)S(1)} %get-tuple-element.63), channel_id=1, source_target_pairs={{0,1},{1,2},{2,3},{4,5},{5,6},{6,7},{8,9},{9,10},{10,11},{12,13},{... | collective-permute-start | bytes 6152 | tf_op jit(solution)/shard_map/ppermute | solution.py:19
  3.1 1.3 %collective-permute-start.1 = (bf16[4,2,128]{2,1,0:T(2,128)(2,1)S(1)}, bf16[4,2,128]{2,1,0:T(2,128)(2,1)S(1)}, u32[]{:S(2)}, u32[]{:S(2)}) collective-permute-start(bf16[4,2,128]{2,1,0:T(2,128)(2,1)S(1)} %get-tuple-element.64), channel_id=1, source_target_pairs={{1,0},{2,1},{3,2},{5,4},{6,5},{7,6},{9,8},{10,9},{11,10},{13,12},{... | collective-permute-start | bytes 6152 | tf_op jit(solution)/shard_map/ppermute | solution.py:22
  4.4 0.0 collective-permute-done
  4.4 3.8 %collective-permute-done.1 = bf16[4,2,128]{2,1,0:T(2,128)(2,1)S(1)} collective-permute-done((bf16[4,2,128]{2,1,0:T(2,128)(2,1)S(1)}, bf16[4,2,128]{2,1,0:T(2,128)(2,1)S(1)}, u32[]{:S(2)}, u32[]{:S(2)}) %collective-permute-start.1) | collective-permute-done | bytes 2080 | tf_op jit(solution)/shard_map/ppermute | solution.py:22
  8.3 0.9 %pad_maximum_fusion.1 = bf16[4,68,128]{2,1,0:T(8,128)(2,1)S(1)} fusion(bf16[4,2,128]{2,1,0:T(2,128)(2,1)S(1)} %collective-permute-done.1, bf16[4,64,128]{2,1,0:T(8,128)(2,1)} %param.6, bf16[4,2,128]{2,1,0:T(2,128)(2,1)S(1)} %collective-permute-done), kind=kLoop, calls=%fused_computation.20 | loop fusion | flops 208896 | bytes 139264 | tf_op jit(solution)/shard_map/concatenate | solution.py:23
  9.1 2.3 %collective-permute-start.4 = (bf16[2048,128]{1,0:T(8,128)(2,1)}, bf16[2048,128]{1,0:T(8,128)(2,1)S(1)}, u32[]{:S(2)}, u32[]{:S(2)}) collective-permute-start(bf16[2048,128]{1,0:T(8,128)(2,1)} %refs_1_), channel_id=1, source_target_pairs={{0,2},{1,3},{2,0},{3,1},{4,6},{5,7},{6,4},{7,5},{8,10},{9,11},{10,... | collective-permute-start | bytes 1572872 | tf_op jit(solution)/shard_map/ppermute | solution.py:197
  11.5 3.4 %collective-permute-start.2 = (bf16[2,68,128]{2,1,0:T(8,128)(2,1)S(1)}, bf16[2,68,128]{2,1,0:T(8,128)(2,1)S(1)}, u32[]{:S(2)}, u32[]{:S(2)}) collective-permute-start(bf16[2,68,128]{2,1,0:T(8,128)(2,1)S(1)} %get-tuple-element.61), channel_id=1, source_target_pairs={{0,4},{4,8},{8,12},{12,16},{16,20},{20,24},{24,28},{1,5},{5,9},{9,... | collective-permute-start | bytes 104456 | tf_op jit(solution)/shard_map/ppermute | solution.py:19
  14.9 1.3 %collective-permute-start.3 = (bf16[2,68,128]{2,1,0:T(8,128)(2,1)S(1)}, bf16[2,68,128]{2,1,0:T(8,128)(2,1)S(1)}, u32[]{:S(2)}, u32[]{:S(2)}) collective-permute-start(bf16[2,68,128]{2,1,0:T(8,128)(2,1)S(1)} %get-tuple-element.62), channel_id=1, source_target_pairs={{4,0},{8,4},{12,8},{16,12},{20,16},{24,20},{28,24},{5,1},{9,5},{13... | collective-permute-start | bytes 104456 | tf_op jit(solution)/shard_map/ppermute | solution.py:22
  16.3 0.1 collective-permute-start.6
  16.3 0.2 collective-permute-done.2
  16.6 4.2 %collective-permute-done.3 = bf16[2,68,128]{2,1,0:T(8,128)(2,1)S(1)} collective-permute-done((bf16[2,68,128]{2,1,0:T(8,128)(2,1)S(1)}, bf16[2,68,128]{2,1,0:T(8,128)(2,1)S(1)}, u32[]{:S(2)}, u32[]{:S(2)}) %collective-permute-start.3) | collective-permute-done | bytes 34848 | tf_op jit(solution)/shard_map/ppermute | solution.py:22
  20.8 0.7 %reshape.81.refs_0_ = bf16[544,128]{1,0:T(8,128)(2,1)} reshape(bf16[8,68,128]{2,1,0:T(8,128)(2,1)S(1)} %pad_maximum_fusion) | data formatting | bytes 278528 | tf_op jit(solution)/shard_map/reshape | solution.py:248
  21.5 5.0 %shard_map.64 = (f32[544,8]{1,0:T(8,128)}, f32[544,128]{1,0:T(8,128)}, f32[544,8]{1,0:T(8,128)}) custom-call(bf16[544,128]{1,0:T(8,128)(2,1)} %reshape.81.refs_0_, bf16[2048,128]{1,0:T(8,128)(2,1)} %refs_1_), custom_call_target="tpu_custom_call" | custom-call | tf_op jit(solution)/shard_map/pallas_call | solution.py:161
  26.5 0.0 collective-permute-done.4.refs_2_
  26.5 0.0 collective-permute-start.5
  26.5 0.1 broadcast_and_fusion
  26.6 0.1 slice.128
  26.7 0.1 copy.24
  26.8 0.7 %copy-done.5 = bf16[2,3,3,128]{3,0,2,1:T(2,128)(2,1)S(1)} copy-done((bf16[2,3,3,128]{3,0,2,1:T(2,128)(2,1)S(1)}, bf16[2,3,3,128]{3,0,2,1:T(2,128)(2,1)}, u32[]{:S(2)}) %copy-start.5) | copy-done | bytes 4632
  27.5 0.7 %copy-done.6 = f32[2,128]{1,0:T(2,128)S(1)} copy-done((f32[2,128]{1,0:T(2,128)S(1)}, f32[2,128]{1,0:T(2,128)}, u32[]{:S(2)}) %copy-start.6) | copy-done | bytes 1048
  28.2 0.0 collective-permute-done.6.refs_1_
  28.2 0.8 %copy-done.3 = bf16[2048,128]{1,0:T(8,128)(2,1)} copy-done((bf16[2048,128]{1,0:T(8,128)(2,1)}, bf16[2048,128]{1,0:T(8,128)(2,1)S(1)}, u32[]{:S(2)}) %copy-start.3) | copy-done | bytes 524312
  29.0 6.3 %shard_map.65 = (f32[544,8]{1,0:T(8,128)}, f32[544,128]{1,0:T(8,128)}, f32[544,8]{1,0:T(8,128)}) custom-call(bf16[544,128]{1,0:T(8,128)(2,1)} %reshape.81.refs_0_, bf16[2048,128]{1,0:T(8,128)(2,1)} %copy-done.3, bf16[2048,128]{1,0:T(8,128)(2,1)} %copy-done.2, f32[544,8]{1,0:T(8,128)} %get-tuple-element.29.refs_3_, f32[544,128]{1,0:T(8,128)} %get-tuple-element.30.refs_4_, ...), custom_call_target="tpu_custom_call" | custom-call | tf_op jit(solution)/shard_map/pallas_call | solution.py:161
  35.3 0.0 collective-permute-done.5.refs_1_
  35.3 0.8 %copy-done.1 = bf16[2048,128]{1,0:T(8,128)(2,1)} copy-done((bf16[2048,128]{1,0:T(8,128)(2,1)}, bf16[2048,128]{1,0:T(8,128)(2,1)S(1)}, u32[]{:S(2)}) %copy-start.1) | copy-done | bytes 524312
  36.1 4.9 %shard_map.66 = (f32[544,128]{1,0:T(8,128)}, f32[544,8]{1,0:T(8,128)}) custom-call(bf16[544,128]{1,0:T(8,128)(2,1)} %reshape.81.refs_0_, bf16[2048,128]{1,0:T(8,128)(2,1)} %copy-done.1, f32[544,8]{1,0:T(8,128)} %get-tuple-element.32.refs_2_, f32[544,128]{1,0:T(8,128)} %get-tuple-element.33.refs_3_, f32[544,8]{1,0:T(8,128)} %get-tuple-element.34.refs_4_), custom_call_target="tpu_custom_call" | custom-call | tf_op jit(solution)/shard_map/pallas_call | solution.py:161
  41.1 1.4 %slice_reduce_fusion.1 = (f32[544]{0:T(1024)S(1)}, f32[544]{0:T(1024)S(1)}) fusion(f32[544,8]{1,0:T(8,128)} %get-tuple-element.35), kind=kLoop, calls=%fused_computation.8 | loop fusion | bytes 8704 | tf_op jit(solution)/shard_map/slice | solution.py:233
  42.5 0.1 reshape_squeeze.7
  42.6 0.1 broadcast_subtract_fusion
  42.6 0.1 slice.131
  42.7 0.1 reshape_squeeze.6
  42.8 0.1 slice.129
  42.9 0.1 slice_bitcast_fusion.1
  43.0 0.1 select_bitcast_fusion
  43.1 0.1 copy.67
  43.2 0.1 copy.27
  43.3 0.0 copy-start.8
  43.3 0.6 %copy-done.8 = pred[8,9]{0,1:T(8,128)(4,1)S(1)} copy-done((pred[8,9]{0,1:T(8,128)(4,1)S(1)}, pred[8,9]{0,1:T(8,128)(4,1)}, u32[]{:S(2)}) %copy-start.8) | copy-done | bytes 96
  44.0 0.9 %convolution_select_fusion = f32[6,8,9,128]{3,1,2,0:T(8,128)S(1)} fusion(bf16[3,3,128,128]{3,2,1,0:T(8,128)(2,1)S(1)} %copy-done, f32[8,1,7,2,128]{4,2,3,0,1:T(8,128)S(1)} %slice.153, f32[8,1,8,9,128]{4,2,3,0,1:T(8,128)S(1)} %copy.27, pred[8,9]{0,1:T(8,128)(4,1)S(1)} %copy-done.8), kind=kOutput, calls=%fused_computation | convolution fusion | flops 764737536 | bytes 868424 | tf_op jit(solution)/shard_map/conv_general_dilated | solution.py:259
  44.9 0.1 copy.28
  45.0 0.1 copy.30
  45.1 0.1 copy.29
  45.2 0.7 %copy-done.7 = f32[128]{0:T(128)S(1)} copy-done((f32[128]{0:T(128)S(1)}, f32[128]{0:T(128)}, u32[]{:S(2)}) %copy-start.7) | copy-done | bytes 536
  45.9 0.3 select_bitcast_fusion.1
  46.1 0.2 fusion.9
  46.3 0.1 fusion.21
  46.5 0.6 %maximum_add_fusion = f32[2,4,64]{2,1,0:T(4,128)} fusion(f32[1,4,64]{2,1,0:T(4,128)S(1)} %get-tuple-element.67, f32[1,4,64]{2,1,0:T(4,128)S(1)} %get-tuple-element.68, f32[1,4,64]{2,1,0:T(4,128)S(1)} %bitcast.103, f32[1,4,64]{2,1,0:T(4,128)S(1)} %bitcast.104, f32[1,4,64]{2,1,0:T(4,128)S(1)} %bitcast.101, f32[1,4,64]{2,1,0:T(4,128)S(1)} %bitcast.102, ...), kind=kLoop, calls=%fused_computation.21 | loop fusion | flops 9728 | bytes 22528 | tf_op jit(solution)/shard_map/add | solution.py:279
  (24 shorter events, 0.2 us)
Async XLA Ops:
  0.0 43.3 %copy-start = (bf16[3,3,128,128]{3,2,1,0:T(8,128)(2,1)S(1)}, bf16[3,3,128,128]{3,2,1,0:T(8,128)(2,1)}, u32[]{:S(2)}) copy-start(bf16[3,3,128,128]{3,2,1,0:T(8,128)(2,1)} %param.8) | copy-start | bytes 884740
  0.8 3.7 %collective-permute-start = (bf16[4,2,128]{2,1,0:T(2,128)(2,1)S(1)}, bf16[4,2,128]{2,1,0:T(2,128)(2,1)S(1)}, u32[]{:S(2)}, u32[]{:S(2)}) collective-permute-start(bf16[4,2,128]{2,1,0:T(2,128)(2,1)S(1)} %get-tuple-element.63), channel_id=1, source_target_pairs={{0,1},{1,2},{2,3},{4,5},{5,6},{6,7},{8,9},{9,10},{10,11},{12,13},{... | collective-permute-start | bytes 6152 | tf_op jit(solution)/shard_map/ppermute | solution.py:19
  3.1 5.2 %collective-permute-start.1 = (bf16[4,2,128]{2,1,0:T(2,128)(2,1)S(1)}, bf16[4,2,128]{2,1,0:T(2,128)(2,1)S(1)}, u32[]{:S(2)}, u32[]{:S(2)}) collective-permute-start(bf16[4,2,128]{2,1,0:T(2,128)(2,1)S(1)} %get-tuple-element.64), channel_id=1, source_target_pairs={{1,0},{2,1},{3,2},{5,4},{6,5},{7,6},{9,8},{10,9},{11,10},{13,12},{... | collective-permute-start | bytes 6152 | tf_op jit(solution)/shard_map/ppermute | solution.py:22
  9.1 17.4 %collective-permute-start.4 = (bf16[2048,128]{1,0:T(8,128)(2,1)}, bf16[2048,128]{1,0:T(8,128)(2,1)S(1)}, u32[]{:S(2)}, u32[]{:S(2)}) collective-permute-start(bf16[2048,128]{1,0:T(8,128)(2,1)} %refs_1_), channel_id=1, source_target_pairs={{0,2},{1,3},{2,0},{3,1},{4,6},{5,7},{6,4},{7,5},{8,10},{9,11},{10,... | collective-permute-start | bytes 1572872 | tf_op jit(solution)/shard_map/ppermute | solution.py:197
  11.5 5.0 %collective-permute-start.2 = (bf16[2,68,128]{2,1,0:T(8,128)(2,1)S(1)}, bf16[2,68,128]{2,1,0:T(8,128)(2,1)S(1)}, u32[]{:S(2)}, u32[]{:S(2)}) collective-permute-start(bf16[2,68,128]{2,1,0:T(8,128)(2,1)S(1)} %get-tuple-element.61), channel_id=1, source_target_pairs={{0,4},{4,8},{8,12},{12,16},{16,20},{20,24},{24,28},{1,5},{5,9},{9,... | collective-permute-start | bytes 104456 | tf_op jit(solution)/shard_map/ppermute | solution.py:19
  14.9 5.9 %collective-permute-start.3 = (bf16[2,68,128]{2,1,0:T(8,128)(2,1)S(1)}, bf16[2,68,128]{2,1,0:T(8,128)(2,1)S(1)}, u32[]{:S(2)}, u32[]{:S(2)}) collective-permute-start(bf16[2,68,128]{2,1,0:T(8,128)(2,1)S(1)} %get-tuple-element.62), channel_id=1, source_target_pairs={{4,0},{8,4},{12,8},{16,12},{20,16},{24,20},{28,24},{5,1},{9,5},{13... | collective-permute-start | bytes 104456 | tf_op jit(solution)/shard_map/ppermute | solution.py:22
  16.3 11.9 %collective-permute-start.6 = (bf16[2048,128]{1,0:T(8,128)(2,1)}, bf16[2048,128]{1,0:T(8,128)(2,1)S(1)}, u32[]{:S(2)}, u32[]{:S(2)}) collective-permute-start(bf16[2048,128]{1,0:T(8,128)(2,1)} %refs_1_), channel_id=1, source_target_pairs={{0,1},{1,0},{2,3},{3,2},{4,5},{5,4},{6,7},{7,6},{8,9},{9,8},{10,11... | collective-permute-start | bytes 1572872 | tf_op jit(solution)/shard_map/ppermute | solution.py:194
  26.5 1.7 %copy-start.2 = (bf16[2048,128]{1,0:T(8,128)(2,1)}, bf16[2048,128]{1,0:T(8,128)(2,1)S(1)}, u32[]{:S(2)}) copy-start(bf16[2048,128]{1,0:T(8,128)(2,1)S(1)} %collective-permute-done.4.refs_2_) | copy-start | bytes 1572868
  26.5 8.8 %collective-permute-start.5 = (bf16[2048,128]{1,0:T(8,128)(2,1)S(1)}, bf16[2048,128]{1,0:T(8,128)(2,1)S(1)}, u32[]{:S(2)}, u32[]{:S(2)}) collective-permute-start(bf16[2048,128]{1,0:T(8,128)(2,1)S(1)} %collective-permute-done.4.refs_2_), channel_id=1, source_target_pairs={{0,1},{1,0},{2,3},{3,2},{4,5},{5,4},{6,7},{7,6},{8,9},{9,8},{10,11... | collective-permute-start | bytes 1572872 | tf_op jit(solution)/shard_map/ppermute | solution.py:220
  26.8 0.7 %copy-start.5 = (bf16[2,3,3,128]{3,0,2,1:T(2,128)(2,1)S(1)}, bf16[2,3,3,128]{3,0,2,1:T(2,128)(2,1)}, u32[]{:S(2)}) copy-start(bf16[2,3,3,128]{3,0,2,1:T(2,128)(2,1)} %param.11) | copy-start | bytes 13828
  27.5 0.7 %copy-start.6 = (f32[2,128]{1,0:T(2,128)S(1)}, f32[2,128]{1,0:T(2,128)}, u32[]{:S(2)}) copy-start(f32[2,128]{1,0:T(2,128)} %param.9) | copy-start | bytes 3076
  28.2 0.8 %copy-start.3 = (bf16[2048,128]{1,0:T(8,128)(2,1)}, bf16[2048,128]{1,0:T(8,128)(2,1)S(1)}, u32[]{:S(2)}) copy-start(bf16[2048,128]{1,0:T(8,128)(2,1)S(1)} %collective-permute-done.6.refs_1_) | copy-start | bytes 1572868
  35.3 0.8 %copy-start.1 = (bf16[2048,128]{1,0:T(8,128)(2,1)}, bf16[2048,128]{1,0:T(8,128)(2,1)S(1)}, u32[]{:S(2)}) copy-start(bf16[2048,128]{1,0:T(8,128)(2,1)S(1)} %collective-permute-done.5.refs_1_) | copy-start | bytes 1572868
  41.1 1.9 %copy-start.4 = (f32[544,128]{1,0:T(8,128)S(1)}, f32[544,128]{1,0:T(8,128)}, u32[]{:S(2)}) copy-start(f32[544,128]{1,0:T(8,128)} %get-tuple-element.36) | copy-start | bytes 835588
  43.3 0.7 %copy-start.8 = (pred[8,9]{0,1:T(8,128)(4,1)S(1)}, pred[8,9]{0,1:T(8,128)(4,1)}, u32[]{:S(2)}) copy-start(pred[8,9]{0,1:T(8,128)(4,1)} %constant.41) | copy-start | bytes 220
  45.2 0.7 %copy-start.7 = (f32[128]{0:T(128)S(1)}, f32[128]{0:T(128)}, u32[]{:S(2)}) copy-start(f32[128]{0:T(128)} %param.10) | copy-start | bytes 1540

commit v17 on v15

--- a/solution.py
+++ b/solution.py
@@ -226,8 +226,10 @@
     row_first = lax.axis_index("space") * rows
     col_first = lax.axis_index("match") * cols
     ext = extended(source, (("match", 1),), HALO)
-    targets, ext, conv_in, flow_proj, in_bias, conv_out = lax.optimization_barrier(
-        (targets, ext, conv_in, flow_proj, in_bias, conv_out)
+    small = jnp.concatenate([flow_proj, in_bias[None, :]], axis=0)
+    taps = jnp.transpose(conv_out, (3, 0, 1, 2)).reshape(chans, -1)
+    targets, ext, conv_in, small, taps = lax.optimization_barrier(
+        (targets, ext, conv_in, small, taps)
     )
     ext = extended(ext, (("space", 0),), HALO)
     erows, ecols = rows + 2 * HALO, cols + 2 * HALO
@@ -250,10 +252,9 @@
     )[0]
     fx1 = flow_x[1:-1, 1:-1]
     fy1 = flow_y[1:-1, 1:-1]
-    pre = pre + fx1[:, :, None] * flow_proj[0] + fy1[:, :, None] * flow_proj[1] + in_bias
+    pre = pre + fx1[:, :, None] * small[0] + fy1[:, :, None] * small[1] + small[2]
     hidden = jax.nn.silu(pre).astype(jnp.bfloat16)
     hidden = jnp.where(inside[1:-1, 1:-1, None], hidden, jnp.zeros((), jnp.bfloat16))
-    taps = jnp.transpose(conv_out, (3, 0, 1, 2)).reshape(chans, -1)
     proj = jnp.einsum("hwc,ck->hwk", hidden, taps, preferred_element_type=jnp.float32)
     delta = None
     for tap_a in range(3):

time: 47.5 us -> 46 us (0.968)
  waiting for transfers between devices: 8.22 us -> 6.84 us
  local copies, waits for them, and re-layouts: 8.91 us -> 8.14 us
  other arithmetic: 1.34 us -> 2.05 us
    ppermute x2, waiting for transfers between devices: 8.02 us -> 6.64 us  [extended(): lax.ppermute(lax.slice_in_dim(block, 0, width, axis=dim), axis, backward)]
    unnamed x21 -> x17, local copies, waits for them, and re-layouts: 4.28 us -> 3.49 us
    concatenate x0 -> x1, other arithmetic: none -> 0.71 us  [local(): small = jnp.concatenate([flow_proj, in_bias[None, :]], axis=0)]
  transfers between devices with their start and end apart: 7 -> 7, of which waited for: 3 -> 3; matrix products, arithmetic and copies ran while one was open for 4% -> 5% of each run, Pallas kernels for 23% -> 24%
where the time goes in v17:
time: 46 us; the launch traced here: 45.7 us
  Pallas kernels  16.4 us (36%)
  starting transfers between devices  10.9 us (24%)
  local copies, waits for them, and re-layouts  8.14 us (18%)
  waiting for transfers between devices  6.84 us (15%)
  other arithmetic  2.05 us (4%)
  matrix products  1.13 us (2%)
    pallas_call x3, Pallas kernels, match_step(): pl.pallas_call(kernel, grid=(nq,), in_specs=in_specs, out_specs=out_specs...  16.4 us
    ppermute x2, waiting for transfers between devices, extended(): lax.ppermute(lax.slice_in_dim(block, 0, width, axis=dim), axis, backward)  6.64 us
    ppermute x2, starting transfers between devices, extended(): lax.ppermute(lax.slice_in_dim(block, block.shape[dim] - width, None, axis...  5.77 us
    unnamed x17, local copies, waits for them, and re-layouts  3.49 us
    ppermute x2, starting transfers between devices, extended(): lax.ppermute(lax.slice_in_dim(block, 0, width, axis=dim), axis, backward)  2.58 us
    ppermute x1, starting transfers between devices, match(): moved = lax.ppermute(targets, 'match', hop)  2.53 us
    slice x1, local copies, waits for them, and re-layouts, match(): return (warped[:count], flow[:count, 0], flow[:count, 1])  1.42 us
    conv_general_dilated x1, matrix products, local(): lax.conv_general_dilated(warped[None], conv_in.astype(jnp.float32), (1, 1...  0.94 us
  transfers between devices with their start and end apart: 7, of which 3 were waited for; matrix products, arithmetic and copies ran while one was open for 5% of the time, Pallas kernels for 24%

profile of v17, /device:TPU:0, one launch (start us, length us, event | category | flops | bytes accessed | tf_op | source)
XLA Modules:
  0.0 45.7 jit_solution(18198378946107625098)
XLA Ops:
  0.0 0.8 %fusion.25 = (bf16[4,2,128]{2,1,0:T(2,128)(2,1)S(1)}, bf16[4,2,128]{2,1,0:T(2,128)(2,1)S(1)}) fusion(bf16[4,64,128]{2,1,0:T(8,128)(2,1)} %param.6), kind=kLoop, calls=%fused_computation.53 | loop fusion | bytes 8192 | tf_op jit(solution)/shard_map/slice | solution.py:20
  0.8 2.3 %collective-permute-start = (bf16[4,2,128]{2,1,0:T(2,128)(2,1)S(1)}, bf16[4,2,128]{2,1,0:T(2,128)(2,1)S(1)}, u32[]{:S(2)}, u32[]{:S(2)}) collective-permute-start(bf16[4,2,128]{2,1,0:T(2,128)(2,1)S(1)} %get-tuple-element.61), channel_id=1, source_target_pairs={{0,1},{1,2},{2,3},{4,5},{5,6},{6,7},{8,9},{9,10},{10,11},{12,13},{... | collective-permute-start | bytes 6152 | tf_op jit(solution)/shard_map/ppermute | solution.py:19
  3.1 1.3 %collective-permute-start.1 = (bf16[4,2,128]{2,1,0:T(2,128)(2,1)S(1)}, bf16[4,2,128]{2,1,0:T(2,128)(2,1)S(1)}, u32[]{:S(2)}, u32[]{:S(2)}) collective-permute-start(bf16[4,2,128]{2,1,0:T(2,128)(2,1)S(1)} %get-tuple-element.62), channel_id=1, source_target_pairs={{1,0},{2,1},{3,2},{5,4},{6,5},{7,6},{9,8},{10,9},{11,10},{13,12},{... | collective-permute-start | bytes 6152 | tf_op jit(solution)/shard_map/ppermute | solution.py:22
  4.5 0.7 %pad_maximum_fusion.2 = f32[3,128]{1,0:T(4,128)S(1)} fusion(f32[1,128]{1,0:T(1,128)} %bitcast.114, f32[2,128]{1,0:T(2,128)} %param.9), kind=kLoop, calls=%fused_computation.31 | loop fusion | flops 384 | bytes 3072 | tf_op jit(solution)/shard_map/concatenate | solution.py:229
  5.2 0.7 %copy-done.6 = bf16[2,3,3,128]{3,0,2,1:T(2,128)(2,1)S(1)} copy-done((bf16[2,3,3,128]{3,0,2,1:T(2,128)(2,1)S(1)}, bf16[2,3,3,128]{3,0,2,1:T(2,128)(2,1)}, u32[]{:S(2)}) %copy-start.6) | copy-done | bytes 4632
  5.9 0.0 collective-permute-done
  5.9 2.4 %collective-permute-done.1 = bf16[4,2,128]{2,1,0:T(2,128)(2,1)S(1)} collective-permute-done((bf16[4,2,128]{2,1,0:T(2,128)(2,1)S(1)}, bf16[4,2,128]{2,1,0:T(2,128)(2,1)S(1)}, u32[]{:S(2)}, u32[]{:S(2)}) %collective-permute-start.1) | collective-permute-done | bytes 2080 | tf_op jit(solution)/shard_map/ppermute | solution.py:22
  8.3 2.5 %collective-permute-start.4 = (bf16[2048,128]{1,0:T(8,128)(2,1)}, bf16[2048,128]{1,0:T(8,128)(2,1)S(1)}, u32[]{:S(2)}, u32[]{:S(2)}) collective-permute-start(bf16[2048,128]{1,0:T(8,128)(2,1)} %refs_1_), channel_id=1, source_target_pairs={{0,2},{1,3},{2,0},{3,1},{4,6},{5,7},{6,4},{7,5},{8,10},{9,11},{10,... | collective-permute-start | bytes 1572872 | tf_op jit(solution)/shard_map/ppermute | solution.py:179
  10.9 3.4 %collective-permute-start.2 = (bf16[2,68,128]{2,1,0:T(8,128)(2,1)S(1)}, bf16[2,68,128]{2,1,0:T(8,128)(2,1)S(1)}, u32[]{:S(2)}, u32[]{:S(2)}) collective-permute-start(bf16[2,68,128]{2,1,0:T(8,128)(2,1)S(1)} %get-tuple-element.59), channel_id=1, source_target_pairs={{0,4},{4,8},{8,12},{12,16},{16,20},{20,24},{24,28},{1,5},{5,9},{9,... | collective-permute-start | bytes 104456 | tf_op jit(solution)/shard_map/ppermute | solution.py:19
  14.3 1.3 %collective-permute-start.3 = (bf16[2,68,128]{2,1,0:T(8,128)(2,1)S(1)}, bf16[2,68,128]{2,1,0:T(8,128)(2,1)S(1)}, u32[]{:S(2)}, u32[]{:S(2)}) collective-permute-start(bf16[2,68,128]{2,1,0:T(8,128)(2,1)S(1)} %get-tuple-element.60), channel_id=1, source_target_pairs={{4,0},{8,4},{12,8},{16,12},{20,16},{24,20},{28,24},{5,1},{9,5},{13... | collective-permute-start | bytes 104456 | tf_op jit(solution)/shard_map/ppermute | solution.py:22
  15.6 0.1 fusion.19
  15.7 0.0 collective-permute-start.6
  15.7 0.2 collective-permute-done.2
  15.9 4.2 %collective-permute-done.3 = bf16[2,68,128]{2,1,0:T(8,128)(2,1)S(1)} collective-permute-done((bf16[2,68,128]{2,1,0:T(8,128)(2,1)S(1)}, bf16[2,68,128]{2,1,0:T(8,128)(2,1)S(1)}, u32[]{:S(2)}, u32[]{:S(2)}) %collective-permute-start.3) | collective-permute-done | bytes 34848 | tf_op jit(solution)/shard_map/ppermute | solution.py:22
  20.2 0.7 %reshape.76.refs_0_ = bf16[544,128]{1,0:T(8,128)(2,1)} reshape(bf16[8,68,128]{2,1,0:T(8,128)(2,1)S(1)} %pad_maximum_fusion) | data formatting | bytes 278528 | tf_op jit(solution)/shard_map/reshape | solution.py:236
  20.9 0.6 %broadcast_in_dim.25.refs_2_.refs_3_ = f32[8,128]{1,0:T(8,128)} broadcast(f32[128]{0:T(128)S(1)} %pad.4), dimensions={1} | broadcast | bytes 4608 | tf_op jit(solution)/shard_map/broadcast_in_dim | solution.py:191
  21.5 4.7 %shard_map.64 = (f32[544,8]{1,0:T(8,128)}, f32[544,128]{1,0:T(8,128)}, f32[544,8]{1,0:T(8,128)}) custom-call(bf16[544,128]{1,0:T(8,128)(2,1)} %reshape.76.refs_0_, bf16[2048,128]{1,0:T(8,128)(2,1)} %refs_1_, f32[8,128]{1,0:T(8,128)} %broadcast_in_dim.25.refs_2_.refs_3_), custom_call_target="tpu_custom_call" | custom-call | tf_op jit(solution)/shard_map/pallas_call | solution.py:151
  26.2 0.0 collective-permute-done.4.refs_2_
  26.2 0.0 collective-permute-start.5
  26.2 0.1 broadcast_and_fusion
  26.3 0.1 slice.131
  26.4 0.1 copy.25
  26.5 0.0 collective-permute-done.6.refs_1_
  26.6 0.5 %copy-done.2 = bf16[2048,128]{1,0:T(8,128)(2,1)} copy-done((bf16[2048,128]{1,0:T(8,128)(2,1)}, bf16[2048,128]{1,0:T(8,128)(2,1)S(1)}, u32[]{:S(2)}) %copy-start.2) | copy-done | bytes 524312
  27.0 0.8 %copy-done.3 = bf16[2048,128]{1,0:T(8,128)(2,1)} copy-done((bf16[2048,128]{1,0:T(8,128)(2,1)}, bf16[2048,128]{1,0:T(8,128)(2,1)S(1)}, u32[]{:S(2)}) %copy-start.3) | copy-done | bytes 524312
  27.8 6.2 %shard_map.65 = (f32[544,8]{1,0:T(8,128)}, f32[544,128]{1,0:T(8,128)}, f32[544,8]{1,0:T(8,128)}) custom-call(bf16[544,128]{1,0:T(8,128)(2,1)} %reshape.76.refs_0_, bf16[2048,128]{1,0:T(8,128)(2,1)} %copy-done.3, bf16[2048,128]{1,0:T(8,128)(2,1)} %copy-done.2, f32[8,128]{1,0:T(8,128)} %broadcast_in_dim.25.refs_2_.refs_3_, ...), custom_call_target="tpu_custom_call" | custom-call | tf_op jit(solution)/shard_map/pallas_call | solution.py:151
  34.0 0.8 %copy-done.1 = bf16[2048,128]{1,0:T(8,128)(2,1)} copy-done((bf16[2048,128]{1,0:T(8,128)(2,1)}, bf16[2048,128]{1,0:T(8,128)(2,1)S(1)}, u32[]{:S(2)}) %copy-start.1) | copy-done | bytes 524312
  34.8 5.4 %shard_map.66 = (f32[544,128]{1,0:T(8,128)}, f32[544,8]{1,0:T(8,128)}) custom-call(bf16[544,128]{1,0:T(8,128)(2,1)} %reshape.76.refs_0_, bf16[2048,128]{1,0:T(8,128)(2,1)} %copy-done.1, f32[8,128]{1,0:T(8,128)} %broadcast_in_dim.25.refs_2_.refs_3_, f32[544,8]{1,0:T(8,128)} %get-tuple-element.31.refs_3_, f32[544,128]{1,0:T(8,128)} %get-tuple-element.32.refs_4_, ...), custom_call_target="tpu_custom_call" | custom-call | tf_op jit(solution)/shard_map/pallas_call | solution.py:151
  40.3 1.4 %slice_reduce_fusion.1 = (f32[544]{0:T(1024)S(1)}, f32[544]{0:T(1024)S(1)}) fusion(f32[544,8]{1,0:T(8,128)} %get-tuple-element.34), kind=kLoop, calls=%fused_computation.8 | loop fusion | bytes 8704 | tf_op jit(solution)/shard_map/slice | solution.py:219
  41.7 0.1 reshape_squeeze.6
  41.8 0.1 slice.132
  41.9 0.1 reshape_squeeze.7
  41.9 0.1 broadcast_subtract_fusion
  42.0 0.1 slice.134
  42.1 0.1 slice_bitcast_fusion.1
  42.2 0.1 select_bitcast_fusion
  42.3 0.1 copy.67
  42.4 0.1 copy.28
  42.5 0.0 copy-start.7
  42.5 0.6 %copy-done.7 = pred[8,9]{0,1:T(8,128)(4,1)S(1)} copy-done((pred[8,9]{0,1:T(8,128)(4,1)S(1)}, pred[8,9]{0,1:T(8,128)(4,1)}, u32[]{:S(2)}) %copy-start.7) | copy-done | bytes 96
  43.2 0.9 %convolution_select_fusion = f32[6,8,9,128]{3,1,2,0:T(8,128)S(1)} fusion(bf16[3,3,128,128]{3,2,1,0:T(8,128)(2,1)S(1)} %copy-done, f32[8,1,7,2,128]{4,2,3,0,1:T(8,128)S(1)} %slice.157, f32[8,1,8,9,128]{4,2,3,0,1:T(8,128)S(1)} %copy.28, pred[8,9]{0,1:T(8,128)(4,1)S(1)} %copy-done.7), kind=kOutput, calls=%fused_computation | convolution fusion | flops 764737536 | bytes 868424 | tf_op jit(solution)/shard_map/conv_general_dilated | solution.py:247
  44.1 0.1 copy.29
  44.2 0.1 copy.30
  44.3 0.1 copy.31
  44.4 0.3 broadcast_select_fusion
  44.7 0.2 fusion.9
  44.9 0.1 fusion.23
  45.0 0.6 %maximum_add_fusion = f32[2,4,64]{2,1,0:T(4,128)} fusion(f32[1,4,64]{2,1,0:T(4,128)S(1)} %get-tuple-element.66, f32[1,4,64]{2,1,0:T(4,128)S(1)} %get-tuple-element.67, f32[1,4,64]{2,1,0:T(4,128)S(1)} %bitcast.110, f32[1,4,64]{2,1,0:T(4,128)S(1)} %bitcast.111, f32[1,4,64]{2,1,0:T(4,128)S(1)} %bitcast.108, f32[1,4,64]{2,1,0:T(4,128)S(1)} %bitcast.109, ...), kind=kLoop, calls=%fused_computation.22 | loop fusion | flops 9728 | bytes 22528 | tf_op jit(solution)/shard_map/add | solution.py:266
  (26 shorter events, 0.2 us)
Async XLA Ops:
  0.0 42.5 %copy-start = (bf16[3,3,128,128]{3,2,1,0:T(8,128)(2,1)S(1)}, bf16[3,3,128,128]{3,2,1,0:T(8,128)(2,1)}, u32[]{:S(2)}) copy-start(bf16[3,3,128,128]{3,2,1,0:T(8,128)(2,1)} %param.8) | copy-start | bytes 884740
  0.0 8.3 %copy-start.5 = (bf16[4,64,128]{2,1,0:T(8,128)(2,1)S(1)}, bf16[4,64,128]{2,1,0:T(8,128)(2,1)}, u32[]{:S(2)}) copy-start(bf16[4,64,128]{2,1,0:T(8,128)(2,1)} %param.6) | copy-start | bytes 196612
  0.8 5.1 %collective-permute-start = (bf16[4,2,128]{2,1,0:T(2,128)(2,1)S(1)}, bf16[4,2,128]{2,1,0:T(2,128)(2,1)S(1)}, u32[]{:S(2)}, u32[]{:S(2)}) collective-permute-start(bf16[4,2,128]{2,1,0:T(2,128)(2,1)S(1)} %get-tuple-element.61), channel_id=1, source_target_pairs={{0,1},{1,2},{2,3},{4,5},{5,6},{6,7},{8,9},{9,10},{10,11},{12,13},{... | collective-permute-start | bytes 6152 | tf_op jit(solution)/shard_map/ppermute | solution.py:19
  3.1 5.2 %collective-permute-start.1 = (bf16[4,2,128]{2,1,0:T(2,128)(2,1)S(1)}, bf16[4,2,128]{2,1,0:T(2,128)(2,1)S(1)}, u32[]{:S(2)}, u32[]{:S(2)}) collective-permute-start(bf16[4,2,128]{2,1,0:T(2,128)(2,1)S(1)} %get-tuple-element.62), channel_id=1, source_target_pairs={{1,0},{2,1},{3,2},{5,4},{6,5},{7,6},{9,8},{10,9},{11,10},{13,12},{... | collective-permute-start | bytes 6152 | tf_op jit(solution)/shard_map/ppermute | solution.py:22
  5.2 0.7 %copy-start.6 = (bf16[2,3,3,128]{3,0,2,1:T(2,128)(2,1)S(1)}, bf16[2,3,3,128]{3,0,2,1:T(2,128)(2,1)}, u32[]{:S(2)}) copy-start(bf16[2,3,3,128]{3,0,2,1:T(2,128)(2,1)} %param.11) | copy-start | bytes 13828
  8.3 17.9 %collective-permute-start.4 = (bf16[2048,128]{1,0:T(8,128)(2,1)}, bf16[2048,128]{1,0:T(8,128)(2,1)S(1)}, u32[]{:S(2)}, u32[]{:S(2)}) collective-permute-start(bf16[2048,128]{1,0:T(8,128)(2,1)} %refs_1_), channel_id=1, source_target_pairs={{0,2},{1,3},{2,0},{3,1},{4,6},{5,7},{6,4},{7,5},{8,10},{9,11},{10,... | collective-permute-start | bytes 1572872 | tf_op jit(solution)/shard_map/ppermute | solution.py:179
  10.9 5.0 %collective-permute-start.2 = (bf16[2,68,128]{2,1,0:T(8,128)(2,1)S(1)}, bf16[2,68,128]{2,1,0:T(8,128)(2,1)S(1)}, u32[]{:S(2)}, u32[]{:S(2)}) collective-permute-start(bf16[2,68,128]{2,1,0:T(8,128)(2,1)S(1)} %get-tuple-element.59), channel_id=1, source_target_pairs={{0,4},{4,8},{8,12},{12,16},{16,20},{20,24},{24,28},{1,5},{5,9},{9,... | collective-permute-start | bytes 104456 | tf_op jit(solution)/shard_map/ppermute | solution.py:19
  14.3 5.9 %collective-permute-start.3 = (bf16[2,68,128]{2,1,0:T(8,128)(2,1)S(1)}, bf16[2,68,128]{2,1,0:T(8,128)(2,1)S(1)}, u32[]{:S(2)}, u32[]{:S(2)}) collective-permute-start(bf16[2,68,128]{2,1,0:T(8,128)(2,1)S(1)} %get-tuple-element.60), channel_id=1, source_target_pairs={{4,0},{8,4},{12,8},{16,12},{20,16},{24,20},{28,24},{5,1},{9,5},{13... | collective-permute-start | bytes 104456 | tf_op jit(solution)/shard_map/ppermute | solution.py:22
  15.7 10.8 %collective-permute-start.6 = (bf16[2048,128]{1,0:T(8,128)(2,1)}, bf16[2048,128]{1,0:T(8,128)(2,1)S(1)}, u32[]{:S(2)}, u32[]{:S(2)}) collective-permute-start(bf16[2048,128]{1,0:T(8,128)(2,1)} %refs_1_), channel_id=1, source_target_pairs={{0,1},{1,0},{2,3},{3,2},{4,5},{5,4},{6,7},{7,6},{8,9},{9,8},{10,11... | collective-permute-start | bytes 1572872 | tf_op jit(solution)/shard_map/ppermute | solution.py:176
  26.2 0.8 %copy-start.2 = (bf16[2048,128]{1,0:T(8,128)(2,1)}, bf16[2048,128]{1,0:T(8,128)(2,1)S(1)}, u32[]{:S(2)}) copy-start(bf16[2048,128]{1,0:T(8,128)(2,1)S(1)} %collective-permute-done.4.refs_2_) | copy-start | bytes 1572868
  26.2 7.8 %collective-permute-start.5 = (bf16[2048,128]{1,0:T(8,128)(2,1)S(1)}, bf16[2048,128]{1,0:T(8,128)(2,1)S(1)}, u32[]{:S(2)}, u32[]{:S(2)}) collective-permute-start(bf16[2048,128]{1,0:T(8,128)(2,1)S(1)} %collective-permute-done.4.refs_2_), channel_id=1, source_target_pairs={{0,1},{1,0},{2,3},{3,2},{4,5},{5,4},{6,7},{7,6},{8,9},{9,8},{10,11... | collective-permute-start | bytes 1572872 | tf_op jit(solution)/shard_map/ppermute | solution.py:206
  27.0 0.8 %copy-start.3 = (bf16[2048,128]{1,0:T(8,128)(2,1)}, bf16[2048,128]{1,0:T(8,128)(2,1)S(1)}, u32[]{:S(2)}) copy-start(bf16[2048,128]{1,0:T(8,128)(2,1)S(1)} %collective-permute-done.6.refs_1_) | copy-start | bytes 1572868
  34.0 0.8 %copy-start.1 = (bf16[2048,128]{1,0:T(8,128)(2,1)}, bf16[2048,128]{1,0:T(8,128)(2,1)S(1)}, u32[]{:S(2)}) copy-start(bf16[2048,128]{1,0:T(8,128)(2,1)S(1)} %collective-permute-done.5.refs_1_) | copy-start | bytes 1572868
  40.3 1.9 %copy-start.4 = (f32[544,128]{1,0:T(8,128)S(1)}, f32[544,128]{1,0:T(8,128)}, u32[]{:S(2)}) copy-start(f32[544,128]{1,0:T(8,128)} %get-tuple-element.35) | copy-start | bytes 835588
  42.5 0.7 %copy-start.7 = (pred[8,9]{0,1:T(8,128)(4,1)S(1)}, pred[8,9]{0,1:T(8,128)(4,1)}, u32[]{:S(2)}) copy-start(pred[8,9]{0,1:T(8,128)(4,1)} %constant.75) | copy-start | bytes 220

commit v18 on v17

--- a/solution.py
+++ b/solution.py
@@ -192,7 +192,7 @@
     pending = None
     whole_rows = tk % width == 0
     if whole_rows and n > 1:
-        groups = [[0]] + ([[1, 2]] if n > 2 else [[1]]) + [[i] for i in range(3, n)]
+        groups = [[i, i + 1] for i in range(0, n, 2)]
     else:
         groups = [[i] for i in range(n)]
     for group in groups:

time: 46 us -> 44.8 us (0.974)
  Pallas kernels: 16.4 us -> 14.5 us
  waiting for transfers between devices: 6.84 us -> 8.47 us
  local copies, waits for them, and re-layouts: 8.14 us -> 7.05 us
    ppermute x1, starting transfers between devices: 0.03 us -> 2.42 us  [match(): shards.append((lax.ppermute(targets, 'match', sibling), me ^ 1, None))]
    ppermute x1, starting transfers between devices: 2.53 us -> 0.2 us  [match(): moved = lax.ppermute(targets, 'match', hop)]
    pallas_call x3 -> x2, Pallas kernels: 16.4 us -> 14.5 us  [match_step(): pl.pallas_call(kernel, grid=(nq,), in_specs=in_specs, out_specs=out_specs...]
    ppermute x1, waiting for transfers between devices: 0.01 us -> 1.59 us  [match(): pending = lax.ppermute(key, 'match', forward)]
    unnamed x17, local copies, waits for them, and re-layouts: 3.49 us -> 2.38 us
  transfers between devices with their start and end apart: 7 -> 7, of which waited for: 3 -> 4; matrix products, arithmetic and copies ran while one was open for 5% -> 6% of each run, Pallas kernels for 24% -> 18%
where the time goes in v18:
time: 44.8 us; the launch traced here: 44.3 us
  Pallas kernels  14.5 us (32%)
  starting transfers between devices  11 us (25%)
  waiting for transfers between devices  8.47 us (19%)
  local copies, waits for them, and re-layouts  7.05 us (16%)
  other arithmetic  2.05 us (5%)
  matrix products  1.13 us (3%)
    pallas_call x2, Pallas kernels, match_step(): pl.pallas_call(kernel, grid=(nq,), in_specs=in_specs, out_specs=out_specs...  14.5 us
    ppermute x2, waiting for transfers between devices, extended(): lax.ppermute(lax.slice_in_dim(block, 0, width, axis=dim), axis, backward)  6.64 us
    ppermute x2, starting transfers between devices, extended(): lax.ppermute(lax.slice_in_dim(block, block.shape[dim] - width, None, axis...  5.77 us
    ppermute x2, starting transfers between devices, extended(): lax.ppermute(lax.slice_in_dim(block, 0, width, axis=dim), axis, backward)  2.58 us
    ppermute x1, starting transfers between devices, match(): shards.append((lax.ppermute(targets, 'match', sibling), me ^ 1, None))  2.42 us
    unnamed x17, local copies, waits for them, and re-layouts  2.38 us
    ppermute x1, waiting for transfers between devices, match(): pending = lax.ppermute(key, 'match', forward)  1.59 us
    slice x1, local copies, waits for them, and re-layouts, match(): return (warped[:count], flow[:count, 0], flow[:count, 1])  1.42 us
  transfers between devices with their start and end apart: 7, of which 4 were waited for; matrix products, arithmetic and copies ran while one was open for 6% of the time, Pallas kernels for 18%

profile of v18, /device:TPU:0, one launch (start us, length us, event | category | flops | bytes accessed | tf_op | source)
XLA Modules:
  0.0 44.3 jit_solution(691193898691543235)
XLA Ops:
  0.0 0.0 copy-start
  0.0 0.8 %fusion.25 = (bf16[4,2,128]{2,1,0:T(2,128)(2,1)S(1)}, bf16[4,2,128]{2,1,0:T(2,128)(2,1)S(1)}) fusion(bf16[4,64,128]{2,1,0:T(8,128)(2,1)} %param.6), kind=kLoop, calls=%fused_computation.53 | loop fusion | bytes 8192 | tf_op jit(solution)/shard_map/slice | solution.py:20
  0.8 2.3 %collective-permute-start = (bf16[4,2,128]{2,1,0:T(2,128)(2,1)S(1)}, bf16[4,2,128]{2,1,0:T(2,128)(2,1)S(1)}, u32[]{:S(2)}, u32[]{:S(2)}) collective-permute-start(bf16[4,2,128]{2,1,0:T(2,128)(2,1)S(1)} %get-tuple-element.55), channel_id=1, source_target_pairs={{0,1},{1,2},{2,3},{4,5},{5,6},{6,7},{8,9},{9,10},{10,11},{12,13},{... | collective-permute-start | bytes 6152 | tf_op jit(solution)/shard_map/ppermute | solution.py:19
  3.1 1.3 %collective-permute-start.1 = (bf16[4,2,128]{2,1,0:T(2,128)(2,1)S(1)}, bf16[4,2,128]{2,1,0:T(2,128)(2,1)S(1)}, u32[]{:S(2)}, u32[]{:S(2)}) collective-permute-start(bf16[4,2,128]{2,1,0:T(2,128)(2,1)S(1)} %get-tuple-element.56), channel_id=1, source_target_pairs={{1,0},{2,1},{3,2},{5,4},{6,5},{7,6},{9,8},{10,9},{11,10},{13,12},{... | collective-permute-start | bytes 6152 | tf_op jit(solution)/shard_map/ppermute | solution.py:22
  4.5 0.7 %pad_maximum_fusion.2 = f32[3,128]{1,0:T(4,128)S(1)} fusion(f32[1,128]{1,0:T(1,128)} %bitcast.114, f32[2,128]{1,0:T(2,128)} %param.9), kind=kLoop, calls=%fused_computation.31 | loop fusion | flops 384 | bytes 3072 | tf_op jit(solution)/shard_map/concatenate | solution.py:229
  5.2 0.7 %copy-done.6 = bf16[2,3,3,128]{3,0,2,1:T(2,128)(2,1)S(1)} copy-done((bf16[2,3,3,128]{3,0,2,1:T(2,128)(2,1)S(1)}, bf16[2,3,3,128]{3,0,2,1:T(2,128)(2,1)}, u32[]{:S(2)}) %copy-start.6) | copy-done | bytes 4632
  5.9 0.0 collective-permute-done
  5.9 2.4 %collective-permute-done.1 = bf16[4,2,128]{2,1,0:T(2,128)(2,1)S(1)} collective-permute-done((bf16[4,2,128]{2,1,0:T(2,128)(2,1)S(1)}, bf16[4,2,128]{2,1,0:T(2,128)(2,1)S(1)}, u32[]{:S(2)}, u32[]{:S(2)}) %collective-permute-start.1) | collective-permute-done | bytes 2080 | tf_op jit(solution)/shard_map/ppermute | solution.py:22
  8.3 2.4 %collective-permute-start.5 = (bf16[2048,128]{1,0:T(8,128)(2,1)}, bf16[2048,128]{1,0:T(8,128)(2,1)S(1)}, u32[]{:S(2)}, u32[]{:S(2)}) collective-permute-start(bf16[2048,128]{1,0:T(8,128)(2,1)} %refs_1_), channel_id=1, source_target_pairs={{0,1},{1,0},{2,3},{3,2},{4,5},{5,4},{6,7},{7,6},{8,9},{9,8},{10,11... | collective-permute-start | bytes 1572872 | tf_op jit(solution)/shard_map/ppermute | solution.py:176
  10.7 0.2 collective-permute-start.4
  11.0 3.4 %collective-permute-start.2 = (bf16[2,68,128]{2,1,0:T(8,128)(2,1)S(1)}, bf16[2,68,128]{2,1,0:T(8,128)(2,1)S(1)}, u32[]{:S(2)}, u32[]{:S(2)}) collective-permute-start(bf16[2,68,128]{2,1,0:T(8,128)(2,1)S(1)} %get-tuple-element.53), channel_id=1, source_target_pairs={{0,4},{4,8},{8,12},{12,16},{16,20},{20,24},{24,28},{1,5},{5,9},{9,... | collective-permute-start | bytes 104456 | tf_op jit(solution)/shard_map/ppermute | solution.py:19
  14.4 1.3 %collective-permute-start.3 = (bf16[2,68,128]{2,1,0:T(8,128)(2,1)S(1)}, bf16[2,68,128]{2,1,0:T(8,128)(2,1)S(1)}, u32[]{:S(2)}, u32[]{:S(2)}) collective-permute-start(bf16[2,68,128]{2,1,0:T(8,128)(2,1)S(1)} %get-tuple-element.54), channel_id=1, source_target_pairs={{4,0},{8,4},{12,8},{16,12},{20,16},{24,20},{28,24},{5,1},{9,5},{13... | collective-permute-start | bytes 104456 | tf_op jit(solution)/shard_map/ppermute | solution.py:22
  15.7 0.1 fusion.19
  15.8 0.2 collective-permute-done.2
  16.0 4.2 %collective-permute-done.3 = bf16[2,68,128]{2,1,0:T(8,128)(2,1)S(1)} collective-permute-done((bf16[2,68,128]{2,1,0:T(8,128)(2,1)S(1)}, bf16[2,68,128]{2,1,0:T(8,128)(2,1)S(1)}, u32[]{:S(2)}, u32[]{:S(2)}) %collective-permute-start.3) | collective-permute-done | bytes 34848 | tf_op jit(solution)/shard_map/ppermute | solution.py:22
  20.3 0.7 %reshape.76.refs_0_ = bf16[544,128]{1,0:T(8,128)(2,1)} reshape(bf16[8,68,128]{2,1,0:T(8,128)(2,1)S(1)} %pad_maximum_fusion) | data formatting | bytes 278528 | tf_op jit(solution)/shard_map/reshape | solution.py:236
  21.0 0.0 collective-permute-done.5.refs_2_
  21.0 0.6 %broadcast_in_dim.25.refs_3_ = f32[8,128]{1,0:T(8,128)} broadcast(f32[128]{0:T(128)S(1)} %pad.4), dimensions={1} | broadcast | bytes 4608 | tf_op jit(solution)/shard_map/broadcast_in_dim | solution.py:191
  21.6 0.2 copy-done.1
  21.8 8.1 %shard_map.64 = (f32[544,8]{1,0:T(8,128)}, f32[544,128]{1,0:T(8,128)}, f32[544,8]{1,0:T(8,128)}) custom-call(bf16[544,128]{1,0:T(8,128)(2,1)} %reshape.76.refs_0_, bf16[2048,128]{1,0:T(8,128)(2,1)} %refs_1_, bf16[2048,128]{1,0:T(8,128)(2,1)} %copy-done.1, f32[8,128]{1,0:T(8,128)} %broadcast_in_dim.25.refs_3_), custom_call_target="tpu_custom_call" | custom-call | tf_op jit(solution)/shard_map/pallas_call | solution.py:151
  29.8 0.0 collective-permute-done.4.refs_1_
  29.8 0.0 collective-permute-start.6
  29.9 0.1 broadcast_and_fusion
  29.9 0.1 slice.131
  30.0 0.1 copy.25
  30.2 1.6 %collective-permute-done.6.refs_2_ = bf16[2048,128]{1,0:T(8,128)(2,1)S(1)} collective-permute-done((bf16[2048,128]{1,0:T(8,128)(2,1)S(1)}, bf16[2048,128]{1,0:T(8,128)(2,1)S(1)}, u32[]{:S(2)}, u32[]{:S(2)}) %collective-permute-start.6) | collective-permute-done | bytes 524320 | tf_op jit(solution)/shard_map/ppermute | solution.py:206
  31.8 0.8 %copy-done.3 = bf16[2048,128]{1,0:T(8,128)(2,1)} copy-done((bf16[2048,128]{1,0:T(8,128)(2,1)}, bf16[2048,128]{1,0:T(8,128)(2,1)S(1)}, u32[]{:S(2)}) %copy-start.3) | copy-done | bytes 524312
  32.6 6.4 %shard_map.65 = (f32[544,128]{1,0:T(8,128)}, f32[544,8]{1,0:T(8,128)}) custom-call(bf16[544,128]{1,0:T(8,128)(2,1)} %reshape.76.refs_0_, bf16[2048,128]{1,0:T(8,128)(2,1)} %copy-done.2, bf16[2048,128]{1,0:T(8,128)(2,1)} %copy-done.3, f32[8,128]{1,0:T(8,128)} %broadcast_in_dim.25.refs_3_, f32[544,8]{1,0:T(8,128)} %get-tuple-element.25.refs_4_, ...), custom_call_target="tpu_custom_call" | custom-call | tf_op jit(solution)/shard_map/pallas_call | solution.py:151
  39.0 1.4 %slice_reduce_fusion.1 = (f32[544]{0:T(1024)S(1)}, f32[544]{0:T(1024)S(1)}) fusion(f32[544,8]{1,0:T(8,128)} %get-tuple-element.28), kind=kLoop, calls=%fused_computation.8 | loop fusion | bytes 8704 | tf_op jit(solution)/shard_map/slice | solution.py:219
  40.4 0.1 reshape_squeeze.6
  40.5 0.1 slice.132
  40.5 0.1 reshape_squeeze.7
  40.6 0.1 broadcast_subtract_fusion
  40.7 0.1 slice.134
  40.8 0.1 slice_bitcast_fusion.1
  40.9 0.1 select_bitcast_fusion
  41.0 0.1 copy.67
  41.1 0.1 copy.28
  41.2 0.0 copy-start.7
  41.2 0.6 %copy-done.7 = pred[8,9]{0,1:T(8,128)(4,1)S(1)} copy-done((pred[8,9]{0,1:T(8,128)(4,1)S(1)}, pred[8,9]{0,1:T(8,128)(4,1)}, u32[]{:S(2)}) %copy-start.7) | copy-done | bytes 96
  41.9 0.9 %convolution_select_fusion = f32[6,8,9,128]{3,1,2,0:T(8,128)S(1)} fusion(bf16[3,3,128,128]{3,2,1,0:T(8,128)(2,1)S(1)} %copy-done, f32[8,1,7,2,128]{4,2,3,0,1:T(8,128)S(1)} %slice.157, f32[8,1,8,9,128]{4,2,3,0,1:T(8,128)S(1)} %copy.28, pred[8,9]{0,1:T(8,128)(4,1)S(1)} %copy-done.7), kind=kOutput, calls=%fused_computation | convolution fusion | flops 764737536 | bytes 868424 | tf_op jit(solution)/shard_map/conv_general_dilated | solution.py:247
  42.8 0.1 copy.29
  42.9 0.1 copy.30
  43.0 0.1 copy.31
  43.1 0.3 broadcast_select_fusion
  43.4 0.2 fusion.9
  43.6 0.1 fusion.23
  43.7 0.6 %maximum_add_fusion = f32[2,4,64]{2,1,0:T(4,128)} fusion(f32[1,4,64]{2,1,0:T(4,128)S(1)} %get-tuple-element.60, f32[1,4,64]{2,1,0:T(4,128)S(1)} %get-tuple-element.61, f32[1,4,64]{2,1,0:T(4,128)S(1)} %bitcast.110, f32[1,4,64]{2,1,0:T(4,128)S(1)} %bitcast.111, f32[1,4,64]{2,1,0:T(4,128)S(1)} %bitcast.108, f32[1,4,64]{2,1,0:T(4,128)S(1)} %bitcast.109, ...), kind=kLoop, calls=%fused_computation.22 | loop fusion | flops 9728 | bytes 22528 | tf_op jit(solution)/shard_map/add | solution.py:266
  (25 shorter events, 0.2 us)
Async XLA Ops:
  0.0 41.2 %copy-start = (bf16[3,3,128,128]{3,2,1,0:T(8,128)(2,1)S(1)}, bf16[3,3,128,128]{3,2,1,0:T(8,128)(2,1)}, u32[]{:S(2)}) copy-start(bf16[3,3,128,128]{3,2,1,0:T(8,128)(2,1)} %param.8) | copy-start | bytes 884740
  0.0 8.3 %copy-start.5 = (bf16[4,64,128]{2,1,0:T(8,128)(2,1)S(1)}, bf16[4,64,128]{2,1,0:T(8,128)(2,1)}, u32[]{:S(2)}) copy-start(bf16[4,64,128]{2,1,0:T(8,128)(2,1)} %param.6) | copy-start | bytes 196612
  0.8 5.1 %collective-permute-start = (bf16[4,2,128]{2,1,0:T(2,128)(2,1)S(1)}, bf16[4,2,128]{2,1,0:T(2,128)(2,1)S(1)}, u32[]{:S(2)}, u32[]{:S(2)}) collective-permute-start(bf16[4,2,128]{2,1,0:T(2,128)(2,1)S(1)} %get-tuple-element.55), channel_id=1, source_target_pairs={{0,1},{1,2},{2,3},{4,5},{5,6},{6,7},{8,9},{9,10},{10,11},{12,13},{... | collective-permute-start | bytes 6152 | tf_op jit(solution)/shard_map/ppermute | solution.py:19
  3.1 5.2 %collective-permute-start.1 = (bf16[4,2,128]{2,1,0:T(2,128)(2,1)S(1)}, bf16[4,2,128]{2,1,0:T(2,128)(2,1)S(1)}, u32[]{:S(2)}, u32[]{:S(2)}) collective-permute-start(bf16[4,2,128]{2,1,0:T(2,128)(2,1)S(1)} %get-tuple-element.56), channel_id=1, source_target_pairs={{1,0},{2,1},{3,2},{5,4},{6,5},{7,6},{9,8},{10,9},{11,10},{13,12},{... | collective-permute-start | bytes 6152 | tf_op jit(solution)/shard_map/ppermute | solution.py:22
  5.2 0.7 %copy-start.6 = (bf16[2,3,3,128]{3,0,2,1:T(2,128)(2,1)S(1)}, bf16[2,3,3,128]{3,0,2,1:T(2,128)(2,1)}, u32[]{:S(2)}) copy-start(bf16[2,3,3,128]{3,0,2,1:T(2,128)(2,1)} %param.11) | copy-start | bytes 13828
  8.3 12.6 %collective-permute-start.5 = (bf16[2048,128]{1,0:T(8,128)(2,1)}, bf16[2048,128]{1,0:T(8,128)(2,1)S(1)}, u32[]{:S(2)}, u32[]{:S(2)}) collective-permute-start(bf16[2048,128]{1,0:T(8,128)(2,1)} %refs_1_), channel_id=1, source_target_pairs={{0,1},{1,0},{2,3},{3,2},{4,5},{5,4},{6,7},{7,6},{8,9},{9,8},{10,11... | collective-permute-start | bytes 1572872 | tf_op jit(solution)/shard_map/ppermute | solution.py:176
  10.7 19.1 %collective-permute-start.4 = (bf16[2048,128]{1,0:T(8,128)(2,1)}, bf16[2048,128]{1,0:T(8,128)(2,1)S(1)}, u32[]{:S(2)}, u32[]{:S(2)}) collective-permute-start(bf16[2048,128]{1,0:T(8,128)(2,1)} %refs_1_), channel_id=1, source_target_pairs={{0,2},{1,3},{2,0},{3,1},{4,6},{5,7},{6,4},{7,5},{8,10},{9,11},{10,... | collective-permute-start | bytes 1572872 | tf_op jit(solution)/shard_map/ppermute | solution.py:179
  11.0 5.0 %collective-permute-start.2 = (bf16[2,68,128]{2,1,0:T(8,128)(2,1)S(1)}, bf16[2,68,128]{2,1,0:T(8,128)(2,1)S(1)}, u32[]{:S(2)}, u32[]{:S(2)}) collective-permute-start(bf16[2,68,128]{2,1,0:T(8,128)(2,1)S(1)} %get-tuple-element.53), channel_id=1, source_target_pairs={{0,4},{4,8},{8,12},{12,16},{16,20},{20,24},{24,28},{1,5},{5,9},{9,... | collective-permute-start | bytes 104456 | tf_op jit(solution)/shard_map/ppermute | solution.py:19
  14.4 5.9 %collective-permute-start.3 = (bf16[2,68,128]{2,1,0:T(8,128)(2,1)S(1)}, bf16[2,68,128]{2,1,0:T(8,128)(2,1)S(1)}, u32[]{:S(2)}, u32[]{:S(2)}) collective-permute-start(bf16[2,68,128]{2,1,0:T(8,128)(2,1)S(1)} %get-tuple-element.54), channel_id=1, source_target_pairs={{4,0},{8,4},{12,8},{16,12},{20,16},{24,20},{28,24},{5,1},{9,5},{13... | collective-permute-start | bytes 104456 | tf_op jit(solution)/shard_map/ppermute | solution.py:22
  21.0 0.8 %copy-start.1 = (bf16[2048,128]{1,0:T(8,128)(2,1)}, bf16[2048,128]{1,0:T(8,128)(2,1)S(1)}, u32[]{:S(2)}) copy-start(bf16[2048,128]{1,0:T(8,128)(2,1)S(1)} %collective-permute-done.5.refs_2_) | copy-start | bytes 1572868
  29.8 1.9 %copy-start.2 = (bf16[2048,128]{1,0:T(8,128)(2,1)}, bf16[2048,128]{1,0:T(8,128)(2,1)S(1)}, u32[]{:S(2)}) copy-start(bf16[2048,128]{1,0:T(8,128)(2,1)S(1)} %collective-permute-done.4.refs_1_) | copy-start | bytes 1572868
  29.8 1.9 %collective-permute-start.6 = (bf16[2048,128]{1,0:T(8,128)(2,1)S(1)}, bf16[2048,128]{1,0:T(8,128)(2,1)S(1)}, u32[]{:S(2)}, u32[]{:S(2)}) collective-permute-start(bf16[2048,128]{1,0:T(8,128)(2,1)S(1)} %collective-permute-done.4.refs_1_), channel_id=1, source_target_pairs={{0,1},{1,0},{2,3},{3,2},{4,5},{5,4},{6,7},{7,6},{8,9},{9,8},{10,11... | collective-permute-start | bytes 1572872 | tf_op jit(solution)/shard_map/ppermute | solution.py:206
  31.8 0.8 %copy-start.3 = (bf16[2048,128]{1,0:T(8,128)(2,1)}, bf16[2048,128]{1,0:T(8,128)(2,1)S(1)}, u32[]{:S(2)}) copy-start(bf16[2048,128]{1,0:T(8,128)(2,1)S(1)} %collective-permute-done.6.refs_2_) | copy-start | bytes 1572868
  39.0 1.9 %copy-start.4 = (f32[544,128]{1,0:T(8,128)S(1)}, f32[544,128]{1,0:T(8,128)}, u32[]{:S(2)}) copy-start(f32[544,128]{1,0:T(8,128)} %get-tuple-element.29) | copy-start | bytes 835588
  41.2 0.7 %copy-start.7 = (pred[8,9]{0,1:T(8,128)(4,1)S(1)}, pred[8,9]{0,1:T(8,128)(4,1)}, u32[]{:S(2)}) copy-start(pred[8,9]{0,1:T(8,128)(4,1)} %constant.75) | copy-start | bytes 220

commit v19 on v18

--- a/solution.py
+++ b/solution.py
@@ -158,7 +158,28 @@
     )(*args)
 
 
-def match(queries, targets, width):
+def shard_owners(n, me):
+    if n % 2:
+        return [(me - shift) % n for shift in range(n)]
+    chips = n // 2
+    owners = [me, me ^ 1]
+    for shift in range(1, chips):
+        owner = ((me // 2 - shift) % chips) * 2 + me % 2
+        owners += [owner, owner ^ 1]
+    return owners
+
+
+def row_table(targets, width):
+    n = lax.axis_size("match")
+    tk = targets.shape[0]
+    if tk % width:
+        return None
+    owners = jnp.stack(shard_owners(n, lax.axis_index("match"))) * (tk // width)
+    owners = jnp.pad(owners.astype(jnp.float32), (0, 128 - n))
+    return jnp.broadcast_to(owners[None, :], (8, 128))
+
+
+def match(queries, targets, width, table):
     count, chans = queries.shape
     tk = targets.shape[0]
     cap = max(8, (1024 * 2048 // tk) // 8 * 8)
@@ -185,10 +206,6 @@
             moved = lax.ppermute(targets, "match", [(j, (j + shift) % n) for j in range(n)])
             shards.append((moved, (me - shift) % n, None))
     state = None
-    if tk % width == 0:
-        owners = jnp.stack([owner for _, owner, _ in shards]) * (tk // width)
-        owners = jnp.pad(owners.astype(jnp.float32), (0, 128 - n))
-        table = jnp.broadcast_to(owners[None, :], (8, 128))
     pending = None
     whole_rows = tk % width == 0
     if whole_rows and n > 1:
@@ -228,12 +245,13 @@
     ext = extended(source, (("match", 1),), HALO)
     small = jnp.concatenate([flow_proj, in_bias[None, :]], axis=0)
     taps = jnp.transpose(conv_out, (3, 0, 1, 2)).reshape(chans, -1)
-    targets, ext, conv_in, small, taps = lax.optimization_barrier(
-        (targets, ext, conv_in, small, taps)
+    table = row_table(targets, width)
+    targets, ext, conv_in, small, taps, table = lax.optimization_barrier(
+        (targets, ext, conv_in, small, taps, table)
     )
     ext = extended(ext, (("space", 0),), HALO)
     erows, ecols = rows + 2 * HALO, cols + 2 * HALO
-    warped, sum_x, sum_y = match(ext.reshape(erows * ecols, chans), targets, width)
+    warped, sum_x, sum_y = match(ext.reshape(erows * ecols, chans), targets, width, table)
     warped = warped.reshape(erows, ecols, chans)
     grow = row_first - HALO + jnp.arange(erows, dtype=jnp.int32)
     gcol = col_first - HALO + jnp.arange(ecols, dtype=jnp.int32)

time: 44.8 us -> 45.5 us (1.016)
  local copies, waits for them, and re-layouts: 7.05 us -> 8.2 us
  other arithmetic: 2.05 us -> 1.35 us
    unnamed x17 -> x21, local copies, waits for them, and re-layouts: 2.38 us -> 3.59 us
    concatenate x1, other arithmetic: 0.71 us -> 0.01 us  [local(): small = jnp.concatenate([flow_proj, in_bias[None, :]], axis=0)]
  transfers between devices with their start and end apart: 7 -> 7, of which waited for: 4 -> 4; matrix products, arithmetic and copies ran while one was open for 6% -> 3% of each run, Pallas kernels for 18% -> 18%
where the time goes in v19:
time: 45.5 us; the launch traced here: 45 us
  Pallas kernels  14.5 us (32%)
  starting transfers between devices  11 us (24%)
  waiting for transfers between devices  8.52 us (19%)
  local copies, waits for them, and re-layouts  8.2 us (18%)
  other arithmetic  1.35 us (3%)
  matrix products  1.13 us (2%)
    pallas_call x2, Pallas kernels, match_step(): pl.pallas_call(kernel, grid=(nq,), in_specs=in_specs, out_specs=out_specs...  14.5 us
    ppermute x2, waiting for transfers between devices, extended(): lax.ppermute(lax.slice_in_dim(block, 0, width, axis=dim), axis, backward)  6.62 us
    ppermute x2, starting transfers between devices, extended(): lax.ppermute(lax.slice_in_dim(block, block.shape[dim] - width, None, axis...  5.77 us
    unnamed x21, local copies, waits for them, and re-layouts  3.59 us
    ppermute x2, starting transfers between devices, extended(): lax.ppermute(lax.slice_in_dim(block, 0, width, axis=dim), axis, backward)  2.72 us
    ppermute x1, starting transfers between devices, match(): shards.append((lax.ppermute(targets, 'match', sibling), me ^ 1, None))  2.35 us
    ppermute x1, waiting for transfers between devices, match(): pending = lax.ppermute(key, 'match', forward)  1.59 us
    slice x1, local copies, waits for them, and re-layouts, match(): return (warped[:count], flow[:count, 0], flow[:count, 1])  1.42 us
  transfers between devices with their start and end apart: 7, of which 4 were waited for; matrix products, arithmetic and copies ran while one was open for 3% of the time, Pallas kernels for 18%

profile of v19, /device:TPU:0, one launch (start us, length us, event | category | flops | bytes accessed | tf_op | source)
XLA Modules:
  0.0 45.0 jit_solution(8570073463881648351)
XLA Ops:
  0.0 0.8 %fusion.25 = (bf16[4,2,128]{2,1,0:T(2,128)(2,1)S(1)}, bf16[4,2,128]{2,1,0:T(2,128)(2,1)S(1)}) fusion(bf16[4,64,128]{2,1,0:T(8,128)(2,1)} %param.6), kind=kLoop, calls=%fused_computation.53 | loop fusion | bytes 8192 | tf_op jit(solution)/shard_map/slice | solution.py:20
  0.8 2.3 %collective-permute-start = (bf16[4,2,128]{2,1,0:T(2,128)(2,1)S(1)}, bf16[4,2,128]{2,1,0:T(2,128)(2,1)S(1)}, u32[]{:S(2)}, u32[]{:S(2)}) collective-permute-start(bf16[4,2,128]{2,1,0:T(2,128)(2,1)S(1)} %get-tuple-element.57), channel_id=1, source_target_pairs={{0,1},{1,2},{2,3},{4,5},{5,6},{6,7},{8,9},{9,10},{10,11},{12,13},{... | collective-permute-start | bytes 6152 | tf_op jit(solution)/shard_map/ppermute | solution.py:19
  3.1 0.0 copy-start.5
  3.1 1.4 %collective-permute-start.1 = (bf16[4,2,128]{2,1,0:T(2,128)(2,1)S(1)}, bf16[4,2,128]{2,1,0:T(2,128)(2,1)S(1)}, u32[]{:S(2)}, u32[]{:S(2)}) collective-permute-start(bf16[4,2,128]{2,1,0:T(2,128)(2,1)S(1)} %get-tuple-element.58), channel_id=1, source_target_pairs={{1,0},{2,1},{3,2},{5,4},{6,5},{7,6},{9,8},{10,9},{11,10},{13,12},{... | collective-permute-start | bytes 6152 | tf_op jit(solution)/shard_map/ppermute | solution.py:22
  4.6 0.0 copy-start.7
  4.6 0.0 copy-start.8
  4.6 0.7 %copy-done.7 = f32[2,128]{1,0:T(2,128)S(1)} copy-done((f32[2,128]{1,0:T(2,128)S(1)}, f32[2,128]{1,0:T(2,128)}, u32[]{:S(2)}) %copy-start.7) | copy-done | bytes 1048
  5.3 0.0 copy-start.6
  5.3 0.1 fusion.19
  5.4 0.6 %copy-done.6 = bf16[2,3,3,128]{3,0,2,1:T(2,128)(2,1)S(1)} copy-done((bf16[2,3,3,128]{3,0,2,1:T(2,128)(2,1)S(1)}, bf16[2,3,3,128]{3,0,2,1:T(2,128)(2,1)}, u32[]{:S(2)}) %copy-start.6) | copy-done | bytes 4632
  6.0 2.4 %collective-permute-done.1 = bf16[4,2,128]{2,1,0:T(2,128)(2,1)S(1)} collective-permute-done((bf16[4,2,128]{2,1,0:T(2,128)(2,1)S(1)}, bf16[4,2,128]{2,1,0:T(2,128)(2,1)S(1)}, u32[]{:S(2)}, u32[]{:S(2)}) %collective-permute-start.1) | collective-permute-done | bytes 2080 | tf_op jit(solution)/shard_map/ppermute | solution.py:22
  8.5 0.6 %broadcast_in_dim.25.refs_3_ = f32[8,128]{1,0:T(8,128)} broadcast(f32[128]{0:T(128)S(1)} %pad.4), dimensions={1} | broadcast | bytes 4608 | tf_op jit(solution)/shard_map/broadcast_in_dim | solution.py:179
  9.1 2.4 %collective-permute-start.5 = (bf16[2048,128]{1,0:T(8,128)(2,1)}, bf16[2048,128]{1,0:T(8,128)(2,1)S(1)}, u32[]{:S(2)}, u32[]{:S(2)}) collective-permute-start(bf16[2048,128]{1,0:T(8,128)(2,1)} %refs_1_), channel_id=1, source_target_pairs={{0,1},{1,0},{2,3},{3,2},{4,5},{5,4},{6,7},{7,6},{8,9},{9,8},{10,11... | collective-permute-start | bytes 1572872 | tf_op jit(solution)/shard_map/ppermute | solution.py:197
  11.4 0.1 collective-permute-start.4
  11.6 3.4 %collective-permute-start.2 = (bf16[2,68,128]{2,1,0:T(8,128)(2,1)S(1)}, bf16[2,68,128]{2,1,0:T(8,128)(2,1)S(1)}, u32[]{:S(2)}, u32[]{:S(2)}) collective-permute-start(bf16[2,68,128]{2,1,0:T(8,128)(2,1)S(1)} %get-tuple-element.55), channel_id=1, source_target_pairs={{0,4},{4,8},{8,12},{12,16},{16,20},{20,24},{24,28},{1,5},{5,9},{9,... | collective-permute-start | bytes 104456 | tf_op jit(solution)/shard_map/ppermute | solution.py:19
  15.0 1.3 %collective-permute-start.3 = (bf16[2,68,128]{2,1,0:T(8,128)(2,1)S(1)}, bf16[2,68,128]{2,1,0:T(8,128)(2,1)S(1)}, u32[]{:S(2)}, u32[]{:S(2)}) collective-permute-start(bf16[2,68,128]{2,1,0:T(8,128)(2,1)S(1)} %get-tuple-element.56), channel_id=1, source_target_pairs={{4,0},{8,4},{12,8},{16,12},{20,16},{24,20},{28,24},{5,1},{9,5},{13... | collective-permute-start | bytes 104456 | tf_op jit(solution)/shard_map/ppermute | solution.py:22
  16.3 0.3 collective-permute-done.2
  16.6 4.2 %collective-permute-done.3 = bf16[2,68,128]{2,1,0:T(8,128)(2,1)S(1)} collective-permute-done((bf16[2,68,128]{2,1,0:T(8,128)(2,1)S(1)}, bf16[2,68,128]{2,1,0:T(8,128)(2,1)S(1)}, u32[]{:S(2)}, u32[]{:S(2)}) %collective-permute-start.3) | collective-permute-done | bytes 34848 | tf_op jit(solution)/shard_map/ppermute | solution.py:22
  20.9 0.7 %reshape.76.refs_0_ = bf16[544,128]{1,0:T(8,128)(2,1)} reshape(bf16[8,68,128]{2,1,0:T(8,128)(2,1)S(1)} %pad_maximum_fusion) | data formatting | bytes 278528 | tf_op jit(solution)/shard_map/reshape | solution.py:254
  21.6 0.8 %copy-done.1 = bf16[2048,128]{1,0:T(8,128)(2,1)} copy-done((bf16[2048,128]{1,0:T(8,128)(2,1)}, bf16[2048,128]{1,0:T(8,128)(2,1)S(1)}, u32[]{:S(2)}) %copy-start.1) | copy-done | bytes 524312
  22.4 8.1 %shard_map.64 = (f32[544,8]{1,0:T(8,128)}, f32[544,128]{1,0:T(8,128)}, f32[544,8]{1,0:T(8,128)}) custom-call(bf16[544,128]{1,0:T(8,128)(2,1)} %reshape.76.refs_0_, bf16[2048,128]{1,0:T(8,128)(2,1)} %refs_1_, bf16[2048,128]{1,0:T(8,128)(2,1)} %copy-done.1, f32[8,128]{1,0:T(8,128)} %broadcast_in_dim.25.refs_3_), custom_call_target="tpu_custom_call" | custom-call | tf_op jit(solution)/shard_map/pallas_call | solution.py:151
  30.4 0.0 collective-permute-done.4.refs_1_
  30.5 0.1 broadcast_and_fusion
  30.5 0.1 slice.131
  30.6 0.1 copy.25
  30.8 1.6 %collective-permute-done.6.refs_2_ = bf16[2048,128]{1,0:T(8,128)(2,1)S(1)} collective-permute-done((bf16[2048,128]{1,0:T(8,128)(2,1)S(1)}, bf16[2048,128]{1,0:T(8,128)(2,1)S(1)}, u32[]{:S(2)}, u32[]{:S(2)}) %collective-permute-start.6) | collective-permute-done | bytes 524320 | tf_op jit(solution)/shard_map/ppermute | solution.py:223
  32.4 0.8 %copy-done.3 = bf16[2048,128]{1,0:T(8,128)(2,1)} copy-done((bf16[2048,128]{1,0:T(8,128)(2,1)}, bf16[2048,128]{1,0:T(8,128)(2,1)S(1)}, u32[]{:S(2)}) %copy-start.3) | copy-done | bytes 524312
  33.2 6.4 %shard_map.65 = (f32[544,128]{1,0:T(8,128)}, f32[544,8]{1,0:T(8,128)}) custom-call(bf16[544,128]{1,0:T(8,128)(2,1)} %reshape.76.refs_0_, bf16[2048,128]{1,0:T(8,128)(2,1)} %copy-done.2, bf16[2048,128]{1,0:T(8,128)(2,1)} %copy-done.3, f32[8,128]{1,0:T(8,128)} %broadcast_in_dim.25.refs_3_, f32[544,8]{1,0:T(8,128)} %get-tuple-element.27.refs_4_, ...), custom_call_target="tpu_custom_call" | custom-call | tf_op jit(solution)/shard_map/pallas_call | solution.py:151
  39.6 1.4 %slice_reduce_fusion.1 = (f32[544]{0:T(1024)S(1)}, f32[544]{0:T(1024)S(1)}) fusion(f32[544,8]{1,0:T(8,128)} %get-tuple-element.30), kind=kLoop, calls=%fused_computation.8 | loop fusion | bytes 8704 | tf_op jit(solution)/shard_map/slice | solution.py:236
  41.0 0.1 reshape_squeeze.6
  41.1 0.1 slice.132
  41.1 0.1 reshape_squeeze.7
  41.2 0.1 broadcast_subtract_fusion
  41.3 0.1 slice.134
  41.4 0.1 slice_bitcast_fusion.1
  41.5 0.1 select_bitcast_fusion
  41.6 0.1 copy.67
  41.7 0.1 copy.28
  41.8 0.0 copy-start.9
  41.8 0.6 %copy-done.9 = pred[8,9]{0,1:T(8,128)(4,1)S(1)} copy-done((pred[8,9]{0,1:T(8,128)(4,1)S(1)}, pred[8,9]{0,1:T(8,128)(4,1)}, u32[]{:S(2)}) %copy-start.9) | copy-done | bytes 96
  42.5 0.9 %convolution_select_fusion = f32[6,8,9,128]{3,1,2,0:T(8,128)S(1)} fusion(bf16[3,3,128,128]{3,2,1,0:T(8,128)(2,1)S(1)} %copy-done, f32[8,1,7,2,128]{4,2,3,0,1:T(8,128)S(1)} %slice.157, f32[8,1,8,9,128]{4,2,3,0,1:T(8,128)S(1)} %copy.28, pred[8,9]{0,1:T(8,128)(4,1)S(1)} %copy-done.9), kind=kOutput, calls=%fused_computation | convolution fusion | flops 764737536 | bytes 868424 | tf_op jit(solution)/shard_map/conv_general_dilated | solution.py:265
  43.4 0.1 copy.29
  43.5 0.1 copy.30
  43.6 0.1 copy.31
  43.7 0.3 broadcast_select_fusion
  44.0 0.2 fusion.9
  44.2 0.1 fusion.23
  44.3 0.6 %maximum_add_fusion = f32[2,4,64]{2,1,0:T(4,128)} fusion(f32[1,4,64]{2,1,0:T(4,128)S(1)} %get-tuple-element.62, f32[1,4,64]{2,1,0:T(4,128)S(1)} %get-tuple-element.63, f32[1,4,64]{2,1,0:T(4,128)S(1)} %bitcast.110, f32[1,4,64]{2,1,0:T(4,128)S(1)} %bitcast.111, f32[1,4,64]{2,1,0:T(4,128)S(1)} %bitcast.108, f32[1,4,64]{2,1,0:T(4,128)S(1)} %bitcast.109, ...), kind=kLoop, calls=%fused_computation.22 | loop fusion | flops 9728 | bytes 22528 | tf_op jit(solution)/shard_map/add | solution.py:284
  (29 shorter events, 0.2 us)
Async XLA Ops:
  0.0 41.8 %copy-start = (bf16[3,3,128,128]{3,2,1,0:T(8,128)(2,1)S(1)}, bf16[3,3,128,128]{3,2,1,0:T(8,128)(2,1)}, u32[]{:S(2)}) copy-start(bf16[3,3,128,128]{3,2,1,0:T(8,128)(2,1)} %param.8) | copy-start | bytes 884740
  0.8 5.3 %collective-permute-start = (bf16[4,2,128]{2,1,0:T(2,128)(2,1)S(1)}, bf16[4,2,128]{2,1,0:T(2,128)(2,1)S(1)}, u32[]{:S(2)}, u32[]{:S(2)}) collective-permute-start(bf16[4,2,128]{2,1,0:T(2,128)(2,1)S(1)} %get-tuple-element.57), channel_id=1, source_target_pairs={{0,1},{1,2},{2,3},{4,5},{5,6},{6,7},{8,9},{9,10},{10,11},{12,13},{... | collective-permute-start | bytes 6152 | tf_op jit(solution)/shard_map/ppermute | solution.py:19
  3.1 5.3 %copy-start.5 = (bf16[4,64,128]{2,1,0:T(8,128)(2,1)S(1)}, bf16[4,64,128]{2,1,0:T(8,128)(2,1)}, u32[]{:S(2)}) copy-start(bf16[4,64,128]{2,1,0:T(8,128)(2,1)} %param.6) | copy-start | bytes 196612
  3.1 5.3 %collective-permute-start.1 = (bf16[4,2,128]{2,1,0:T(2,128)(2,1)S(1)}, bf16[4,2,128]{2,1,0:T(2,128)(2,1)S(1)}, u32[]{:S(2)}, u32[]{:S(2)}) collective-permute-start(bf16[4,2,128]{2,1,0:T(2,128)(2,1)S(1)} %get-tuple-element.58), channel_id=1, source_target_pairs={{1,0},{2,1},{3,2},{5,4},{6,5},{7,6},{9,8},{10,9},{11,10},{13,12},{... | collective-permute-start | bytes 6152 | tf_op jit(solution)/shard_map/ppermute | solution.py:22
  4.6 0.7 %copy-start.7 = (f32[2,128]{1,0:T(2,128)S(1)}, f32[2,128]{1,0:T(2,128)}, u32[]{:S(2)}) copy-start(f32[2,128]{1,0:T(2,128)} %param.9) | copy-start | bytes 3076
  4.6 0.7 %copy-start.8 = (f32[128]{0:T(128)S(1)}, f32[128]{0:T(128)}, u32[]{:S(2)}) copy-start(f32[128]{0:T(128)} %param.10) | copy-start | bytes 1540
  5.3 0.7 %copy-start.6 = (bf16[2,3,3,128]{3,0,2,1:T(2,128)(2,1)S(1)}, bf16[2,3,3,128]{3,0,2,1:T(2,128)(2,1)}, u32[]{:S(2)}) copy-start(bf16[2,3,3,128]{3,0,2,1:T(2,128)(2,1)} %param.11) | copy-start | bytes 13828
  9.1 12.5 %collective-permute-start.5 = (bf16[2048,128]{1,0:T(8,128)(2,1)}, bf16[2048,128]{1,0:T(8,128)(2,1)S(1)}, u32[]{:S(2)}, u32[]{:S(2)}) collective-permute-start(bf16[2048,128]{1,0:T(8,128)(2,1)} %refs_1_), channel_id=1, source_target_pairs={{0,1},{1,0},{2,3},{3,2},{4,5},{5,4},{6,7},{7,6},{8,9},{9,8},{10,11... | collective-permute-start | bytes 1572872 | tf_op jit(solution)/shard_map/ppermute | solution.py:197
  11.4 19.0 %collective-permute-start.4 = (bf16[2048,128]{1,0:T(8,128)(2,1)}, bf16[2048,128]{1,0:T(8,128)(2,1)S(1)}, u32[]{:S(2)}, u32[]{:S(2)}) collective-permute-start(bf16[2048,128]{1,0:T(8,128)(2,1)} %refs_1_), channel_id=1, source_target_pairs={{0,2},{1,3},{2,0},{3,1},{4,6},{5,7},{6,4},{7,5},{8,10},{9,11},{10,... | collective-permute-start | bytes 1572872 | tf_op jit(solution)/shard_map/ppermute | solution.py:200
  11.6 5.0 %collective-permute-start.2 = (bf16[2,68,128]{2,1,0:T(8,128)(2,1)S(1)}, bf16[2,68,128]{2,1,0:T(8,128)(2,1)S(1)}, u32[]{:S(2)}, u32[]{:S(2)}) collective-permute-start(bf16[2,68,128]{2,1,0:T(8,128)(2,1)S(1)} %get-tuple-element.55), channel_id=1, source_target_pairs={{0,4},{4,8},{8,12},{12,16},{16,20},{20,24},{24,28},{1,5},{5,9},{9,... | collective-permute-start | bytes 104456 | tf_op jit(solution)/shard_map/ppermute | solution.py:19
  15.0 5.9 %collective-permute-start.3 = (bf16[2,68,128]{2,1,0:T(8,128)(2,1)S(1)}, bf16[2,68,128]{2,1,0:T(8,128)(2,1)S(1)}, u32[]{:S(2)}, u32[]{:S(2)}) collective-permute-start(bf16[2,68,128]{2,1,0:T(8,128)(2,1)S(1)} %get-tuple-element.56), channel_id=1, source_target_pairs={{4,0},{8,4},{12,8},{16,12},{20,16},{24,20},{28,24},{5,1},{9,5},{13... | collective-permute-start | bytes 104456 | tf_op jit(solution)/shard_map/ppermute | solution.py:22
  21.6 0.8 %copy-start.1 = (bf16[2048,128]{1,0:T(8,128)(2,1)}, bf16[2048,128]{1,0:T(8,128)(2,1)S(1)}, u32[]{:S(2)}) copy-start(bf16[2048,128]{1,0:T(8,128)(2,1)S(1)} %collective-permute-done.5.refs_2_) | copy-start | bytes 1572868
  30.5 1.9 %copy-start.2 = (bf16[2048,128]{1,0:T(8,128)(2,1)}, bf16[2048,128]{1,0:T(8,128)(2,1)S(1)}, u32[]{:S(2)}) copy-start(bf16[2048,128]{1,0:T(8,128)(2,1)S(1)} %collective-permute-done.4.refs_1_) | copy-start | bytes 1572868
  30.5 1.9 %collective-permute-start.6 = (bf16[2048,128]{1,0:T(8,128)(2,1)S(1)}, bf16[2048,128]{1,0:T(8,128)(2,1)S(1)}, u32[]{:S(2)}, u32[]{:S(2)}) collective-permute-start(bf16[2048,128]{1,0:T(8,128)(2,1)S(1)} %collective-permute-done.4.refs_1_), channel_id=1, source_target_pairs={{0,1},{1,0},{2,3},{3,2},{4,5},{5,4},{6,7},{7,6},{8,9},{9,8},{10,11... | collective-permute-start | bytes 1572872 | tf_op jit(solution)/shard_map/ppermute | solution.py:223
  32.4 0.8 %copy-start.3 = (bf16[2048,128]{1,0:T(8,128)(2,1)}, bf16[2048,128]{1,0:T(8,128)(2,1)S(1)}, u32[]{:S(2)}) copy-start(bf16[2048,128]{1,0:T(8,128)(2,1)S(1)} %collective-permute-done.6.refs_2_) | copy-start | bytes 1572868
  39.6 1.9 %copy-start.4 = (f32[544,128]{1,0:T(8,128)S(1)}, f32[544,128]{1,0:T(8,128)}, u32[]{:S(2)}) copy-start(f32[544,128]{1,0:T(8,128)} %get-tuple-element.31) | copy-start | bytes 835588
  41.8 0.7 %copy-start.9 = (pred[8,9]{0,1:T(8,128)(4,1)S(1)}, pred[8,9]{0,1:T(8,128)(4,1)}, u32[]{:S(2)}) copy-start(pred[8,9]{0,1:T(8,128)(4,1)} %constant.75) | copy-start | bytes 220

commit v20 on v18

--- a/solution.py
+++ b/solution.py
@@ -226,14 +226,15 @@
     row_first = lax.axis_index("space") * rows
     col_first = lax.axis_index("match") * cols
     ext = extended(source, (("match", 1),), HALO)
+    ext = ext.reshape(rows * (cols + 2 * HALO), chans)
     small = jnp.concatenate([flow_proj, in_bias[None, :]], axis=0)
     taps = jnp.transpose(conv_out, (3, 0, 1, 2)).reshape(chans, -1)
     targets, ext, conv_in, small, taps = lax.optimization_barrier(
         (targets, ext, conv_in, small, taps)
     )
-    ext = extended(ext, (("space", 0),), HALO)
+    ext = extended(ext, (("space", 0),), HALO * (cols + 2 * HALO))
     erows, ecols = rows + 2 * HALO, cols + 2 * HALO
-    warped, sum_x, sum_y = match(ext.reshape(erows * ecols, chans), targets, width)
+    warped, sum_x, sum_y = match(ext, targets, width)
     warped = warped.reshape(erows, ecols, chans)
     grow = row_first - HALO + jnp.arange(erows, dtype=jnp.int32)
     gcol = col_first - HALO + jnp.arange(ecols, dtype=jnp.int32)

time: 44.8 us -> 44.2 us (0.987)
  local copies, waits for them, and re-layouts: 7.05 us -> 6.44 us
    reshape x1, local copies, waits for them, and re-layouts: 0.69 us -> 0.02 us  [local(): ext = ext.reshape(rows * (cols + 2 * HALO), chans)]
    unnamed x17 -> x21, local copies, waits for them, and re-layouts: 2.38 us -> 2.39 us
  transfers between devices with their start and end apart: 7 -> 7, of which waited for: 4 -> 4; matrix products, arithmetic and copies ran while one was open for 6% -> 4% of each run, Pallas kernels for 18% -> 18%
where the time goes in v20:
time: 44.2 us; the launch traced here: 43.8 us
  Pallas kernels  14.5 us (33%)
  starting transfers between devices  11 us (25%)
  waiting for transfers between devices  8.5 us (19%)
  local copies, waits for them, and re-layouts  6.44 us (15%)
  other arithmetic  2.03 us (5%)
  matrix products  1.13 us (3%)
    pallas_call x2, Pallas kernels, match_step(): pl.pallas_call(kernel, grid=(nq,), in_specs=in_specs, out_specs=out_specs...  14.5 us
    ppermute x2, waiting for transfers between devices, extended(): lax.ppermute(lax.slice_in_dim(block, 0, width, axis=dim), axis, backward)  6.69 us
    ppermute x2, starting transfers between devices, extended(): lax.ppermute(lax.slice_in_dim(block, block.shape[dim] - width, None, axis...  5.76 us
    ppermute x2, starting transfers between devices, extended(): lax.ppermute(lax.slice_in_dim(block, 0, width, axis=dim), axis, backward)  2.57 us
    ppermute x1, starting transfers between devices, match(): shards.append((lax.ppermute(targets, 'match', sibling), me ^ 1, None))  2.42 us
    unnamed x21, local copies, waits for them, and re-layouts  2.39 us
    ppermute x1, waiting for transfers between devices, match(): pending = lax.ppermute(key, 'match', forward)  1.59 us
    slice x1, local copies, waits for them, and re-layouts, match(): return (warped[:count], flow[:count, 0], flow[:count, 1])  1.42 us
  transfers between devices with their start and end apart: 7, of which 4 were waited for; matrix products, arithmetic and copies ran while one was open for 4% of the time, Pallas kernels for 18%

profile of v20, /device:TPU:0, one launch (start us, length us, event | category | flops | bytes accessed | tf_op | source)
XLA Modules:
  0.0 43.8 jit_solution(8479466655452565783)
XLA Ops:
  0.0 0.8 %fusion.25 = (bf16[4,2,128]{2,1,0:T(2,128)(2,1)S(1)}, bf16[4,2,128]{2,1,0:T(2,128)(2,1)S(1)}) fusion(bf16[4,64,128]{2,1,0:T(8,128)(2,1)} %param.6), kind=kLoop, calls=%fused_computation.55 | loop fusion | bytes 8192 | tf_op jit(solution)/shard_map/slice | solution.py:20
  0.8 2.3 %collective-permute-start = (bf16[4,2,128]{2,1,0:T(2,128)(2,1)S(1)}, bf16[4,2,128]{2,1,0:T(2,128)(2,1)S(1)}, u32[]{:S(2)}, u32[]{:S(2)}) collective-permute-start(bf16[4,2,128]{2,1,0:T(2,128)(2,1)S(1)} %get-tuple-element.55), channel_id=1, source_target_pairs={{0,1},{1,2},{2,3},{4,5},{5,6},{6,7},{8,9},{9,10},{10,11},{12,13},{... | collective-permute-start | bytes 6152 | tf_op jit(solution)/shard_map/ppermute | solution.py:19
  3.1 1.3 %collective-permute-start.1 = (bf16[4,2,128]{2,1,0:T(2,128)(2,1)S(1)}, bf16[4,2,128]{2,1,0:T(2,128)(2,1)S(1)}, u32[]{:S(2)}, u32[]{:S(2)}) collective-permute-start(bf16[4,2,128]{2,1,0:T(2,128)(2,1)S(1)} %get-tuple-element.56), channel_id=1, source_target_pairs={{1,0},{2,1},{3,2},{5,4},{6,5},{7,6},{9,8},{10,9},{11,10},{13,12},{... | collective-permute-start | bytes 6152 | tf_op jit(solution)/shard_map/ppermute | solution.py:22
  4.5 0.7 %pad_maximum_fusion.1 = f32[3,128]{1,0:T(4,128)S(1)} fusion(f32[1,128]{1,0:T(1,128)} %bitcast.114, f32[2,128]{1,0:T(2,128)} %param.9), kind=kLoop, calls=%fused_computation.33 | loop fusion | flops 384 | bytes 3072 | tf_op jit(solution)/shard_map/concatenate | solution.py:230
  5.2 0.7 %copy-done.7 = bf16[2,3,3,128]{3,0,2,1:T(2,128)(2,1)S(1)} copy-done((bf16[2,3,3,128]{3,0,2,1:T(2,128)(2,1)S(1)}, bf16[2,3,3,128]{3,0,2,1:T(2,128)(2,1)}, u32[]{:S(2)}) %copy-start.7) | copy-done | bytes 4632
  5.9 0.0 collective-permute-done
  5.9 2.4 %collective-permute-done.1 = bf16[4,2,128]{2,1,0:T(2,128)(2,1)S(1)} collective-permute-done((bf16[4,2,128]{2,1,0:T(2,128)(2,1)S(1)}, bf16[4,2,128]{2,1,0:T(2,128)(2,1)S(1)}, u32[]{:S(2)}, u32[]{:S(2)}) %collective-permute-start.1) | collective-permute-done | bytes 2080 | tf_op jit(solution)/shard_map/ppermute | solution.py:22
  8.4 2.4 %collective-permute-start.5 = (bf16[2048,128]{1,0:T(8,128)(2,1)}, bf16[2048,128]{1,0:T(8,128)(2,1)S(1)}, u32[]{:S(2)}, u32[]{:S(2)}) collective-permute-start(bf16[2048,128]{1,0:T(8,128)(2,1)} %refs_1_), channel_id=1, source_target_pairs={{0,1},{1,0},{2,3},{3,2},{4,5},{5,4},{6,7},{7,6},{8,9},{9,8},{10,11... | collective-permute-start | bytes 1572872 | tf_op jit(solution)/shard_map/ppermute | solution.py:176
  10.8 0.2 collective-permute-start.4
  11.0 3.4 %collective-permute-start.2 = (bf16[136,128]{1,0:T(8,128)(2,1)S(1)}, bf16[136,128]{1,0:T(8,128)(2,1)S(1)}, u32[]{:S(2)}, u32[]{:S(2)}) collective-permute-start(bf16[136,128]{1,0:T(8,128)(2,1)S(1)} %get-tuple-element.54), channel_id=1, source_target_pairs={{0,4},{4,8},{8,12},{12,16},{16,20},{20,24},{24,28},{1,5},{5,9},{9,... | collective-permute-start | bytes 104456 | tf_op jit(solution)/shard_map/ppermute | solution.py:19
  14.4 0.1 fusion.19
  14.5 1.3 %collective-permute-start.3 = (bf16[136,128]{1,0:T(8,128)(2,1)S(1)}, bf16[136,128]{1,0:T(8,128)(2,1)S(1)}, u32[]{:S(2)}, u32[]{:S(2)}) collective-permute-start(bf16[136,128]{1,0:T(8,128)(2,1)S(1)} %get-tuple-element.53), channel_id=1, source_target_pairs={{4,0},{8,4},{12,8},{16,12},{20,16},{24,20},{28,24},{5,1},{9,5},{13... | collective-permute-start | bytes 104456 | tf_op jit(solution)/shard_map/ppermute | solution.py:22
  15.8 0.2 collective-permute-done.2
  16.0 4.3 %collective-permute-done.3 = bf16[136,128]{1,0:T(8,128)(2,1)S(1)} collective-permute-done((bf16[136,128]{1,0:T(8,128)(2,1)S(1)}, bf16[136,128]{1,0:T(8,128)(2,1)S(1)}, u32[]{:S(2)}, u32[]{:S(2)}) %collective-permute-start.3) | collective-permute-done | bytes 34848 | tf_op jit(solution)/shard_map/ppermute | solution.py:22
  20.3 0.0 collective-permute-done.5.refs_2_
  20.4 0.7 %broadcast_in_dim.25.refs_3_ = f32[8,128]{1,0:T(8,128)} broadcast(f32[128]{0:T(128)S(1)} %pad.4), dimensions={1} | broadcast | bytes 4608 | tf_op jit(solution)/shard_map/broadcast_in_dim | solution.py:191
  21.0 0.0 copy-done.1
  21.0 0.2 copy-done.2
  21.2 8.1 %shard_map.64 = (f32[544,8]{1,0:T(8,128)}, f32[544,128]{1,0:T(8,128)}, f32[544,8]{1,0:T(8,128)}) custom-call(bf16[544,128]{1,0:T(8,128)(2,1)} %copy-done.1, bf16[2048,128]{1,0:T(8,128)(2,1)} %refs_1_, bf16[2048,128]{1,0:T(8,128)(2,1)} %copy-done.2, f32[8,128]{1,0:T(8,128)} %broadcast_in_dim.25.refs_3_), custom_call_target="tpu_custom_call" | custom-call | tf_op jit(solution)/shard_map/pallas_call | solution.py:151
  29.3 0.0 collective-permute-done.4.refs_1_
  29.3 0.0 collective-permute-start.6
  29.3 0.1 broadcast_and_fusion
  29.4 0.1 slice.131
  29.4 0.1 copy.25
  29.6 1.6 %collective-permute-done.6.refs_2_ = bf16[2048,128]{1,0:T(8,128)(2,1)S(1)} collective-permute-done((bf16[2048,128]{1,0:T(8,128)(2,1)S(1)}, bf16[2048,128]{1,0:T(8,128)(2,1)S(1)}, u32[]{:S(2)}, u32[]{:S(2)}) %collective-permute-start.6) | collective-permute-done | bytes 524320 | tf_op jit(solution)/shard_map/ppermute | solution.py:206
  31.2 0.0 copy-done.3
  31.2 0.8 %copy-done.4 = bf16[2048,128]{1,0:T(8,128)(2,1)} copy-done((bf16[2048,128]{1,0:T(8,128)(2,1)}, bf16[2048,128]{1,0:T(8,128)(2,1)S(1)}, u32[]{:S(2)}) %copy-start.4) | copy-done | bytes 524312
  32.0 6.4 %shard_map.65 = (f32[544,128]{1,0:T(8,128)}, f32[544,8]{1,0:T(8,128)}) custom-call(bf16[544,128]{1,0:T(8,128)(2,1)} %copy-done.1, bf16[2048,128]{1,0:T(8,128)(2,1)} %copy-done.3, bf16[2048,128]{1,0:T(8,128)(2,1)} %copy-done.4, f32[8,128]{1,0:T(8,128)} %broadcast_in_dim.25.refs_3_, f32[544,8]{1,0:T(8,128)} %get-tuple-element.25.refs_4_, ...), custom_call_target="tpu_custom_call" | custom-call | tf_op jit(solution)/shard_map/pallas_call | solution.py:151
  38.4 1.4 %slice_reduce_fusion.1 = (f32[544]{0:T(1024)S(1)}, f32[544]{0:T(1024)S(1)}) fusion(f32[544,8]{1,0:T(8,128)} %get-tuple-element.28), kind=kLoop, calls=%fused_computation.8 | loop fusion | bytes 8704 | tf_op jit(solution)/shard_map/slice | solution.py:219
  39.8 0.1 reshape_squeeze.6
  39.9 0.1 slice.132
  40.0 0.1 reshape_squeeze.7
  40.0 0.1 broadcast_subtract_fusion
  40.1 0.1 slice.134
  40.2 0.1 slice_bitcast_fusion.1
  40.3 0.1 select_bitcast_fusion
  40.4 0.1 copy.67
  40.5 0.1 copy.28
  40.6 0.0 copy-start.8
  40.6 0.6 %copy-done.8 = pred[8,9]{0,1:T(8,128)(4,1)S(1)} copy-done((pred[8,9]{0,1:T(8,128)(4,1)S(1)}, pred[8,9]{0,1:T(8,128)(4,1)}, u32[]{:S(2)}) %copy-start.8) | copy-done | bytes 96
  41.3 0.9 %convolution_select_fusion = f32[6,8,9,128]{3,1,2,0:T(8,128)S(1)} fusion(bf16[3,3,128,128]{3,2,1,0:T(8,128)(2,1)S(1)} %copy-done, f32[8,1,7,2,128]{4,2,3,0,1:T(8,128)S(1)} %slice.157, f32[8,1,8,9,128]{4,2,3,0,1:T(8,128)S(1)} %copy.28, pred[8,9]{0,1:T(8,128)(4,1)S(1)} %copy-done.8), kind=kOutput, calls=%fused_computation | convolution fusion | flops 764737536 | bytes 868424 | tf_op jit(solution)/shard_map/conv_general_dilated | solution.py:248
  42.2 0.1 copy.29
  42.3 0.1 copy.30
  42.4 0.1 copy.31
  42.5 0.3 broadcast_select_fusion
  42.8 0.2 fusion.9
  43.0 0.1 fusion.23
  43.2 0.6 %maximum_add_fusion = f32[2,4,64]{2,1,0:T(4,128)} fusion(f32[1,4,64]{2,1,0:T(4,128)S(1)} %get-tuple-element.60, f32[1,4,64]{2,1,0:T(4,128)S(1)} %get-tuple-element.61, f32[1,4,64]{2,1,0:T(4,128)S(1)} %bitcast.110, f32[1,4,64]{2,1,0:T(4,128)S(1)} %bitcast.111, f32[1,4,64]{2,1,0:T(4,128)S(1)} %bitcast.108, f32[1,4,64]{2,1,0:T(4,128)S(1)} %bitcast.109, ...), kind=kLoop, calls=%fused_computation.24 | loop fusion | flops 9728 | bytes 22528 | tf_op jit(solution)/shard_map/add | solution.py:267
  (29 shorter events, 0.2 us)
Async XLA Ops:
  0.0 40.6 %copy-start = (bf16[3,3,128,128]{3,2,1,0:T(8,128)(2,1)S(1)}, bf16[3,3,128,128]{3,2,1,0:T(8,128)(2,1)}, u32[]{:S(2)}) copy-start(bf16[3,3,128,128]{3,2,1,0:T(8,128)(2,1)} %param.8) | copy-start | bytes 884740
  0.0 8.3 %copy-start.6 = (bf16[4,64,128]{2,1,0:T(8,128)(2,1)S(1)}, bf16[4,64,128]{2,1,0:T(8,128)(2,1)}, u32[]{:S(2)}) copy-start(bf16[4,64,128]{2,1,0:T(8,128)(2,1)} %param.6) | copy-start | bytes 196612
  0.8 5.1 %collective-permute-start = (bf16[4,2,128]{2,1,0:T(2,128)(2,1)S(1)}, bf16[4,2,128]{2,1,0:T(2,128)(2,1)S(1)}, u32[]{:S(2)}, u32[]{:S(2)}) collective-permute-start(bf16[4,2,128]{2,1,0:T(2,128)(2,1)S(1)} %get-tuple-element.55), channel_id=1, source_target_pairs={{0,1},{1,2},{2,3},{4,5},{5,6},{6,7},{8,9},{9,10},{10,11},{12,13},{... | collective-permute-start | bytes 6152 | tf_op jit(solution)/shard_map/ppermute | solution.py:19
  3.1 5.2 %collective-permute-start.1 = (bf16[4,2,128]{2,1,0:T(2,128)(2,1)S(1)}, bf16[4,2,128]{2,1,0:T(2,128)(2,1)S(1)}, u32[]{:S(2)}, u32[]{:S(2)}) collective-permute-start(bf16[4,2,128]{2,1,0:T(2,128)(2,1)S(1)} %get-tuple-element.56), channel_id=1, source_target_pairs={{1,0},{2,1},{3,2},{5,4},{6,5},{7,6},{9,8},{10,9},{11,10},{13,12},{... | collective-permute-start | bytes 6152 | tf_op jit(solution)/shard_map/ppermute | solution.py:22
  5.2 0.7 %copy-start.7 = (bf16[2,3,3,128]{3,0,2,1:T(2,128)(2,1)S(1)}, bf16[2,3,3,128]{3,0,2,1:T(2,128)(2,1)}, u32[]{:S(2)}) copy-start(bf16[2,3,3,128]{3,0,2,1:T(2,128)(2,1)} %param.11) | copy-start | bytes 13828
  8.4 12.0 %collective-permute-start.5 = (bf16[2048,128]{1,0:T(8,128)(2,1)}, bf16[2048,128]{1,0:T(8,128)(2,1)S(1)}, u32[]{:S(2)}, u32[]{:S(2)}) collective-permute-start(bf16[2048,128]{1,0:T(8,128)(2,1)} %refs_1_), channel_id=1, source_target_pairs={{0,1},{1,0},{2,3},{3,2},{4,5},{5,4},{6,7},{7,6},{8,9},{9,8},{10,11... | collective-permute-start | bytes 1572872 | tf_op jit(solution)/shard_map/ppermute | solution.py:176
  10.8 18.5 %collective-permute-start.4 = (bf16[2048,128]{1,0:T(8,128)(2,1)}, bf16[2048,128]{1,0:T(8,128)(2,1)S(1)}, u32[]{:S(2)}, u32[]{:S(2)}) collective-permute-start(bf16[2048,128]{1,0:T(8,128)(2,1)} %refs_1_), channel_id=1, source_target_pairs={{0,2},{1,3},{2,0},{3,1},{4,6},{5,7},{6,4},{7,5},{8,10},{9,11},{10,... | collective-permute-start | bytes 1572872 | tf_op jit(solution)/shard_map/ppermute | solution.py:179
  11.0 5.0 %collective-permute-start.2 = (bf16[136,128]{1,0:T(8,128)(2,1)S(1)}, bf16[136,128]{1,0:T(8,128)(2,1)S(1)}, u32[]{:S(2)}, u32[]{:S(2)}) collective-permute-start(bf16[136,128]{1,0:T(8,128)(2,1)S(1)} %get-tuple-element.54), channel_id=1, source_target_pairs={{0,4},{4,8},{8,12},{12,16},{16,20},{20,24},{24,28},{1,5},{5,9},{9,... | collective-permute-start | bytes 104456 | tf_op jit(solution)/shard_map/ppermute | solution.py:19
  14.5 5.8 %collective-permute-start.3 = (bf16[136,128]{1,0:T(8,128)(2,1)S(1)}, bf16[136,128]{1,0:T(8,128)(2,1)S(1)}, u32[]{:S(2)}, u32[]{:S(2)}) collective-permute-start(bf16[136,128]{1,0:T(8,128)(2,1)S(1)} %get-tuple-element.53), channel_id=1, source_target_pairs={{4,0},{8,4},{12,8},{16,12},{20,16},{24,20},{28,24},{5,1},{9,5},{13... | collective-permute-start | bytes 104456 | tf_op jit(solution)/shard_map/ppermute | solution.py:22
  20.3 0.7 %copy-start.1 = (bf16[544,128]{1,0:T(8,128)(2,1)}, bf16[544,128]{1,0:T(8,128)(2,1)S(1)}, u32[]{:S(2)}) copy-start(bf16[544,128]{1,0:T(8,128)(2,1)S(1)} %constant_dynamic-update-slice_fusion.refs_0_) | copy-start | bytes 417796
  20.3 0.8 %copy-start.2 = (bf16[2048,128]{1,0:T(8,128)(2,1)}, bf16[2048,128]{1,0:T(8,128)(2,1)S(1)}, u32[]{:S(2)}) copy-start(bf16[2048,128]{1,0:T(8,128)(2,1)S(1)} %collective-permute-done.5.refs_2_) | copy-start | bytes 1572868
  29.3 1.9 %copy-start.3 = (bf16[2048,128]{1,0:T(8,128)(2,1)}, bf16[2048,128]{1,0:T(8,128)(2,1)S(1)}, u32[]{:S(2)}) copy-start(bf16[2048,128]{1,0:T(8,128)(2,1)S(1)} %collective-permute-done.4.refs_1_) | copy-start | bytes 1572868
  29.3 1.9 %collective-permute-start.6 = (bf16[2048,128]{1,0:T(8,128)(2,1)S(1)}, bf16[2048,128]{1,0:T(8,128)(2,1)S(1)}, u32[]{:S(2)}, u32[]{:S(2)}) collective-permute-start(bf16[2048,128]{1,0:T(8,128)(2,1)S(1)} %collective-permute-done.4.refs_1_), channel_id=1, source_target_pairs={{0,1},{1,0},{2,3},{3,2},{4,5},{5,4},{6,7},{7,6},{8,9},{9,8},{10,11... | collective-permute-start | bytes 1572872 | tf_op jit(solution)/shard_map/ppermute | solution.py:206
  31.2 0.8 %copy-start.4 = (bf16[2048,128]{1,0:T(8,128)(2,1)}, bf16[2048,128]{1,0:T(8,128)(2,1)S(1)}, u32[]{:S(2)}) copy-start(bf16[2048,128]{1,0:T(8,128)(2,1)S(1)} %collective-permute-done.6.refs_2_) | copy-start | bytes 1572868
  38.4 1.9 %copy-start.5 = (f32[544,128]{1,0:T(8,128)S(1)}, f32[544,128]{1,0:T(8,128)}, u32[]{:S(2)}) copy-start(f32[544,128]{1,0:T(8,128)} %get-tuple-element.29) | copy-start | bytes 835588
  40.6 0.7 %copy-start.8 = (pred[8,9]{0,1:T(8,128)(4,1)S(1)}, pred[8,9]{0,1:T(8,128)(4,1)}, u32[]{:S(2)}) copy-start(pred[8,9]{0,1:T(8,128)(4,1)} %constant.75) | copy-start | bytes 220

commit v21 on v20

--- a/solution.py
+++ b/solution.py
@@ -46,7 +46,7 @@
     return jnp.where(lane8 == 0, total, jnp.where(lane8 == 1, sum_x, jnp.where(lane8 == 3, sum_y, zero)))
 
 
-def shard_kernel(*refs, scale, chans, first, last, width, slots):
+def shard_kernel(*refs, scale, chans, first, last, width, slots, flip):
     parts = len(slots)
     q_ref = refs[0]
     k_refs = refs[1:1 + parts]
@@ -90,7 +90,25 @@
         alpha = jnp.exp2((old - peak) * rate)
         acc = acc_ref[...] * alpha + acc
         st = st_ref[...] * alpha + st
-    if last:
+    if last and flip:
+        warped_ref, flow_ref = outs
+        total = st[:, 0:1]
+        warped_ref[...] = acc / total
+        fx = (st[:, 1:2] + st[:, 2:3]) / total
+        fy = (st[:, 3:4] + st[:, 4:5]) / total
+        lane = lax.broadcasted_iota(jnp.int32, (st.shape[0], 128), 1)
+        flow = jnp.where(lane == 0, fx, jnp.where(lane == 1, fy, 0.0))
+        eye = (lax.broadcasted_iota(jnp.int32, (8, 128), 0)
+               == lax.broadcasted_iota(jnp.int32, (8, 128), 1)).astype(jnp.bfloat16)
+        flipped = None
+        for _ in range(3):
+            piece = flow.astype(jnp.bfloat16)
+            flow = flow - piece.astype(jnp.float32)
+            part = lax.dot_general(eye, piece, (((1,), (1,)), ((), ())),
+                                   preferred_element_type=jnp.float32)
+            flipped = part if flipped is None else flipped + part
+        flow_ref[...] = flipped
+    elif last:
         warped_ref, flow_ref = outs
         total = st[:, 0:1]
         warped_ref[...] = acc / total
@@ -125,7 +143,7 @@
     tk = keys[0].shape[0]
     kernel = functools.partial(
         shard_kernel, scale=1.0 / math.sqrt(chans), chans=chans, first=first, last=last,
-        width=width, slots=slots,
+        width=width, slots=slots, flip=nq == 1,
     )
     row_spec = lambda width: pl.BlockSpec((tq, width), lambda i: (i, 0))
     in_specs = [row_spec(chans)]
@@ -135,7 +153,13 @@
     if not first:
         in_specs += [row_spec(8), row_spec(chans), row_spec(8)]
         args += list(state)
-    if last:
+    if last and nq == 1:
+        out_specs = [row_spec(chans), pl.BlockSpec((8, tq), lambda i: (0, i))]
+        out_shape = [
+            jax.ShapeDtypeStruct((padded, chans), jnp.float32),
+            jax.ShapeDtypeStruct((8, padded), jnp.float32),
+        ]
+    elif last:
         out_specs = [row_spec(chans), row_spec(8)]
         out_shape = [
             jax.ShapeDtypeStruct((padded, chans), jnp.float32),
@@ -216,6 +240,8 @@
             tuple(step % 128 for step in group),
         )
     warped, flow = state
+    if nq == 1:
+        return warped[:count], flow[0, :count], flow[1, :count]
     return warped[:count], flow[:count, 0], flow[:count, 1]
 
 

time: 44.2 us -> 44.7 us (1.011)
    reshape x1, local copies, waits for them, and re-layouts: 0.03 us -> 0.99 us  [local(): warped = warped.reshape(erows, ecols, chans)]
    slice x1, local copies, waits for them, and re-layouts: 1.42 us -> 0.82 us  [match(): return (warped[:count], flow[0, :count], flow[1, :count])]
    unnamed x21 -> x19, local copies, waits for them, and re-layouts: 2.39 us -> 2.41 us
where the time goes in v21:
time: 44.7 us; the launch traced here: 44.2 us
  Pallas kernels  14.6 us (33%)
  starting transfers between devices  11 us (25%)
  waiting for transfers between devices  8.5 us (19%)
  local copies, waits for them, and re-layouts  6.81 us (15%)
  other arithmetic  2.03 us (5%)
  matrix products  1.13 us (3%)
    pallas_call x2, Pallas kernels, match_step(): pl.pallas_call(kernel, grid=(nq,), in_specs=in_specs, out_specs=out_specs...  14.6 us
    ppermute x2, waiting for transfers between devices, extended(): lax.ppermute(lax.slice_in_dim(block, 0, width, axis=dim), axis, backward)  6.69 us
    ppermute x2, starting transfers between devices, extended(): lax.ppermute(lax.slice_in_dim(block, block.shape[dim] - width, None, axis...  5.76 us
    ppermute x2, starting transfers between devices, extended(): lax.ppermute(lax.slice_in_dim(block, 0, width, axis=dim), axis, backward)  2.57 us
    ppermute x1, starting transfers between devices, match(): shards.append((lax.ppermute(targets, 'match', sibling), me ^ 1, None))  2.42 us
    unnamed x19, local copies, waits for them, and re-layouts  2.41 us
    ppermute x1, waiting for transfers between devices, match(): pending = lax.ppermute(key, 'match', forward)  1.59 us
    reshape x1, local copies, waits for them, and re-layouts, local(): warped = warped.reshape(erows, ecols, chans)  0.99 us
  transfers between devices with their start and end apart: 7, of which 4 were waited for; matrix products, arithmetic and copies ran while one was open for 4% of the time, Pallas kernels for 18%

profile of v21, /device:TPU:0, one launch (start us, length us, event | category | flops | bytes accessed | tf_op | source)
XLA Modules:
  0.0 44.2 jit_solution(5878368595657727691)
XLA Ops:
  0.0 0.8 %fusion.25 = (bf16[4,2,128]{2,1,0:T(2,128)(2,1)S(1)}, bf16[4,2,128]{2,1,0:T(2,128)(2,1)S(1)}) fusion(bf16[4,64,128]{2,1,0:T(8,128)(2,1)} %param.6), kind=kLoop, calls=%fused_computation.55 | loop fusion | bytes 8192 | tf_op jit(solution)/shard_map/slice | solution.py:20
  0.8 2.3 %collective-permute-start = (bf16[4,2,128]{2,1,0:T(2,128)(2,1)S(1)}, bf16[4,2,128]{2,1,0:T(2,128)(2,1)S(1)}, u32[]{:S(2)}, u32[]{:S(2)}) collective-permute-start(bf16[4,2,128]{2,1,0:T(2,128)(2,1)S(1)} %get-tuple-element.55), channel_id=1, source_target_pairs={{0,1},{1,2},{2,3},{4,5},{5,6},{6,7},{8,9},{9,10},{10,11},{12,13},{... | collective-permute-start | bytes 6152 | tf_op jit(solution)/shard_map/ppermute | solution.py:19
  3.1 1.3 %collective-permute-start.1 = (bf16[4,2,128]{2,1,0:T(2,128)(2,1)S(1)}, bf16[4,2,128]{2,1,0:T(2,128)(2,1)S(1)}, u32[]{:S(2)}, u32[]{:S(2)}) collective-permute-start(bf16[4,2,128]{2,1,0:T(2,128)(2,1)S(1)} %get-tuple-element.56), channel_id=1, source_target_pairs={{1,0},{2,1},{3,2},{5,4},{6,5},{7,6},{9,8},{10,9},{11,10},{13,12},{... | collective-permute-start | bytes 6152 | tf_op jit(solution)/shard_map/ppermute | solution.py:22
  4.5 0.7 %pad_maximum_fusion.1 = f32[3,128]{1,0:T(4,128)S(1)} fusion(f32[1,128]{1,0:T(1,128)} %bitcast.114, f32[2,128]{1,0:T(2,128)} %param.9), kind=kLoop, calls=%fused_computation.33 | loop fusion | flops 384 | bytes 3072 | tf_op jit(solution)/shard_map/concatenate | solution.py:256
  5.2 0.7 %copy-done.6 = bf16[2,3,3,128]{3,0,2,1:T(2,128)(2,1)S(1)} copy-done((bf16[2,3,3,128]{3,0,2,1:T(2,128)(2,1)S(1)}, bf16[2,3,3,128]{3,0,2,1:T(2,128)(2,1)}, u32[]{:S(2)}) %copy-start.6) | copy-done | bytes 4632
  5.9 0.0 collective-permute-done
  5.9 2.4 %collective-permute-done.1 = bf16[4,2,128]{2,1,0:T(2,128)(2,1)S(1)} collective-permute-done((bf16[4,2,128]{2,1,0:T(2,128)(2,1)S(1)}, bf16[4,2,128]{2,1,0:T(2,128)(2,1)S(1)}, u32[]{:S(2)}, u32[]{:S(2)}) %collective-permute-start.1) | collective-permute-done | bytes 2080 | tf_op jit(solution)/shard_map/ppermute | solution.py:22
  8.3 0.0 copy-done.5
  8.4 2.4 %collective-permute-start.5 = (bf16[2048,128]{1,0:T(8,128)(2,1)}, bf16[2048,128]{1,0:T(8,128)(2,1)S(1)}, u32[]{:S(2)}, u32[]{:S(2)}) collective-permute-start(bf16[2048,128]{1,0:T(8,128)(2,1)} %refs_1_), channel_id=1, source_target_pairs={{0,1},{1,0},{2,3},{3,2},{4,5},{5,4},{6,7},{7,6},{8,9},{9,8},{10,11... | collective-permute-start | bytes 1572872 | tf_op jit(solution)/shard_map/ppermute | solution.py:200
  10.8 0.2 collective-permute-start.4
  11.0 3.4 %collective-permute-start.2 = (bf16[136,128]{1,0:T(8,128)(2,1)S(1)}, bf16[136,128]{1,0:T(8,128)(2,1)S(1)}, u32[]{:S(2)}, u32[]{:S(2)}) collective-permute-start(bf16[136,128]{1,0:T(8,128)(2,1)S(1)} %get-tuple-element.54), channel_id=1, source_target_pairs={{0,4},{4,8},{8,12},{12,16},{16,20},{20,24},{24,28},{1,5},{5,9},{9,... | collective-permute-start | bytes 104456 | tf_op jit(solution)/shard_map/ppermute | solution.py:19
  14.4 0.1 fusion.19
  14.5 1.3 %collective-permute-start.3 = (bf16[136,128]{1,0:T(8,128)(2,1)S(1)}, bf16[136,128]{1,0:T(8,128)(2,1)S(1)}, u32[]{:S(2)}, u32[]{:S(2)}) collective-permute-start(bf16[136,128]{1,0:T(8,128)(2,1)S(1)} %get-tuple-element.53), channel_id=1, source_target_pairs={{4,0},{8,4},{12,8},{16,12},{20,16},{24,20},{28,24},{5,1},{9,5},{13... | collective-permute-start | bytes 104456 | tf_op jit(solution)/shard_map/ppermute | solution.py:22
  15.8 0.2 collective-permute-done.2
  16.0 4.3 %collective-permute-done.3 = bf16[136,128]{1,0:T(8,128)(2,1)S(1)} collective-permute-done((bf16[136,128]{1,0:T(8,128)(2,1)S(1)}, bf16[136,128]{1,0:T(8,128)(2,1)S(1)}, u32[]{:S(2)}, u32[]{:S(2)}) %collective-permute-start.3) | collective-permute-done | bytes 34848 | tf_op jit(solution)/shard_map/ppermute | solution.py:22
  20.3 0.0 collective-permute-done.5.refs_2_
  20.4 0.7 %broadcast_in_dim.25.refs_3_ = f32[8,128]{1,0:T(8,128)} broadcast(f32[128]{0:T(128)S(1)} %pad.4), dimensions={1} | broadcast | bytes 4608 | tf_op jit(solution)/shard_map/broadcast_in_dim | solution.py:215
  21.0 0.2 copy-done.2
  21.2 8.1 %shard_map.64 = (f32[544,8]{1,0:T(8,128)}, f32[544,128]{1,0:T(8,128)}, f32[544,8]{1,0:T(8,128)}) custom-call(bf16[544,128]{1,0:T(8,128)(2,1)} %copy-done.1, bf16[2048,128]{1,0:T(8,128)(2,1)} %refs_1_, bf16[2048,128]{1,0:T(8,128)(2,1)} %copy-done.2, f32[8,128]{1,0:T(8,128)} %broadcast_in_dim.25.refs_3_), custom_call_target="tpu_custom_call" | custom-call | tf_op jit(solution)/shard_map/pallas_call | solution.py:175
  29.3 0.0 collective-permute-done.4.refs_1_
  29.3 0.0 collective-permute-start.6
  29.3 0.1 broadcast_and_fusion
  29.4 0.1 slice.131
  29.4 0.1 copy.25
  29.6 1.6 %collective-permute-done.6.refs_2_ = bf16[2048,128]{1,0:T(8,128)(2,1)S(1)} collective-permute-done((bf16[2048,128]{1,0:T(8,128)(2,1)S(1)}, bf16[2048,128]{1,0:T(8,128)(2,1)S(1)}, u32[]{:S(2)}, u32[]{:S(2)}) %collective-permute-start.6) | collective-permute-done | bytes 524320 | tf_op jit(solution)/shard_map/ppermute | solution.py:230
  31.2 0.8 %copy-done.4 = bf16[2048,128]{1,0:T(8,128)(2,1)} copy-done((bf16[2048,128]{1,0:T(8,128)(2,1)}, bf16[2048,128]{1,0:T(8,128)(2,1)S(1)}, u32[]{:S(2)}) %copy-start.4) | copy-done | bytes 524312
  32.0 6.5 %shard_map.65 = (f32[544,128]{1,0:T(8,128)}, f32[8,544]{1,0:T(8,128)}) custom-call(bf16[544,128]{1,0:T(8,128)(2,1)} %copy-done.1, bf16[2048,128]{1,0:T(8,128)(2,1)} %copy-done.3, bf16[2048,128]{1,0:T(8,128)(2,1)} %copy-done.4, f32[8,128]{1,0:T(8,128)} %broadcast_in_dim.25.refs_3_, f32[544,8]{1,0:T(8,128)} %get-tuple-element.25.refs_4_, ...), custom_call_target="tpu_custom_call" | custom-call | tf_op jit(solution)/shard_map/pallas_call | solution.py:175
  38.5 0.8 %slice_reduce_fusion.1 = (f32[544]{0:T(1024)S(1)}, f32[544]{0:T(1024)S(1)}) fusion(f32[8,544]{1,0:T(8,128)} %get-tuple-element.28), kind=kLoop, calls=%fused_computation.32 | loop fusion | bytes 8704 | tf_op jit(solution)/shard_map/slice | solution.py:244
  39.3 0.1 reshape_squeeze.6
  39.4 0.1 slice.132
  39.5 0.1 reshape_squeeze.7
  39.5 0.1 broadcast_subtract_fusion
  39.6 0.1 slice.134
  39.7 0.1 slice_bitcast_fusion.1
  39.8 1.0 %reshape.77 = f32[1,8,68,128]{3,2,1,0:T(8,128)S(1)} reshape(f32[544,128]{1,0:T(8,128)} %get-tuple-element.29) | data formatting | bytes 557056 | tf_op jit(solution)/shard_map/reshape | solution.py:264
  40.8 0.1 select_bitcast_fusion
  40.9 0.1 copy.67
  41.0 0.1 copy.28
  41.1 0.0 copy-start.7
  41.1 0.6 %copy-done.7 = pred[8,9]{0,1:T(8,128)(4,1)S(1)} copy-done((pred[8,9]{0,1:T(8,128)(4,1)S(1)}, pred[8,9]{0,1:T(8,128)(4,1)}, u32[]{:S(2)}) %copy-start.7) | copy-done | bytes 96
  41.8 0.9 %convolution_select_fusion = f32[6,8,9,128]{3,1,2,0:T(8,128)S(1)} fusion(bf16[3,3,128,128]{3,2,1,0:T(8,128)(2,1)S(1)} %copy-done, f32[8,1,7,2,128]{4,2,3,0,1:T(8,128)S(1)} %slice.157, f32[8,1,8,9,128]{4,2,3,0,1:T(8,128)S(1)} %copy.28, pred[8,9]{0,1:T(8,128)(4,1)S(1)} %copy-done.7), kind=kOutput, calls=%fused_computation | convolution fusion | flops 764737536 | bytes 868424 | tf_op jit(solution)/shard_map/conv_general_dilated | solution.py:274
  42.7 0.1 copy.29
  42.8 0.1 copy.30
  42.9 0.1 copy.31
  43.0 0.3 broadcast_select_fusion
  43.3 0.2 fusion.9
  43.5 0.1 fusion.23
  43.6 0.6 %maximum_add_fusion = f32[2,4,64]{2,1,0:T(4,128)} fusion(f32[1,4,64]{2,1,0:T(4,128)S(1)} %get-tuple-element.60, f32[1,4,64]{2,1,0:T(4,128)S(1)} %get-tuple-element.61, f32[1,4,64]{2,1,0:T(4,128)S(1)} %bitcast.110, f32[1,4,64]{2,1,0:T(4,128)S(1)} %bitcast.111, f32[1,4,64]{2,1,0:T(4,128)S(1)} %bitcast.108, f32[1,4,64]{2,1,0:T(4,128)S(1)} %bitcast.109, ...), kind=kLoop, calls=%fused_computation.22 | loop fusion | flops 9728 | bytes 22528 | tf_op jit(solution)/shard_map/add | solution.py:293
  (27 shorter events, 0.2 us)
Async XLA Ops:
  0.0 41.1 %copy-start = (bf16[3,3,128,128]{3,2,1,0:T(8,128)(2,1)S(1)}, bf16[3,3,128,128]{3,2,1,0:T(8,128)(2,1)}, u32[]{:S(2)}) copy-start(bf16[3,3,128,128]{3,2,1,0:T(8,128)(2,1)} %param.8) | copy-start | bytes 884740
  0.0 8.3 %copy-start.5 = (bf16[4,64,128]{2,1,0:T(8,128)(2,1)S(1)}, bf16[4,64,128]{2,1,0:T(8,128)(2,1)}, u32[]{:S(2)}) copy-start(bf16[4,64,128]{2,1,0:T(8,128)(2,1)} %param.6) | copy-start | bytes 196612
  0.8 5.1 %collective-permute-start = (bf16[4,2,128]{2,1,0:T(2,128)(2,1)S(1)}, bf16[4,2,128]{2,1,0:T(2,128)(2,1)S(1)}, u32[]{:S(2)}, u32[]{:S(2)}) collective-permute-start(bf16[4,2,128]{2,1,0:T(2,128)(2,1)S(1)} %get-tuple-element.55), channel_id=1, source_target_pairs={{0,1},{1,2},{2,3},{4,5},{5,6},{6,7},{8,9},{9,10},{10,11},{12,13},{... | collective-permute-start | bytes 6152 | tf_op jit(solution)/shard_map/ppermute | solution.py:19
  3.1 5.2 %collective-permute-start.1 = (bf16[4,2,128]{2,1,0:T(2,128)(2,1)S(1)}, bf16[4,2,128]{2,1,0:T(2,128)(2,1)S(1)}, u32[]{:S(2)}, u32[]{:S(2)}) collective-permute-start(bf16[4,2,128]{2,1,0:T(2,128)(2,1)S(1)} %get-tuple-element.56), channel_id=1, source_target_pairs={{1,0},{2,1},{3,2},{5,4},{6,5},{7,6},{9,8},{10,9},{11,10},{13,12},{... | collective-permute-start | bytes 6152 | tf_op jit(solution)/shard_map/ppermute | solution.py:22
  5.2 0.7 %copy-start.6 = (bf16[2,3,3,128]{3,0,2,1:T(2,128)(2,1)S(1)}, bf16[2,3,3,128]{3,0,2,1:T(2,128)(2,1)}, u32[]{:S(2)}) copy-start(bf16[2,3,3,128]{3,0,2,1:T(2,128)(2,1)} %param.11) | copy-start | bytes 13828
  8.4 12.0 %collective-permute-start.5 = (bf16[2048,128]{1,0:T(8,128)(2,1)}, bf16[2048,128]{1,0:T(8,128)(2,1)S(1)}, u32[]{:S(2)}, u32[]{:S(2)}) collective-permute-start(bf16[2048,128]{1,0:T(8,128)(2,1)} %refs_1_), channel_id=1, source_target_pairs={{0,1},{1,0},{2,3},{3,2},{4,5},{5,4},{6,7},{7,6},{8,9},{9,8},{10,11... | collective-permute-start | bytes 1572872 | tf_op jit(solution)/shard_map/ppermute | solution.py:200
  10.8 18.5 %collective-permute-start.4 = (bf16[2048,128]{1,0:T(8,128)(2,1)}, bf16[2048,128]{1,0:T(8,128)(2,1)S(1)}, u32[]{:S(2)}, u32[]{:S(2)}) collective-permute-start(bf16[2048,128]{1,0:T(8,128)(2,1)} %refs_1_), channel_id=1, source_target_pairs={{0,2},{1,3},{2,0},{3,1},{4,6},{5,7},{6,4},{7,5},{8,10},{9,11},{10,... | collective-permute-start | bytes 1572872 | tf_op jit(solution)/shard_map/ppermute | solution.py:203
  11.0 5.0 %collective-permute-start.2 = (bf16[136,128]{1,0:T(8,128)(2,1)S(1)}, bf16[136,128]{1,0:T(8,128)(2,1)S(1)}, u32[]{:S(2)}, u32[]{:S(2)}) collective-permute-start(bf16[136,128]{1,0:T(8,128)(2,1)S(1)} %get-tuple-element.54), channel_id=1, source_target_pairs={{0,4},{4,8},{8,12},{12,16},{16,20},{20,24},{24,28},{1,5},{5,9},{9,... | collective-permute-start | bytes 104456 | tf_op jit(solution)/shard_map/ppermute | solution.py:19
  14.5 5.8 %collective-permute-start.3 = (bf16[136,128]{1,0:T(8,128)(2,1)S(1)}, bf16[136,128]{1,0:T(8,128)(2,1)S(1)}, u32[]{:S(2)}, u32[]{:S(2)}) collective-permute-start(bf16[136,128]{1,0:T(8,128)(2,1)S(1)} %get-tuple-element.53), channel_id=1, source_target_pairs={{4,0},{8,4},{12,8},{16,12},{20,16},{24,20},{28,24},{5,1},{9,5},{13... | collective-permute-start | bytes 104456 | tf_op jit(solution)/shard_map/ppermute | solution.py:22
  20.3 0.7 %copy-start.1 = (bf16[544,128]{1,0:T(8,128)(2,1)}, bf16[544,128]{1,0:T(8,128)(2,1)S(1)}, u32[]{:S(2)}) copy-start(bf16[544,128]{1,0:T(8,128)(2,1)S(1)} %constant_dynamic-update-slice_fusion.refs_0_) | copy-start | bytes 417796
  20.3 0.8 %copy-start.2 = (bf16[2048,128]{1,0:T(8,128)(2,1)}, bf16[2048,128]{1,0:T(8,128)(2,1)S(1)}, u32[]{:S(2)}) copy-start(bf16[2048,128]{1,0:T(8,128)(2,1)S(1)} %collective-permute-done.5.refs_2_) | copy-start | bytes 1572868
  29.3 1.9 %copy-start.3 = (bf16[2048,128]{1,0:T(8,128)(2,1)}, bf16[2048,128]{1,0:T(8,128)(2,1)S(1)}, u32[]{:S(2)}) copy-start(bf16[2048,128]{1,0:T(8,128)(2,1)S(1)} %collective-permute-done.4.refs_1_) | copy-start | bytes 1572868
  29.3 1.9 %collective-permute-start.6 = (bf16[2048,128]{1,0:T(8,128)(2,1)S(1)}, bf16[2048,128]{1,0:T(8,128)(2,1)S(1)}, u32[]{:S(2)}, u32[]{:S(2)}) collective-permute-start(bf16[2048,128]{1,0:T(8,128)(2,1)S(1)} %collective-permute-done.4.refs_1_), channel_id=1, source_target_pairs={{0,1},{1,0},{2,3},{3,2},{4,5},{5,4},{6,7},{7,6},{8,9},{9,8},{10,11... | collective-permute-start | bytes 1572872 | tf_op jit(solution)/shard_map/ppermute | solution.py:230
  31.2 0.8 %copy-start.4 = (bf16[2048,128]{1,0:T(8,128)(2,1)}, bf16[2048,128]{1,0:T(8,128)(2,1)S(1)}, u32[]{:S(2)}) copy-start(bf16[2048,128]{1,0:T(8,128)(2,1)S(1)} %collective-permute-done.6.refs_2_) | copy-start | bytes 1572868
  41.1 0.7 %copy-start.7 = (pred[8,9]{0,1:T(8,128)(4,1)S(1)}, pred[8,9]{0,1:T(8,128)(4,1)}, u32[]{:S(2)}) copy-start(pred[8,9]{0,1:T(8,128)(4,1)} %constant.75) | copy-start | bytes 220

commit v22 on v19

--- a/solution.py
+++ b/solution.py
@@ -243,15 +243,16 @@
     row_first = lax.axis_index("space") * rows
     col_first = lax.axis_index("match") * cols
     ext = extended(source, (("match", 1),), HALO)
+    ext = ext.reshape(rows * (cols + 2 * HALO), chans)
     small = jnp.concatenate([flow_proj, in_bias[None, :]], axis=0)
     taps = jnp.transpose(conv_out, (3, 0, 1, 2)).reshape(chans, -1)
     table = row_table(targets, width)
     targets, ext, conv_in, small, taps, table = lax.optimization_barrier(
         (targets, ext, conv_in, small, taps, table)
     )
-    ext = extended(ext, (("space", 0),), HALO)
+    ext = extended(ext, (("space", 0),), HALO * (cols + 2 * HALO))
     erows, ecols = rows + 2 * HALO, cols + 2 * HALO
-    warped, sum_x, sum_y = match(ext.reshape(erows * ecols, chans), targets, width, table)
+    warped, sum_x, sum_y = match(ext, targets, width, table)
     warped = warped.reshape(erows, ecols, chans)
     grow = row_first - HALO + jnp.arange(erows, dtype=jnp.int32)
     gcol = col_first - HALO + jnp.arange(ecols, dtype=jnp.int32)

time: 45.5 us -> 45.3 us (level)
    reshape x1, local copies, waits for them, and re-layouts: 0.68 us -> 0.02 us  [local(): ext = ext.reshape(rows * (cols + 2 * HALO), chans)]
    unnamed x21 -> x25, local copies, waits for them, and re-layouts: 3.59 us -> 4.24 us
  transfers between devices with their start and end apart: 7 -> 7, of which waited for: 4 -> 4; matrix products, arithmetic and copies ran while one was open for 3% -> 1% of each run, Pallas kernels for 18% -> 18%
where the time goes in v22:
time: 45.3 us; the launch traced here: 44.8 us
  Pallas kernels  14.5 us (32%)
  starting transfers between devices  10.9 us (24%)
  waiting for transfers between devices  8.47 us (19%)
  local copies, waits for them, and re-layouts  8.21 us (18%)
  other arithmetic  1.33 us (3%)
  matrix products  1.13 us (2%)
    pallas_call x2, Pallas kernels, match_step(): pl.pallas_call(kernel, grid=(nq,), in_specs=in_specs, out_specs=out_specs...  14.5 us
    ppermute x2, waiting for transfers between devices, extended(): lax.ppermute(lax.slice_in_dim(block, 0, width, axis=dim), axis, backward)  6.59 us
    ppermute x2, starting transfers between devices, extended(): lax.ppermute(lax.slice_in_dim(block, block.shape[dim] - width, None, axis...  5.76 us
    unnamed x25, local copies, waits for them, and re-layouts  4.24 us
    ppermute x2, starting transfers between devices, extended(): lax.ppermute(lax.slice_in_dim(block, 0, width, axis=dim), axis, backward)  2.58 us
    ppermute x1, starting transfers between devices, match(): shards.append((lax.ppermute(targets, 'match', sibling), me ^ 1, None))  2.35 us
    ppermute x1, waiting for transfers between devices, match(): pending = lax.ppermute(key, 'match', forward)  1.59 us
    slice x1, local copies, waits for them, and re-layouts, match(): return (warped[:count], flow[:count, 0], flow[:count, 1])  1.42 us
  transfers between devices with their start and end apart: 7, of which 4 were waited for; matrix products, arithmetic and copies ran while one was open for 1% of the time, Pallas kernels for 18%

profile of v22, /device:TPU:0, one launch (start us, length us, event | category | flops | bytes accessed | tf_op | source)
XLA Modules:
  0.0 44.8 jit_solution(6193993965921698631)
XLA Ops:
  0.0 0.8 %fusion.25 = (bf16[4,2,128]{2,1,0:T(2,128)(2,1)S(1)}, bf16[4,2,128]{2,1,0:T(2,128)(2,1)S(1)}) fusion(bf16[4,64,128]{2,1,0:T(8,128)(2,1)} %param.6), kind=kLoop, calls=%fused_computation.55 | loop fusion | bytes 8192 | tf_op jit(solution)/shard_map/slice | solution.py:20
  0.8 2.3 %collective-permute-start = (bf16[4,2,128]{2,1,0:T(2,128)(2,1)S(1)}, bf16[4,2,128]{2,1,0:T(2,128)(2,1)S(1)}, u32[]{:S(2)}, u32[]{:S(2)}) collective-permute-start(bf16[4,2,128]{2,1,0:T(2,128)(2,1)S(1)} %get-tuple-element.57), channel_id=1, source_target_pairs={{0,1},{1,2},{2,3},{4,5},{5,6},{6,7},{8,9},{9,10},{10,11},{12,13},{... | collective-permute-start | bytes 6152 | tf_op jit(solution)/shard_map/ppermute | solution.py:19
  3.1 1.3 %collective-permute-start.1 = (bf16[4,2,128]{2,1,0:T(2,128)(2,1)S(1)}, bf16[4,2,128]{2,1,0:T(2,128)(2,1)S(1)}, u32[]{:S(2)}, u32[]{:S(2)}) collective-permute-start(bf16[4,2,128]{2,1,0:T(2,128)(2,1)S(1)} %get-tuple-element.58), channel_id=1, source_target_pairs={{1,0},{2,1},{3,2},{5,4},{6,5},{7,6},{9,8},{10,9},{11,10},{13,12},{... | collective-permute-start | bytes 6152 | tf_op jit(solution)/shard_map/ppermute | solution.py:22
  4.4 0.0 copy-start.6
  4.5 0.0 copy-start.8
  4.5 0.0 copy-start.9
  4.5 0.7 %copy-done.8 = f32[2,128]{1,0:T(2,128)S(1)} copy-done((f32[2,128]{1,0:T(2,128)S(1)}, f32[2,128]{1,0:T(2,128)}, u32[]{:S(2)}) %copy-start.8) | copy-done | bytes 1048
  5.2 0.0 copy-start.7
  5.2 0.1 fusion.19
  5.3 0.6 %copy-done.7 = bf16[2,3,3,128]{3,0,2,1:T(2,128)(2,1)S(1)} copy-done((bf16[2,3,3,128]{3,0,2,1:T(2,128)(2,1)S(1)}, bf16[2,3,3,128]{3,0,2,1:T(2,128)(2,1)}, u32[]{:S(2)}) %copy-start.7) | copy-done | bytes 4632
  5.9 2.4 %collective-permute-done.1 = bf16[4,2,128]{2,1,0:T(2,128)(2,1)S(1)} collective-permute-done((bf16[4,2,128]{2,1,0:T(2,128)(2,1)S(1)}, bf16[4,2,128]{2,1,0:T(2,128)(2,1)S(1)}, u32[]{:S(2)}, u32[]{:S(2)}) %collective-permute-start.1) | collective-permute-done | bytes 2080 | tf_op jit(solution)/shard_map/ppermute | solution.py:22
  8.3 0.6 %broadcast_in_dim.25.refs_3_ = f32[8,128]{1,0:T(8,128)} broadcast(f32[128]{0:T(128)S(1)} %pad.4), dimensions={1} | broadcast | bytes 4608 | tf_op jit(solution)/shard_map/broadcast_in_dim | solution.py:179
  8.9 2.4 %collective-permute-start.5 = (bf16[2048,128]{1,0:T(8,128)(2,1)}, bf16[2048,128]{1,0:T(8,128)(2,1)S(1)}, u32[]{:S(2)}, u32[]{:S(2)}) collective-permute-start(bf16[2048,128]{1,0:T(8,128)(2,1)} %refs_1_), channel_id=1, source_target_pairs={{0,1},{1,0},{2,3},{3,2},{4,5},{5,4},{6,7},{7,6},{8,9},{9,8},{10,11... | collective-permute-start | bytes 1572872 | tf_op jit(solution)/shard_map/ppermute | solution.py:197
  11.3 0.2 collective-permute-start.4
  11.5 3.4 %collective-permute-start.2 = (bf16[136,128]{1,0:T(8,128)(2,1)S(1)}, bf16[136,128]{1,0:T(8,128)(2,1)S(1)}, u32[]{:S(2)}, u32[]{:S(2)}) collective-permute-start(bf16[136,128]{1,0:T(8,128)(2,1)S(1)} %get-tuple-element.56), channel_id=1, source_target_pairs={{0,4},{4,8},{8,12},{12,16},{16,20},{20,24},{24,28},{1,5},{5,9},{9,... | collective-permute-start | bytes 104456 | tf_op jit(solution)/shard_map/ppermute | solution.py:19
  14.9 1.3 %collective-permute-start.3 = (bf16[136,128]{1,0:T(8,128)(2,1)S(1)}, bf16[136,128]{1,0:T(8,128)(2,1)S(1)}, u32[]{:S(2)}, u32[]{:S(2)}) collective-permute-start(bf16[136,128]{1,0:T(8,128)(2,1)S(1)} %get-tuple-element.55), channel_id=1, source_target_pairs={{4,0},{8,4},{12,8},{16,12},{20,16},{24,20},{28,24},{5,1},{9,5},{13... | collective-permute-start | bytes 104456 | tf_op jit(solution)/shard_map/ppermute | solution.py:22
  16.2 0.3 collective-permute-done.2
  16.5 4.2 %collective-permute-done.3 = bf16[136,128]{1,0:T(8,128)(2,1)S(1)} collective-permute-done((bf16[136,128]{1,0:T(8,128)(2,1)S(1)}, bf16[136,128]{1,0:T(8,128)(2,1)S(1)}, u32[]{:S(2)}, u32[]{:S(2)}) %collective-permute-start.3) | collective-permute-done | bytes 34848 | tf_op jit(solution)/shard_map/ppermute | solution.py:22
  20.7 0.6 %copy-done.1 = bf16[544,128]{1,0:T(8,128)(2,1)} copy-done((bf16[544,128]{1,0:T(8,128)(2,1)}, bf16[544,128]{1,0:T(8,128)(2,1)S(1)}, u32[]{:S(2)}) %copy-start.1) | copy-done | bytes 139288
  21.4 0.8 %copy-done.2 = bf16[2048,128]{1,0:T(8,128)(2,1)} copy-done((bf16[2048,128]{1,0:T(8,128)(2,1)}, bf16[2048,128]{1,0:T(8,128)(2,1)S(1)}, u32[]{:S(2)}) %copy-start.2) | copy-done | bytes 524312
  22.2 8.1 %shard_map.64 = (f32[544,8]{1,0:T(8,128)}, f32[544,128]{1,0:T(8,128)}, f32[544,8]{1,0:T(8,128)}) custom-call(bf16[544,128]{1,0:T(8,128)(2,1)} %copy-done.1, bf16[2048,128]{1,0:T(8,128)(2,1)} %refs_1_, bf16[2048,128]{1,0:T(8,128)(2,1)} %copy-done.2, f32[8,128]{1,0:T(8,128)} %broadcast_in_dim.25.refs_3_), custom_call_target="tpu_custom_call" | custom-call | tf_op jit(solution)/shard_map/pallas_call | solution.py:151
  30.3 0.0 collective-permute-start.6
  30.3 0.1 broadcast_and_fusion
  30.4 0.1 slice.131
  30.4 0.1 copy.25
  30.6 1.6 %collective-permute-done.6.refs_2_ = bf16[2048,128]{1,0:T(8,128)(2,1)S(1)} collective-permute-done((bf16[2048,128]{1,0:T(8,128)(2,1)S(1)}, bf16[2048,128]{1,0:T(8,128)(2,1)S(1)}, u32[]{:S(2)}, u32[]{:S(2)}) %collective-permute-start.6) | collective-permute-done | bytes 524320 | tf_op jit(solution)/shard_map/ppermute | solution.py:223
  32.2 0.8 %copy-done.4 = bf16[2048,128]{1,0:T(8,128)(2,1)} copy-done((bf16[2048,128]{1,0:T(8,128)(2,1)}, bf16[2048,128]{1,0:T(8,128)(2,1)S(1)}, u32[]{:S(2)}) %copy-start.4) | copy-done | bytes 524312
  33.0 6.4 %shard_map.65 = (f32[544,128]{1,0:T(8,128)}, f32[544,8]{1,0:T(8,128)}) custom-call(bf16[544,128]{1,0:T(8,128)(2,1)} %copy-done.1, bf16[2048,128]{1,0:T(8,128)(2,1)} %copy-done.3, bf16[2048,128]{1,0:T(8,128)(2,1)} %copy-done.4, f32[8,128]{1,0:T(8,128)} %broadcast_in_dim.25.refs_3_, f32[544,8]{1,0:T(8,128)} %get-tuple-element.27.refs_4_, ...), custom_call_target="tpu_custom_call" | custom-call | tf_op jit(solution)/shard_map/pallas_call | solution.py:151
  39.4 1.4 %slice_reduce_fusion.1 = (f32[544]{0:T(1024)S(1)}, f32[544]{0:T(1024)S(1)}) fusion(f32[544,8]{1,0:T(8,128)} %get-tuple-element.30), kind=kLoop, calls=%fused_computation.8 | loop fusion | bytes 8704 | tf_op jit(solution)/shard_map/slice | solution.py:236
  40.8 0.1 reshape_squeeze.6
  40.9 0.1 slice.132
  41.0 0.1 reshape_squeeze.7
  41.0 0.1 broadcast_subtract_fusion
  41.1 0.1 slice.134
  41.2 0.1 slice_bitcast_fusion.1
  41.3 0.1 select_bitcast_fusion
  41.5 0.1 copy.67
  41.6 0.1 copy.28
  41.6 0.0 copy-start.10
  41.7 0.6 %copy-done.10 = pred[8,9]{0,1:T(8,128)(4,1)S(1)} copy-done((pred[8,9]{0,1:T(8,128)(4,1)S(1)}, pred[8,9]{0,1:T(8,128)(4,1)}, u32[]{:S(2)}) %copy-start.10) | copy-done | bytes 96
  42.3 0.9 %convolution_select_fusion = f32[6,8,9,128]{3,1,2,0:T(8,128)S(1)} fusion(bf16[3,3,128,128]{3,2,1,0:T(8,128)(2,1)S(1)} %copy-done, f32[8,1,7,2,128]{4,2,3,0,1:T(8,128)S(1)} %slice.157, f32[8,1,8,9,128]{4,2,3,0,1:T(8,128)S(1)} %copy.28, pred[8,9]{0,1:T(8,128)(4,1)S(1)} %copy-done.10), kind=kOutput, calls=%fused_computation | convolution fusion | flops 764737536 | bytes 868424 | tf_op jit(solution)/shard_map/conv_general_dilated | solution.py:266
  43.2 0.1 copy.29
  43.3 0.1 copy.30
  43.4 0.1 copy.31
  43.5 0.3 broadcast_select_fusion
  43.8 0.2 fusion.9
  44.0 0.1 fusion.23
  44.2 0.6 %maximum_add_fusion = f32[2,4,64]{2,1,0:T(4,128)} fusion(f32[1,4,64]{2,1,0:T(4,128)S(1)} %get-tuple-element.62, f32[1,4,64]{2,1,0:T(4,128)S(1)} %get-tuple-element.63, f32[1,4,64]{2,1,0:T(4,128)S(1)} %bitcast.110, f32[1,4,64]{2,1,0:T(4,128)S(1)} %bitcast.111, f32[1,4,64]{2,1,0:T(4,128)S(1)} %bitcast.108, f32[1,4,64]{2,1,0:T(4,128)S(1)} %bitcast.109, ...), kind=kLoop, calls=%fused_computation.24 | loop fusion | flops 9728 | bytes 22528 | tf_op jit(solution)/shard_map/add | solution.py:285
  (33 shorter events, 0.2 us)
Async XLA Ops:
  0.0 41.6 %copy-start = (bf16[3,3,128,128]{3,2,1,0:T(8,128)(2,1)S(1)}, bf16[3,3,128,128]{3,2,1,0:T(8,128)(2,1)}, u32[]{:S(2)}) copy-start(bf16[3,3,128,128]{3,2,1,0:T(8,128)(2,1)} %param.8) | copy-start | bytes 884740
  0.8 5.1 %collective-permute-start = (bf16[4,2,128]{2,1,0:T(2,128)(2,1)S(1)}, bf16[4,2,128]{2,1,0:T(2,128)(2,1)S(1)}, u32[]{:S(2)}, u32[]{:S(2)}) collective-permute-start(bf16[4,2,128]{2,1,0:T(2,128)(2,1)S(1)} %get-tuple-element.57), channel_id=1, source_target_pairs={{0,1},{1,2},{2,3},{4,5},{5,6},{6,7},{8,9},{9,10},{10,11},{12,13},{... | collective-permute-start | bytes 6152 | tf_op jit(solution)/shard_map/ppermute | solution.py:19
  3.1 5.2 %collective-permute-start.1 = (bf16[4,2,128]{2,1,0:T(2,128)(2,1)S(1)}, bf16[4,2,128]{2,1,0:T(2,128)(2,1)S(1)}, u32[]{:S(2)}, u32[]{:S(2)}) collective-permute-start(bf16[4,2,128]{2,1,0:T(2,128)(2,1)S(1)} %get-tuple-element.58), channel_id=1, source_target_pairs={{1,0},{2,1},{3,2},{5,4},{6,5},{7,6},{9,8},{10,9},{11,10},{13,12},{... | collective-permute-start | bytes 6152 | tf_op jit(solution)/shard_map/ppermute | solution.py:22
  4.4 3.9 %copy-start.6 = (bf16[4,64,128]{2,1,0:T(8,128)(2,1)S(1)}, bf16[4,64,128]{2,1,0:T(8,128)(2,1)}, u32[]{:S(2)}) copy-start(bf16[4,64,128]{2,1,0:T(8,128)(2,1)} %param.6) | copy-start | bytes 196612
  4.5 0.7 %copy-start.8 = (f32[2,128]{1,0:T(2,128)S(1)}, f32[2,128]{1,0:T(2,128)}, u32[]{:S(2)}) copy-start(f32[2,128]{1,0:T(2,128)} %param.9) | copy-start | bytes 3076
  4.5 0.7 %copy-start.9 = (f32[128]{0:T(128)S(1)}, f32[128]{0:T(128)}, u32[]{:S(2)}) copy-start(f32[128]{0:T(128)} %param.10) | copy-start | bytes 1540
  5.2 0.7 %copy-start.7 = (bf16[2,3,3,128]{3,0,2,1:T(2,128)(2,1)S(1)}, bf16[2,3,3,128]{3,0,2,1:T(2,128)(2,1)}, u32[]{:S(2)}) copy-start(bf16[2,3,3,128]{3,0,2,1:T(2,128)(2,1)} %param.11) | copy-start | bytes 13828
  8.9 11.8 %collective-permute-start.5 = (bf16[2048,128]{1,0:T(8,128)(2,1)}, bf16[2048,128]{1,0:T(8,128)(2,1)S(1)}, u32[]{:S(2)}, u32[]{:S(2)}) collective-permute-start(bf16[2048,128]{1,0:T(8,128)(2,1)} %refs_1_), channel_id=1, source_target_pairs={{0,1},{1,0},{2,3},{3,2},{4,5},{5,4},{6,7},{7,6},{8,9},{9,8},{10,11... | collective-permute-start | bytes 1572872 | tf_op jit(solution)/shard_map/ppermute | solution.py:197
  11.3 19.0 %collective-permute-start.4 = (bf16[2048,128]{1,0:T(8,128)(2,1)}, bf16[2048,128]{1,0:T(8,128)(2,1)S(1)}, u32[]{:S(2)}, u32[]{:S(2)}) collective-permute-start(bf16[2048,128]{1,0:T(8,128)(2,1)} %refs_1_), channel_id=1, source_target_pairs={{0,2},{1,3},{2,0},{3,1},{4,6},{5,7},{6,4},{7,5},{8,10},{9,11},{10,... | collective-permute-start | bytes 1572872 | tf_op jit(solution)/shard_map/ppermute | solution.py:200
  11.5 5.0 %collective-permute-start.2 = (bf16[136,128]{1,0:T(8,128)(2,1)S(1)}, bf16[136,128]{1,0:T(8,128)(2,1)S(1)}, u32[]{:S(2)}, u32[]{:S(2)}) collective-permute-start(bf16[136,128]{1,0:T(8,128)(2,1)S(1)} %get-tuple-element.56), channel_id=1, source_target_pairs={{0,4},{4,8},{8,12},{12,16},{16,20},{20,24},{24,28},{1,5},{5,9},{9,... | collective-permute-start | bytes 104456 | tf_op jit(solution)/shard_map/ppermute | solution.py:19
  14.9 5.8 %collective-permute-start.3 = (bf16[136,128]{1,0:T(8,128)(2,1)S(1)}, bf16[136,128]{1,0:T(8,128)(2,1)S(1)}, u32[]{:S(2)}, u32[]{:S(2)}) collective-permute-start(bf16[136,128]{1,0:T(8,128)(2,1)S(1)} %get-tuple-element.55), channel_id=1, source_target_pairs={{4,0},{8,4},{12,8},{16,12},{20,16},{24,20},{28,24},{5,1},{9,5},{13... | collective-permute-start | bytes 104456 | tf_op jit(solution)/shard_map/ppermute | solution.py:22
  20.7 0.7 %copy-start.1 = (bf16[544,128]{1,0:T(8,128)(2,1)}, bf16[544,128]{1,0:T(8,128)(2,1)S(1)}, u32[]{:S(2)}) copy-start(bf16[544,128]{1,0:T(8,128)(2,1)S(1)} %constant_dynamic-update-slice_fusion.refs_0_) | copy-start | bytes 417796
  21.4 0.8 %copy-start.2 = (bf16[2048,128]{1,0:T(8,128)(2,1)}, bf16[2048,128]{1,0:T(8,128)(2,1)S(1)}, u32[]{:S(2)}) copy-start(bf16[2048,128]{1,0:T(8,128)(2,1)S(1)} %collective-permute-done.5.refs_2_) | copy-start | bytes 1572868
  30.3 1.9 %copy-start.3 = (bf16[2048,128]{1,0:T(8,128)(2,1)}, bf16[2048,128]{1,0:T(8,128)(2,1)S(1)}, u32[]{:S(2)}) copy-start(bf16[2048,128]{1,0:T(8,128)(2,1)S(1)} %collective-permute-done.4.refs_1_) | copy-start | bytes 1572868
  30.3 1.9 %collective-permute-start.6 = (bf16[2048,128]{1,0:T(8,128)(2,1)S(1)}, bf16[2048,128]{1,0:T(8,128)(2,1)S(1)}, u32[]{:S(2)}, u32[]{:S(2)}) collective-permute-start(bf16[2048,128]{1,0:T(8,128)(2,1)S(1)} %collective-permute-done.4.refs_1_), channel_id=1, source_target_pairs={{0,1},{1,0},{2,3},{3,2},{4,5},{5,4},{6,7},{7,6},{8,9},{9,8},{10,11... | collective-permute-start | bytes 1572872 | tf_op jit(solution)/shard_map/ppermute | solution.py:223
  32.2 0.8 %copy-start.4 = (bf16[2048,128]{1,0:T(8,128)(2,1)}, bf16[2048,128]{1,0:T(8,128)(2,1)S(1)}, u32[]{:S(2)}) copy-start(bf16[2048,128]{1,0:T(8,128)(2,1)S(1)} %collective-permute-done.6.refs_2_) | copy-start | bytes 1572868
  39.4 1.9 %copy-start.5 = (f32[544,128]{1,0:T(8,128)S(1)}, f32[544,128]{1,0:T(8,128)}, u32[]{:S(2)}) copy-start(f32[544,128]{1,0:T(8,128)} %get-tuple-element.31) | copy-start | bytes 835588
  41.6 0.7 %copy-start.10 = (pred[8,9]{0,1:T(8,128)(4,1)S(1)}, pred[8,9]{0,1:T(8,128)(4,1)}, u32[]{:S(2)}) copy-start(pred[8,9]{0,1:T(8,128)(4,1)} %constant.75) | copy-start | bytes 220

commit v23 on v20

--- a/solution.py
+++ b/solution.py
@@ -188,7 +188,7 @@
     if tk % width == 0:
         owners = jnp.stack([owner for _, owner, _ in shards]) * (tk // width)
         owners = jnp.pad(owners.astype(jnp.float32), (0, 128 - n))
-        table = jnp.broadcast_to(owners[None, :], (8, 128))
+        table = owners[None, :]
     pending = None
     whole_rows = tk % width == 0
     if whole_rows and n > 1:

time: 44.2 us -> 45.2 us (1.023)
  local copies, waits for them, and re-layouts: 6.44 us -> 8.22 us
  other arithmetic: 2.03 us -> 1.33 us
  waiting for transfers between devices: 8.5 us -> 7.89 us
  starting transfers between devices: 11 us -> 11.6 us
    unnamed x21 -> x25, local copies, waits for them, and re-layouts: 2.39 us -> 4.32 us
    concatenate x1, other arithmetic: 0.71 us -> 0.01 us  [local(): small = jnp.concatenate([flow_proj, in_bias[None, :]], axis=0)]
    ppermute x2, waiting for transfers between devices: 6.69 us -> 6.01 us  [extended(): lax.ppermute(lax.slice_in_dim(block, 0, width, axis=dim), axis, backward)]
    ppermute x1, starting transfers between devices: 0.21 us -> 0.82 us  [match(): moved = lax.ppermute(targets, 'match', hop)]
  transfers between devices with their start and end apart: 7 -> 7, of which waited for: 4 -> 4; matrix products, arithmetic and copies ran while one was open for 4% -> 2% of each run, Pallas kernels for 18% -> 18%
where the time goes in v23:
time: 45.2 us; the launch traced here: 44.9 us
  Pallas kernels  14.5 us (32%)
  starting transfers between devices  11.6 us (26%)
  local copies, waits for them, and re-layouts  8.22 us (18%)
  waiting for transfers between devices  7.89 us (17%)
  other arithmetic  1.33 us (3%)
  matrix products  1.13 us (2%)
    pallas_call x2, Pallas kernels, match_step(): pl.pallas_call(kernel, grid=(nq,), in_specs=in_specs, out_specs=out_specs...  14.5 us
    ppermute x2, waiting for transfers between devices, extended(): lax.ppermute(lax.slice_in_dim(block, 0, width, axis=dim), axis, backward)  6.01 us
    ppermute x2, starting transfers between devices, extended(): lax.ppermute(lax.slice_in_dim(block, block.shape[dim] - width, None, axis...  5.76 us
    unnamed x25, local copies, waits for them, and re-layouts  4.32 us
    ppermute x2, starting transfers between devices, extended(): lax.ppermute(lax.slice_in_dim(block, 0, width, axis=dim), axis, backward)  2.58 us
    ppermute x1, starting transfers between devices, match(): shards.append((lax.ppermute(targets, 'match', sibling), me ^ 1, None))  2.42 us
    ppermute x1, waiting for transfers between devices, match(): pending = lax.ppermute(key, 'match', forward)  1.59 us
    slice x1, local copies, waits for them, and re-layouts, match(): return (warped[:count], flow[:count, 0], flow[:count, 1])  1.42 us
  transfers between devices with their start and end apart: 7, of which 4 were waited for; matrix products, arithmetic and copies ran while one was open for 2% of the time, Pallas kernels for 18%

profile of v23, /device:TPU:0, one launch (start us, length us, event | category | flops | bytes accessed | tf_op | source)
XLA Modules:
  0.0 44.9 jit_solution(9755770376157113950)
XLA Ops:
  0.0 0.8 %fusion.25 = (bf16[4,2,128]{2,1,0:T(2,128)(2,1)S(1)}, bf16[4,2,128]{2,1,0:T(2,128)(2,1)S(1)}) fusion(bf16[4,64,128]{2,1,0:T(8,128)(2,1)} %param.6), kind=kLoop, calls=%fused_computation.56 | loop fusion | bytes 8192 | tf_op jit(solution)/shard_map/slice | solution.py:20
  0.8 2.3 %collective-permute-start = (bf16[4,2,128]{2,1,0:T(2,128)(2,1)S(1)}, bf16[4,2,128]{2,1,0:T(2,128)(2,1)S(1)}, u32[]{:S(2)}, u32[]{:S(2)}) collective-permute-start(bf16[4,2,128]{2,1,0:T(2,128)(2,1)S(1)} %get-tuple-element.55), channel_id=1, source_target_pairs={{0,1},{1,2},{2,3},{4,5},{5,6},{6,7},{8,9},{9,10},{10,11},{12,13},{... | collective-permute-start | bytes 6152 | tf_op jit(solution)/shard_map/ppermute | solution.py:19
  3.1 1.3 %collective-permute-start.1 = (bf16[4,2,128]{2,1,0:T(2,128)(2,1)S(1)}, bf16[4,2,128]{2,1,0:T(2,128)(2,1)S(1)}, u32[]{:S(2)}, u32[]{:S(2)}) collective-permute-start(bf16[4,2,128]{2,1,0:T(2,128)(2,1)S(1)} %get-tuple-element.56), channel_id=1, source_target_pairs={{1,0},{2,1},{3,2},{5,4},{6,5},{7,6},{9,8},{10,9},{11,10},{13,12},{... | collective-permute-start | bytes 6152 | tf_op jit(solution)/shard_map/ppermute | solution.py:22
  4.4 0.0 copy-start.6
  4.5 0.1 fusion.19
  4.6 0.5 %pad_bitcast_fusion.refs_3_ = f32[1,128]{1,0:T(1,128)} fusion(f32[4]{0:T(128)S(1)} %fusion.19), kind=kLoop, calls=%fused_computation.50 | loop fusion | bytes 528 | tf_op jit(solution)/shard_map/broadcast_in_dim | solution.py:191
  5.1 0.7 %copy-done.8 = f32[2,128]{1,0:T(2,128)S(1)} copy-done((f32[2,128]{1,0:T(2,128)S(1)}, f32[2,128]{1,0:T(2,128)}, u32[]{:S(2)}) %copy-start.8) | copy-done | bytes 1048
  5.8 0.7 %copy-done.7 = bf16[2,3,3,128]{3,0,2,1:T(2,128)(2,1)S(1)} copy-done((bf16[2,3,3,128]{3,0,2,1:T(2,128)(2,1)S(1)}, bf16[2,3,3,128]{3,0,2,1:T(2,128)(2,1)}, u32[]{:S(2)}) %copy-start.7) | copy-done | bytes 4632
  6.5 0.0 collective-permute-done
  6.5 1.8 %collective-permute-done.1 = bf16[4,2,128]{2,1,0:T(2,128)(2,1)S(1)} collective-permute-done((bf16[4,2,128]{2,1,0:T(2,128)(2,1)S(1)}, bf16[4,2,128]{2,1,0:T(2,128)(2,1)S(1)}, u32[]{:S(2)}, u32[]{:S(2)}) %collective-permute-start.1) | collective-permute-done | bytes 2080 | tf_op jit(solution)/shard_map/ppermute | solution.py:22
  8.3 2.4 %collective-permute-start.5 = (bf16[2048,128]{1,0:T(8,128)(2,1)}, bf16[2048,128]{1,0:T(8,128)(2,1)S(1)}, u32[]{:S(2)}, u32[]{:S(2)}) collective-permute-start(bf16[2048,128]{1,0:T(8,128)(2,1)} %refs_1_), channel_id=1, source_target_pairs={{0,1},{1,0},{2,3},{3,2},{4,5},{5,4},{6,7},{7,6},{8,9},{9,8},{10,11... | collective-permute-start | bytes 1572872 | tf_op jit(solution)/shard_map/ppermute | solution.py:176
  10.8 0.8 %collective-permute-start.4 = (bf16[2048,128]{1,0:T(8,128)(2,1)}, bf16[2048,128]{1,0:T(8,128)(2,1)S(1)}, u32[]{:S(2)}, u32[]{:S(2)}) collective-permute-start(bf16[2048,128]{1,0:T(8,128)(2,1)} %refs_1_), channel_id=1, source_target_pairs={{0,2},{1,3},{2,0},{3,1},{4,6},{5,7},{6,4},{7,5},{8,10},{9,11},{10,... | collective-permute-start | bytes 1572872 | tf_op jit(solution)/shard_map/ppermute | solution.py:179
  11.6 3.4 %collective-permute-start.2 = (bf16[136,128]{1,0:T(8,128)(2,1)S(1)}, bf16[136,128]{1,0:T(8,128)(2,1)S(1)}, u32[]{:S(2)}, u32[]{:S(2)}) collective-permute-start(bf16[136,128]{1,0:T(8,128)(2,1)S(1)} %get-tuple-element.54), channel_id=1, source_target_pairs={{0,4},{4,8},{8,12},{12,16},{16,20},{20,24},{24,28},{1,5},{5,9},{9,... | collective-permute-start | bytes 104456 | tf_op jit(solution)/shard_map/ppermute | solution.py:19
  15.0 1.3 %collective-permute-start.3 = (bf16[136,128]{1,0:T(8,128)(2,1)S(1)}, bf16[136,128]{1,0:T(8,128)(2,1)S(1)}, u32[]{:S(2)}, u32[]{:S(2)}) collective-permute-start(bf16[136,128]{1,0:T(8,128)(2,1)S(1)} %get-tuple-element.53), channel_id=1, source_target_pairs={{4,0},{8,4},{12,8},{16,12},{20,16},{24,20},{28,24},{5,1},{9,5},{13... | collective-permute-start | bytes 104456 | tf_op jit(solution)/shard_map/ppermute | solution.py:22
  16.3 0.3 collective-permute-done.2
  16.6 4.2 %collective-permute-done.3 = bf16[136,128]{1,0:T(8,128)(2,1)S(1)} collective-permute-done((bf16[136,128]{1,0:T(8,128)(2,1)S(1)}, bf16[136,128]{1,0:T(8,128)(2,1)S(1)}, u32[]{:S(2)}, u32[]{:S(2)}) %collective-permute-start.3) | collective-permute-done | bytes 34848 | tf_op jit(solution)/shard_map/ppermute | solution.py:22
  20.9 0.0 collective-permute-done.5.refs_2_
  20.9 0.6 %copy-done.1 = bf16[544,128]{1,0:T(8,128)(2,1)} copy-done((bf16[544,128]{1,0:T(8,128)(2,1)}, bf16[544,128]{1,0:T(8,128)(2,1)S(1)}, u32[]{:S(2)}) %copy-start.1) | copy-done | bytes 139288
  21.5 0.8 %copy-done.4 = bf16[2048,128]{1,0:T(8,128)(2,1)} copy-done((bf16[2048,128]{1,0:T(8,128)(2,1)}, bf16[2048,128]{1,0:T(8,128)(2,1)S(1)}, u32[]{:S(2)}) %copy-start.4) | copy-done | bytes 524312
  22.3 8.1 %shard_map.64 = (f32[544,8]{1,0:T(8,128)}, f32[544,128]{1,0:T(8,128)}, f32[544,8]{1,0:T(8,128)}) custom-call(bf16[544,128]{1,0:T(8,128)(2,1)} %copy-done.1, bf16[2048,128]{1,0:T(8,128)(2,1)} %refs_1_, bf16[2048,128]{1,0:T(8,128)(2,1)} %copy-done.4, f32[1,128]{1,0:T(1,128)} %pad_bitcast_fusion.refs_3_), custom_call_target="tpu_custom_call" | custom-call | tf_op jit(solution)/shard_map/pallas_call | solution.py:151
  30.4 0.0 collective-permute-done.4.refs_1_
  30.4 0.0 collective-permute-start.6
  30.4 0.1 broadcast_and_fusion
  30.5 0.1 slice.131
  30.6 0.1 copy.25
  30.7 1.6 %collective-permute-done.6.refs_2_ = bf16[2048,128]{1,0:T(8,128)(2,1)S(1)} collective-permute-done((bf16[2048,128]{1,0:T(8,128)(2,1)S(1)}, bf16[2048,128]{1,0:T(8,128)(2,1)S(1)}, u32[]{:S(2)}, u32[]{:S(2)}) %collective-permute-start.6) | collective-permute-done | bytes 524320 | tf_op jit(solution)/shard_map/ppermute | solution.py:206
  32.3 0.8 %copy-done.3 = bf16[2048,128]{1,0:T(8,128)(2,1)} copy-done((bf16[2048,128]{1,0:T(8,128)(2,1)}, bf16[2048,128]{1,0:T(8,128)(2,1)S(1)}, u32[]{:S(2)}) %copy-start.3) | copy-done | bytes 524312
  33.1 6.4 %shard_map.65 = (f32[544,128]{1,0:T(8,128)}, f32[544,8]{1,0:T(8,128)}) custom-call(bf16[544,128]{1,0:T(8,128)(2,1)} %copy-done.1, bf16[2048,128]{1,0:T(8,128)(2,1)} %copy-done.2, bf16[2048,128]{1,0:T(8,128)(2,1)} %copy-done.3, f32[1,128]{1,0:T(1,128)} %pad_bitcast_fusion.refs_3_, f32[544,8]{1,0:T(8,128)} %get-tuple-element.25.refs_4_, ...), custom_call_target="tpu_custom_call" | custom-call | tf_op jit(solution)/shard_map/pallas_call | solution.py:151
  39.5 1.4 %slice_reduce_fusion.1 = (f32[544]{0:T(1024)S(1)}, f32[544]{0:T(1024)S(1)}) fusion(f32[544,8]{1,0:T(8,128)} %get-tuple-element.28), kind=kLoop, calls=%fused_computation.8 | loop fusion | bytes 8704 | tf_op jit(solution)/shard_map/slice | solution.py:219
  40.9 0.1 reshape_squeeze.6
  41.0 0.1 slice.132
  41.1 0.1 reshape_squeeze.7
  41.2 0.1 broadcast_subtract_fusion
  41.2 0.1 slice.134
  41.3 0.1 slice_bitcast_fusion.1
  41.4 0.1 select_bitcast_fusion
  41.6 0.1 copy.67
  41.7 0.1 copy.28
  41.7 0.0 copy-start.10
  41.8 0.6 %copy-done.10 = pred[8,9]{0,1:T(8,128)(4,1)S(1)} copy-done((pred[8,9]{0,1:T(8,128)(4,1)S(1)}, pred[8,9]{0,1:T(8,128)(4,1)}, u32[]{:S(2)}) %copy-start.10) | copy-done | bytes 96
  42.4 0.9 %convolution_select_fusion = f32[6,8,9,128]{3,1,2,0:T(8,128)S(1)} fusion(bf16[3,3,128,128]{3,2,1,0:T(8,128)(2,1)S(1)} %copy-done, f32[8,1,7,2,128]{4,2,3,0,1:T(8,128)S(1)} %slice.157, f32[8,1,8,9,128]{4,2,3,0,1:T(8,128)S(1)} %copy.28, pred[8,9]{0,1:T(8,128)(4,1)S(1)} %copy-done.10), kind=kOutput, calls=%fused_computation | convolution fusion | flops 764737536 | bytes 868424 | tf_op jit(solution)/shard_map/conv_general_dilated | solution.py:248
  43.4 0.1 copy.29
  43.4 0.1 copy.30
  43.5 0.1 copy.31
  43.6 0.3 broadcast_select_fusion
  43.9 0.2 fusion.9
  44.1 0.1 fusion.23
  44.3 0.6 %maximum_add_fusion = f32[2,4,64]{2,1,0:T(4,128)} fusion(f32[1,4,64]{2,1,0:T(4,128)S(1)} %get-tuple-element.60, f32[1,4,64]{2,1,0:T(4,128)S(1)} %get-tuple-element.61, f32[1,4,64]{2,1,0:T(4,128)S(1)} %bitcast.112, f32[1,4,64]{2,1,0:T(4,128)S(1)} %bitcast.113, f32[1,4,64]{2,1,0:T(4,128)S(1)} %bitcast.110, f32[1,4,64]{2,1,0:T(4,128)S(1)} %bitcast.111, ...), kind=kLoop, calls=%fused_computation.24 | loop fusion | flops 9728 | bytes 22528 | tf_op jit(solution)/shard_map/add | solution.py:267
  (32 shorter events, 0.2 us)
Async XLA Ops:
  0.0 41.8 %copy-start = (bf16[3,3,128,128]{3,2,1,0:T(8,128)(2,1)S(1)}, bf16[3,3,128,128]{3,2,1,0:T(8,128)(2,1)}, u32[]{:S(2)}) copy-start(bf16[3,3,128,128]{3,2,1,0:T(8,128)(2,1)} %param.8) | copy-start | bytes 884740
  0.8 5.7 %collective-permute-start = (bf16[4,2,128]{2,1,0:T(2,128)(2,1)S(1)}, bf16[4,2,128]{2,1,0:T(2,128)(2,1)S(1)}, u32[]{:S(2)}, u32[]{:S(2)}) collective-permute-start(bf16[4,2,128]{2,1,0:T(2,128)(2,1)S(1)} %get-tuple-element.55), channel_id=1, source_target_pairs={{0,1},{1,2},{2,3},{4,5},{5,6},{6,7},{8,9},{9,10},{10,11},{12,13},{... | collective-permute-start | bytes 6152 | tf_op jit(solution)/shard_map/ppermute | solution.py:19
  3.1 5.2 %collective-permute-start.1 = (bf16[4,2,128]{2,1,0:T(2,128)(2,1)S(1)}, bf16[4,2,128]{2,1,0:T(2,128)(2,1)S(1)}, u32[]{:S(2)}, u32[]{:S(2)}) collective-permute-start(bf16[4,2,128]{2,1,0:T(2,128)(2,1)S(1)} %get-tuple-element.56), channel_id=1, source_target_pairs={{1,0},{2,1},{3,2},{5,4},{6,5},{7,6},{9,8},{10,9},{11,10},{13,12},{... | collective-permute-start | bytes 6152 | tf_op jit(solution)/shard_map/ppermute | solution.py:22
  4.4 3.9 %copy-start.6 = (bf16[4,64,128]{2,1,0:T(8,128)(2,1)S(1)}, bf16[4,64,128]{2,1,0:T(8,128)(2,1)}, u32[]{:S(2)}) copy-start(bf16[4,64,128]{2,1,0:T(8,128)(2,1)} %param.6) | copy-start | bytes 196612
  5.1 0.7 %copy-start.8 = (f32[2,128]{1,0:T(2,128)S(1)}, f32[2,128]{1,0:T(2,128)}, u32[]{:S(2)}) copy-start(f32[2,128]{1,0:T(2,128)} %param.9) | copy-start | bytes 3076
  5.1 0.7 %copy-start.9 = (f32[128]{0:T(128)S(1)}, f32[128]{0:T(128)}, u32[]{:S(2)}) copy-start(f32[128]{0:T(128)} %param.10) | copy-start | bytes 1540
  5.8 0.7 %copy-start.7 = (bf16[2,3,3,128]{3,0,2,1:T(2,128)(2,1)S(1)}, bf16[2,3,3,128]{3,0,2,1:T(2,128)(2,1)}, u32[]{:S(2)}) copy-start(bf16[2,3,3,128]{3,0,2,1:T(2,128)(2,1)} %param.11) | copy-start | bytes 13828
  8.3 12.5 %collective-permute-start.5 = (bf16[2048,128]{1,0:T(8,128)(2,1)}, bf16[2048,128]{1,0:T(8,128)(2,1)S(1)}, u32[]{:S(2)}, u32[]{:S(2)}) collective-permute-start(bf16[2048,128]{1,0:T(8,128)(2,1)} %refs_1_), channel_id=1, source_target_pairs={{0,1},{1,0},{2,3},{3,2},{4,5},{5,4},{6,7},{7,6},{8,9},{9,8},{10,11... | collective-permute-start | bytes 1572872 | tf_op jit(solution)/shard_map/ppermute | solution.py:176
  10.8 19.6 %collective-permute-start.4 = (bf16[2048,128]{1,0:T(8,128)(2,1)}, bf16[2048,128]{1,0:T(8,128)(2,1)S(1)}, u32[]{:S(2)}, u32[]{:S(2)}) collective-permute-start(bf16[2048,128]{1,0:T(8,128)(2,1)} %refs_1_), channel_id=1, source_target_pairs={{0,2},{1,3},{2,0},{3,1},{4,6},{5,7},{6,4},{7,5},{8,10},{9,11},{10,... | collective-permute-start | bytes 1572872 | tf_op jit(solution)/shard_map/ppermute | solution.py:179
  11.6 5.0 %collective-permute-start.2 = (bf16[136,128]{1,0:T(8,128)(2,1)S(1)}, bf16[136,128]{1,0:T(8,128)(2,1)S(1)}, u32[]{:S(2)}, u32[]{:S(2)}) collective-permute-start(bf16[136,128]{1,0:T(8,128)(2,1)S(1)} %get-tuple-element.54), channel_id=1, source_target_pairs={{0,4},{4,8},{8,12},{12,16},{16,20},{20,24},{24,28},{1,5},{5,9},{9,... | collective-permute-start | bytes 104456 | tf_op jit(solution)/shard_map/ppermute | solution.py:19
  15.0 5.8 %collective-permute-start.3 = (bf16[136,128]{1,0:T(8,128)(2,1)S(1)}, bf16[136,128]{1,0:T(8,128)(2,1)S(1)}, u32[]{:S(2)}, u32[]{:S(2)}) collective-permute-start(bf16[136,128]{1,0:T(8,128)(2,1)S(1)} %get-tuple-element.53), channel_id=1, source_target_pairs={{4,0},{8,4},{12,8},{16,12},{20,16},{24,20},{28,24},{5,1},{9,5},{13... | collective-permute-start | bytes 104456 | tf_op jit(solution)/shard_map/ppermute | solution.py:22
  20.9 0.7 %copy-start.1 = (bf16[544,128]{1,0:T(8,128)(2,1)}, bf16[544,128]{1,0:T(8,128)(2,1)S(1)}, u32[]{:S(2)}) copy-start(bf16[544,128]{1,0:T(8,128)(2,1)S(1)} %constant_dynamic-update-slice_fusion.refs_0_) | copy-start | bytes 417796
  21.5 0.8 %copy-start.4 = (bf16[2048,128]{1,0:T(8,128)(2,1)}, bf16[2048,128]{1,0:T(8,128)(2,1)S(1)}, u32[]{:S(2)}) copy-start(bf16[2048,128]{1,0:T(8,128)(2,1)S(1)} %collective-permute-done.5.refs_2_) | copy-start | bytes 1572868
  30.4 1.9 %copy-start.2 = (bf16[2048,128]{1,0:T(8,128)(2,1)}, bf16[2048,128]{1,0:T(8,128)(2,1)S(1)}, u32[]{:S(2)}) copy-start(bf16[2048,128]{1,0:T(8,128)(2,1)S(1)} %collective-permute-done.4.refs_1_) | copy-start | bytes 1572868
  30.4 1.9 %collective-permute-start.6 = (bf16[2048,128]{1,0:T(8,128)(2,1)S(1)}, bf16[2048,128]{1,0:T(8,128)(2,1)S(1)}, u32[]{:S(2)}, u32[]{:S(2)}) collective-permute-start(bf16[2048,128]{1,0:T(8,128)(2,1)S(1)} %collective-permute-done.4.refs_1_), channel_id=1, source_target_pairs={{0,1},{1,0},{2,3},{3,2},{4,5},{5,4},{6,7},{7,6},{8,9},{9,8},{10,11... | collective-permute-start | bytes 1572872 | tf_op jit(solution)/shard_map/ppermute | solution.py:206
  32.3 0.8 %copy-start.3 = (bf16[2048,128]{1,0:T(8,128)(2,1)}, bf16[2048,128]{1,0:T(8,128)(2,1)S(1)}, u32[]{:S(2)}) copy-start(bf16[2048,128]{1,0:T(8,128)(2,1)S(1)} %collective-permute-done.6.refs_2_) | copy-start | bytes 1572868
  39.5 1.9 %copy-start.5 = (f32[544,128]{1,0:T(8,128)S(1)}, f32[544,128]{1,0:T(8,128)}, u32[]{:S(2)}) copy-start(f32[544,128]{1,0:T(8,128)} %get-tuple-element.29) | copy-start | bytes 835588
  41.7 0.7 %copy-start.10 = (pred[8,9]{0,1:T(8,128)(4,1)S(1)}, pred[8,9]{0,1:T(8,128)(4,1)}, u32[]{:S(2)}) copy-start(pred[8,9]{0,1:T(8,128)(4,1)} %constant.75) | copy-start | bytes 220

commit v24 on v20

--- a/solution.py
+++ b/solution.py
@@ -245,10 +245,12 @@
     flow_x = sum_x.reshape(erows, ecols) - col_pos[None, :]
     flow_y = sum_y.reshape(erows, ecols) - row_pos[:, None]
 
+    hi, rest = split_bf16(warped)
+    mid, lo = split_bf16(rest.astype(jnp.float32) + (warped - hi.astype(jnp.float32) - rest.astype(jnp.float32)))
+    pieces = jnp.concatenate([hi, mid, lo], axis=-1)
     pre = lax.conv_general_dilated(
-        warped[None], conv_in.astype(jnp.float32), (1, 1), "VALID",
+        pieces[None], jnp.concatenate([conv_in] * 3, axis=2), (1, 1), "VALID",
         dimension_numbers=("NHWC", "HWIO", "NHWC"),
-        precision=lax.Precision.HIGHEST,
         preferred_element_type=jnp.float32,
     )[0]
     fx1 = flow_x[1:-1, 1:-1]

time: 44.2 us -> 46.1 us (1.043)
  other arithmetic: 2.03 us -> 3.09 us
  local copies, waits for them, and re-layouts: 6.44 us -> 7.12 us
    slice x1, local copies, waits for them, and re-layouts: 1.42 us -> 0.33 us  [match(): return (warped[:count], flow[:count, 0], flow[:count, 1])]
    reshape x1, local copies, waits for them, and re-layouts: 0.03 us -> 0.97 us  [local(): warped = warped.reshape(erows, ecols, chans)]
    concatenate x1, other arithmetic: 0.03 us -> 0.87 us  [extended(): block = jnp.concatenate([low, block, high], axis=dim)]
    transpose x1, local copies, waits for them, and re-layouts: 0.01 us -> 0.69 us  [local(): taps = jnp.transpose(conv_out, (3, 0, 1, 2)).reshape(chans, -1)]
    unnamed x21 -> x17, local copies, waits for them, and re-layouts: 2.39 us -> 2.55 us
  transfers between devices with their start and end apart: 7 -> 7, of which waited for: 4 -> 4; matrix products, arithmetic and copies ran while one was open for 4% -> 6% of each run, Pallas kernels for 18% -> 18%
where the time goes in v24:
time: 46.1 us; the launch traced here: 45.5 us
  Pallas kernels  14.5 us (31%)
  starting transfers between devices  11 us (24%)
  waiting for transfers between devices  8.5 us (18%)
  local copies, waits for them, and re-layouts  7.12 us (15%)
  other arithmetic  3.09 us (7%)
  matrix products  1.14 us (2%)
    pallas_call x2, Pallas kernels, match_step(): pl.pallas_call(kernel, grid=(nq,), in_specs=in_specs, out_specs=out_specs...  14.5 us
    ppermute x2, waiting for transfers between devices, extended(): lax.ppermute(lax.slice_in_dim(block, 0, width, axis=dim), axis, backward)  6.69 us
    ppermute x2, starting transfers between devices, extended(): lax.ppermute(lax.slice_in_dim(block, block.shape[dim] - width, None, axis...  5.76 us
    ppermute x2, starting transfers between devices, extended(): lax.ppermute(lax.slice_in_dim(block, 0, width, axis=dim), axis, backward)  2.57 us
    unnamed x17, local copies, waits for them, and re-layouts  2.55 us
    ppermute x1, starting transfers between devices, match(): shards.append((lax.ppermute(targets, 'match', sibling), me ^ 1, None))  2.42 us
    ppermute x1, waiting for transfers between devices, match(): pending = lax.ppermute(key, 'match', forward)  1.59 us
    reshape x1, local copies, waits for them, and re-layouts, local(): warped = warped.reshape(erows, ecols, chans)  0.97 us
  transfers between devices with their start and end apart: 7, of which 4 were waited for; matrix products, arithmetic and copies ran while one was open for 6% of the time, Pallas kernels for 18%

profile of v24, /device:TPU:0, one launch (start us, length us, event | category | flops | bytes accessed | tf_op | source)
XLA Modules:
  0.0 45.5 jit_solution(15729911624839111352)
XLA Ops:
  0.0 0.7 %fusion.34 = (bf16[4,2,128]{2,1,0:T(2,128)(2,1)S(1)}, bf16[4,2,128]{2,1,0:T(2,128)(2,1)S(1)}) fusion(bf16[4,64,128]{2,1,0:T(8,128)(2,1)} %param.6), kind=kLoop, calls=%fused_computation.67 | loop fusion | bytes 8192 | tf_op jit(solution)/shard_map/slice | solution.py:20
  0.7 2.3 %collective-permute-start = (bf16[4,2,128]{2,1,0:T(2,128)(2,1)S(1)}, bf16[4,2,128]{2,1,0:T(2,128)(2,1)S(1)}, u32[]{:S(2)}, u32[]{:S(2)}) collective-permute-start(bf16[4,2,128]{2,1,0:T(2,128)(2,1)S(1)} %get-tuple-element.57), channel_id=1, source_target_pairs={{0,1},{1,2},{2,3},{4,5},{5,6},{6,7},{8,9},{9,10},{10,11},{12,13},{... | collective-permute-start | bytes 6152 | tf_op jit(solution)/shard_map/ppermute | solution.py:19
  3.1 1.3 %collective-permute-start.1 = (bf16[4,2,128]{2,1,0:T(2,128)(2,1)S(1)}, bf16[4,2,128]{2,1,0:T(2,128)(2,1)S(1)}, u32[]{:S(2)}, u32[]{:S(2)}) collective-permute-start(bf16[4,2,128]{2,1,0:T(2,128)(2,1)S(1)} %get-tuple-element.58), channel_id=1, source_target_pairs={{1,0},{2,1},{3,2},{5,4},{6,5},{7,6},{9,8},{10,9},{11,10},{13,12},{... | collective-permute-start | bytes 6152 | tf_op jit(solution)/shard_map/ppermute | solution.py:22
  4.4 0.7 %pad_maximum_fusion.1 = f32[3,128]{1,0:T(4,128)S(1)} fusion(f32[1,128]{1,0:T(1,128)} %bitcast.113, f32[2,128]{1,0:T(2,128)} %param.9), kind=kLoop, calls=%fused_computation.45 | loop fusion | flops 384 | bytes 3072 | tf_op jit(solution)/shard_map/concatenate | solution.py:230
  5.1 0.7 %copy.24 = bf16[128,2,3,3]{0,3,2,1:T(4,128)(2,1)S(1)} copy(bf16[128,2,3,3]{0,1,3,2:T(2,128)(2,1)} %bitcast.112) | data formatting | bytes 9216 | tf_op jit(solution)/shard_map/transpose | solution.py:231
  5.8 2.4 %collective-permute-done.1 = bf16[4,2,128]{2,1,0:T(2,128)(2,1)S(1)} collective-permute-done((bf16[4,2,128]{2,1,0:T(2,128)(2,1)S(1)}, bf16[4,2,128]{2,1,0:T(2,128)(2,1)S(1)}, u32[]{:S(2)}, u32[]{:S(2)}) %collective-permute-start.1) | collective-permute-done | bytes 2080 | tf_op jit(solution)/shard_map/ppermute | solution.py:22
  8.2 0.9 %pad_maximum_fusion = bf16[4,68,128]{2,1,0:T(8,128)(2,1)S(1)} fusion(bf16[4,2,128]{2,1,0:T(2,128)(2,1)S(1)} %collective-permute-done.1, bf16[4,64,128]{2,1,0:T(8,128)(2,1)} %param.6, bf16[4,2,128]{2,1,0:T(2,128)(2,1)S(1)} %collective-permute-done), kind=kLoop, calls=%fused_computation.31 | loop fusion | flops 208896 | bytes 139264 | tf_op jit(solution)/shard_map/concatenate | solution.py:23
  9.1 2.4 %collective-permute-start.5 = (bf16[2048,128]{1,0:T(8,128)(2,1)}, bf16[2048,128]{1,0:T(8,128)(2,1)S(1)}, u32[]{:S(2)}, u32[]{:S(2)}) collective-permute-start(bf16[2048,128]{1,0:T(8,128)(2,1)} %refs_1_), channel_id=1, source_target_pairs={{0,1},{1,0},{2,3},{3,2},{4,5},{5,4},{6,7},{7,6},{8,9},{9,8},{10,11... | collective-permute-start | bytes 1572872 | tf_op jit(solution)/shard_map/ppermute | solution.py:176
  11.5 0.2 collective-permute-start.4
  11.8 3.4 %collective-permute-start.2 = (bf16[136,128]{1,0:T(8,128)(2,1)S(1)}, bf16[136,128]{1,0:T(8,128)(2,1)S(1)}, u32[]{:S(2)}, u32[]{:S(2)}) collective-permute-start(bf16[136,128]{1,0:T(8,128)(2,1)S(1)} %get-tuple-element.56), channel_id=1, source_target_pairs={{0,4},{4,8},{8,12},{12,16},{16,20},{20,24},{24,28},{1,5},{5,9},{9,... | collective-permute-start | bytes 104456 | tf_op jit(solution)/shard_map/ppermute | solution.py:19
  15.2 0.1 fusion.28
  15.3 1.3 %collective-permute-start.3 = (bf16[136,128]{1,0:T(8,128)(2,1)S(1)}, bf16[136,128]{1,0:T(8,128)(2,1)S(1)}, u32[]{:S(2)}, u32[]{:S(2)}) collective-permute-start(bf16[136,128]{1,0:T(8,128)(2,1)S(1)} %get-tuple-element.55), channel_id=1, source_target_pairs={{4,0},{8,4},{12,8},{16,12},{20,16},{24,20},{28,24},{5,1},{9,5},{13... | collective-permute-start | bytes 104456 | tf_op jit(solution)/shard_map/ppermute | solution.py:22
  16.6 0.2 collective-permute-done.2
  16.8 4.3 %collective-permute-done.3 = bf16[136,128]{1,0:T(8,128)(2,1)S(1)} collective-permute-done((bf16[136,128]{1,0:T(8,128)(2,1)S(1)}, bf16[136,128]{1,0:T(8,128)(2,1)S(1)}, u32[]{:S(2)}, u32[]{:S(2)}) %collective-permute-start.3) | collective-permute-done | bytes 34848 | tf_op jit(solution)/shard_map/ppermute | solution.py:22
  21.1 0.7 %broadcast_in_dim.45.refs_3_ = f32[8,128]{1,0:T(8,128)} broadcast(f32[128]{0:T(128)S(1)} %pad.4), dimensions={1} | broadcast | bytes 4608 | tf_op jit(solution)/shard_map/broadcast_in_dim | solution.py:191
  21.8 0.2 copy-done.2
  22.0 8.1 %shard_map.64 = (f32[544,8]{1,0:T(8,128)}, f32[544,128]{1,0:T(8,128)}, f32[544,8]{1,0:T(8,128)}) custom-call(bf16[544,128]{1,0:T(8,128)(2,1)} %copy-done.1, bf16[2048,128]{1,0:T(8,128)(2,1)} %refs_1_, bf16[2048,128]{1,0:T(8,128)(2,1)} %copy-done.2, f32[8,128]{1,0:T(8,128)} %broadcast_in_dim.45.refs_3_), custom_call_target="tpu_custom_call" | custom-call | tf_op jit(solution)/shard_map/pallas_call | solution.py:151
  30.1 0.1 broadcast_and_fusion
  30.1 0.1 slice.131
  30.2 0.1 copy.25
  30.4 1.6 %collective-permute-done.6.refs_2_ = bf16[2048,128]{1,0:T(8,128)(2,1)S(1)} collective-permute-done((bf16[2048,128]{1,0:T(8,128)(2,1)S(1)}, bf16[2048,128]{1,0:T(8,128)(2,1)S(1)}, u32[]{:S(2)}, u32[]{:S(2)}) %collective-permute-start.6) | collective-permute-done | bytes 524320 | tf_op jit(solution)/shard_map/ppermute | solution.py:206
  32.0 0.8 %copy-done.4 = bf16[2048,128]{1,0:T(8,128)(2,1)} copy-done((bf16[2048,128]{1,0:T(8,128)(2,1)}, bf16[2048,128]{1,0:T(8,128)(2,1)S(1)}, u32[]{:S(2)}) %copy-start.4) | copy-done | bytes 524312
  32.8 6.4 %shard_map.65 = (f32[544,128]{1,0:T(8,128)}, f32[544,8]{1,0:T(8,128)}) custom-call(bf16[544,128]{1,0:T(8,128)(2,1)} %copy-done.1, bf16[2048,128]{1,0:T(8,128)(2,1)} %copy-done.3, bf16[2048,128]{1,0:T(8,128)(2,1)} %copy-done.4, f32[8,128]{1,0:T(8,128)} %broadcast_in_dim.45.refs_3_, f32[544,8]{1,0:T(8,128)} %get-tuple-element.25.refs_4_, ...), custom_call_target="tpu_custom_call" | custom-call | tf_op jit(solution)/shard_map/pallas_call | solution.py:151
  39.2 1.0 %reshape.67 = f32[8,68,128]{2,1,0:T(8,128)S(1)} reshape(f32[544,128]{1,0:T(8,128)} %get-tuple-element.29) | data formatting | bytes 557056 | tf_op jit(solution)/shard_map/reshape | solution.py:238
  40.1 0.1 fusion.17
  40.3 0.1 select_convert_fusion
  40.5 0.6 %copy-done = f32[544,8]{1,0:T(8,128)S(1)} copy-done((f32[544,8]{1,0:T(8,128)S(1)}, f32[544,8]{1,0:T(8,128)}, u32[]{:S(2)}) %copy-start) | copy-done | bytes 17432
  41.1 0.3 slice_reduce_fusion.1
  41.4 0.1 reshape_squeeze.6
  41.5 0.1 slice.132
  41.6 0.1 reshape_squeeze.7
  41.7 0.1 broadcast_subtract_fusion
  41.7 0.1 slice.134
  41.8 0.1 slice_bitcast_fusion.1
  41.9 0.1 maximum_bitcast_fusion
  42.0 0.1 copy.67
  42.1 0.0 copy-start.5
  42.1 0.0 copy-start.6
  42.1 0.1 copy.28
  42.2 0.8 %copy-done.5 = bf16[3,3,128,128]{3,2,1,0:T(8,128)(2,1)S(1)} copy-done((bf16[3,3,128,128]{3,2,1,0:T(8,128)(2,1)S(1)}, bf16[3,3,128,128]{3,2,1,0:T(8,128)(2,1)}, u32[]{:S(2)}) %copy-start.5) | copy-done | bytes 294936
  43.0 0.9 %convolution_select_fusion = f32[6,8,9,128]{3,1,2,0:T(8,128)S(1)} fusion(bf16[3,3,128,128]{3,2,1,0:T(8,128)(2,1)S(1)} %copy-done.5, bf16[8,1,7,2,384]{4,2,3,0,1:T(8,128)(2,1)S(1)} %slice.157, bf16[8,1,8,9,384]{4,2,3,0,1:T(8,128)(2,1)S(1)} %copy.28, pred[8,9]{0,1:T(8,128)(4,1)S(1)} %copy-done.6), kind=kOutput, calls=%fused_computation | convolution fusion | flops 386537472 | bytes 1044552 | tf_op jit(solution)/shard_map/conv_general_dilated | solution.py:251
  44.0 0.1 copy.29
  44.1 0.1 copy.30
  44.2 0.1 copy.31
  44.3 0.3 broadcast_select_fusion
  44.6 0.2 fusion.18
  44.8 0.1 fusion.32
  44.9 0.6 %maximum_add_fusion = f32[2,4,64]{2,1,0:T(4,128)} fusion(f32[1,4,64]{2,1,0:T(4,128)S(1)} %get-tuple-element.62, f32[1,4,64]{2,1,0:T(4,128)S(1)} %get-tuple-element.63, f32[1,4,64]{2,1,0:T(4,128)S(1)} %bitcast.109, f32[1,4,64]{2,1,0:T(4,128)S(1)} %bitcast.110, f32[1,4,64]{2,1,0:T(4,128)S(1)} %bitcast.107, f32[1,4,64]{2,1,0:T(4,128)S(1)} %bitcast.108, ...), kind=kLoop, calls=%fused_computation.36 | loop fusion | flops 9728 | bytes 22528 | tf_op jit(solution)/shard_map/add | solution.py:269
  (27 shorter events, 0.2 us)
Async XLA Ops:
  0.7 5.1 %collective-permute-start = (bf16[4,2,128]{2,1,0:T(2,128)(2,1)S(1)}, bf16[4,2,128]{2,1,0:T(2,128)(2,1)S(1)}, u32[]{:S(2)}, u32[]{:S(2)}) collective-permute-start(bf16[4,2,128]{2,1,0:T(2,128)(2,1)S(1)} %get-tuple-element.57), channel_id=1, source_target_pairs={{0,1},{1,2},{2,3},{4,5},{5,6},{6,7},{8,9},{9,10},{10,11},{12,13},{... | collective-permute-start | bytes 6152 | tf_op jit(solution)/shard_map/ppermute | solution.py:19
  3.1 5.2 %collective-permute-start.1 = (bf16[4,2,128]{2,1,0:T(2,128)(2,1)S(1)}, bf16[4,2,128]{2,1,0:T(2,128)(2,1)S(1)}, u32[]{:S(2)}, u32[]{:S(2)}) collective-permute-start(bf16[4,2,128]{2,1,0:T(2,128)(2,1)S(1)} %get-tuple-element.58), channel_id=1, source_target_pairs={{1,0},{2,1},{3,2},{5,4},{6,5},{7,6},{9,8},{10,9},{11,10},{13,12},{... | collective-permute-start | bytes 6152 | tf_op jit(solution)/shard_map/ppermute | solution.py:22
  9.1 12.0 %collective-permute-start.5 = (bf16[2048,128]{1,0:T(8,128)(2,1)}, bf16[2048,128]{1,0:T(8,128)(2,1)S(1)}, u32[]{:S(2)}, u32[]{:S(2)}) collective-permute-start(bf16[2048,128]{1,0:T(8,128)(2,1)} %refs_1_), channel_id=1, source_target_pairs={{0,1},{1,0},{2,3},{3,2},{4,5},{5,4},{6,7},{7,6},{8,9},{9,8},{10,11... | collective-permute-start | bytes 1572872 | tf_op jit(solution)/shard_map/ppermute | solution.py:176
  11.5 18.5 %collective-permute-start.4 = (bf16[2048,128]{1,0:T(8,128)(2,1)}, bf16[2048,128]{1,0:T(8,128)(2,1)S(1)}, u32[]{:S(2)}, u32[]{:S(2)}) collective-permute-start(bf16[2048,128]{1,0:T(8,128)(2,1)} %refs_1_), channel_id=1, source_target_pairs={{0,2},{1,3},{2,0},{3,1},{4,6},{5,7},{6,4},{7,5},{8,10},{9,11},{10,... | collective-permute-start | bytes 1572872 | tf_op jit(solution)/shard_map/ppermute | solution.py:179
  11.8 5.0 %collective-permute-start.2 = (bf16[136,128]{1,0:T(8,128)(2,1)S(1)}, bf16[136,128]{1,0:T(8,128)(2,1)S(1)}, u32[]{:S(2)}, u32[]{:S(2)}) collective-permute-start(bf16[136,128]{1,0:T(8,128)(2,1)S(1)} %get-tuple-element.56), channel_id=1, source_target_pairs={{0,4},{4,8},{8,12},{12,16},{16,20},{20,24},{24,28},{1,5},{5,9},{9,... | collective-permute-start | bytes 104456 | tf_op jit(solution)/shard_map/ppermute | solution.py:19
  15.3 5.8 %collective-permute-start.3 = (bf16[136,128]{1,0:T(8,128)(2,1)S(1)}, bf16[136,128]{1,0:T(8,128)(2,1)S(1)}, u32[]{:S(2)}, u32[]{:S(2)}) collective-permute-start(bf16[136,128]{1,0:T(8,128)(2,1)S(1)} %get-tuple-element.55), channel_id=1, source_target_pairs={{4,0},{8,4},{12,8},{16,12},{20,16},{24,20},{28,24},{5,1},{9,5},{13... | collective-permute-start | bytes 104456 | tf_op jit(solution)/shard_map/ppermute | solution.py:22
  21.1 0.7 %copy-start.1 = (bf16[544,128]{1,0:T(8,128)(2,1)}, bf16[544,128]{1,0:T(8,128)(2,1)S(1)}, u32[]{:S(2)}) copy-start(bf16[544,128]{1,0:T(8,128)(2,1)S(1)} %constant_dynamic-update-slice_fusion.refs_0_) | copy-start | bytes 417796
  21.1 0.8 %copy-start.2 = (bf16[2048,128]{1,0:T(8,128)(2,1)}, bf16[2048,128]{1,0:T(8,128)(2,1)S(1)}, u32[]{:S(2)}) copy-start(bf16[2048,128]{1,0:T(8,128)(2,1)S(1)} %collective-permute-done.5.refs_2_) | copy-start | bytes 1572868
  30.0 1.9 %copy-start.3 = (bf16[2048,128]{1,0:T(8,128)(2,1)}, bf16[2048,128]{1,0:T(8,128)(2,1)S(1)}, u32[]{:S(2)}) copy-start(bf16[2048,128]{1,0:T(8,128)(2,1)S(1)} %collective-permute-done.4.refs_1_) | copy-start | bytes 1572868
  30.0 1.9 %collective-permute-start.6 = (bf16[2048,128]{1,0:T(8,128)(2,1)S(1)}, bf16[2048,128]{1,0:T(8,128)(2,1)S(1)}, u32[]{:S(2)}, u32[]{:S(2)}) collective-permute-start(bf16[2048,128]{1,0:T(8,128)(2,1)S(1)} %collective-permute-done.4.refs_1_), channel_id=1, source_target_pairs={{0,1},{1,0},{2,3},{3,2},{4,5},{5,4},{6,7},{7,6},{8,9},{9,8},{10,11... | collective-permute-start | bytes 1572872 | tf_op jit(solution)/shard_map/ppermute | solution.py:206
  32.0 0.8 %copy-start.4 = (bf16[2048,128]{1,0:T(8,128)(2,1)}, bf16[2048,128]{1,0:T(8,128)(2,1)S(1)}, u32[]{:S(2)}) copy-start(bf16[2048,128]{1,0:T(8,128)(2,1)S(1)} %collective-permute-done.6.refs_2_) | copy-start | bytes 1572868
  40.1 1.0 %copy-start = (f32[544,8]{1,0:T(8,128)S(1)}, f32[544,8]{1,0:T(8,128)}, u32[]{:S(2)}) copy-start(f32[544,8]{1,0:T(8,128)} %get-tuple-element.28) | copy-start | bytes 52228
  42.1 1.0 %copy-start.5 = (bf16[3,3,128,128]{3,2,1,0:T(8,128)(2,1)S(1)}, bf16[3,3,128,128]{3,2,1,0:T(8,128)(2,1)}, u32[]{:S(2)}) copy-start(bf16[3,3,128,128]{3,2,1,0:T(8,128)(2,1)} %param.8) | copy-start | bytes 884740
  42.1 1.0 %copy-start.6 = (pred[8,9]{0,1:T(8,128)(4,1)S(1)}, pred[8,9]{0,1:T(8,128)(4,1)}, u32[]{:S(2)}) copy-start(pred[8,9]{0,1:T(8,128)(4,1)} %constant.75) | copy-start | bytes 220

commit v25 on v20

--- a/solution.py
+++ b/solution.py
@@ -93,7 +93,8 @@
     if last:
         warped_ref, flow_ref = outs
         total = st[:, 0:1]
-        warped_ref[...] = acc / total
+        inverse = 1.0 / total
+        warped_ref[...] = acc * inverse
         fx = (st[:, 1:2] + st[:, 2:3]) / total
         fy = (st[:, 3:4] + st[:, 4:5]) / total
         lane = lax.broadcasted_iota(jnp.int32, flow_ref.shape, 1)

time: 44.2 us -> 44.2 us (level)
  no operation moved by 1% of the time
where the time goes in v25:
time: 44.2 us; the launch traced here: 43.8 us
  Pallas kernels  14.5 us (33%)
  starting transfers between devices  11 us (25%)
  waiting for transfers between devices  8.5 us (19%)
  local copies, waits for them, and re-layouts  6.44 us (15%)
  other arithmetic  2.03 us (5%)
  matrix products  1.13 us (3%)
    pallas_call x2, Pallas kernels, match_step(): pl.pallas_call(kernel, grid=(nq,), in_specs=in_specs, out_specs=out_specs...  14.5 us
    ppermute x2, waiting for transfers between devices, extended(): lax.ppermute(lax.slice_in_dim(block, 0, width, axis=dim), axis, backward)  6.69 us
    ppermute x2, starting transfers between devices, extended(): lax.ppermute(lax.slice_in_dim(block, block.shape[dim] - width, None, axis...  5.76 us
    ppermute x2, starting transfers between devices, extended(): lax.ppermute(lax.slice_in_dim(block, 0, width, axis=dim), axis, backward)  2.57 us
    ppermute x1, starting transfers between devices, match(): shards.append((lax.ppermute(targets, 'match', sibling), me ^ 1, None))  2.42 us
    unnamed x21, local copies, waits for them, and re-layouts  2.39 us
    ppermute x1, waiting for transfers between devices, match(): pending = lax.ppermute(key, 'match', forward)  1.59 us
    slice x1, local copies, waits for them, and re-layouts, match(): return (warped[:count], flow[:count, 0], flow[:count, 1])  1.42 us
  transfers between devices with their start and end apart: 7, of which 4 were waited for; matrix products, arithmetic and copies ran while one was open for 4% of the time, Pallas kernels for 18%

profile of v25, /device:TPU:0, one launch (start us, length us, event | category | flops | bytes accessed | tf_op | source)
XLA Modules:
  0.0 43.8 jit_solution(11545235549412654866)
XLA Ops:
  0.0 0.0 copy-start
  0.0 0.8 %fusion.25 = (bf16[4,2,128]{2,1,0:T(2,128)(2,1)S(1)}, bf16[4,2,128]{2,1,0:T(2,128)(2,1)S(1)}) fusion(bf16[4,64,128]{2,1,0:T(8,128)(2,1)} %param.6), kind=kLoop, calls=%fused_computation.55 | loop fusion | bytes 8192 | tf_op jit(solution)/shard_map/slice | solution.py:20
  0.8 2.3 %collective-permute-start = (bf16[4,2,128]{2,1,0:T(2,128)(2,1)S(1)}, bf16[4,2,128]{2,1,0:T(2,128)(2,1)S(1)}, u32[]{:S(2)}, u32[]{:S(2)}) collective-permute-start(bf16[4,2,128]{2,1,0:T(2,128)(2,1)S(1)} %get-tuple-element.55), channel_id=1, source_target_pairs={{0,1},{1,2},{2,3},{4,5},{5,6},{6,7},{8,9},{9,10},{10,11},{12,13},{... | collective-permute-start | bytes 6152 | tf_op jit(solution)/shard_map/ppermute | solution.py:19
  3.1 1.3 %collective-permute-start.1 = (bf16[4,2,128]{2,1,0:T(2,128)(2,1)S(1)}, bf16[4,2,128]{2,1,0:T(2,128)(2,1)S(1)}, u32[]{:S(2)}, u32[]{:S(2)}) collective-permute-start(bf16[4,2,128]{2,1,0:T(2,128)(2,1)S(1)} %get-tuple-element.56), channel_id=1, source_target_pairs={{1,0},{2,1},{3,2},{5,4},{6,5},{7,6},{9,8},{10,9},{11,10},{13,12},{... | collective-permute-start | bytes 6152 | tf_op jit(solution)/shard_map/ppermute | solution.py:22
  4.5 0.7 %pad_maximum_fusion.1 = f32[3,128]{1,0:T(4,128)S(1)} fusion(f32[1,128]{1,0:T(1,128)} %bitcast.114, f32[2,128]{1,0:T(2,128)} %param.9), kind=kLoop, calls=%fused_computation.33 | loop fusion | flops 384 | bytes 3072 | tf_op jit(solution)/shard_map/concatenate | solution.py:231
  5.2 0.7 %copy-done.7 = bf16[2,3,3,128]{3,0,2,1:T(2,128)(2,1)S(1)} copy-done((bf16[2,3,3,128]{3,0,2,1:T(2,128)(2,1)S(1)}, bf16[2,3,3,128]{3,0,2,1:T(2,128)(2,1)}, u32[]{:S(2)}) %copy-start.7) | copy-done | bytes 4632
  5.9 0.0 collective-permute-done
  5.9 2.4 %collective-permute-done.1 = bf16[4,2,128]{2,1,0:T(2,128)(2,1)S(1)} collective-permute-done((bf16[4,2,128]{2,1,0:T(2,128)(2,1)S(1)}, bf16[4,2,128]{2,1,0:T(2,128)(2,1)S(1)}, u32[]{:S(2)}, u32[]{:S(2)}) %collective-permute-start.1) | collective-permute-done | bytes 2080 | tf_op jit(solution)/shard_map/ppermute | solution.py:22
  8.4 2.4 %collective-permute-start.5 = (bf16[2048,128]{1,0:T(8,128)(2,1)}, bf16[2048,128]{1,0:T(8,128)(2,1)S(1)}, u32[]{:S(2)}, u32[]{:S(2)}) collective-permute-start(bf16[2048,128]{1,0:T(8,128)(2,1)} %refs_1_), channel_id=1, source_target_pairs={{0,1},{1,0},{2,3},{3,2},{4,5},{5,4},{6,7},{7,6},{8,9},{9,8},{10,11... | collective-permute-start | bytes 1572872 | tf_op jit(solution)/shard_map/ppermute | solution.py:177
  10.8 0.2 collective-permute-start.4
  11.0 3.4 %collective-permute-start.2 = (bf16[136,128]{1,0:T(8,128)(2,1)S(1)}, bf16[136,128]{1,0:T(8,128)(2,1)S(1)}, u32[]{:S(2)}, u32[]{:S(2)}) collective-permute-start(bf16[136,128]{1,0:T(8,128)(2,1)S(1)} %get-tuple-element.54), channel_id=1, source_target_pairs={{0,4},{4,8},{8,12},{12,16},{16,20},{20,24},{24,28},{1,5},{5,9},{9,... | collective-permute-start | bytes 104456 | tf_op jit(solution)/shard_map/ppermute | solution.py:19
  14.4 0.1 fusion.19
  14.5 1.3 %collective-permute-start.3 = (bf16[136,128]{1,0:T(8,128)(2,1)S(1)}, bf16[136,128]{1,0:T(8,128)(2,1)S(1)}, u32[]{:S(2)}, u32[]{:S(2)}) collective-permute-start(bf16[136,128]{1,0:T(8,128)(2,1)S(1)} %get-tuple-element.53), channel_id=1, source_target_pairs={{4,0},{8,4},{12,8},{16,12},{20,16},{24,20},{28,24},{5,1},{9,5},{13... | collective-permute-start | bytes 104456 | tf_op jit(solution)/shard_map/ppermute | solution.py:22
  15.8 0.2 collective-permute-done.2
  16.0 4.3 %collective-permute-done.3 = bf16[136,128]{1,0:T(8,128)(2,1)S(1)} collective-permute-done((bf16[136,128]{1,0:T(8,128)(2,1)S(1)}, bf16[136,128]{1,0:T(8,128)(2,1)S(1)}, u32[]{:S(2)}, u32[]{:S(2)}) %collective-permute-start.3) | collective-permute-done | bytes 34848 | tf_op jit(solution)/shard_map/ppermute | solution.py:22
  20.3 0.0 collective-permute-done.5.refs_2_
  20.4 0.7 %broadcast_in_dim.25.refs_3_ = f32[8,128]{1,0:T(8,128)} broadcast(f32[128]{0:T(128)S(1)} %pad.4), dimensions={1} | broadcast | bytes 4608 | tf_op jit(solution)/shard_map/broadcast_in_dim | solution.py:192
  21.0 0.0 copy-done.1
  21.0 0.2 copy-done.2
  21.2 8.1 %shard_map.64 = (f32[544,8]{1,0:T(8,128)}, f32[544,128]{1,0:T(8,128)}, f32[544,8]{1,0:T(8,128)}) custom-call(bf16[544,128]{1,0:T(8,128)(2,1)} %copy-done.1, bf16[2048,128]{1,0:T(8,128)(2,1)} %refs_1_, bf16[2048,128]{1,0:T(8,128)(2,1)} %copy-done.2, f32[8,128]{1,0:T(8,128)} %broadcast_in_dim.25.refs_3_), custom_call_target="tpu_custom_call" | custom-call | tf_op jit(solution)/shard_map/pallas_call | solution.py:152
  29.3 0.0 collective-permute-done.4.refs_1_
  29.3 0.0 collective-permute-start.6
  29.3 0.1 broadcast_and_fusion
  29.4 0.1 slice.131
  29.4 0.1 copy.25
  29.6 1.6 %collective-permute-done.6.refs_2_ = bf16[2048,128]{1,0:T(8,128)(2,1)S(1)} collective-permute-done((bf16[2048,128]{1,0:T(8,128)(2,1)S(1)}, bf16[2048,128]{1,0:T(8,128)(2,1)S(1)}, u32[]{:S(2)}, u32[]{:S(2)}) %collective-permute-start.6) | collective-permute-done | bytes 524320 | tf_op jit(solution)/shard_map/ppermute | solution.py:207
  31.2 0.8 %copy-done.4 = bf16[2048,128]{1,0:T(8,128)(2,1)} copy-done((bf16[2048,128]{1,0:T(8,128)(2,1)}, bf16[2048,128]{1,0:T(8,128)(2,1)S(1)}, u32[]{:S(2)}) %copy-start.4) | copy-done | bytes 524312
  32.0 6.4 %shard_map.65 = (f32[544,128]{1,0:T(8,128)}, f32[544,8]{1,0:T(8,128)}) custom-call(bf16[544,128]{1,0:T(8,128)(2,1)} %copy-done.1, bf16[2048,128]{1,0:T(8,128)(2,1)} %copy-done.3, bf16[2048,128]{1,0:T(8,128)(2,1)} %copy-done.4, f32[8,128]{1,0:T(8,128)} %broadcast_in_dim.25.refs_3_, f32[544,8]{1,0:T(8,128)} %get-tuple-element.25.refs_4_, ...), custom_call_target="tpu_custom_call" | custom-call | tf_op jit(solution)/shard_map/pallas_call | solution.py:152
  38.4 1.4 %slice_reduce_fusion.1 = (f32[544]{0:T(1024)S(1)}, f32[544]{0:T(1024)S(1)}) fusion(f32[544,8]{1,0:T(8,128)} %get-tuple-element.28), kind=kLoop, calls=%fused_computation.8 | loop fusion | bytes 8704 | tf_op jit(solution)/shard_map/slice | solution.py:220
  39.8 0.1 reshape_squeeze.6
  39.9 0.1 slice.132
  40.0 0.1 reshape_squeeze.7
  40.0 0.1 broadcast_subtract_fusion
  40.1 0.1 slice.134
  40.2 0.1 slice_bitcast_fusion.1
  40.3 0.1 select_bitcast_fusion
  40.4 0.1 copy.67
  40.5 0.1 copy.28
  40.6 0.0 copy-start.8
  40.6 0.6 %copy-done.8 = pred[8,9]{0,1:T(8,128)(4,1)S(1)} copy-done((pred[8,9]{0,1:T(8,128)(4,1)S(1)}, pred[8,9]{0,1:T(8,128)(4,1)}, u32[]{:S(2)}) %copy-start.8) | copy-done | bytes 96
  41.3 0.9 %convolution_select_fusion = f32[6,8,9,128]{3,1,2,0:T(8,128)S(1)} fusion(bf16[3,3,128,128]{3,2,1,0:T(8,128)(2,1)S(1)} %copy-done, f32[8,1,7,2,128]{4,2,3,0,1:T(8,128)S(1)} %slice.157, f32[8,1,8,9,128]{4,2,3,0,1:T(8,128)S(1)} %copy.28, pred[8,9]{0,1:T(8,128)(4,1)S(1)} %copy-done.8), kind=kOutput, calls=%fused_computation | convolution fusion | flops 764737536 | bytes 868424 | tf_op jit(solution)/shard_map/conv_general_dilated | solution.py:249
  42.2 0.1 copy.29
  42.3 0.1 copy.30
  42.4 0.1 copy.31
  42.5 0.3 broadcast_select_fusion
  42.8 0.2 fusion.9
  43.0 0.1 fusion.23
  43.2 0.6 %maximum_add_fusion = f32[2,4,64]{2,1,0:T(4,128)} fusion(f32[1,4,64]{2,1,0:T(4,128)S(1)} %get-tuple-element.60, f32[1,4,64]{2,1,0:T(4,128)S(1)} %get-tuple-element.61, f32[1,4,64]{2,1,0:T(4,128)S(1)} %bitcast.110, f32[1,4,64]{2,1,0:T(4,128)S(1)} %bitcast.111, f32[1,4,64]{2,1,0:T(4,128)S(1)} %bitcast.108, f32[1,4,64]{2,1,0:T(4,128)S(1)} %bitcast.109, ...), kind=kLoop, calls=%fused_computation.24 | loop fusion | flops 9728 | bytes 22528 | tf_op jit(solution)/shard_map/add | solution.py:268
  (29 shorter events, 0.2 us)
Async XLA Ops:
  0.0 40.6 %copy-start = (bf16[3,3,128,128]{3,2,1,0:T(8,128)(2,1)S(1)}, bf16[3,3,128,128]{3,2,1,0:T(8,128)(2,1)}, u32[]{:S(2)}) copy-start(bf16[3,3,128,128]{3,2,1,0:T(8,128)(2,1)} %param.8) | copy-start | bytes 884740
  0.0 8.3 %copy-start.6 = (bf16[4,64,128]{2,1,0:T(8,128)(2,1)S(1)}, bf16[4,64,128]{2,1,0:T(8,128)(2,1)}, u32[]{:S(2)}) copy-start(bf16[4,64,128]{2,1,0:T(8,128)(2,1)} %param.6) | copy-start | bytes 196612
  0.8 5.1 %collective-permute-start = (bf16[4,2,128]{2,1,0:T(2,128)(2,1)S(1)}, bf16[4,2,128]{2,1,0:T(2,128)(2,1)S(1)}, u32[]{:S(2)}, u32[]{:S(2)}) collective-permute-start(bf16[4,2,128]{2,1,0:T(2,128)(2,1)S(1)} %get-tuple-element.55), channel_id=1, source_target_pairs={{0,1},{1,2},{2,3},{4,5},{5,6},{6,7},{8,9},{9,10},{10,11},{12,13},{... | collective-permute-start | bytes 6152 | tf_op jit(solution)/shard_map/ppermute | solution.py:19
  3.1 5.2 %collective-permute-start.1 = (bf16[4,2,128]{2,1,0:T(2,128)(2,1)S(1)}, bf16[4,2,128]{2,1,0:T(2,128)(2,1)S(1)}, u32[]{:S(2)}, u32[]{:S(2)}) collective-permute-start(bf16[4,2,128]{2,1,0:T(2,128)(2,1)S(1)} %get-tuple-element.56), channel_id=1, source_target_pairs={{1,0},{2,1},{3,2},{5,4},{6,5},{7,6},{9,8},{10,9},{11,10},{13,12},{... | collective-permute-start | bytes 6152 | tf_op jit(solution)/shard_map/ppermute | solution.py:22
  5.2 0.7 %copy-start.7 = (bf16[2,3,3,128]{3,0,2,1:T(2,128)(2,1)S(1)}, bf16[2,3,3,128]{3,0,2,1:T(2,128)(2,1)}, u32[]{:S(2)}) copy-start(bf16[2,3,3,128]{3,0,2,1:T(2,128)(2,1)} %param.11) | copy-start | bytes 13828
  8.4 12.0 %collective-permute-start.5 = (bf16[2048,128]{1,0:T(8,128)(2,1)}, bf16[2048,128]{1,0:T(8,128)(2,1)S(1)}, u32[]{:S(2)}, u32[]{:S(2)}) collective-permute-start(bf16[2048,128]{1,0:T(8,128)(2,1)} %refs_1_), channel_id=1, source_target_pairs={{0,1},{1,0},{2,3},{3,2},{4,5},{5,4},{6,7},{7,6},{8,9},{9,8},{10,11... | collective-permute-start | bytes 1572872 | tf_op jit(solution)/shard_map/ppermute | solution.py:177
  10.8 18.5 %collective-permute-start.4 = (bf16[2048,128]{1,0:T(8,128)(2,1)}, bf16[2048,128]{1,0:T(8,128)(2,1)S(1)}, u32[]{:S(2)}, u32[]{:S(2)}) collective-permute-start(bf16[2048,128]{1,0:T(8,128)(2,1)} %refs_1_), channel_id=1, source_target_pairs={{0,2},{1,3},{2,0},{3,1},{4,6},{5,7},{6,4},{7,5},{8,10},{9,11},{10,... | collective-permute-start | bytes 1572872 | tf_op jit(solution)/shard_map/ppermute | solution.py:180
  11.0 5.0 %collective-permute-start.2 = (bf16[136,128]{1,0:T(8,128)(2,1)S(1)}, bf16[136,128]{1,0:T(8,128)(2,1)S(1)}, u32[]{:S(2)}, u32[]{:S(2)}) collective-permute-start(bf16[136,128]{1,0:T(8,128)(2,1)S(1)} %get-tuple-element.54), channel_id=1, source_target_pairs={{0,4},{4,8},{8,12},{12,16},{16,20},{20,24},{24,28},{1,5},{5,9},{9,... | collective-permute-start | bytes 104456 | tf_op jit(solution)/shard_map/ppermute | solution.py:19
  14.5 5.8 %collective-permute-start.3 = (bf16[136,128]{1,0:T(8,128)(2,1)S(1)}, bf16[136,128]{1,0:T(8,128)(2,1)S(1)}, u32[]{:S(2)}, u32[]{:S(2)}) collective-permute-start(bf16[136,128]{1,0:T(8,128)(2,1)S(1)} %get-tuple-element.53), channel_id=1, source_target_pairs={{4,0},{8,4},{12,8},{16,12},{20,16},{24,20},{28,24},{5,1},{9,5},{13... | collective-permute-start | bytes 104456 | tf_op jit(solution)/shard_map/ppermute | solution.py:22
  20.3 0.7 %copy-start.1 = (bf16[544,128]{1,0:T(8,128)(2,1)}, bf16[544,128]{1,0:T(8,128)(2,1)S(1)}, u32[]{:S(2)}) copy-start(bf16[544,128]{1,0:T(8,128)(2,1)S(1)} %constant_dynamic-update-slice_fusion.refs_0_) | copy-start | bytes 417796
  20.3 0.8 %copy-start.2 = (bf16[2048,128]{1,0:T(8,128)(2,1)}, bf16[2048,128]{1,0:T(8,128)(2,1)S(1)}, u32[]{:S(2)}) copy-start(bf16[2048,128]{1,0:T(8,128)(2,1)S(1)} %collective-permute-done.5.refs_2_) | copy-start | bytes 1572868
  29.3 1.9 %copy-start.3 = (bf16[2048,128]{1,0:T(8,128)(2,1)}, bf16[2048,128]{1,0:T(8,128)(2,1)S(1)}, u32[]{:S(2)}) copy-start(bf16[2048,128]{1,0:T(8,128)(2,1)S(1)} %collective-permute-done.4.refs_1_) | copy-start | bytes 1572868
  29.3 1.9 %collective-permute-start.6 = (bf16[2048,128]{1,0:T(8,128)(2,1)S(1)}, bf16[2048,128]{1,0:T(8,128)(2,1)S(1)}, u32[]{:S(2)}, u32[]{:S(2)}) collective-permute-start(bf16[2048,128]{1,0:T(8,128)(2,1)S(1)} %collective-permute-done.4.refs_1_), channel_id=1, source_target_pairs={{0,1},{1,0},{2,3},{3,2},{4,5},{5,4},{6,7},{7,6},{8,9},{9,8},{10,11... | collective-permute-start | bytes 1572872 | tf_op jit(solution)/shard_map/ppermute | solution.py:207
  31.2 0.8 %copy-start.4 = (bf16[2048,128]{1,0:T(8,128)(2,1)}, bf16[2048,128]{1,0:T(8,128)(2,1)S(1)}, u32[]{:S(2)}) copy-start(bf16[2048,128]{1,0:T(8,128)(2,1)S(1)} %collective-permute-done.6.refs_2_) | copy-start | bytes 1572868
  38.4 1.9 %copy-start.5 = (f32[544,128]{1,0:T(8,128)S(1)}, f32[544,128]{1,0:T(8,128)}, u32[]{:S(2)}) copy-start(f32[544,128]{1,0:T(8,128)} %get-tuple-element.29) | copy-start | bytes 835588
  40.6 0.7 %copy-start.8 = (pred[8,9]{0,1:T(8,128)(4,1)S(1)}, pred[8,9]{0,1:T(8,128)(4,1)}, u32[]{:S(2)}) copy-start(pred[8,9]{0,1:T(8,128)(4,1)} %constant.75) | copy-start | bytes 220
